TPU v7x, 32 devices: a whole 2x2x4 slice. The times are simulated.
32 devices in a mesh: gx: 8 (over y, x, core), gy: 4 (over z).
Axes of the slice: x: 2, y: 2, z: 4, core: 2. Of those that a mesh axis runs over, the one named last changes fastest.
Arguments:
- prior_gas_warmth: float32 [128, 128, 512], P(None, 'gx', 'gy'), may hold values from -8 to 8
- fire_power_output: float32 [128, 128, 512], P(None, 'gx', 'gy'), may hold values from -6 to 6
- measured_warmth: float32 [32768], P(('gx', 'gy')), may hold values from -8 to 8
- reading_noise_spread: float32 [32768], P(('gx', 'gy')), may hold values from 1.15 to 6
- reading_local_location: int32 [32768], P(('gx', 'gy')), may hold values from 0 to 2047
Outputs:
- temperature_analysis: float32 [128, 128, 512], P(None, 'gx', 'gy')
- heat_analysis: float32 [128, 128, 512], P(None, 'gx', 'gy')
All inputs are finite; a program needn't handle non-finite values.
Results may differ from a plain program's by a relative error of at most 0.0003.
Values sent between devices are 32-bit elements; how exact they have to be, the bound alone decides.
No kernel may reach another device: no remote copies, remote signals or barrier semaphores. Data moves between devices by JAX's collectives and lax.ppermute only.
A program may use at most 64 MiB of HBM per device.

v0:
```python
import math

import jax
import jax.numpy as jnp
from jax import lax
from jax.sharding import PartitionSpec as P

diffusion = 0.2
heating = 0.5


def with_halo(block, sides, width):
    for axis, dim in sides:
        count = lax.axis_size(axis)
        forward = [(i, i + 1) for i in range(count - 1)]
        backward = [(target, source) for source, target in forward]
        low = lax.ppermute(
            lax.slice_in_dim(block, block.shape[dim] - width, None, axis=dim), axis, forward
        )
        high = lax.ppermute(lax.slice_in_dim(block, 0, width, axis=dim), axis, backward)
        block = jnp.concatenate([low, block, high], axis=dim)
    return block


def propagate_model(padded_field, source_term):
    laplacian = (
        padded_field[:, 2:, 1:-1]
        + padded_field[:, :-2, 1:-1]
        + padded_field[:, 1:-1, 2:]
        + padded_field[:, 1:-1, :-2]
        - 4.0 * padded_field[:, 1:-1, 1:-1]
    )
    return padded_field[:, 1:-1, 1:-1] + diffusion * laplacian + heating * source_term


def shards(
    prior_gas_warmth,
    fire_power_output,
    measured_warmth,
    reading_noise_spread,
    reading_local_location,
):
    sample_number, block_height_number, block_width_number = prior_gas_warmth.shape
    devices_all = lax.axis_size(("gx", "gy"))
    predicted_vector = prior_gas_warmth
    for section in range(2):
        bordered_vector = with_halo(predicted_vector, (("gx", 1), ("gy", 2)), 1)
        predicted_vector = propagate_model(bordered_vector, fire_power_output)
    grid_points_number = block_height_number * block_width_number
    warmth_vectorised = predicted_vector.reshape(sample_number, grid_points_number)
    heat_flat = fire_power_output.reshape(sample_number, grid_points_number)
    average_gas_warmth = jnp.mean(warmth_vectorised, axis=0)
    mean_heat = jnp.mean(heat_flat, axis=0)
    sample_deviation_matrix = warmth_vectorised - average_gas_warmth
    heat_anomaly = heat_flat - mean_heat
    picked = jnp.take(sample_deviation_matrix, reading_local_location, axis=1)
    coefficient_line = 1.0 / (reading_noise_spread * math.sqrt(sample_number - 1))
    s_matrix = picked * coefficient_line
    measurement_residual = (
        measured_warmth - jnp.take(average_gas_warmth, reading_local_location)
    ) * coefficient_line
    identity = jnp.eye(sample_number, dtype=jnp.float32)
    gram_local = (
        jnp.dot(s_matrix, s_matrix.T, precision=lax.Precision.HIGHEST) + identity / devices_all
    )
    projected = jnp.dot(s_matrix, measurement_residual, precision=lax.Precision.HIGHEST)
    gram_sum, projected_sum = lax.psum((gram_local, projected), ("gx", "gy"))
    lower = jnp.linalg.cholesky(gram_sum)
    mean_weights = jax.scipy.linalg.cho_solve((lower, True), projected_sum)
    inverse_factor = jax.scipy.linalg.solve_triangular(lower, identity, lower=True, trans=1)
    combination_matrix = mean_weights[:, None] + inverse_factor
    updated_warmth = average_gas_warmth + jnp.dot(
        combination_matrix.T, sample_deviation_matrix, precision=lax.Precision.HIGHEST
    )
    heat_out = mean_heat + jnp.dot(
        combination_matrix.T, heat_anomaly, precision=lax.Precision.HIGHEST
    )
    return (
        updated_warmth.reshape(sample_number, block_height_number, block_width_number),
        heat_out.reshape(sample_number, block_height_number, block_width_number),
    )


def solution(mesh):
    placed = (
        P(None, "gx", "gy"),
        P(None, "gx", "gy"),
        P(("gx", "gy")),
        P(("gx", "gy")),
        P(("gx", "gy")),
    )
    return jax.shard_map(
        shards,
        mesh=mesh,
        in_specs=placed,
        out_specs=(P(None, "gx", "gy"), P(None, "gx", "gy")),
        check_vma=False,
    )
```

profile of v0, /device:TPU:0, one launch (start us, length us, event | category | flops | bytes accessed | tf_op | source)
XLA Modules:
  0.0 213.8 jit_solution(14382763396117944814)
XLA Ops:
  7.2 0.0 all-reduce.2.cloned.1.call-start
  7.2 1.8 copy.128
  9.1 0.0 copy-start
  9.1 0.1 fusion.37
  9.2 1.4 collective-permute-start
  10.6 3.0 %collective-permute-start.1 = (f32[128,1,128]{0,1,2:T(1,128)S(1)}, f32[128,1,128]{0,1,2:T(1,128)S(1)}, u32[]{:S(2)}, u32[]{:S(2)}) collective-permute-start(f32[128,1,128]{0,1,2:T(1,128)S(1)} %get-tuple-element.12), channel_id=1, source_target_pairs={{0,4},{4,8},{8,12},{12,16},{16,20},{20,24},{24,28},{1,5},{5,9},{9,... | collective-permute-start | bytes 196616 | tf_op jit(solution)/shard_map/ppermute | solution.py:17
  13.7 0.0 collective-permute-done
  13.7 0.9 collective-permute-done.1
  14.5 1.3 collective-permute-start.2
  15.8 5.6 %collective-permute-start.3 = (f32[128,18,1]{0,1,2:T(8,128)S(1)}, f32[128,18,1]{0,1,2:T(8,128)S(1)}, u32[]{:S(2)}, u32[]{:S(2)}) collective-permute-start(f32[128,18,1]{0,1,2:T(8,128)S(1)} %get-tuple-element.9), channel_id=1, source_target_pairs={{0,1},{1,2},{2,3},{4,5},{5,6},{6,7},{8,9},{9,10},{10,11},{12,13},{... | collective-permute-start | bytes 27656 | tf_op jit(solution)/shard_map/ppermute | solution.py:17
  21.4 0.0 copy-done
  21.4 0.7 copy.129
  22.1 0.1 reduce_sum.19
  22.2 0.0 collective-permute-done.2
  22.3 0.5 collective-permute-done.3
  22.8 0.6 fusion.14
  23.4 0.1 fusion.36
  23.5 1.3 collective-permute-start.4
  24.8 3.4 %collective-permute-start.5 = (f32[128,1,128]{0,1,2:T(1,128)S(1)}, f32[128,1,128]{0,1,2:T(1,128)S(1)}, u32[]{:S(2)}, u32[]{:S(2)}) collective-permute-start(f32[128,1,128]{0,1,2:T(1,128)S(1)} %get-tuple-element.10), channel_id=1, source_target_pairs={{0,4},{4,8},{8,12},{12,16},{16,20},{20,24},{24,28},{1,5},{5,9},{9,... | collective-permute-start | bytes 196616 | tf_op jit(solution)/shard_map/ppermute | solution.py:17
  28.2 0.0 collective-permute-done.4
  28.3 0.9 collective-permute-done.5
  29.1 0.0 copy-start.4
  29.1 1.3 collective-permute-start.6
  30.4 4.5 %collective-permute-start.7 = (f32[128,18,1]{0,1,2:T(8,128)S(1)}, f32[128,18,1]{0,1,2:T(8,128)S(1)}, u32[]{:S(2)}, u32[]{:S(2)}) collective-permute-start(f32[128,18,1]{0,1,2:T(8,128)S(1)} %get-tuple-element.7), channel_id=1, source_target_pairs={{0,1},{1,2},{2,3},{4,5},{5,6},{6,7},{8,9},{9,10},{10,11},{12,13},{... | collective-permute-start | bytes 27656 | tf_op jit(solution)/shard_map/ppermute | solution.py:17
  35.0 0.0 copy-done.4
  35.0 0.0 collective-permute-done.6
  35.0 1.4 collective-permute-done.7
  36.4 0.7 fusion.34
  37.1 0.7 copy.131
  37.8 0.0 copy-start.1
  37.8 0.1 copy.130
  37.8 0.9 copy-done.1
  38.7 0.4 bitcast_subtract_fusion.2
  39.1 0.3 copy.132
  39.4 6.2 %gather_fusion.1 = f32[1024]{0:T(1024)S(1)} fusion(f32[2048]{0:T(1024)S(1)} %multiply_bitcast_fusion.1, s32[1024]{0:T(1024)S(1)} %fusion.30), kind=kCustom, calls=%fused_computation.1 | custom fusion | bytes 12288 | tf_op jit(solution)/shard_map/jit(_take)/gather | solution.py:60
  45.6 0.0 copy-start.5
  45.6 0.0 copy-start.6
  45.6 2.8 %gather_fusion = f32[1024,128]{1,0:T(8,128)S(1)} fusion(f32[128,2048]{0,1:T(8,128)S(1)} %copy.132, s32[1024]{0:T(1024)S(1)} %fusion.30), kind=kCustom, calls=%fused_computation | custom fusion | bytes 1052672 | tf_op jit(solution)/shard_map/jit(_take)/gather | solution.py:56
  48.4 0.0 copy-done.5
  48.5 0.0 copy-done.6
  48.5 0.0 copy-start.2
  48.5 2.3 %convolution_add_fusion.3 = f32[128,128]{1,0:T(8,128)} fusion(f32[1024,128]{1,0:T(8,128)S(1)} %gather_fusion, f32[1024]{0:T(1024)S(1)} %get-tuple-element.14, pred[1024]{0:T(1024)(128)(4,1)S(1)} %get-tuple-element.3), kind=kOutput, calls=%fused_computation.7 | convolution fusion | flops 201637888 | bytes 594944 | tf_op jit(solution)/shard_map/dot_general | solution.py:64
  50.8 0.0 all-reduce.2.cloned.1.call-update
  50.8 0.6 convolution_bitcast_fusion.2
  51.4 48.0 %psum.15 = f32[128]{0:T(128)S(1)} all-reduce(f32[128]{0:T(128)S(1)} %convolution_bitcast_fusion.2), channel_id=1, replica_groups=mesh['gx'=8,'gy'=4] {'gx','gy'}, use_global_device_ids=true, to_apply=%region_4.5 | all-reduce | flops 128 | bytes 1024 | tf_op jit(solution)/shard_map/psum | solution.py:67
  99.4 78.1 %all-reduce.2.cloned.1.call-done = f32[128,128]{1,0:T(8,128)} async-done(((f32[128,128]{1,0:T(8,128)}), f32[128,128]{1,0:T(8,128)}) %all-reduce.2.cloned.1.call-update) | async-done | bytes 65552 | tf_op jit(solution)/shard_map/psum | solution.py:67
  177.5 0.0 copy-start.3
  177.5 1.0 copy.133
  178.5 0.0 copy-done.3
  178.5 11.7 %cholesky.17 = f32[128,128]{1,0:T(8,128)S(1)} custom-call(f32[128,128]{1,0:T(8,128)S(1)} %fusion.29), custom_call_target="Cholesky" | custom-call | tf_op jit(solution)/shard_map/jit(cholesky)/cholesky | solution.py:68
  190.3 0.6 compare_reduce_fusion
  190.9 0.7 fusion.25
  191.6 9.8 %custom-call.13 = f32[1,128,128]{1,2,0:T(8,128)S(1)} custom-call(f32[1,128,128]{2,1,0:T(8,128)S(1)} %fusion.25), custom_call_target="InvertDiagBlocksLowerTriangular" | custom-call | tf_op jit(solution)/shard_map/jit(_cho_solve)/triangular_solve | solution.py:69
  201.4 0.2 convolution_bitcast_fusion.1
  201.6 0.2 convolution_bitcast_fusion
  201.8 0.2 convolution_add_fusion.2
  202.0 0.0 copy-done.2
  202.0 1.3 fusion
  203.3 1.3 fusion.1
  204.6 1.2 copy.137
  205.8 1.2 copy.135
  (8 shorter events, 0.1 us)
Async XLA Ops:
  7.2 170.3 %all-reduce.2.cloned.1.call-start = ((), (), s32[]{:S(2)}) async-start(), calls=%async_computation | async-start | bytes 131072 | tf_op jit(solution)/shard_map/psum | solution.py:67
  9.1 12.3 %copy-start = (f32[128,16,128]{2,1,0:T(8,128)S(1)}, f32[128,16,128]{2,1,0:T(8,128)}, u32[]{:S(2)}) copy-start(f32[128,16,128]{2,1,0:T(8,128)} %param.6) | copy-start | bytes 3145732
  9.2 4.5 %collective-permute-start = (f32[128,1,128]{0,1,2:T(1,128)S(1)}, f32[128,1,128]{0,1,2:T(1,128)S(1)}, u32[]{:S(2)}, u32[]{:S(2)}) collective-permute-start(f32[128,1,128]{0,1,2:T(1,128)S(1)} %get-tuple-element.13), channel_id=1, source_target_pairs={{4,0},{8,4},{12,8},{16,12},{20,16},{24,20},{28,24},{5,1},{9,5},{13... | collective-permute-start | bytes 196616 | tf_op jit(solution)/shard_map/ppermute | solution.py:20
  10.6 3.9 %collective-permute-start.1 = (f32[128,1,128]{0,1,2:T(1,128)S(1)}, f32[128,1,128]{0,1,2:T(1,128)S(1)}, u32[]{:S(2)}, u32[]{:S(2)}) collective-permute-start(f32[128,1,128]{0,1,2:T(1,128)S(1)} %get-tuple-element.12), channel_id=1, source_target_pairs={{0,4},{4,8},{8,12},{12,16},{16,20},{20,24},{24,28},{1,5},{5,9},{9,... | collective-permute-start | bytes 196616 | tf_op jit(solution)/shard_map/ppermute | solution.py:17
  14.5 7.7 %collective-permute-start.2 = (f32[128,18,1]{0,1,2:T(8,128)S(1)}, f32[128,18,1]{0,1,2:T(8,128)S(1)}, u32[]{:S(2)}, u32[]{:S(2)}) collective-permute-start(f32[128,18,1]{0,1,2:T(8,128)S(1)} %get-tuple-element.8), channel_id=1, source_target_pairs={{1,0},{2,1},{3,2},{5,4},{6,5},{7,6},{9,8},{10,9},{11,10},{13,12},{... | collective-permute-start | bytes 27656 | tf_op jit(solution)/shard_map/ppermute | solution.py:20
  15.8 7.0 %collective-permute-start.3 = (f32[128,18,1]{0,1,2:T(8,128)S(1)}, f32[128,18,1]{0,1,2:T(8,128)S(1)}, u32[]{:S(2)}, u32[]{:S(2)}) collective-permute-start(f32[128,18,1]{0,1,2:T(8,128)S(1)} %get-tuple-element.9), channel_id=1, source_target_pairs={{0,1},{1,2},{2,3},{4,5},{5,6},{6,7},{8,9},{9,10},{10,11},{12,13},{... | collective-permute-start | bytes 27656 | tf_op jit(solution)/shard_map/ppermute | solution.py:17
  23.5 4.8 %collective-permute-start.4 = (f32[128,1,128]{0,1,2:T(1,128)S(1)}, f32[128,1,128]{0,1,2:T(1,128)S(1)}, u32[]{:S(2)}, u32[]{:S(2)}) collective-permute-start(f32[128,1,128]{0,1,2:T(1,128)S(1)} %get-tuple-element.11), channel_id=1, source_target_pairs={{4,0},{8,4},{12,8},{16,12},{20,16},{24,20},{28,24},{5,1},{9,5},{13... | collective-permute-start | bytes 196616 | tf_op jit(solution)/shard_map/ppermute | solution.py:20
  24.8 4.3 %collective-permute-start.5 = (f32[128,1,128]{0,1,2:T(1,128)S(1)}, f32[128,1,128]{0,1,2:T(1,128)S(1)}, u32[]{:S(2)}, u32[]{:S(2)}) collective-permute-start(f32[128,1,128]{0,1,2:T(1,128)S(1)} %get-tuple-element.10), channel_id=1, source_target_pairs={{0,4},{4,8},{8,12},{12,16},{16,20},{20,24},{24,28},{1,5},{5,9},{9,... | collective-permute-start | bytes 196616 | tf_op jit(solution)/shard_map/ppermute | solution.py:17
  29.1 5.9 %copy-start.4 = (s32[1024]{0:T(1024)S(1)}, s32[1024]{0:T(1024)}, u32[]{:S(2)}) copy-start(s32[1024]{0:T(1024)} %param.9) | copy-start | bytes 12292
  29.1 5.9 %collective-permute-start.6 = (f32[128,18,1]{0,1,2:T(8,128)S(1)}, f32[128,18,1]{0,1,2:T(8,128)S(1)}, u32[]{:S(2)}, u32[]{:S(2)}) collective-permute-start(f32[128,18,1]{0,1,2:T(8,128)S(1)} %get-tuple-element.6), channel_id=1, source_target_pairs={{1,0},{2,1},{3,2},{5,4},{6,5},{7,6},{9,8},{10,9},{11,10},{13,12},{... | collective-permute-start | bytes 27656 | tf_op jit(solution)/shard_map/ppermute | solution.py:20
  30.4 5.9 %collective-permute-start.7 = (f32[128,18,1]{0,1,2:T(8,128)S(1)}, f32[128,18,1]{0,1,2:T(8,128)S(1)}, u32[]{:S(2)}, u32[]{:S(2)}) collective-permute-start(f32[128,18,1]{0,1,2:T(8,128)S(1)} %get-tuple-element.7), channel_id=1, source_target_pairs={{0,1},{1,2},{2,3},{4,5},{5,6},{6,7},{8,9},{9,10},{10,11},{12,13},{... | collective-permute-start | bytes 27656 | tf_op jit(solution)/shard_map/ppermute | solution.py:17
  37.8 1.0 copy-start.1
  45.6 2.8 %copy-start.5 = (f32[1024]{0:T(1024)S(1)}, f32[1024]{0:T(1024)}, u32[]{:S(2)}) copy-start(f32[1024]{0:T(1024)} %param.7) | copy-start | bytes 12292
  45.6 2.8 %copy-start.6 = (f32[1024]{0:T(1024)S(1)}, f32[1024]{0:T(1024)}, u32[]{:S(2)}) copy-start(f32[1024]{0:T(1024)} %param.8) | copy-start | bytes 12292
  48.5 153.5 %copy-start.2 = (f32[128,16,128]{2,1,0:T(8,128)S(1)}, f32[128,16,128]{2,1,0:T(8,128)}, u32[]{:S(2)}) copy-start(f32[128,16,128]{2,1,0:T(8,128)} %copy-done.1) | copy-start | bytes 3145732
  177.5 1.0 copy-start.3
Sparse Core Ops, SparseCore 0:
  50.9 126.5 all-reduce.1
where the time goes:
time: 215 us; the launch traced here: 214 us
  waiting for transfers between devices  81.7 us (38%)
  blocking collectives  48 us (22%)
  other arithmetic  24.7 us (11%)
  starting transfers between devices  21.9 us (10%)
  local copies, waits for them, and re-layouts  17 us (8%)
  between operations  14.4 us (7%)
  matrix products  6.05 us (3%)
    psum x1, waiting for transfers between devices, shards(): gram_sum, projected_sum = lax.psum((gram_local, projected), ('gx', 'gy'))  78.1 us
    psum x1, blocking collectives, shards(): gram_sum, projected_sum = lax.psum((gram_local, projected), ('gx', 'gy'))  48 us
    ppermute x4, starting transfers between devices, with_halo(): lax.ppermute(lax.slice_in_dim(block, block.shape[dim] - width, None, axis...  16.6 us
    another operation x3, other arithmetic, shards(): lower = jnp.linalg.cholesky(gram_sum)  12.4 us
    another operation x2, other arithmetic, shards(): mean_weights = jax.scipy.linalg.cho_solve((lower, True), projected_sum)  10.5 us
    gather x1, local copies, waits for them, and re-layouts, shards(): jnp.take(average_gas_warmth, reading_local_location)  6.15 us
    unnamed x18, local copies, waits for them, and re-layouts  5.79 us
    ppermute x4, starting transfers between devices, with_halo(): lax.ppermute(lax.slice_in_dim(block, 0, width, axis=dim), axis, backward)  5.29 us
  transfers between devices with their start and end apart: 9, of which 5 were waited for; matrix products, arithmetic and copies ran while one was open for 1% of the time, Pallas kernels for 0%

commit v1 on v0

--- a/solution.py
+++ b/solution.py
@@ -22,6 +22,20 @@
     return block
 
 
+def butterfly_sum(value, axes):
+    for axis in axes:
+        count = lax.axis_size(axis)
+        if count & (count - 1):
+            value = lax.psum(value, axis)
+            continue
+        stride = 1
+        while stride < count:
+            pairs = [(i, i ^ stride) for i in range(count)]
+            value = value + lax.ppermute(value, axis, pairs)
+            stride *= 2
+    return value
+
+
 def propagate_model(padded_field, source_term):
     laplacian = (
         padded_field[:, 2:, 1:-1]
@@ -41,7 +55,6 @@
     reading_local_location,
 ):
     sample_number, block_height_number, block_width_number = prior_gas_warmth.shape
-    devices_all = lax.axis_size(("gx", "gy"))
     predicted_vector = prior_gas_warmth
     for section in range(2):
         bordered_vector = with_halo(predicted_vector, (("gx", 1), ("gy", 2)), 1)
@@ -60,11 +73,13 @@
         measured_warmth - jnp.take(average_gas_warmth, reading_local_location)
     ) * coefficient_line
     identity = jnp.eye(sample_number, dtype=jnp.float32)
-    gram_local = (
-        jnp.dot(s_matrix, s_matrix.T, precision=lax.Precision.HIGHEST) + identity / devices_all
+    gram_local = jnp.dot(s_matrix, s_matrix.T, precision=lax.Precision.HIGHEST)
+    projected = jnp.dot(s_matrix, measurement_residual, precision=lax.Precision.HIGHEST)
+    stacked = butterfly_sum(
+        jnp.concatenate([gram_local, projected[None, :]], axis=0), ("gx", "gy")
     )
-    projected = jnp.dot(s_matrix, measurement_residual, precision=lax.Precision.HIGHEST)
-    gram_sum, projected_sum = lax.psum((gram_local, projected), ("gx", "gy"))
+    gram_sum = stacked[:sample_number] + identity
+    projected_sum = stacked[sample_number]
     lower = jnp.linalg.cholesky(gram_sum)
     mean_weights = jax.scipy.linalg.cho_solve((lower, True), projected_sum)
     inverse_factor = jax.scipy.linalg.solve_triangular(lower, identity, lower=True, trans=1)

time: 215 us -> 104 us (0.48)
  waiting for transfers between devices: 81.7 us -> 14.7 us
  blocking collectives: 48 us -> 0 us
  starting transfers between devices: 21.9 us -> 39.7 us
  between operations: 14.4 us -> 0.99 us
    psum x1 -> x0, waiting for transfers between devices: 78.1 us -> none  [shards(): gram_sum, projected_sum = lax.psum((gram_local, projected), ('gx', 'gy'))]
    psum x1 -> x0, blocking collectives: 48 us -> none  [shards(): gram_sum, projected_sum = lax.psum((gram_local, projected), ('gx', 'gy'))]
    ppermute x0 -> x5, starting transfers between devices: none -> 17.9 us  [butterfly_sum(): value = value + lax.ppermute(value, axis, pairs)]
    ppermute x0 -> x5, waiting for transfers between devices: none -> 10.9 us  [butterfly_sum(): value = value + lax.ppermute(value, axis, pairs)]
    unnamed x18 -> x16, local copies, waits for them, and re-layouts: 5.79 us -> 5.78 us
  transfers between devices with their start and end apart: 9 -> 13, of which waited for: 5 -> 9; matrix products, arithmetic and copies ran while one was open for 1% -> 1% of each run, Pallas kernels for 0% -> 0%
where the time goes in v1:
time: 104 us
  starting transfers between devices  39.7 us (38%)
  other arithmetic  25.8 us (25%)
  local copies, waits for them, and re-layouts  17.5 us (17%)
  waiting for transfers between devices  14.7 us (14%)
  matrix products  5.42 us (5%)
    ppermute x5, starting transfers between devices, butterfly_sum(): value = value + lax.ppermute(value, axis, pairs)  17.9 us
    ppermute x4, starting transfers between devices, with_halo(): lax.ppermute(lax.slice_in_dim(block, block.shape[dim] - width, None, axis...  16.5 us
    another operation x3, other arithmetic, shards(): lower = jnp.linalg.cholesky(gram_sum)  12.4 us
    ppermute x5, waiting for transfers between devices, butterfly_sum(): value = value + lax.ppermute(value, axis, pairs)  10.9 us
    another operation x2, other arithmetic, shards(): mean_weights = jax.scipy.linalg.cho_solve((lower, True), projected_sum)  10.5 us
    gather x1, local copies, waits for them, and re-layouts, shards(): jnp.take(average_gas_warmth, reading_local_location)  6.15 us
    unnamed x16, local copies, waits for them, and re-layouts  5.78 us
    ppermute x4, starting transfers between devices, with_halo(): lax.ppermute(lax.slice_in_dim(block, 0, width, axis=dim), axis, backward)  5.29 us
  transfers between devices with their start and end apart: 13, of which 9 were waited for; matrix products, arithmetic and copies ran while one was open for 1% of the time, Pallas kernels for 0%

profile of v1, /device:TPU:0, one launch (start us, length us, event | category | flops | bytes accessed | tf_op | source)
XLA Modules:
  0.0 104.0 jit_solution(10158028881385614367)
XLA Ops:
  0.6 1.8 %copy.128 = f32[128,16,128]{0,1,2:T(8,128)S(1)} copy(f32[128,16,128]{2,1,0:T(8,128)} %param.5) | data formatting | bytes 2097152 | tf_op args[0]
  2.5 0.0 copy-start
  2.5 0.1 fusion.39
  2.6 1.4 %collective-permute-start = (f32[128,1,128]{0,1,2:T(1,128)S(1)}, f32[128,1,128]{0,1,2:T(1,128)S(1)}, u32[]{:S(2)}, u32[]{:S(2)}) collective-permute-start(f32[128,1,128]{0,1,2:T(1,128)S(1)} %get-tuple-element.13), channel_id=1, source_target_pairs={{4,0},{8,4},{12,8},{16,12},{20,16},{24,20},{28,24},{5,1},{9,5},{13... | collective-permute-start | bytes 196616 | tf_op jit(solution)/shard_map/ppermute | solution.py:20
  4.0 3.0 %collective-permute-start.1 = (f32[128,1,128]{0,1,2:T(1,128)S(1)}, f32[128,1,128]{0,1,2:T(1,128)S(1)}, u32[]{:S(2)}, u32[]{:S(2)}) collective-permute-start(f32[128,1,128]{0,1,2:T(1,128)S(1)} %get-tuple-element.12), channel_id=1, source_target_pairs={{0,4},{4,8},{8,12},{12,16},{16,20},{20,24},{24,28},{1,5},{5,9},{9,... | collective-permute-start | bytes 196616 | tf_op jit(solution)/shard_map/ppermute | solution.py:17
  7.1 0.0 collective-permute-done
  7.1 0.9 collective-permute-done.1
  8.0 1.3 %collective-permute-start.2 = (f32[128,18,1]{0,1,2:T(8,128)S(1)}, f32[128,18,1]{0,1,2:T(8,128)S(1)}, u32[]{:S(2)}, u32[]{:S(2)}) collective-permute-start(f32[128,18,1]{0,1,2:T(8,128)S(1)} %get-tuple-element.8), channel_id=1, source_target_pairs={{1,0},{2,1},{3,2},{5,4},{6,5},{7,6},{9,8},{10,9},{11,10},{13,12},{... | collective-permute-start | bytes 27656 | tf_op jit(solution)/shard_map/ppermute | solution.py:20
  9.2 5.6 %collective-permute-start.3 = (f32[128,18,1]{0,1,2:T(8,128)S(1)}, f32[128,18,1]{0,1,2:T(8,128)S(1)}, u32[]{:S(2)}, u32[]{:S(2)}) collective-permute-start(f32[128,18,1]{0,1,2:T(8,128)S(1)} %get-tuple-element.9), channel_id=1, source_target_pairs={{0,1},{1,2},{2,3},{4,5},{5,6},{6,7},{8,9},{9,10},{10,11},{12,13},{... | collective-permute-start | bytes 27656 | tf_op jit(solution)/shard_map/ppermute | solution.py:17
  14.8 0.0 copy-done
  14.8 0.7 copy.129
  15.5 0.0 collective-permute-done.2
  15.5 0.7 collective-permute-done.3
  16.2 0.6 fusion.14
  16.8 0.1 fusion.38
  16.9 1.3 %collective-permute-start.4 = (f32[128,1,128]{0,1,2:T(1,128)S(1)}, f32[128,1,128]{0,1,2:T(1,128)S(1)}, u32[]{:S(2)}, u32[]{:S(2)}) collective-permute-start(f32[128,1,128]{0,1,2:T(1,128)S(1)} %get-tuple-element.11), channel_id=1, source_target_pairs={{4,0},{8,4},{12,8},{16,12},{20,16},{24,20},{28,24},{5,1},{9,5},{13... | collective-permute-start | bytes 196616 | tf_op jit(solution)/shard_map/ppermute | solution.py:20
  18.2 3.4 %collective-permute-start.5 = (f32[128,1,128]{0,1,2:T(1,128)S(1)}, f32[128,1,128]{0,1,2:T(1,128)S(1)}, u32[]{:S(2)}, u32[]{:S(2)}) collective-permute-start(f32[128,1,128]{0,1,2:T(1,128)S(1)} %get-tuple-element.10), channel_id=1, source_target_pairs={{0,4},{4,8},{8,12},{12,16},{16,20},{20,24},{24,28},{1,5},{5,9},{9,... | collective-permute-start | bytes 196616 | tf_op jit(solution)/shard_map/ppermute | solution.py:17
  21.6 0.0 collective-permute-done.4
  21.6 0.9 collective-permute-done.5
  22.5 1.3 %collective-permute-start.6 = (f32[128,18,1]{0,1,2:T(8,128)S(1)}, f32[128,18,1]{0,1,2:T(8,128)S(1)}, u32[]{:S(2)}, u32[]{:S(2)}) collective-permute-start(f32[128,18,1]{0,1,2:T(8,128)S(1)} %get-tuple-element.6), channel_id=1, source_target_pairs={{1,0},{2,1},{3,2},{5,4},{6,5},{7,6},{9,8},{10,9},{11,10},{13,12},{... | collective-permute-start | bytes 27656 | tf_op jit(solution)/shard_map/ppermute | solution.py:20
  23.8 4.5 %collective-permute-start.7 = (f32[128,18,1]{0,1,2:T(8,128)S(1)}, f32[128,18,1]{0,1,2:T(8,128)S(1)}, u32[]{:S(2)}, u32[]{:S(2)}) collective-permute-start(f32[128,18,1]{0,1,2:T(8,128)S(1)} %get-tuple-element.7), channel_id=1, source_target_pairs={{0,1},{1,2},{2,3},{4,5},{5,6},{6,7},{8,9},{9,10},{10,11},{12,13},{... | collective-permute-start | bytes 27656 | tf_op jit(solution)/shard_map/ppermute | solution.py:17
  28.3 0.0 copy-done.3
  28.4 0.0 collective-permute-done.6
  28.4 1.4 %collective-permute-done.7 = f32[128,18,1]{0,1,2:T(8,128)S(1)} collective-permute-done((f32[128,18,1]{0,1,2:T(8,128)S(1)}, f32[128,18,1]{0,1,2:T(8,128)S(1)}, u32[]{:S(2)}, u32[]{:S(2)}) %collective-permute-start.7) | collective-permute-done | bytes 9248 | tf_op jit(solution)/shard_map/ppermute | solution.py:17
  29.7 0.7 fusion.36
  30.4 0.7 copy.131
  31.1 0.0 copy-start.1
  31.1 0.1 copy.130
  31.2 0.9 copy-done.1
  32.1 1.3 %bitcast_subtract_fusion.2 = f32[128,2048]{1,0:T(8,128)} fusion(f32[16,8,16,128]{3,2,1,0:T(8,128)S(1)} %bitcast.50, f32[2048]{0:T(1024)S(1)} %multiply_bitcast_fusion.1), kind=kLoop, calls=%fused_computation.11 | loop fusion | flops 262144 | bytes 2105344 | tf_op jit(solution)/shard_map/sub | solution.py:67
  33.4 1.5 %copy.132 = f32[128,2048]{0,1:T(8,128)S(1)} copy(f32[128,2048]{1,0:T(8,128)} %bitcast_subtract_fusion.2) | data formatting | bytes 2097152 | tf_op jit(solution)/shard_map/sub | solution.py:67
  35.0 6.2 %gather_fusion.1 = f32[1024]{0:T(1024)S(1)} fusion(f32[2048]{0:T(1024)S(1)} %multiply_bitcast_fusion.1, s32[1024]{0:T(1024)S(1)} %fusion.32), kind=kCustom, calls=%fused_computation.1 | custom fusion | bytes 12288 | tf_op jit(solution)/shard_map/jit(_take)/gather | solution.py:73
  41.1 0.0 copy-start.4
  41.2 0.0 copy-start.5
  41.2 3.0 %gather_fusion = f32[1024,128]{1,0:T(8,128)S(1)} fusion(f32[128,2048]{0,1:T(8,128)S(1)} %copy.132, s32[1024]{0:T(1024)S(1)} %fusion.32), kind=kCustom, calls=%fused_computation | custom fusion | bytes 1052672 | tf_op jit(solution)/shard_map/jit(_take)/gather | solution.py:69
  44.2 0.0 copy-done.4
  44.2 0.0 copy-done.5
  44.2 1.6 %fusion.20 = f32[128,128]{1,0:T(8,128)S(1)} fusion(f32[1024,128]{1,0:T(8,128)S(1)} %gather_fusion, f32[1024]{0:T(1024)S(1)} %get-tuple-element.14, pred[1024]{0:T(1024)(128)(4,1)S(1)} %get-tuple-element.3), kind=kOutput, calls=%fused_computation.46 | convolution fusion | flops 201588736 | bytes 594944 | tf_op jit(solution)/shard_map/dot_general | solution.py:76
  45.8 0.6 fusion.17
  46.5 3.4 %collective-permute-start.8 = (f32[129,128]{1,0:T(8,128)S(1)}, f32[129,128]{1,0:T(8,128)S(1)}, u32[]{:S(2)}, u32[]{:S(2)}) collective-permute-start(f32[129,128]{1,0:T(8,128)S(1)} %pad_maximum_fusion.16), channel_id=1, source_target_pairs={{0,4},{4,0},{8,12},{12,8},{16,20},{20,16},{24,28},{28,24},{1,5},{5... | collective-permute-start | bytes 198152 | tf_op jit(solution)/shard_map/ppermute | solution.py:34
  49.9 0.9 collective-permute-done.8
  50.8 3.5 %collective-permute-start.9 = (f32[129,128]{1,0:T(8,128)S(1)}, f32[129,128]{1,0:T(8,128)S(1)}, u32[]{:S(2)}, u32[]{:S(2)}) collective-permute-start(f32[129,128]{1,0:T(8,128)S(1)} %fusion.35), channel_id=1, source_target_pairs={{0,8},{4,12},{8,0},{12,4},{16,24},{20,28},{24,16},{28,20},{1,9},{5... | collective-permute-start | bytes 198152 | tf_op jit(solution)/shard_map/ppermute | solution.py:34
  54.3 2.5 %collective-permute-done.9 = f32[129,128]{1,0:T(8,128)S(1)} collective-permute-done((f32[129,128]{1,0:T(8,128)S(1)}, f32[129,128]{1,0:T(8,128)S(1)}, u32[]{:S(2)}, u32[]{:S(2)}) %collective-permute-start.9) | collective-permute-done | bytes 66080 | tf_op jit(solution)/shard_map/ppermute | solution.py:34
  56.9 4.6 %collective-permute-start.10 = (f32[129,128]{1,0:T(8,128)S(1)}, f32[129,128]{1,0:T(8,128)S(1)}, u32[]{:S(2)}, u32[]{:S(2)}) collective-permute-start(f32[129,128]{1,0:T(8,128)S(1)} %add.116), channel_id=1, source_target_pairs={{0,16},{4,20},{8,24},{12,28},{16,0},{20,4},{24,8},{28,12},{1,17},{... | collective-permute-start | bytes 198152 | tf_op jit(solution)/shard_map/ppermute | solution.py:34
  61.4 2.3 %collective-permute-done.10 = f32[129,128]{1,0:T(8,128)S(1)} collective-permute-done((f32[129,128]{1,0:T(8,128)S(1)}, f32[129,128]{1,0:T(8,128)S(1)}, u32[]{:S(2)}, u32[]{:S(2)}) %collective-permute-start.10) | collective-permute-done | bytes 66080 | tf_op jit(solution)/shard_map/ppermute | solution.py:34
  63.7 0.0 copy-start.2
  63.7 2.4 %collective-permute-start.11 = (f32[129,128]{1,0:T(8,128)S(1)}, f32[129,128]{1,0:T(8,128)S(1)}, u32[]{:S(2)}, u32[]{:S(2)}) collective-permute-start(f32[129,128]{1,0:T(8,128)S(1)} %add.117), channel_id=1, source_target_pairs={{0,1},{1,0},{2,3},{3,2},{4,5},{5,4},{6,7},{7,6},{8,9},{9,8},{10,11... | collective-permute-start | bytes 198152 | tf_op jit(solution)/shard_map/ppermute | solution.py:34
  66.1 0.1 reduce_sum.19
  66.2 2.1 %collective-permute-done.11 = f32[129,128]{1,0:T(8,128)S(1)} collective-permute-done((f32[129,128]{1,0:T(8,128)S(1)}, f32[129,128]{1,0:T(8,128)S(1)}, u32[]{:S(2)}, u32[]{:S(2)}) %collective-permute-start.11) | collective-permute-done | bytes 66080 | tf_op jit(solution)/shard_map/ppermute | solution.py:34
  68.4 4.0 %collective-permute-start.12 = (f32[129,128]{1,0:T(8,128)S(1)}, f32[129,128]{1,0:T(8,128)S(1)}, u32[]{:S(2)}, u32[]{:S(2)}) collective-permute-start(f32[129,128]{1,0:T(8,128)S(1)} %add.118), channel_id=1, source_target_pairs={{0,2},{1,3},{2,0},{3,1},{4,6},{5,7},{6,4},{7,5},{8,10},{9,11},{10,... | collective-permute-start | bytes 198152 | tf_op jit(solution)/shard_map/ppermute | solution.py:34
  72.4 3.0 %collective-permute-done.12 = f32[129,128]{1,0:T(8,128)S(1)} collective-permute-done((f32[129,128]{1,0:T(8,128)S(1)}, f32[129,128]{1,0:T(8,128)S(1)}, u32[]{:S(2)}, u32[]{:S(2)}) %collective-permute-start.12) | collective-permute-done | bytes 66080 | tf_op jit(solution)/shard_map/ppermute | solution.py:34
  75.5 0.1 copy.133
  75.6 11.7 %cholesky.18 = f32[128,128]{1,0:T(8,128)S(1)} custom-call(f32[128,128]{1,0:T(8,128)S(1)} %fusion.31), custom_call_target="Cholesky" | custom-call | tf_op jit(solution)/shard_map/jit(cholesky)/cholesky | solution.py:83
  87.4 0.6 compare_reduce_fusion
  88.0 0.7 fusion.27
  88.7 9.8 %custom-call.13 = f32[1,128,128]{1,2,0:T(8,128)S(1)} custom-call(f32[1,128,128]{2,1,0:T(8,128)S(1)} %fusion.27), custom_call_target="InvertDiagBlocksLowerTriangular" | custom-call | tf_op jit(solution)/shard_map/jit(_cho_solve)/triangular_solve | solution.py:84
  98.5 0.2 convolution_bitcast_fusion.1
  98.7 0.2 convolution_bitcast_fusion
  98.8 0.2 convolution_add_fusion.2
  99.1 0.0 copy-done.2
  99.1 1.3 %fusion = f32[16,8,16,128]{3,1,2,0:T(8,128)S(1)} fusion(f32[128,128]{1,0:T(8,128)S(1)} %convolution_add_fusion.2, f32[2048]{0:T(1024)S(1)} %multiply_bitcast_fusion.1, f32[16,8,16,128]{3,2,1,0:T(8,128)S(1)} %bitcast.51), kind=kOutput, calls=%fused_computation.4 | convolution fusion | flops 403177472 | bytes 2170880 | tf_op jit(solution)/shard_map/dot_general | solution.py:87
  100.4 1.3 %fusion.1 = f32[16,8,16,128]{3,1,2,0:T(8,128)S(1)} fusion(f32[128,128]{1,0:T(8,128)S(1)} %convolution_add_fusion.2, f32[16,8,16,128]{3,2,1,0:T(8,128)S(1)} %bitcast.49, f32[2048]{0:T(1024)S(1)} %multiply_bitcast_fusion), kind=kOutput, calls=%fused_computation.5 | convolution fusion | flops 403177472 | bytes 2170880 | tf_op jit(solution)/shard_map/dot_general | solution.py:90
  101.7 1.2 %copy.137 = f32[16,8,16,128]{3,2,1,0:T(8,128)} copy(f32[16,8,16,128]{3,1,2,0:T(8,128)S(1)} %fusion.1) | data formatting | bytes 2097152
  102.9 1.2 %copy.135 = f32[16,8,16,128]{3,2,1,0:T(8,128)} copy(f32[16,8,16,128]{3,1,2,0:T(8,128)S(1)} %fusion) | data formatting | bytes 2097152
  (16 shorter events, 0.2 us)
Async XLA Ops:
  2.5 12.3 %copy-start = (f32[128,16,128]{2,1,0:T(8,128)S(1)}, f32[128,16,128]{2,1,0:T(8,128)}, u32[]{:S(2)}) copy-start(f32[128,16,128]{2,1,0:T(8,128)} %param.6) | copy-start | bytes 3145732
  2.6 4.5 %collective-permute-start = (f32[128,1,128]{0,1,2:T(1,128)S(1)}, f32[128,1,128]{0,1,2:T(1,128)S(1)}, u32[]{:S(2)}, u32[]{:S(2)}) collective-permute-start(f32[128,1,128]{0,1,2:T(1,128)S(1)} %get-tuple-element.13), channel_id=1, source_target_pairs={{4,0},{8,4},{12,8},{16,12},{20,16},{24,20},{28,24},{5,1},{9,5},{13... | collective-permute-start | bytes 196616 | tf_op jit(solution)/shard_map/ppermute | solution.py:20
  4.0 3.9 %collective-permute-start.1 = (f32[128,1,128]{0,1,2:T(1,128)S(1)}, f32[128,1,128]{0,1,2:T(1,128)S(1)}, u32[]{:S(2)}, u32[]{:S(2)}) collective-permute-start(f32[128,1,128]{0,1,2:T(1,128)S(1)} %get-tuple-element.12), channel_id=1, source_target_pairs={{0,4},{4,8},{8,12},{12,16},{16,20},{20,24},{24,28},{1,5},{5,9},{9,... | collective-permute-start | bytes 196616 | tf_op jit(solution)/shard_map/ppermute | solution.py:17
  8.0 7.6 %collective-permute-start.2 = (f32[128,18,1]{0,1,2:T(8,128)S(1)}, f32[128,18,1]{0,1,2:T(8,128)S(1)}, u32[]{:S(2)}, u32[]{:S(2)}) collective-permute-start(f32[128,18,1]{0,1,2:T(8,128)S(1)} %get-tuple-element.8), channel_id=1, source_target_pairs={{1,0},{2,1},{3,2},{5,4},{6,5},{7,6},{9,8},{10,9},{11,10},{13,12},{... | collective-permute-start | bytes 27656 | tf_op jit(solution)/shard_map/ppermute | solution.py:20
  9.2 7.0 %collective-permute-start.3 = (f32[128,18,1]{0,1,2:T(8,128)S(1)}, f32[128,18,1]{0,1,2:T(8,128)S(1)}, u32[]{:S(2)}, u32[]{:S(2)}) collective-permute-start(f32[128,18,1]{0,1,2:T(8,128)S(1)} %get-tuple-element.9), channel_id=1, source_target_pairs={{0,1},{1,2},{2,3},{4,5},{5,6},{6,7},{8,9},{9,10},{10,11},{12,13},{... | collective-permute-start | bytes 27656 | tf_op jit(solution)/shard_map/ppermute | solution.py:17
  16.9 4.7 %collective-permute-start.4 = (f32[128,1,128]{0,1,2:T(1,128)S(1)}, f32[128,1,128]{0,1,2:T(1,128)S(1)}, u32[]{:S(2)}, u32[]{:S(2)}) collective-permute-start(f32[128,1,128]{0,1,2:T(1,128)S(1)} %get-tuple-element.11), channel_id=1, source_target_pairs={{4,0},{8,4},{12,8},{16,12},{20,16},{24,20},{28,24},{5,1},{9,5},{13... | collective-permute-start | bytes 196616 | tf_op jit(solution)/shard_map/ppermute | solution.py:20
  18.2 4.3 %collective-permute-start.5 = (f32[128,1,128]{0,1,2:T(1,128)S(1)}, f32[128,1,128]{0,1,2:T(1,128)S(1)}, u32[]{:S(2)}, u32[]{:S(2)}) collective-permute-start(f32[128,1,128]{0,1,2:T(1,128)S(1)} %get-tuple-element.10), channel_id=1, source_target_pairs={{0,4},{4,8},{8,12},{12,16},{16,20},{20,24},{24,28},{1,5},{5,9},{9,... | collective-permute-start | bytes 196616 | tf_op jit(solution)/shard_map/ppermute | solution.py:17
  22.5 5.9 %copy-start.3 = (s32[1024]{0:T(1024)S(1)}, s32[1024]{0:T(1024)}, u32[]{:S(2)}) copy-start(s32[1024]{0:T(1024)} %param.9) | copy-start | bytes 12292
  22.5 5.9 %collective-permute-start.6 = (f32[128,18,1]{0,1,2:T(8,128)S(1)}, f32[128,18,1]{0,1,2:T(8,128)S(1)}, u32[]{:S(2)}, u32[]{:S(2)}) collective-permute-start(f32[128,18,1]{0,1,2:T(8,128)S(1)} %get-tuple-element.6), channel_id=1, source_target_pairs={{1,0},{2,1},{3,2},{5,4},{6,5},{7,6},{9,8},{10,9},{11,10},{13,12},{... | collective-permute-start | bytes 27656 | tf_op jit(solution)/shard_map/ppermute | solution.py:20
  23.8 5.9 %collective-permute-start.7 = (f32[128,18,1]{0,1,2:T(8,128)S(1)}, f32[128,18,1]{0,1,2:T(8,128)S(1)}, u32[]{:S(2)}, u32[]{:S(2)}) collective-permute-start(f32[128,18,1]{0,1,2:T(8,128)S(1)} %get-tuple-element.7), channel_id=1, source_target_pairs={{0,1},{1,2},{2,3},{4,5},{5,6},{6,7},{8,9},{9,10},{10,11},{12,13},{... | collective-permute-start | bytes 27656 | tf_op jit(solution)/shard_map/ppermute | solution.py:17
  31.1 1.0 copy-start.1
  41.1 3.0 %copy-start.4 = (f32[1024]{0:T(1024)S(1)}, f32[1024]{0:T(1024)}, u32[]{:S(2)}) copy-start(f32[1024]{0:T(1024)} %param.7) | copy-start | bytes 12292
  41.2 3.0 %copy-start.5 = (f32[1024]{0:T(1024)S(1)}, f32[1024]{0:T(1024)}, u32[]{:S(2)}) copy-start(f32[1024]{0:T(1024)} %param.8) | copy-start | bytes 12292
  46.5 4.3 %collective-permute-start.8 = (f32[129,128]{1,0:T(8,128)S(1)}, f32[129,128]{1,0:T(8,128)S(1)}, u32[]{:S(2)}, u32[]{:S(2)}) collective-permute-start(f32[129,128]{1,0:T(8,128)S(1)} %pad_maximum_fusion.16), channel_id=1, source_target_pairs={{0,4},{4,0},{8,12},{12,8},{16,20},{20,16},{24,28},{28,24},{1,5},{5... | collective-permute-start | bytes 198152 | tf_op jit(solution)/shard_map/ppermute | solution.py:34
  50.8 6.0 %collective-permute-start.9 = (f32[129,128]{1,0:T(8,128)S(1)}, f32[129,128]{1,0:T(8,128)S(1)}, u32[]{:S(2)}, u32[]{:S(2)}) collective-permute-start(f32[129,128]{1,0:T(8,128)S(1)} %fusion.35), channel_id=1, source_target_pairs={{0,8},{4,12},{8,0},{12,4},{16,24},{20,28},{24,16},{28,20},{1,9},{5... | collective-permute-start | bytes 198152 | tf_op jit(solution)/shard_map/ppermute | solution.py:34
  56.9 6.8 %collective-permute-start.10 = (f32[129,128]{1,0:T(8,128)S(1)}, f32[129,128]{1,0:T(8,128)S(1)}, u32[]{:S(2)}, u32[]{:S(2)}) collective-permute-start(f32[129,128]{1,0:T(8,128)S(1)} %add.116), channel_id=1, source_target_pairs={{0,16},{4,20},{8,24},{12,28},{16,0},{20,4},{24,8},{28,12},{1,17},{... | collective-permute-start | bytes 198152 | tf_op jit(solution)/shard_map/ppermute | solution.py:34
  63.7 35.4 %copy-start.2 = (f32[128,16,128]{2,1,0:T(8,128)S(1)}, f32[128,16,128]{2,1,0:T(8,128)}, u32[]{:S(2)}) copy-start(f32[128,16,128]{2,1,0:T(8,128)} %copy-done.1) | copy-start | bytes 3145732
  63.7 4.6 %collective-permute-start.11 = (f32[129,128]{1,0:T(8,128)S(1)}, f32[129,128]{1,0:T(8,128)S(1)}, u32[]{:S(2)}, u32[]{:S(2)}) collective-permute-start(f32[129,128]{1,0:T(8,128)S(1)} %add.117), channel_id=1, source_target_pairs={{0,1},{1,0},{2,3},{3,2},{4,5},{5,4},{6,7},{7,6},{8,9},{9,8},{10,11... | collective-permute-start | bytes 198152 | tf_op jit(solution)/shard_map/ppermute | solution.py:34
  68.4 7.1 %collective-permute-start.12 = (f32[129,128]{1,0:T(8,128)S(1)}, f32[129,128]{1,0:T(8,128)S(1)}, u32[]{:S(2)}, u32[]{:S(2)}) collective-permute-start(f32[129,128]{1,0:T(8,128)S(1)} %add.118), channel_id=1, source_target_pairs={{0,2},{1,3},{2,0},{3,1},{4,6},{5,7},{6,4},{7,5},{8,10},{9,11},{10,... | collective-permute-start | bytes 198152 | tf_op jit(solution)/shard_map/ppermute | solution.py:34

commit v2 on v1

--- a/solution.py
+++ b/solution.py
@@ -9,17 +9,72 @@
 heating = 0.5
 
 
-def with_halo(block, sides, width):
-    for axis, dim in sides:
-        count = lax.axis_size(axis)
-        forward = [(i, i + 1) for i in range(count - 1)]
-        backward = [(target, source) for source, target in forward]
-        low = lax.ppermute(
-            lax.slice_in_dim(block, block.shape[dim] - width, None, axis=dim), axis, forward
-        )
-        high = lax.ppermute(lax.slice_in_dim(block, 0, width, axis=dim), axis, backward)
-        block = jnp.concatenate([low, block, high], axis=dim)
-    return block
+def from_neighbour(block, axis, step):
+    count = lax.axis_size(axis)
+    if step > 0:
+        pairs = [(i, i + 1) for i in range(count - 1)]
+    else:
+        pairs = [(i + 1, i) for i in range(count - 1)]
+    return lax.ppermute(block, axis, pairs)
+
+
+def from_diagonal(block, step_x, step_y):
+    rows, cols = lax.axis_size("gx"), lax.axis_size("gy")
+    pairs = []
+    for a in range(rows):
+        for b in range(cols):
+            if 0 <= a + step_x < rows and 0 <= b + step_y < cols:
+                pairs.append((a * cols + b, (a + step_x) * cols + b + step_y))
+    return lax.ppermute(block, ("gx", "gy"), pairs)
+
+
+def forecast_two_steps(warmth, heat):
+    height, width = warmth.shape[1], warmth.shape[2]
+    top = from_neighbour(
+        jnp.concatenate([warmth[:, -2:, :], heat[:, -1:, :]], axis=1), "gx", 1
+    )
+    bottom = from_neighbour(
+        jnp.concatenate([warmth[:, :2, :], heat[:, :1, :]], axis=1), "gx", -1
+    )
+    left = from_neighbour(
+        jnp.concatenate([warmth[:, :, -2:], heat[:, :, -1:]], axis=2), "gy", 1
+    )
+    right = from_neighbour(
+        jnp.concatenate([warmth[:, :, :2], heat[:, :, :1]], axis=2), "gy", -1
+    )
+    top_left = from_diagonal(warmth[:, -2:, -2:], 1, 1)
+    top_right = from_diagonal(warmth[:, -2:, :2], 1, -1)
+    bottom_left = from_diagonal(warmth[:, :2, -2:], -1, 1)
+    bottom_right = from_diagonal(warmth[:, :2, :2], -1, -1)
+    warmth_wide = jnp.concatenate(
+        [
+            jnp.concatenate([top_left, top[:, :2], top_right], axis=2),
+            jnp.concatenate([left[:, :, :2], warmth, right[:, :, :2]], axis=2),
+            jnp.concatenate([bottom_left, bottom[:, :2], bottom_right], axis=2),
+        ],
+        axis=1,
+    )
+    corner = jnp.zeros_like(heat[:, :1, :1])
+    heat_wide = jnp.concatenate(
+        [
+            jnp.concatenate([corner, top[:, 2:], corner], axis=2),
+            jnp.concatenate([left[:, :, 2:], heat, right[:, :, 2:]], axis=2),
+            jnp.concatenate([corner, bottom[:, 2:], corner], axis=2),
+        ],
+        axis=1,
+    )
+    first = propagate_model(warmth_wide, heat_wide)
+    row = lax.broadcasted_iota(jnp.int32, (height + 2, width + 2), 0)
+    col = lax.broadcasted_iota(jnp.int32, (height + 2, width + 2), 1)
+    at_x, at_y = lax.axis_index("gx"), lax.axis_index("gy")
+    outside = (
+        ((row == 0) & (at_x == 0))
+        | ((row == height + 1) & (at_x == lax.axis_size("gx") - 1))
+        | ((col == 0) & (at_y == 0))
+        | ((col == width + 1) & (at_y == lax.axis_size("gy") - 1))
+    )
+    first = jnp.where(outside[None], 0.0, first)
+    return propagate_model(first, heat)
 
 
 def butterfly_sum(value, axes):
@@ -55,10 +110,7 @@
     reading_local_location,
 ):
     sample_number, block_height_number, block_width_number = prior_gas_warmth.shape
-    predicted_vector = prior_gas_warmth
-    for section in range(2):
-        bordered_vector = with_halo(predicted_vector, (("gx", 1), ("gy", 2)), 1)
-        predicted_vector = propagate_model(bordered_vector, fire_power_output)
+    predicted_vector = forecast_two_steps(prior_gas_warmth, fire_power_output)
     grid_points_number = block_height_number * block_width_number
     warmth_vectorised = predicted_vector.reshape(sample_number, grid_points_number)
     heat_flat = fire_power_output.reshape(sample_number, grid_points_number)

time: 104 us -> 124 us (1.19)
  local copies, waits for them, and re-layouts: 17.5 us -> 35.7 us
  starting transfers between devices: 39.7 us -> 33.2 us
  other arithmetic: 25.8 us -> 31.8 us
  matrix products: 5.42 us -> 7.41 us
    slice x2 -> x19, local copies, waits for them, and re-layouts: 0.19 us -> 11.3 us  [the longest x2 2.4 us: forecast_two_steps(): bottom[:, 2:]]
    unnamed x16 -> x30, local copies, waits for them, and re-layouts: 5.78 us -> 11.1 us
    select_n x0 -> x1, other arithmetic: none -> 3.83 us  [forecast_two_steps(): first = jnp.where(outside[None], 0.0, first)]
    ppermute x5, starting transfers between devices: 17.9 us -> 14.3 us  [butterfly_sum(): value = value + lax.ppermute(value, axis, pairs)]
    ppermute x8, starting transfers between devices: 21.8 us -> 18.9 us  [the longest x4 10.2 us: from_neighbour(): return lax.ppermute(block, axis, pairs)]
    ppermute x8, waiting for transfers between devices: 3.77 us -> 1.95 us  [the longest x4 1.94 us: from_neighbour(): return lax.ppermute(block, axis, pairs)]
    concatenate x0 -> x5, other arithmetic: none -> 1.58 us  [the longest x1 0.87 us: forecast_two_steps(): jnp.concatenate([jnp.concatenate([top_left, top[:, :2], top_right], axis=...]
    reshape x0 -> x1, local copies, waits for them, and re-layouts: none -> 1.55 us  [shards(): predicted_vector.reshape(sample_number, grid_points_number)]
  transfers between devices with their start and end apart: 13 -> 13, of which waited for: 9 -> 7; matrix products, arithmetic and copies ran while one was open for 1% -> 16% of each run, Pallas kernels for 0% -> 0%
where the time goes in v2:
time: 124 us; the launch traced here: 123 us
  local copies, waits for them, and re-layouts  35.7 us (29%)
  starting transfers between devices  33.2 us (27%)
  other arithmetic  31.8 us (26%)
  waiting for transfers between devices  13.6 us (11%)
  matrix products  7.41 us (6%)
    ppermute x5, starting transfers between devices, butterfly_sum(): value = value + lax.ppermute(value, axis, pairs)  14.3 us
    another operation x3, other arithmetic, shards(): lower = jnp.linalg.cholesky(gram_sum)  12.4 us
    ppermute x5, waiting for transfers between devices, butterfly_sum(): value = value + lax.ppermute(value, axis, pairs)  11.7 us
    unnamed x30, local copies, waits for them, and re-layouts  11.1 us
    another operation x2, other arithmetic, shards(): mean_weights = jax.scipy.linalg.cho_solve((lower, True), projected_sum)  10.5 us
    ppermute x4, starting transfers between devices, from_neighbour(): return lax.ppermute(block, axis, pairs)  10.2 us
    ppermute x4, starting transfers between devices, from_diagonal(): return lax.ppermute(block, ('gx', 'gy'), pairs)  8.69 us
    gather x1, local copies, waits for them, and re-layouts, shards(): jnp.take(average_gas_warmth, reading_local_location)  6.15 us
  transfers between devices with their start and end apart: 13, of which 7 were waited for; matrix products, arithmetic and copies ran while one was open for 16% of the time, Pallas kernels for 0%

profile of v2, /device:TPU:0, one launch (start us, length us, event | category | flops | bytes accessed | tf_op | source)
XLA Modules:
  0.0 123.0 jit_solution(15647468841808727004)
XLA Ops:
  0.6 1.7 %copy.11 = f32[128,16,128]{0,2,1:T(8,128)S(1)} copy(f32[128,16,128]{2,1,0:T(8,128)} %param.5) | data formatting | bytes 2097152 | tf_op args[0]
  2.3 0.6 fusion.36
  2.9 4.9 %collective-permute-start = (f32[128,2,2]{0,2,1:T(2,128)}, f32[128,2,2]{0,2,1:T(2,128)}, u32[]{:S(2)}, u32[]{:S(2)}) collective-permute-start(f32[128,2,2]{0,2,1:T(2,128)} %get-tuple-element.6), channel_id=1, source_target_pairs={{0,5},{1,6},{2,7},{4,9},{5,10},{6,11},{8,13},{9,14},{10,15},{12,17... | collective-permute-start | bytes 6152 | tf_op jit(solution)/shard_map/ppermute | solution.py:28
  7.9 1.2 collective-permute-start.2
  9.1 1.6 %fusion.39 = (f32[128,16,2]{2,1,0:T(8,128)}, f32[128,16,2]{2,1,0:T(8,128)}) fusion(f32[128,16,128]{2,1,0:T(8,128)S(1)} %copy-done.1), kind=kLoop, calls=%fused_computation.86 | loop fusion | bytes 65536 | tf_op jit(solution)/shard_map/slice | solution.py:40
  10.7 1.7 %copy.40 = f32[128,16,2]{0,1,2:T(8,128)S(1)} copy(f32[128,16,2]{2,1,0:T(8,128)} %get-tuple-element.14) | data formatting | bytes 32768
  12.4 1.6 %fusion.40 = (f32[128,16,1]{2,1,0:T(8,128)}, f32[128,16,1]{2,1,0:T(8,128)}) fusion(f32[128,16,128]{2,1,0:T(8,128)S(1)} %copy-done), kind=kLoop, calls=%fused_computation.87 | loop fusion | bytes 32768 | tf_op jit(solution)/shard_map/slice | solution.py:40
  14.1 1.6 %copy.41 = f32[128,16,1]{0,1,2:T(8,128)S(1)} copy(f32[128,16,1]{2,1,0:T(8,128)} %get-tuple-element.16) | data formatting | bytes 16384
  15.7 6.4 %collective-permute-start.3 = (f32[128,16,3]{0,1,2:T(8,128)S(1)}, f32[128,16,3]{0,1,2:T(8,128)S(1)}, u32[]{:S(2)}, u32[]{:S(2)}) collective-permute-start(f32[128,16,3]{0,1,2:T(8,128)S(1)} %pad_maximum_fusion.11), channel_id=1, source_target_pairs={{0,1},{1,2},{2,3},{4,5},{5,6},{6,7},{8,9},{9,10},{10,11},{12,13},{... | collective-permute-start | bytes 73736 | tf_op jit(solution)/shard_map/ppermute | solution.py:18
  22.1 1.6 %copy.42 = f32[128,16,2]{0,1,2:T(8,128)S(1)} copy(f32[128,16,2]{2,1,0:T(8,128)} %get-tuple-element.15) | data formatting | bytes 32768
  23.7 1.6 %copy.43 = f32[128,16,1]{0,1,2:T(8,128)S(1)} copy(f32[128,16,1]{2,1,0:T(8,128)} %get-tuple-element.17) | data formatting | bytes 16384
  25.4 1.3 %collective-permute-start.4 = (f32[128,16,3]{0,1,2:T(8,128)S(1)}, f32[128,16,3]{0,1,2:T(8,128)S(1)}, u32[]{:S(2)}, u32[]{:S(2)}) collective-permute-start(f32[128,16,3]{0,1,2:T(8,128)S(1)} %pad_maximum_fusion.12), channel_id=1, source_target_pairs={{1,0},{2,1},{3,2},{5,4},{6,5},{7,6},{9,8},{10,9},{11,10},{13,12},{... | collective-permute-start | bytes 73736 | tf_op jit(solution)/shard_map/ppermute | solution.py:18
  26.8 0.1 fusion.38
  26.9 1.3 %collective-permute-start.1 = (f32[128,3,128]{2,0,1:T(8,128)S(1)}, f32[128,3,128]{2,0,1:T(8,128)S(1)}, u32[]{:S(2)}, u32[]{:S(2)}) collective-permute-start(f32[128,3,128]{2,0,1:T(8,128)S(1)} %pad_maximum_fusion.8), channel_id=1, source_target_pairs={{0,4},{4,8},{8,12},{12,16},{16,20},{20,24},{24,28},{1,5},{5,9},{9,... | collective-permute-start | bytes 589832 | tf_op jit(solution)/shard_map/ppermute | solution.py:18
  28.3 0.7 pad_maximum_fusion.9
  29.0 1.3 %collective-permute-start.5 = (f32[128,2,2]{0,2,1:T(2,128)}, f32[128,2,2]{0,2,1:T(2,128)}, u32[]{:S(2)}, u32[]{:S(2)}) collective-permute-start(f32[128,2,2]{0,2,1:T(2,128)} %get-tuple-element.8), channel_id=1, source_target_pairs={{4,1},{5,2},{6,3},{8,5},{9,6},{10,7},{12,9},{13,10},{14,11},{16,13... | collective-permute-start | bytes 6152 | tf_op jit(solution)/shard_map/ppermute | solution.py:28
  30.3 0.8 collective-permute-done.4
  31.1 1.3 %collective-permute-start.7 = (f32[128,2,2]{0,2,1:T(2,128)}, f32[128,2,2]{0,2,1:T(2,128)}, u32[]{:S(2)}, u32[]{:S(2)}) collective-permute-start(f32[128,2,2]{0,2,1:T(2,128)} %get-tuple-element.7), channel_id=1, source_target_pairs={{5,0},{6,1},{7,2},{9,4},{10,5},{11,6},{13,8},{14,9},{15,10},{17,12... | collective-permute-start | bytes 6152 | tf_op jit(solution)/shard_map/ppermute | solution.py:28
  32.4 1.3 %collective-permute-start.6 = (f32[128,3,128]{2,0,1:T(8,128)}, f32[128,3,128]{2,0,1:T(8,128)}, u32[]{:S(2)}, u32[]{:S(2)}) collective-permute-start(f32[128,3,128]{2,0,1:T(8,128)} %pad_maximum_fusion.9), channel_id=1, source_target_pairs={{4,0},{8,4},{12,8},{16,12},{20,16},{24,20},{28,24},{5,1},{9,5},{13... | collective-permute-start | bytes 589832 | tf_op jit(solution)/shard_map/ppermute | solution.py:18
  33.7 0.7 or_or_fusion
  34.4 0.4 copy.30
  34.8 0.6 copy.20
  35.4 0.6 copy.22
  36.0 0.6 slice.173
  36.6 0.9 slice.161
  37.6 0.1 copy.15
  37.7 1.1 collective-permute-done.6
  38.7 0.9 slice.166
  39.7 0.1 copy.27
  39.8 0.8 slice.171
  40.7 1.5 %slice.174 = f32[128,1,128]{2,0,1:T(8,128)} slice(f32[128,3,128]{2,0,1:T(8,128)} %collective-permute-done.6), slice={[0:128], [2:3], [0:128]} | slice | bytes 131072 | tf_op jit(solution)/shard_map/slice | solution.py:62
  42.2 0.9 copy.32
  43.2 0.9 maximum_maximum_fusion
  44.1 3.8 %fusion.6 = f32[128,18,130]{0,2,1:T(8,128)S(1)} fusion(f32[128,20,132]{0,2,1:T(8,128)S(1)} %maximum_maximum_fusion, f32[128,16,2]{0,2,1:T(2,128)S(1)} %copy-done.4, f32[128,2,2]{0,2,1:T(2,128)} %collective-permute-done.2, f32[128,16,128]{0,2,1:T(8,128)S(1)} %copy.11, f32[128,16,2]{0,2,1:T(2,128)S(1)} %copy-done.3, f32[128,2,128]{0,2,1:T(8,128)S(1)} %copy.15, ...), kind=kLoop, calls=%fused_computation.12 | loop fusion | flops 8386560 | bytes 7342884 | tf_op jit(solution)/shard_map/jit(_where)/select_n | solution.py:76
  48.0 1.5 %fusion.34 = (f32[16,128]{1,0:T(8,128)S(1)}, f32[128,16,128]{0,2,1:T(8,128)}) fusion(f32[128,16,128]{0,2,1:T(8,128)S(1)} %copy.30, f32[128,18,130]{0,2,1:T(8,128)S(1)} %fusion.6), kind=kLoop, calls=%fused_computation.82 | loop fusion | flops 2619392 | bytes 7348224 | tf_op jit(solution)/shard_map/reduce_sum | solution.py:117
  49.5 1.6 %copy.37 = f32[128,2048]{1,0:T(8,128)S(1)} copy(f32[128,2048]{0,1:T(8,128)} %bitcast.51) | data formatting | bytes 2097152 | tf_op jit(solution)/shard_map/reshape | solution.py:115
  51.1 1.1 broadcast_subtract_fusion
  52.2 1.5 %copy.35 = f32[128,2048]{0,1:T(8,128)S(1)} copy(f32[128,2048]{1,0:T(8,128)} %broadcast_subtract_fusion) | data formatting | bytes 2097152 | tf_op jit(solution)/shard_map/sub | solution.py:119
  53.7 6.2 %gather_fusion.1 = f32[1024]{0:T(1024)S(1)} fusion(f32[2048]{0:T(1024)S(1)} %multiply_bitcast_fusion.1, s32[1024]{0:T(1024)S(1)} %fusion.30), kind=kCustom, calls=%fused_computation.1 | custom fusion | bytes 12288 | tf_op jit(solution)/shard_map/jit(_take)/gather | solution.py:125
  59.9 4.0 %gather_fusion = f32[1024,128]{1,0:T(8,128)} fusion(f32[128,2048]{0,1:T(8,128)S(1)} %copy.35, s32[1024]{0:T(1024)S(1)} %fusion.30), kind=kCustom, calls=%fused_computation | custom fusion | bytes 1052672 | tf_op jit(solution)/shard_map/jit(_take)/gather | solution.py:121
  64.0 2.8 %fusion.18 = f32[128,128]{1,0:T(8,128)S(1)} fusion(f32[1024,128]{1,0:T(8,128)} %gather_fusion, f32[1024]{0:T(1024)S(1)} %get-tuple-element.18, pred[1024]{0:T(1024)(128)(4,1)S(1)} %get-tuple-element.3), kind=kOutput, calls=%fused_computation.43 | convolution fusion | flops 201588736 | bytes 594944 | tf_op jit(solution)/shard_map/dot_general | solution.py:128
  66.8 1.7 %fusion.15 = f32[1,128]{1,0:T(1,128)S(1)} fusion(f32[1024,1]{0,1:T(1,128)S(1)} %bitcast.58, f32[1024,128]{1,0:T(8,128)} %gather_fusion, f32[1024]{0:T(1024)S(1)} %get-tuple-element.18, pred[1024]{0:T(1024)(128)(4,1)S(1)} %get-tuple-element.3), kind=kOutput, calls=%fused_computation.38 | convolution fusion | flops 1835008 | bytes 534016 | tf_op jit(solution)/shard_map/dot_general | solution.py:129
  68.5 5.2 %collective-permute-start.8 = (f32[129,128]{1,0:T(8,128)S(1)}, f32[129,128]{1,0:T(8,128)S(1)}, u32[]{:S(2)}, u32[]{:S(2)}) collective-permute-start(f32[129,128]{1,0:T(8,128)S(1)} %pad_maximum_fusion.10), channel_id=1, source_target_pairs={{0,4},{4,0},{8,12},{12,8},{16,20},{20,16},{24,28},{28,24},{1,5},{5... | collective-permute-start | bytes 198152 | tf_op jit(solution)/shard_map/ppermute | solution.py:89
  73.7 0.9 collective-permute-done.8
  74.6 2.5 %collective-permute-start.9 = (f32[129,128]{1,0:T(8,128)S(1)}, f32[129,128]{1,0:T(8,128)S(1)}, u32[]{:S(2)}, u32[]{:S(2)}) collective-permute-start(f32[129,128]{1,0:T(8,128)S(1)} %fusion.33), channel_id=1, source_target_pairs={{0,8},{4,12},{8,0},{12,4},{16,24},{20,28},{24,16},{28,20},{1,9},{5... | collective-permute-start | bytes 198152 | tf_op jit(solution)/shard_map/ppermute | solution.py:89
  77.0 2.7 %collective-permute-done.9 = f32[129,128]{1,0:T(8,128)S(1)} collective-permute-done((f32[129,128]{1,0:T(8,128)S(1)}, f32[129,128]{1,0:T(8,128)S(1)}, u32[]{:S(2)}, u32[]{:S(2)}) %collective-permute-start.9) | collective-permute-done | bytes 66080 | tf_op jit(solution)/shard_map/ppermute | solution.py:89
  79.7 1.0 collective-permute-start.10
  80.8 3.3 %collective-permute-done.10 = f32[129,128]{1,0:T(8,128)S(1)} collective-permute-done((f32[129,128]{1,0:T(8,128)S(1)}, f32[129,128]{1,0:T(8,128)S(1)}, u32[]{:S(2)}, u32[]{:S(2)}) %collective-permute-start.10) | collective-permute-done | bytes 66080 | tf_op jit(solution)/shard_map/ppermute | solution.py:89
  84.1 3.0 %collective-permute-start.11 = (f32[129,128]{1,0:T(8,128)S(1)}, f32[129,128]{1,0:T(8,128)S(1)}, u32[]{:S(2)}, u32[]{:S(2)}) collective-permute-start(f32[129,128]{1,0:T(8,128)S(1)} %add.117), channel_id=1, source_target_pairs={{0,1},{1,0},{2,3},{3,2},{4,5},{5,4},{6,7},{7,6},{8,9},{9,8},{10,11... | collective-permute-start | bytes 198152 | tf_op jit(solution)/shard_map/ppermute | solution.py:89
  87.1 0.1 reduce_sum.19
  87.2 2.1 %collective-permute-done.11 = f32[129,128]{1,0:T(8,128)S(1)} collective-permute-done((f32[129,128]{1,0:T(8,128)S(1)}, f32[129,128]{1,0:T(8,128)S(1)}, u32[]{:S(2)}, u32[]{:S(2)}) %collective-permute-start.11) | collective-permute-done | bytes 66080 | tf_op jit(solution)/shard_map/ppermute | solution.py:89
  89.4 2.6 %collective-permute-start.12 = (f32[129,128]{1,0:T(8,128)S(1)}, f32[129,128]{1,0:T(8,128)S(1)}, u32[]{:S(2)}, u32[]{:S(2)}) collective-permute-start(f32[129,128]{1,0:T(8,128)S(1)} %add.118), channel_id=1, source_target_pairs={{0,2},{1,3},{2,0},{3,1},{4,6},{5,7},{6,4},{7,5},{8,10},{9,11},{10,... | collective-permute-start | bytes 198152 | tf_op jit(solution)/shard_map/ppermute | solution.py:89
  92.0 2.6 %collective-permute-done.12 = f32[129,128]{1,0:T(8,128)S(1)} collective-permute-done((f32[129,128]{1,0:T(8,128)S(1)}, f32[129,128]{1,0:T(8,128)S(1)}, u32[]{:S(2)}, u32[]{:S(2)}) %collective-permute-start.12) | collective-permute-done | bytes 66080 | tf_op jit(solution)/shard_map/ppermute | solution.py:89
  94.8 11.7 %cholesky.18 = f32[128,128]{1,0:T(8,128)S(1)} custom-call(f32[128,128]{1,0:T(8,128)S(1)} %fusion.29), custom_call_target="Cholesky" | custom-call | tf_op jit(solution)/shard_map/jit(cholesky)/cholesky | solution.py:135
  106.6 0.6 compare_reduce_fusion
  107.2 0.7 fusion.25
  107.9 9.8 %custom-call.13 = f32[1,128,128]{1,2,0:T(8,128)S(1)} custom-call(f32[1,128,128]{2,1,0:T(8,128)S(1)} %fusion.25), custom_call_target="InvertDiagBlocksLowerTriangular" | custom-call | tf_op jit(solution)/shard_map/jit(_cho_solve)/triangular_solve | solution.py:136
  117.7 0.2 convolution_bitcast_fusion.1
  117.9 0.2 convolution_bitcast_fusion
  118.0 0.2 convolution_add_fusion.2
  118.3 1.0 fusion
  119.3 1.3 %fusion.1 = f32[16,8,16,128]{3,1,2,0:T(8,128)S(1)} fusion(f32[128,128]{1,0:T(8,128)S(1)} %convolution_add_fusion.2, f32[16,8,16,128]{3,2,1,0:T(8,128)S(1)} %bitcast.50, f32[2048]{0:T(1024)S(1)} %multiply_bitcast_fusion), kind=kOutput, calls=%fused_computation.6 | convolution fusion | flops 403177472 | bytes 2170880 | tf_op jit(solution)/shard_map/dot_general | solution.py:142
  120.6 1.2 copy.48
  121.8 1.2 copy.46
  (53 shorter events, 0.6 us)
Async XLA Ops:
  0.6 8.4 %copy-start.1 = (f32[128,16,128]{2,1,0:T(8,128)S(1)}, f32[128,16,128]{2,1,0:T(8,128)}, u32[]{:S(2)}) copy-start(f32[128,16,128]{2,1,0:T(8,128)} %param.5) | copy-start | bytes 3145732
  2.9 40.3 %collective-permute-start = (f32[128,2,2]{0,2,1:T(2,128)}, f32[128,2,2]{0,2,1:T(2,128)}, u32[]{:S(2)}, u32[]{:S(2)}) collective-permute-start(f32[128,2,2]{0,2,1:T(2,128)} %get-tuple-element.6), channel_id=1, source_target_pairs={{0,5},{1,6},{2,7},{4,9},{5,10},{6,11},{8,13},{9,14},{10,15},{12,17... | collective-permute-start | bytes 6152 | tf_op jit(solution)/shard_map/ppermute | solution.py:28
  7.9 35.3 %collective-permute-start.2 = (f32[128,2,2]{0,2,1:T(2,128)}, f32[128,2,2]{0,2,1:T(2,128)}, u32[]{:S(2)}, u32[]{:S(2)}) collective-permute-start(f32[128,2,2]{0,2,1:T(2,128)} %get-tuple-element.9), channel_id=1, source_target_pairs={{1,4},{2,5},{3,6},{5,8},{6,9},{7,10},{9,12},{10,13},{11,14},{13,16... | collective-permute-start | bytes 6152 | tf_op jit(solution)/shard_map/ppermute | solution.py:28
  10.7 1.7 %copy-start = (f32[128,16,128]{2,1,0:T(8,128)S(1)}, f32[128,16,128]{2,1,0:T(8,128)}, u32[]{:S(2)}) copy-start(f32[128,16,128]{2,1,0:T(8,128)} %param.6) | copy-start | bytes 3145732
  15.7 13.3 %collective-permute-start.3 = (f32[128,16,3]{0,1,2:T(8,128)S(1)}, f32[128,16,3]{0,1,2:T(8,128)S(1)}, u32[]{:S(2)}, u32[]{:S(2)}) collective-permute-start(f32[128,16,3]{0,1,2:T(8,128)S(1)} %pad_maximum_fusion.11), channel_id=1, source_target_pairs={{0,1},{1,2},{2,3},{4,5},{5,6},{6,7},{8,9},{9,10},{10,11},{12,13},{... | collective-permute-start | bytes 73736 | tf_op jit(solution)/shard_map/ppermute | solution.py:18
  23.7 4.5 %copy-start.7 = (s32[1024]{0:T(1024)S(1)}, s32[1024]{0:T(1024)}, u32[]{:S(2)}) copy-start(s32[1024]{0:T(1024)} %param.9) | copy-start | bytes 12292
  25.4 5.7 %collective-permute-start.4 = (f32[128,16,3]{0,1,2:T(8,128)S(1)}, f32[128,16,3]{0,1,2:T(8,128)S(1)}, u32[]{:S(2)}, u32[]{:S(2)}) collective-permute-start(f32[128,16,3]{0,1,2:T(8,128)S(1)} %pad_maximum_fusion.12), channel_id=1, source_target_pairs={{1,0},{2,1},{3,2},{5,4},{6,5},{7,6},{9,8},{10,9},{11,10},{13,12},{... | collective-permute-start | bytes 73736 | tf_op jit(solution)/shard_map/ppermute | solution.py:18
  26.9 5.5 %collective-permute-start.1 = (f32[128,3,128]{2,0,1:T(8,128)S(1)}, f32[128,3,128]{2,0,1:T(8,128)S(1)}, u32[]{:S(2)}, u32[]{:S(2)}) collective-permute-start(f32[128,3,128]{2,0,1:T(8,128)S(1)} %pad_maximum_fusion.8), channel_id=1, source_target_pairs={{0,4},{4,8},{8,12},{12,16},{16,20},{20,24},{24,28},{1,5},{5,9},{9,... | collective-permute-start | bytes 589832 | tf_op jit(solution)/shard_map/ppermute | solution.py:18
  29.0 14.2 %collective-permute-start.5 = (f32[128,2,2]{0,2,1:T(2,128)}, f32[128,2,2]{0,2,1:T(2,128)}, u32[]{:S(2)}, u32[]{:S(2)}) collective-permute-start(f32[128,2,2]{0,2,1:T(2,128)} %get-tuple-element.8), channel_id=1, source_target_pairs={{4,1},{5,2},{6,3},{8,5},{9,6},{10,7},{12,9},{13,10},{14,11},{16,13... | collective-permute-start | bytes 6152 | tf_op jit(solution)/shard_map/ppermute | solution.py:28
  31.1 12.1 %collective-permute-start.7 = (f32[128,2,2]{0,2,1:T(2,128)}, f32[128,2,2]{0,2,1:T(2,128)}, u32[]{:S(2)}, u32[]{:S(2)}) collective-permute-start(f32[128,2,2]{0,2,1:T(2,128)} %get-tuple-element.7), channel_id=1, source_target_pairs={{5,0},{6,1},{7,2},{9,4},{10,5},{11,6},{13,8},{14,9},{15,10},{17,12... | collective-permute-start | bytes 6152 | tf_op jit(solution)/shard_map/ppermute | solution.py:28
  32.4 1.3 %copy-start.2 = (f32[128,3,128]{2,0,1:T(8,128)}, f32[128,3,128]{2,0,1:T(8,128)S(1)}, u32[]{:S(2)}) copy-start(f32[128,3,128]{2,0,1:T(8,128)S(1)} %collective-permute-done.1) | copy-start | bytes 589828
  32.4 6.3 %collective-permute-start.6 = (f32[128,3,128]{2,0,1:T(8,128)}, f32[128,3,128]{2,0,1:T(8,128)}, u32[]{:S(2)}, u32[]{:S(2)}) collective-permute-start(f32[128,3,128]{2,0,1:T(8,128)} %pad_maximum_fusion.9), channel_id=1, source_target_pairs={{4,0},{8,4},{12,8},{16,12},{20,16},{24,20},{28,24},{5,1},{9,5},{13... | collective-permute-start | bytes 589832 | tf_op jit(solution)/shard_map/ppermute | solution.py:18
  43.1 1.0 copy-start.3
  43.1 1.0 copy-start.4
  43.1 1.0 copy-start.5
  43.2 1.0 copy-start.6
  59.9 4.1 %copy-start.8 = (f32[1024]{0:T(1024)S(1)}, f32[1024]{0:T(1024)}, u32[]{:S(2)}) copy-start(f32[1024]{0:T(1024)} %param.7) | copy-start | bytes 12292
  59.9 4.1 %copy-start.9 = (f32[1024]{0:T(1024)S(1)}, f32[1024]{0:T(1024)}, u32[]{:S(2)}) copy-start(f32[1024]{0:T(1024)} %param.8) | copy-start | bytes 12292
  68.5 6.1 %collective-permute-start.8 = (f32[129,128]{1,0:T(8,128)S(1)}, f32[129,128]{1,0:T(8,128)S(1)}, u32[]{:S(2)}, u32[]{:S(2)}) collective-permute-start(f32[129,128]{1,0:T(8,128)S(1)} %pad_maximum_fusion.10), channel_id=1, source_target_pairs={{0,4},{4,0},{8,12},{12,8},{16,20},{20,16},{24,28},{28,24},{1,5},{5... | collective-permute-start | bytes 198152 | tf_op jit(solution)/shard_map/ppermute | solution.py:89
  74.6 5.2 %collective-permute-start.9 = (f32[129,128]{1,0:T(8,128)S(1)}, f32[129,128]{1,0:T(8,128)S(1)}, u32[]{:S(2)}, u32[]{:S(2)}) collective-permute-start(f32[129,128]{1,0:T(8,128)S(1)} %fusion.33), channel_id=1, source_target_pairs={{0,8},{4,12},{8,0},{12,4},{16,24},{20,28},{24,16},{28,20},{1,9},{5... | collective-permute-start | bytes 198152 | tf_op jit(solution)/shard_map/ppermute | solution.py:89
  79.7 4.4 %collective-permute-start.10 = (f32[129,128]{1,0:T(8,128)S(1)}, f32[129,128]{1,0:T(8,128)S(1)}, u32[]{:S(2)}, u32[]{:S(2)}) collective-permute-start(f32[129,128]{1,0:T(8,128)S(1)} %add.116), channel_id=1, source_target_pairs={{0,16},{4,20},{8,24},{12,28},{16,0},{20,4},{24,8},{28,12},{1,17},{... | collective-permute-start | bytes 198152 | tf_op jit(solution)/shard_map/ppermute | solution.py:89
  84.1 5.2 %collective-permute-start.11 = (f32[129,128]{1,0:T(8,128)S(1)}, f32[129,128]{1,0:T(8,128)S(1)}, u32[]{:S(2)}, u32[]{:S(2)}) collective-permute-start(f32[129,128]{1,0:T(8,128)S(1)} %add.117), channel_id=1, source_target_pairs={{0,1},{1,0},{2,3},{3,2},{4,5},{5,4},{6,7},{7,6},{8,9},{9,8},{10,11... | collective-permute-start | bytes 198152 | tf_op jit(solution)/shard_map/ppermute | solution.py:89
  89.4 5.3 %collective-permute-start.12 = (f32[129,128]{1,0:T(8,128)S(1)}, f32[129,128]{1,0:T(8,128)S(1)}, u32[]{:S(2)}, u32[]{:S(2)}) collective-permute-start(f32[129,128]{1,0:T(8,128)S(1)} %add.118), channel_id=1, source_target_pairs={{0,2},{1,3},{2,0},{3,1},{4,6},{5,7},{6,4},{7,5},{8,10},{9,11},{10,... | collective-permute-start | bytes 198152 | tf_op jit(solution)/shard_map/ppermute | solution.py:89

commit v3 on v1

--- a/solution.py
+++ b/solution.py
@@ -22,17 +22,32 @@
     return block
 
 
+def xor_tree(received, base, strides):
+    if not strides:
+        return received[base]
+    return xor_tree(received, base, strides[:-1]) + xor_tree(
+        received, base ^ strides[-1], strides[:-1]
+    )
+
+
 def butterfly_sum(value, axes):
     for axis in axes:
         count = lax.axis_size(axis)
         if count & (count - 1):
             value = lax.psum(value, axis)
             continue
-        stride = 1
-        while stride < count:
-            pairs = [(i, i ^ stride) for i in range(count)]
-            value = value + lax.ppermute(value, axis, pairs)
-            stride *= 2
+        bits = [1 << b for b in range(count.bit_length() - 1)]
+        for first in range(0, len(bits), 2):
+            strides = bits[first : first + 2]
+            received = {0: value}
+            for mask in range(1, 1 << len(strides)):
+                offset = 0
+                for position, stride in enumerate(strides):
+                    if mask >> position & 1:
+                        offset ^= stride
+                pairs = [(i, i ^ offset) for i in range(count)]
+                received[offset] = lax.ppermute(value, axis, pairs)
+            value = xor_tree(received, 0, strides)
     return value
 
 

time: 104 us -> 104 us (level)
  starting transfers between devices: 39.7 us -> 37.4 us
  waiting for transfers between devices: 14.7 us -> 16.4 us
    ppermute x5 -> x7, starting transfers between devices: 17.9 us -> 15.6 us  [butterfly_sum(): received[offset] = lax.ppermute(value, axis, pairs)]
    ppermute x5 -> x7, waiting for transfers between devices: 10.9 us -> 12.6 us  [butterfly_sum(): received[offset] = lax.ppermute(value, axis, pairs)]
  transfers between devices with their start and end apart: 13 -> 15, of which waited for: 9 -> 9; matrix products, arithmetic and copies ran while one was open for 1% -> 1% of each run, Pallas kernels for 0% -> 0%
where the time goes in v3:
time: 104 us
  starting transfers between devices  37.4 us (36%)
  other arithmetic  25.8 us (25%)
  local copies, waits for them, and re-layouts  17.5 us (17%)
  waiting for transfers between devices  16.4 us (16%)
  matrix products  5.41 us (5%)
    ppermute x4, starting transfers between devices, with_halo(): lax.ppermute(lax.slice_in_dim(block, block.shape[dim] - width, None, axis...  16.5 us
    ppermute x7, starting transfers between devices, butterfly_sum(): received[offset] = lax.ppermute(value, axis, pairs)  15.6 us
    ppermute x7, waiting for transfers between devices, butterfly_sum(): received[offset] = lax.ppermute(value, axis, pairs)  12.6 us
    another operation x3, other arithmetic, shards(): lower = jnp.linalg.cholesky(gram_sum)  12.4 us
    another operation x2, other arithmetic, shards(): mean_weights = jax.scipy.linalg.cho_solve((lower, True), projected_sum)  10.5 us
    gather x1, local copies, waits for them, and re-layouts, shards(): jnp.take(average_gas_warmth, reading_local_location)  6.15 us
    unnamed x16, local copies, waits for them, and re-layouts  5.78 us
    ppermute x4, starting transfers between devices, with_halo(): lax.ppermute(lax.slice_in_dim(block, 0, width, axis=dim), axis, backward)  5.29 us
  transfers between devices with their start and end apart: 15, of which 9 were waited for; matrix products, arithmetic and copies ran while one was open for 1% of the time, Pallas kernels for 0%

profile of v3, /device:TPU:0, one launch (start us, length us, event | category | flops | bytes accessed | tf_op | source)
XLA Modules:
  0.0 103.5 jit_solution(8575528152628703875)
XLA Ops:
  0.6 1.8 %copy.128 = f32[128,16,128]{0,1,2:T(8,128)S(1)} copy(f32[128,16,128]{2,1,0:T(8,128)} %param.5) | data formatting | bytes 2097152 | tf_op args[0]
  2.5 0.0 copy-start
  2.5 0.1 fusion.38
  2.6 1.4 %collective-permute-start = (f32[128,1,128]{0,1,2:T(1,128)S(1)}, f32[128,1,128]{0,1,2:T(1,128)S(1)}, u32[]{:S(2)}, u32[]{:S(2)}) collective-permute-start(f32[128,1,128]{0,1,2:T(1,128)S(1)} %get-tuple-element.13), channel_id=1, source_target_pairs={{4,0},{8,4},{12,8},{16,12},{20,16},{24,20},{28,24},{5,1},{9,5},{13... | collective-permute-start | bytes 196616 | tf_op jit(solution)/shard_map/ppermute | solution.py:20
  4.0 3.0 %collective-permute-start.1 = (f32[128,1,128]{0,1,2:T(1,128)S(1)}, f32[128,1,128]{0,1,2:T(1,128)S(1)}, u32[]{:S(2)}, u32[]{:S(2)}) collective-permute-start(f32[128,1,128]{0,1,2:T(1,128)S(1)} %get-tuple-element.12), channel_id=1, source_target_pairs={{0,4},{4,8},{8,12},{12,16},{16,20},{20,24},{24,28},{1,5},{5,9},{9,... | collective-permute-start | bytes 196616 | tf_op jit(solution)/shard_map/ppermute | solution.py:17
  7.1 0.0 collective-permute-done
  7.1 0.9 collective-permute-done.1
  8.0 1.3 %collective-permute-start.2 = (f32[128,18,1]{0,1,2:T(8,128)S(1)}, f32[128,18,1]{0,1,2:T(8,128)S(1)}, u32[]{:S(2)}, u32[]{:S(2)}) collective-permute-start(f32[128,18,1]{0,1,2:T(8,128)S(1)} %get-tuple-element.8), channel_id=1, source_target_pairs={{1,0},{2,1},{3,2},{5,4},{6,5},{7,6},{9,8},{10,9},{11,10},{13,12},{... | collective-permute-start | bytes 27656 | tf_op jit(solution)/shard_map/ppermute | solution.py:20
  9.2 5.6 %collective-permute-start.3 = (f32[128,18,1]{0,1,2:T(8,128)S(1)}, f32[128,18,1]{0,1,2:T(8,128)S(1)}, u32[]{:S(2)}, u32[]{:S(2)}) collective-permute-start(f32[128,18,1]{0,1,2:T(8,128)S(1)} %get-tuple-element.9), channel_id=1, source_target_pairs={{0,1},{1,2},{2,3},{4,5},{5,6},{6,7},{8,9},{9,10},{10,11},{12,13},{... | collective-permute-start | bytes 27656 | tf_op jit(solution)/shard_map/ppermute | solution.py:17
  14.8 0.0 copy-done
  14.8 0.7 copy.129
  15.5 0.0 collective-permute-done.2
  15.5 0.7 collective-permute-done.3
  16.2 0.6 fusion.14
  16.8 0.1 fusion.37
  16.9 1.3 %collective-permute-start.4 = (f32[128,1,128]{0,1,2:T(1,128)S(1)}, f32[128,1,128]{0,1,2:T(1,128)S(1)}, u32[]{:S(2)}, u32[]{:S(2)}) collective-permute-start(f32[128,1,128]{0,1,2:T(1,128)S(1)} %get-tuple-element.11), channel_id=1, source_target_pairs={{4,0},{8,4},{12,8},{16,12},{20,16},{24,20},{28,24},{5,1},{9,5},{13... | collective-permute-start | bytes 196616 | tf_op jit(solution)/shard_map/ppermute | solution.py:20
  18.2 3.4 %collective-permute-start.5 = (f32[128,1,128]{0,1,2:T(1,128)S(1)}, f32[128,1,128]{0,1,2:T(1,128)S(1)}, u32[]{:S(2)}, u32[]{:S(2)}) collective-permute-start(f32[128,1,128]{0,1,2:T(1,128)S(1)} %get-tuple-element.10), channel_id=1, source_target_pairs={{0,4},{4,8},{8,12},{12,16},{16,20},{20,24},{24,28},{1,5},{5,9},{9,... | collective-permute-start | bytes 196616 | tf_op jit(solution)/shard_map/ppermute | solution.py:17
  21.6 0.0 collective-permute-done.4
  21.6 0.9 collective-permute-done.5
  22.5 1.3 %collective-permute-start.6 = (f32[128,18,1]{0,1,2:T(8,128)S(1)}, f32[128,18,1]{0,1,2:T(8,128)S(1)}, u32[]{:S(2)}, u32[]{:S(2)}) collective-permute-start(f32[128,18,1]{0,1,2:T(8,128)S(1)} %get-tuple-element.6), channel_id=1, source_target_pairs={{1,0},{2,1},{3,2},{5,4},{6,5},{7,6},{9,8},{10,9},{11,10},{13,12},{... | collective-permute-start | bytes 27656 | tf_op jit(solution)/shard_map/ppermute | solution.py:20
  23.8 4.5 %collective-permute-start.7 = (f32[128,18,1]{0,1,2:T(8,128)S(1)}, f32[128,18,1]{0,1,2:T(8,128)S(1)}, u32[]{:S(2)}, u32[]{:S(2)}) collective-permute-start(f32[128,18,1]{0,1,2:T(8,128)S(1)} %get-tuple-element.7), channel_id=1, source_target_pairs={{0,1},{1,2},{2,3},{4,5},{5,6},{6,7},{8,9},{9,10},{10,11},{12,13},{... | collective-permute-start | bytes 27656 | tf_op jit(solution)/shard_map/ppermute | solution.py:17
  28.4 0.0 collective-permute-done.6
  28.4 1.4 %collective-permute-done.7 = f32[128,18,1]{0,1,2:T(8,128)S(1)} collective-permute-done((f32[128,18,1]{0,1,2:T(8,128)S(1)}, f32[128,18,1]{0,1,2:T(8,128)S(1)}, u32[]{:S(2)}, u32[]{:S(2)}) %collective-permute-start.7) | collective-permute-done | bytes 9248 | tf_op jit(solution)/shard_map/ppermute | solution.py:17
  29.7 0.7 fusion.35
  30.4 0.7 copy.131
  31.1 0.0 copy-start.1
  31.1 0.1 copy.130
  31.2 0.9 copy-done.1
  32.1 1.3 %bitcast_subtract_fusion.2 = f32[128,2048]{1,0:T(8,128)} fusion(f32[16,8,16,128]{3,2,1,0:T(8,128)S(1)} %bitcast.50, f32[2048]{0:T(1024)S(1)} %multiply_bitcast_fusion.1), kind=kLoop, calls=%fused_computation.11 | loop fusion | flops 262144 | bytes 2105344 | tf_op jit(solution)/shard_map/sub | solution.py:82
  33.4 1.5 %copy.132 = f32[128,2048]{0,1:T(8,128)S(1)} copy(f32[128,2048]{1,0:T(8,128)} %bitcast_subtract_fusion.2) | data formatting | bytes 2097152 | tf_op jit(solution)/shard_map/sub | solution.py:82
  35.0 6.2 %gather_fusion.1 = f32[1024]{0:T(1024)S(1)} fusion(f32[2048]{0:T(1024)S(1)} %multiply_bitcast_fusion.1, s32[1024]{0:T(1024)S(1)} %fusion.32), kind=kCustom, calls=%fused_computation.1 | custom fusion | bytes 12288 | tf_op jit(solution)/shard_map/jit(_take)/gather | solution.py:88
  41.1 0.0 copy-start.4
  41.2 0.0 copy-start.5
  41.2 3.0 %gather_fusion = f32[1024,128]{1,0:T(8,128)S(1)} fusion(f32[128,2048]{0,1:T(8,128)S(1)} %copy.132, s32[1024]{0:T(1024)S(1)} %fusion.32), kind=kCustom, calls=%fused_computation | custom fusion | bytes 1052672 | tf_op jit(solution)/shard_map/jit(_take)/gather | solution.py:84
  44.2 1.6 %fusion.20 = f32[128,128]{1,0:T(8,128)S(1)} fusion(f32[1024,128]{1,0:T(8,128)S(1)} %gather_fusion, f32[1024]{0:T(1024)S(1)} %get-tuple-element.14, pred[1024]{0:T(1024)(128)(4,1)S(1)} %get-tuple-element.3), kind=kOutput, calls=%fused_computation.46 | convolution fusion | flops 201588736 | bytes 594944 | tf_op jit(solution)/shard_map/dot_general | solution.py:91
  45.8 0.6 fusion.17
  46.5 6.3 %collective-permute-start.10 = (f32[129,128]{1,0:T(8,128)S(1)}, f32[129,128]{1,0:T(8,128)S(1)}, u32[]{:S(2)}, u32[]{:S(2)}) collective-permute-start(f32[129,128]{1,0:T(8,128)S(1)} %pad_maximum_fusion.16), channel_id=1, source_target_pairs={{0,12},{4,8},{8,4},{12,0},{16,28},{20,24},{24,20},{28,16},{1,13},{... | collective-permute-start | bytes 198152 | tf_op jit(solution)/shard_map/ppermute | solution.py:49
  52.8 0.4 collective-permute-start.8
  53.1 0.1 collective-permute-start.9
  53.2 2.1 %collective-permute-done.10 = f32[129,128]{1,0:T(8,128)S(1)} collective-permute-done((f32[129,128]{1,0:T(8,128)S(1)}, f32[129,128]{1,0:T(8,128)S(1)}, u32[]{:S(2)}, u32[]{:S(2)}) %collective-permute-start.10) | collective-permute-done | bytes 66080 | tf_op jit(solution)/shard_map/ppermute | solution.py:49
  55.3 0.0 collective-permute-done.8
  55.3 2.1 %collective-permute-done.9 = f32[129,128]{1,0:T(8,128)S(1)} collective-permute-done((f32[129,128]{1,0:T(8,128)S(1)}, f32[129,128]{1,0:T(8,128)S(1)}, u32[]{:S(2)}, u32[]{:S(2)}) %collective-permute-start.9) | collective-permute-done | bytes 66080 | tf_op jit(solution)/shard_map/ppermute | solution.py:49
  57.4 0.0 copy-start.2
  57.5 3.5 %collective-permute-start.11 = (f32[129,128]{1,0:T(8,128)S(1)}, f32[129,128]{1,0:T(8,128)S(1)}, u32[]{:S(2)}, u32[]{:S(2)}) collective-permute-start(f32[129,128]{1,0:T(8,128)S(1)} %add_add_fusion.1), channel_id=1, source_target_pairs={{0,16},{4,20},{8,24},{12,28},{16,0},{20,4},{24,8},{28,12},{1,17},{... | collective-permute-start | bytes 198152 | tf_op jit(solution)/shard_map/ppermute | solution.py:49
  61.0 0.1 reduce_sum.19
  61.1 2.3 %collective-permute-done.11 = f32[129,128]{1,0:T(8,128)S(1)} collective-permute-done((f32[129,128]{1,0:T(8,128)S(1)}, f32[129,128]{1,0:T(8,128)S(1)}, u32[]{:S(2)}, u32[]{:S(2)}) %collective-permute-start.11) | collective-permute-done | bytes 66080 | tf_op jit(solution)/shard_map/ppermute | solution.py:49
  63.4 2.4 %collective-permute-start.12 = (f32[129,128]{1,0:T(8,128)S(1)}, f32[129,128]{1,0:T(8,128)S(1)}, u32[]{:S(2)}, u32[]{:S(2)}) collective-permute-start(f32[129,128]{1,0:T(8,128)S(1)} %add.124), channel_id=1, source_target_pairs={{0,1},{1,0},{2,3},{3,2},{4,5},{5,4},{6,7},{7,6},{8,9},{9,8},{10,11... | collective-permute-start | bytes 198152 | tf_op jit(solution)/shard_map/ppermute | solution.py:49
  65.8 3.0 %collective-permute-start.13 = (f32[129,128]{1,0:T(8,128)S(1)}, f32[129,128]{1,0:T(8,128)S(1)}, u32[]{:S(2)}, u32[]{:S(2)}) collective-permute-start(f32[129,128]{1,0:T(8,128)S(1)} %add.124), channel_id=1, source_target_pairs={{0,2},{1,3},{2,0},{3,1},{4,6},{5,7},{6,4},{7,5},{8,10},{9,11},{10,... | collective-permute-start | bytes 198152 | tf_op jit(solution)/shard_map/ppermute | solution.py:49
  68.8 0.0 collective-permute-start.14
  68.8 0.0 collective-permute-done.12
  68.8 4.6 %collective-permute-done.13 = f32[129,128]{1,0:T(8,128)S(1)} collective-permute-done((f32[129,128]{1,0:T(8,128)S(1)}, f32[129,128]{1,0:T(8,128)S(1)}, u32[]{:S(2)}, u32[]{:S(2)}) %collective-permute-start.13) | collective-permute-done | bytes 66080 | tf_op jit(solution)/shard_map/ppermute | solution.py:49
  73.5 1.5 %collective-permute-done.14 = f32[129,128]{1,0:T(8,128)S(1)} collective-permute-done((f32[129,128]{1,0:T(8,128)S(1)}, f32[129,128]{1,0:T(8,128)S(1)}, u32[]{:S(2)}, u32[]{:S(2)}) %collective-permute-start.14) | collective-permute-done | bytes 66080 | tf_op jit(solution)/shard_map/ppermute | solution.py:49
  75.0 0.1 copy.133
  75.1 11.7 %cholesky.18 = f32[128,128]{1,0:T(8,128)S(1)} custom-call(f32[128,128]{1,0:T(8,128)S(1)} %fusion.31), custom_call_target="Cholesky" | custom-call | tf_op jit(solution)/shard_map/jit(cholesky)/cholesky | solution.py:98
  86.9 0.6 compare_reduce_fusion
  87.5 0.7 fusion.27
  88.2 9.8 %custom-call.13 = f32[1,128,128]{1,2,0:T(8,128)S(1)} custom-call(f32[1,128,128]{2,1,0:T(8,128)S(1)} %fusion.27), custom_call_target="InvertDiagBlocksLowerTriangular" | custom-call | tf_op jit(solution)/shard_map/jit(_cho_solve)/triangular_solve | solution.py:99
  98.0 0.2 convolution_bitcast_fusion.1
  98.1 0.2 convolution_bitcast_fusion
  98.3 0.2 convolution_add_fusion.2
  98.6 1.3 %fusion = f32[16,8,16,128]{3,1,2,0:T(8,128)S(1)} fusion(f32[128,128]{1,0:T(8,128)S(1)} %convolution_add_fusion.2, f32[2048]{0:T(1024)S(1)} %multiply_bitcast_fusion.1, f32[16,8,16,128]{3,2,1,0:T(8,128)S(1)} %bitcast.51), kind=kOutput, calls=%fused_computation.4 | convolution fusion | flops 403177472 | bytes 2170880 | tf_op jit(solution)/shard_map/dot_general | solution.py:102
  99.9 1.3 %fusion.1 = f32[16,8,16,128]{3,1,2,0:T(8,128)S(1)} fusion(f32[128,128]{1,0:T(8,128)S(1)} %convolution_add_fusion.2, f32[16,8,16,128]{3,2,1,0:T(8,128)S(1)} %bitcast.49, f32[2048]{0:T(1024)S(1)} %multiply_bitcast_fusion), kind=kOutput, calls=%fused_computation.5 | convolution fusion | flops 403177472 | bytes 2170880 | tf_op jit(solution)/shard_map/dot_general | solution.py:105
  101.2 1.2 %copy.137 = f32[16,8,16,128]{3,2,1,0:T(8,128)} copy(f32[16,8,16,128]{3,1,2,0:T(8,128)S(1)} %fusion.1) | data formatting | bytes 2097152
  102.3 1.2 %copy.135 = f32[16,8,16,128]{3,2,1,0:T(8,128)} copy(f32[16,8,16,128]{3,1,2,0:T(8,128)S(1)} %fusion) | data formatting | bytes 2097152
  (18 shorter events, 0.2 us)
Async XLA Ops:
  2.5 12.3 %copy-start = (f32[128,16,128]{2,1,0:T(8,128)S(1)}, f32[128,16,128]{2,1,0:T(8,128)}, u32[]{:S(2)}) copy-start(f32[128,16,128]{2,1,0:T(8,128)} %param.6) | copy-start | bytes 3145732
  2.6 4.5 %collective-permute-start = (f32[128,1,128]{0,1,2:T(1,128)S(1)}, f32[128,1,128]{0,1,2:T(1,128)S(1)}, u32[]{:S(2)}, u32[]{:S(2)}) collective-permute-start(f32[128,1,128]{0,1,2:T(1,128)S(1)} %get-tuple-element.13), channel_id=1, source_target_pairs={{4,0},{8,4},{12,8},{16,12},{20,16},{24,20},{28,24},{5,1},{9,5},{13... | collective-permute-start | bytes 196616 | tf_op jit(solution)/shard_map/ppermute | solution.py:20
  4.0 3.9 %collective-permute-start.1 = (f32[128,1,128]{0,1,2:T(1,128)S(1)}, f32[128,1,128]{0,1,2:T(1,128)S(1)}, u32[]{:S(2)}, u32[]{:S(2)}) collective-permute-start(f32[128,1,128]{0,1,2:T(1,128)S(1)} %get-tuple-element.12), channel_id=1, source_target_pairs={{0,4},{4,8},{8,12},{12,16},{16,20},{20,24},{24,28},{1,5},{5,9},{9,... | collective-permute-start | bytes 196616 | tf_op jit(solution)/shard_map/ppermute | solution.py:17
  8.0 7.6 %collective-permute-start.2 = (f32[128,18,1]{0,1,2:T(8,128)S(1)}, f32[128,18,1]{0,1,2:T(8,128)S(1)}, u32[]{:S(2)}, u32[]{:S(2)}) collective-permute-start(f32[128,18,1]{0,1,2:T(8,128)S(1)} %get-tuple-element.8), channel_id=1, source_target_pairs={{1,0},{2,1},{3,2},{5,4},{6,5},{7,6},{9,8},{10,9},{11,10},{13,12},{... | collective-permute-start | bytes 27656 | tf_op jit(solution)/shard_map/ppermute | solution.py:20
  9.2 7.0 %collective-permute-start.3 = (f32[128,18,1]{0,1,2:T(8,128)S(1)}, f32[128,18,1]{0,1,2:T(8,128)S(1)}, u32[]{:S(2)}, u32[]{:S(2)}) collective-permute-start(f32[128,18,1]{0,1,2:T(8,128)S(1)} %get-tuple-element.9), channel_id=1, source_target_pairs={{0,1},{1,2},{2,3},{4,5},{5,6},{6,7},{8,9},{9,10},{10,11},{12,13},{... | collective-permute-start | bytes 27656 | tf_op jit(solution)/shard_map/ppermute | solution.py:17
  16.9 4.7 %collective-permute-start.4 = (f32[128,1,128]{0,1,2:T(1,128)S(1)}, f32[128,1,128]{0,1,2:T(1,128)S(1)}, u32[]{:S(2)}, u32[]{:S(2)}) collective-permute-start(f32[128,1,128]{0,1,2:T(1,128)S(1)} %get-tuple-element.11), channel_id=1, source_target_pairs={{4,0},{8,4},{12,8},{16,12},{20,16},{24,20},{28,24},{5,1},{9,5},{13... | collective-permute-start | bytes 196616 | tf_op jit(solution)/shard_map/ppermute | solution.py:20
  18.2 4.3 %collective-permute-start.5 = (f32[128,1,128]{0,1,2:T(1,128)S(1)}, f32[128,1,128]{0,1,2:T(1,128)S(1)}, u32[]{:S(2)}, u32[]{:S(2)}) collective-permute-start(f32[128,1,128]{0,1,2:T(1,128)S(1)} %get-tuple-element.10), channel_id=1, source_target_pairs={{0,4},{4,8},{8,12},{12,16},{16,20},{20,24},{24,28},{1,5},{5,9},{9,... | collective-permute-start | bytes 196616 | tf_op jit(solution)/shard_map/ppermute | solution.py:17
  22.5 5.9 %copy-start.3 = (s32[1024]{0:T(1024)S(1)}, s32[1024]{0:T(1024)}, u32[]{:S(2)}) copy-start(s32[1024]{0:T(1024)} %param.9) | copy-start | bytes 12292
  22.5 5.9 %collective-permute-start.6 = (f32[128,18,1]{0,1,2:T(8,128)S(1)}, f32[128,18,1]{0,1,2:T(8,128)S(1)}, u32[]{:S(2)}, u32[]{:S(2)}) collective-permute-start(f32[128,18,1]{0,1,2:T(8,128)S(1)} %get-tuple-element.6), channel_id=1, source_target_pairs={{1,0},{2,1},{3,2},{5,4},{6,5},{7,6},{9,8},{10,9},{11,10},{13,12},{... | collective-permute-start | bytes 27656 | tf_op jit(solution)/shard_map/ppermute | solution.py:20
  23.8 5.9 %collective-permute-start.7 = (f32[128,18,1]{0,1,2:T(8,128)S(1)}, f32[128,18,1]{0,1,2:T(8,128)S(1)}, u32[]{:S(2)}, u32[]{:S(2)}) collective-permute-start(f32[128,18,1]{0,1,2:T(8,128)S(1)} %get-tuple-element.7), channel_id=1, source_target_pairs={{0,1},{1,2},{2,3},{4,5},{5,6},{6,7},{8,9},{9,10},{10,11},{12,13},{... | collective-permute-start | bytes 27656 | tf_op jit(solution)/shard_map/ppermute | solution.py:17
  31.1 1.0 copy-start.1
  41.1 3.0 %copy-start.4 = (f32[1024]{0:T(1024)S(1)}, f32[1024]{0:T(1024)}, u32[]{:S(2)}) copy-start(f32[1024]{0:T(1024)} %param.7) | copy-start | bytes 12292
  41.2 3.0 %copy-start.5 = (f32[1024]{0:T(1024)S(1)}, f32[1024]{0:T(1024)}, u32[]{:S(2)}) copy-start(f32[1024]{0:T(1024)} %param.8) | copy-start | bytes 12292
  46.5 8.8 %collective-permute-start.10 = (f32[129,128]{1,0:T(8,128)S(1)}, f32[129,128]{1,0:T(8,128)S(1)}, u32[]{:S(2)}, u32[]{:S(2)}) collective-permute-start(f32[129,128]{1,0:T(8,128)S(1)} %pad_maximum_fusion.16), channel_id=1, source_target_pairs={{0,12},{4,8},{8,4},{12,0},{16,28},{20,24},{24,20},{28,16},{1,13},{... | collective-permute-start | bytes 198152 | tf_op jit(solution)/shard_map/ppermute | solution.py:49
  52.8 2.6 %collective-permute-start.8 = (f32[129,128]{1,0:T(8,128)S(1)}, f32[129,128]{1,0:T(8,128)S(1)}, u32[]{:S(2)}, u32[]{:S(2)}) collective-permute-start(f32[129,128]{1,0:T(8,128)S(1)} %pad_maximum_fusion.16), channel_id=1, source_target_pairs={{0,4},{4,0},{8,12},{12,8},{16,20},{20,16},{24,28},{28,24},{1,5},{5... | collective-permute-start | bytes 198152 | tf_op jit(solution)/shard_map/ppermute | solution.py:49
  53.1 4.3 %collective-permute-start.9 = (f32[129,128]{1,0:T(8,128)S(1)}, f32[129,128]{1,0:T(8,128)S(1)}, u32[]{:S(2)}, u32[]{:S(2)}) collective-permute-start(f32[129,128]{1,0:T(8,128)S(1)} %pad_maximum_fusion.16), channel_id=1, source_target_pairs={{0,8},{4,12},{8,0},{12,4},{16,24},{20,28},{24,16},{28,20},{1,9},{5... | collective-permute-start | bytes 198152 | tf_op jit(solution)/shard_map/ppermute | solution.py:49
  57.4 41.1 %copy-start.2 = (f32[128,16,128]{2,1,0:T(8,128)S(1)}, f32[128,16,128]{2,1,0:T(8,128)}, u32[]{:S(2)}) copy-start(f32[128,16,128]{2,1,0:T(8,128)} %copy-done.1) | copy-start | bytes 3145732
  57.5 6.0 %collective-permute-start.11 = (f32[129,128]{1,0:T(8,128)S(1)}, f32[129,128]{1,0:T(8,128)S(1)}, u32[]{:S(2)}, u32[]{:S(2)}) collective-permute-start(f32[129,128]{1,0:T(8,128)S(1)} %add_add_fusion.1), channel_id=1, source_target_pairs={{0,16},{4,20},{8,24},{12,28},{16,0},{20,4},{24,8},{28,12},{1,17},{... | collective-permute-start | bytes 198152 | tf_op jit(solution)/shard_map/ppermute | solution.py:49
  63.4 5.4 %collective-permute-start.12 = (f32[129,128]{1,0:T(8,128)S(1)}, f32[129,128]{1,0:T(8,128)S(1)}, u32[]{:S(2)}, u32[]{:S(2)}) collective-permute-start(f32[129,128]{1,0:T(8,128)S(1)} %add.124), channel_id=1, source_target_pairs={{0,1},{1,0},{2,3},{3,2},{4,5},{5,4},{6,7},{7,6},{8,9},{9,8},{10,11... | collective-permute-start | bytes 198152 | tf_op jit(solution)/shard_map/ppermute | solution.py:49
  65.8 7.7 %collective-permute-start.13 = (f32[129,128]{1,0:T(8,128)S(1)}, f32[129,128]{1,0:T(8,128)S(1)}, u32[]{:S(2)}, u32[]{:S(2)}) collective-permute-start(f32[129,128]{1,0:T(8,128)S(1)} %add.124), channel_id=1, source_target_pairs={{0,2},{1,3},{2,0},{3,1},{4,6},{5,7},{6,4},{7,5},{8,10},{9,11},{10,... | collective-permute-start | bytes 198152 | tf_op jit(solution)/shard_map/ppermute | solution.py:49
  68.8 6.1 %collective-permute-start.14 = (f32[129,128]{1,0:T(8,128)S(1)}, f32[129,128]{1,0:T(8,128)S(1)}, u32[]{:S(2)}, u32[]{:S(2)}) collective-permute-start(f32[129,128]{1,0:T(8,128)S(1)} %add.124), channel_id=1, source_target_pairs={{0,3},{1,2},{2,1},{3,0},{4,7},{5,6},{6,5},{7,4},{8,11},{9,10},{10,... | collective-permute-start | bytes 198152 | tf_op jit(solution)/shard_map/ppermute | solution.py:49

commit v4 on v3

--- a/solution.py
+++ b/solution.py
@@ -3,6 +3,8 @@
 import jax
 import jax.numpy as jnp
 from jax import lax
+from jax.experimental import pallas as pl
+from jax.experimental.pallas import tpu as pltpu
 from jax.sharding import PartitionSpec as P
 
 diffusion = 0.2
@@ -51,6 +53,42 @@
     return value
 
 
+def inverse_factor_kernel(gram_ref, inverse_ref, work_ref):
+    size = gram_ref.shape[0]
+    work_ref[...] = gram_ref[...]
+    square_row = lax.broadcasted_iota(jnp.int32, (size, size), 0)
+    square_col = lax.broadcasted_iota(jnp.int32, (size, size), 1)
+    inverse_ref[...] = jnp.where(square_row == square_col, 1.0, 0.0).astype(jnp.float32)
+    lane = lax.broadcasted_iota(jnp.int32, (1, size), 1)
+    sublane = lax.broadcasted_iota(jnp.int32, (size, 1), 0)
+
+    def step(k, carry):
+        row = work_ref[pl.ds(k, 1), :]
+        column = jnp.sum(jnp.where(square_col == k, work_ref[...], 0.0), axis=1, keepdims=True)
+        pivot = jnp.sum(jnp.where(lane == k, row, 0.0), axis=1, keepdims=True)
+        root = jnp.sqrt(pivot)
+        factor_row = jnp.where(lane >= k, row / root, 0.0)
+        factor_col = jnp.where(sublane >= k, column / root, 0.0)
+        work_ref[...] = work_ref[...] - factor_col * factor_row
+        inverse_row = inverse_ref[pl.ds(k, 1), :] / root
+        below = jnp.where(sublane > k, factor_col, 0.0)
+        inverse_ref[...] = inverse_ref[...] - below * inverse_row
+        inverse_ref[pl.ds(k, 1), :] = inverse_row
+        return carry
+
+    lax.fori_loop(0, size, step, 0)
+
+
+def inverse_factor(gram):
+    size = gram.shape[0]
+    return pl.pallas_call(
+        inverse_factor_kernel,
+        out_shape=jax.ShapeDtypeStruct((size, size), jnp.float32),
+        in_specs=[pl.BlockSpec(memory_space=pltpu.VMEM)],
+        out_specs=pl.BlockSpec(memory_space=pltpu.VMEM),
+        scratch_shapes=[pltpu.VMEM((size, size), jnp.float32)],
+    )(gram)
+
 def propagate_model(padded_field, source_term):
     laplacian = (
         padded_field[:, 2:, 1:-1]
@@ -95,15 +133,15 @@
     )
     gram_sum = stacked[:sample_number] + identity
     projected_sum = stacked[sample_number]
-    lower = jnp.linalg.cholesky(gram_sum)
-    mean_weights = jax.scipy.linalg.cho_solve((lower, True), projected_sum)
-    inverse_factor = jax.scipy.linalg.solve_triangular(lower, identity, lower=True, trans=1)
-    combination_matrix = mean_weights[:, None] + inverse_factor
+    lower_inverse = inverse_factor(gram_sum)
+    whitened = jnp.dot(lower_inverse, projected_sum, precision=lax.Precision.HIGHEST)
+    mean_weights = jnp.dot(lower_inverse.T, whitened, precision=lax.Precision.HIGHEST)
+    combination_transposed = lower_inverse + mean_weights[None, :]
     updated_warmth = average_gas_warmth + jnp.dot(
-        combination_matrix.T, sample_deviation_matrix, precision=lax.Precision.HIGHEST
+        combination_transposed, sample_deviation_matrix, precision=lax.Precision.HIGHEST
     )
     heat_out = mean_heat + jnp.dot(
-        combination_matrix.T, heat_anomaly, precision=lax.Precision.HIGHEST
+        combination_transposed, heat_anomaly, precision=lax.Precision.HIGHEST
     )
     return (
         updated_warmth.reshape(sample_number, block_height_number, block_width_number),

time: 104 us -> 98.4 us (0.946)
  other arithmetic: 25.8 us -> 3.52 us
  Pallas kernels: 0 us -> 16.2 us
    another operation x5 -> x0, other arithmetic: 22.9 us -> none  [the longest x3 12.4 us: shards(): lower = jnp.linalg.cholesky(gram_sum)]
    pallas_call x0 -> x1, Pallas kernels: none -> 16.2 us  [inverse_factor(): pl.pallas_call(inverse_factor_kernel, out_shape=jax.ShapeDtypeStruct((siz...]
    dot_general x2 -> x4, matrix products: 2.59 us -> 3.92 us  [the longest x1 1.33 us: shards(): jnp.dot(combination_transposed, sample_deviation_matrix, precision=lax.Pr...]
    unnamed x16 -> x18, local copies, waits for them, and re-layouts: 5.78 us -> 5.79 us
where the time goes in v4:
time: 98.4 us; the launch traced here: 97.9 us
  starting transfers between devices  37.4 us (38%)
  local copies, waits for them, and re-layouts  17.2 us (17%)
  waiting for transfers between devices  16.4 us (17%)
  Pallas kernels  16.2 us (16%)
  matrix products  6.16 us (6%)
  other arithmetic  3.52 us (4%)
    ppermute x4, starting transfers between devices, with_halo(): lax.ppermute(lax.slice_in_dim(block, block.shape[dim] - width, None, axis...  16.5 us
    pallas_call x1, Pallas kernels, inverse_factor(): pl.pallas_call(inverse_factor_kernel, out_shape=jax.ShapeDtypeStruct((siz...  16.2 us
    ppermute x7, starting transfers between devices, butterfly_sum(): received[offset] = lax.ppermute(value, axis, pairs)  15.6 us
    ppermute x7, waiting for transfers between devices, butterfly_sum(): received[offset] = lax.ppermute(value, axis, pairs)  12.6 us
    gather x1, local copies, waits for them, and re-layouts, shards(): jnp.take(average_gas_warmth, reading_local_location)  6.15 us
    unnamed x18, local copies, waits for them, and re-layouts  5.79 us
    ppermute x4, starting transfers between devices, with_halo(): lax.ppermute(lax.slice_in_dim(block, 0, width, axis=dim), axis, backward)  5.29 us
    ppermute x4, waiting for transfers between devices, with_halo(): lax.ppermute(lax.slice_in_dim(block, block.shape[dim] - width, None, axis...  3.76 us
  transfers between devices with their start and end apart: 15, of which 9 were waited for; matrix products, arithmetic and copies ran while one was open for 1% of the time, Pallas kernels for 0%

profile of v4, /device:TPU:0, one launch (start us, length us, event | category | flops | bytes accessed | tf_op | source)
XLA Modules:
  0.0 97.9 jit_solution(11817244906922588127)
XLA Ops:
  0.6 1.8 %copy.121 = f32[128,16,128]{0,1,2:T(8,128)S(1)} copy(f32[128,16,128]{2,1,0:T(8,128)} %param.5) | data formatting | bytes 2097152 | tf_op args[0]
  2.5 0.0 copy-start
  2.5 0.1 fusion.38
  2.6 1.4 %collective-permute-start = (f32[128,1,128]{0,1,2:T(1,128)S(1)}, f32[128,1,128]{0,1,2:T(1,128)S(1)}, u32[]{:S(2)}, u32[]{:S(2)}) collective-permute-start(f32[128,1,128]{0,1,2:T(1,128)S(1)} %get-tuple-element.13), channel_id=1, source_target_pairs={{4,0},{8,4},{12,8},{16,12},{20,16},{24,20},{28,24},{5,1},{9,5},{13... | collective-permute-start | bytes 196616 | tf_op jit(solution)/shard_map/ppermute | solution.py:22
  4.0 3.0 %collective-permute-start.1 = (f32[128,1,128]{0,1,2:T(1,128)S(1)}, f32[128,1,128]{0,1,2:T(1,128)S(1)}, u32[]{:S(2)}, u32[]{:S(2)}) collective-permute-start(f32[128,1,128]{0,1,2:T(1,128)S(1)} %get-tuple-element.12), channel_id=1, source_target_pairs={{0,4},{4,8},{8,12},{12,16},{16,20},{20,24},{24,28},{1,5},{5,9},{9,... | collective-permute-start | bytes 196616 | tf_op jit(solution)/shard_map/ppermute | solution.py:19
  7.1 0.0 collective-permute-done
  7.1 0.9 collective-permute-done.1
  8.0 1.3 %collective-permute-start.2 = (f32[128,18,1]{0,1,2:T(8,128)S(1)}, f32[128,18,1]{0,1,2:T(8,128)S(1)}, u32[]{:S(2)}, u32[]{:S(2)}) collective-permute-start(f32[128,18,1]{0,1,2:T(8,128)S(1)} %get-tuple-element.8), channel_id=1, source_target_pairs={{1,0},{2,1},{3,2},{5,4},{6,5},{7,6},{9,8},{10,9},{11,10},{13,12},{... | collective-permute-start | bytes 27656 | tf_op jit(solution)/shard_map/ppermute | solution.py:22
  9.2 5.6 %collective-permute-start.3 = (f32[128,18,1]{0,1,2:T(8,128)S(1)}, f32[128,18,1]{0,1,2:T(8,128)S(1)}, u32[]{:S(2)}, u32[]{:S(2)}) collective-permute-start(f32[128,18,1]{0,1,2:T(8,128)S(1)} %get-tuple-element.9), channel_id=1, source_target_pairs={{0,1},{1,2},{2,3},{4,5},{5,6},{6,7},{8,9},{9,10},{10,11},{12,13},{... | collective-permute-start | bytes 27656 | tf_op jit(solution)/shard_map/ppermute | solution.py:19
  14.8 0.0 copy-done
  14.8 0.7 copy.122
  15.5 0.0 collective-permute-done.2
  15.5 0.7 collective-permute-done.3
  16.2 0.6 fusion.14
  16.8 0.1 fusion.37
  16.9 1.3 %collective-permute-start.4 = (f32[128,1,128]{0,1,2:T(1,128)S(1)}, f32[128,1,128]{0,1,2:T(1,128)S(1)}, u32[]{:S(2)}, u32[]{:S(2)}) collective-permute-start(f32[128,1,128]{0,1,2:T(1,128)S(1)} %get-tuple-element.11), channel_id=1, source_target_pairs={{4,0},{8,4},{12,8},{16,12},{20,16},{24,20},{28,24},{5,1},{9,5},{13... | collective-permute-start | bytes 196616 | tf_op jit(solution)/shard_map/ppermute | solution.py:22
  18.2 3.4 %collective-permute-start.5 = (f32[128,1,128]{0,1,2:T(1,128)S(1)}, f32[128,1,128]{0,1,2:T(1,128)S(1)}, u32[]{:S(2)}, u32[]{:S(2)}) collective-permute-start(f32[128,1,128]{0,1,2:T(1,128)S(1)} %get-tuple-element.10), channel_id=1, source_target_pairs={{0,4},{4,8},{8,12},{12,16},{16,20},{20,24},{24,28},{1,5},{5,9},{9,... | collective-permute-start | bytes 196616 | tf_op jit(solution)/shard_map/ppermute | solution.py:19
  21.6 0.0 collective-permute-done.4
  21.6 0.9 collective-permute-done.5
  22.5 1.3 %collective-permute-start.6 = (f32[128,18,1]{0,1,2:T(8,128)S(1)}, f32[128,18,1]{0,1,2:T(8,128)S(1)}, u32[]{:S(2)}, u32[]{:S(2)}) collective-permute-start(f32[128,18,1]{0,1,2:T(8,128)S(1)} %get-tuple-element.6), channel_id=1, source_target_pairs={{1,0},{2,1},{3,2},{5,4},{6,5},{7,6},{9,8},{10,9},{11,10},{13,12},{... | collective-permute-start | bytes 27656 | tf_op jit(solution)/shard_map/ppermute | solution.py:22
  23.8 4.5 %collective-permute-start.7 = (f32[128,18,1]{0,1,2:T(8,128)S(1)}, f32[128,18,1]{0,1,2:T(8,128)S(1)}, u32[]{:S(2)}, u32[]{:S(2)}) collective-permute-start(f32[128,18,1]{0,1,2:T(8,128)S(1)} %get-tuple-element.7), channel_id=1, source_target_pairs={{0,1},{1,2},{2,3},{4,5},{5,6},{6,7},{8,9},{9,10},{10,11},{12,13},{... | collective-permute-start | bytes 27656 | tf_op jit(solution)/shard_map/ppermute | solution.py:19
  28.4 0.0 collective-permute-done.6
  28.4 1.4 %collective-permute-done.7 = f32[128,18,1]{0,1,2:T(8,128)S(1)} collective-permute-done((f32[128,18,1]{0,1,2:T(8,128)S(1)}, f32[128,18,1]{0,1,2:T(8,128)S(1)}, u32[]{:S(2)}, u32[]{:S(2)}) %collective-permute-start.7) | collective-permute-done | bytes 9248 | tf_op jit(solution)/shard_map/ppermute | solution.py:19
  29.7 0.7 fusion.35
  30.4 0.7 copy.124
  31.1 0.0 copy-start.1
  31.1 0.1 copy.123
  31.2 0.9 copy-done.1
  32.1 1.3 %bitcast_subtract_fusion.2 = f32[128,2048]{1,0:T(8,128)} fusion(f32[16,8,16,128]{3,2,1,0:T(8,128)S(1)} %bitcast.39, f32[2048]{0:T(1024)S(1)} %multiply_bitcast_fusion.1), kind=kLoop, calls=%fused_computation.10 | loop fusion | flops 262144 | bytes 2105344 | tf_op jit(solution)/shard_map/sub | solution.py:120
  33.4 1.5 %copy.125 = f32[128,2048]{0,1:T(8,128)S(1)} copy(f32[128,2048]{1,0:T(8,128)} %bitcast_subtract_fusion.2) | data formatting | bytes 2097152 | tf_op jit(solution)/shard_map/sub | solution.py:120
  35.0 6.2 %gather_fusion.1 = f32[1024]{0:T(1024)S(1)} fusion(f32[2048]{0:T(1024)S(1)} %multiply_bitcast_fusion.1, s32[1024]{0:T(1024)S(1)} %fusion.32), kind=kCustom, calls=%fused_computation.1 | custom fusion | bytes 12288 | tf_op jit(solution)/shard_map/jit(_take)/gather | solution.py:126
  41.1 0.0 copy-start.5
  41.2 0.0 copy-start.6
  41.2 2.8 %gather_fusion = f32[1024,128]{1,0:T(8,128)S(1)} fusion(f32[128,2048]{0,1:T(8,128)S(1)} %copy.125, s32[1024]{0:T(1024)S(1)} %fusion.32), kind=kCustom, calls=%fused_computation | custom fusion | bytes 1052672 | tf_op jit(solution)/shard_map/jit(_take)/gather | solution.py:122
  44.0 0.0 copy-done.5
  44.0 0.0 copy-done.6
  44.0 1.6 %fusion.20 = f32[128,128]{1,0:T(8,128)S(1)} fusion(f32[1024,128]{1,0:T(8,128)S(1)} %gather_fusion, f32[1024]{0:T(1024)S(1)} %get-tuple-element.14, pred[1024]{0:T(1024)(128)(4,1)S(1)} %get-tuple-element.3), kind=kOutput, calls=%fused_computation.45 | convolution fusion | flops 201588736 | bytes 594944 | tf_op jit(solution)/shard_map/dot_general | solution.py:129
  45.7 0.6 fusion.17
  46.3 6.3 %collective-permute-start.10 = (f32[129,128]{1,0:T(8,128)S(1)}, f32[129,128]{1,0:T(8,128)S(1)}, u32[]{:S(2)}, u32[]{:S(2)}) collective-permute-start(f32[129,128]{1,0:T(8,128)S(1)} %pad_maximum_fusion.16), channel_id=1, source_target_pairs={{0,12},{4,8},{8,4},{12,0},{16,28},{20,24},{24,20},{28,16},{1,13},{... | collective-permute-start | bytes 198152 | tf_op jit(solution)/shard_map/ppermute | solution.py:51
  52.6 0.4 collective-permute-start.8
  52.9 0.1 collective-permute-start.9
  53.1 2.1 %collective-permute-done.10 = f32[129,128]{1,0:T(8,128)S(1)} collective-permute-done((f32[129,128]{1,0:T(8,128)S(1)}, f32[129,128]{1,0:T(8,128)S(1)}, u32[]{:S(2)}, u32[]{:S(2)}) %collective-permute-start.10) | collective-permute-done | bytes 66080 | tf_op jit(solution)/shard_map/ppermute | solution.py:51
  55.2 0.0 collective-permute-done.8
  55.2 2.1 %collective-permute-done.9 = f32[129,128]{1,0:T(8,128)S(1)} collective-permute-done((f32[129,128]{1,0:T(8,128)S(1)}, f32[129,128]{1,0:T(8,128)S(1)}, u32[]{:S(2)}, u32[]{:S(2)}) %collective-permute-start.9) | collective-permute-done | bytes 66080 | tf_op jit(solution)/shard_map/ppermute | solution.py:51
  57.3 0.0 copy-start.2
  57.3 3.5 %collective-permute-start.11 = (f32[129,128]{1,0:T(8,128)S(1)}, f32[129,128]{1,0:T(8,128)S(1)}, u32[]{:S(2)}, u32[]{:S(2)}) collective-permute-start(f32[129,128]{1,0:T(8,128)S(1)} %add_add_fusion.1), channel_id=1, source_target_pairs={{0,16},{4,20},{8,24},{12,28},{16,0},{20,4},{24,8},{28,12},{1,17},{... | collective-permute-start | bytes 198152 | tf_op jit(solution)/shard_map/ppermute | solution.py:51
  60.8 0.1 reduce_sum.19
  60.9 2.3 %collective-permute-done.11 = f32[129,128]{1,0:T(8,128)S(1)} collective-permute-done((f32[129,128]{1,0:T(8,128)S(1)}, f32[129,128]{1,0:T(8,128)S(1)}, u32[]{:S(2)}, u32[]{:S(2)}) %collective-permute-start.11) | collective-permute-done | bytes 66080 | tf_op jit(solution)/shard_map/ppermute | solution.py:51
  63.3 2.4 %collective-permute-start.12 = (f32[129,128]{1,0:T(8,128)S(1)}, f32[129,128]{1,0:T(8,128)S(1)}, u32[]{:S(2)}, u32[]{:S(2)}) collective-permute-start(f32[129,128]{1,0:T(8,128)S(1)} %add.106), channel_id=1, source_target_pairs={{0,1},{1,0},{2,3},{3,2},{4,5},{5,4},{6,7},{7,6},{8,9},{9,8},{10,11... | collective-permute-start | bytes 198152 | tf_op jit(solution)/shard_map/ppermute | solution.py:51
  65.6 3.0 %collective-permute-start.13 = (f32[129,128]{1,0:T(8,128)S(1)}, f32[129,128]{1,0:T(8,128)S(1)}, u32[]{:S(2)}, u32[]{:S(2)}) collective-permute-start(f32[129,128]{1,0:T(8,128)S(1)} %add.106), channel_id=1, source_target_pairs={{0,2},{1,3},{2,0},{3,1},{4,6},{5,7},{6,4},{7,5},{8,10},{9,11},{10,... | collective-permute-start | bytes 198152 | tf_op jit(solution)/shard_map/ppermute | solution.py:51
  68.6 0.0 collective-permute-start.14
  68.6 0.0 collective-permute-done.12
  68.6 4.6 %collective-permute-done.13 = f32[129,128]{1,0:T(8,128)S(1)} collective-permute-done((f32[129,128]{1,0:T(8,128)S(1)}, f32[129,128]{1,0:T(8,128)S(1)}, u32[]{:S(2)}, u32[]{:S(2)}) %collective-permute-start.13) | collective-permute-done | bytes 66080 | tf_op jit(solution)/shard_map/ppermute | solution.py:51
  73.3 1.5 %collective-permute-done.14 = f32[129,128]{1,0:T(8,128)S(1)} collective-permute-done((f32[129,128]{1,0:T(8,128)S(1)}, f32[129,128]{1,0:T(8,128)S(1)}, u32[]{:S(2)}, u32[]{:S(2)}) %collective-permute-start.14) | collective-permute-done | bytes 66080 | tf_op jit(solution)/shard_map/ppermute | solution.py:51
  74.8 0.6 slice_add_fusion.gram_ref
  75.4 16.2 %shard_map.68 = f32[128,128]{1,0:T(8,128)} custom-call(f32[128,128]{1,0:T(8,128)} %slice_add_fusion.gram_ref), custom_call_target="tpu_custom_call" | custom-call | tf_op jit(solution)/shard_map/pallas_call | solution.py:84
  91.6 1.1 %convolution_bitcast_fusion.1 = f32[128,1]{0,1:T(1,128)S(1)} fusion(f32[128,128]{1,0:T(8,128)} %shard_map.68, f32[129,128]{1,0:T(8,128)S(1)} %add_add_fusion), kind=kOutput, calls=%fused_computation.7 | convolution fusion | flops 196608 | bytes 66560 | tf_op jit(solution)/shard_map/dot_general | solution.py:137
  92.7 0.0 copy-done.3
  92.7 0.2 convolution_bitcast_fusion
  92.9 0.0 copy-done.2
  92.9 1.3 %fusion = f32[16,8,16,128]{3,1,2,0:T(8,128)S(1)} fusion(f32[2048]{0:T(1024)S(1)} %multiply_bitcast_fusion.1, f32[128,128]{1,0:T(8,128)S(1)} %copy-done.3, f32[128]{0:T(128)S(1)} %convolution_bitcast_fusion, f32[16,8,16,128]{3,2,1,0:T(8,128)S(1)} %bitcast.40), kind=kOutput, calls=%fused_computation.4 | convolution fusion | flops 403193856 | bytes 2171392 | tf_op jit(solution)/shard_map/dot_general | solution.py:140
  94.2 1.3 %fusion.1 = f32[16,8,16,128]{3,1,2,0:T(8,128)S(1)} fusion(f32[16,8,16,128]{3,2,1,0:T(8,128)S(1)} %bitcast.38, f32[2048]{0:T(1024)S(1)} %multiply_bitcast_fusion, f32[128,128]{1,0:T(8,128)S(1)} %copy-done.3, f32[128]{0:T(128)S(1)} %convolution_bitcast_fusion), kind=kOutput, calls=%fused_computation.5 | convolution fusion | flops 403193856 | bytes 2171392 | tf_op jit(solution)/shard_map/dot_general | solution.py:143
  95.6 1.2 %copy.129 = f32[16,8,16,128]{3,2,1,0:T(8,128)} copy(f32[16,8,16,128]{3,1,2,0:T(8,128)S(1)} %fusion.1) | data formatting | bytes 2097152
  96.7 1.2 %copy.127 = f32[16,8,16,128]{3,2,1,0:T(8,128)} copy(f32[16,8,16,128]{3,1,2,0:T(8,128)S(1)} %fusion) | data formatting | bytes 2097152
  (13 shorter events, 0.1 us)
Async XLA Ops:
  2.5 12.3 %copy-start = (f32[128,16,128]{2,1,0:T(8,128)S(1)}, f32[128,16,128]{2,1,0:T(8,128)}, u32[]{:S(2)}) copy-start(f32[128,16,128]{2,1,0:T(8,128)} %param.6) | copy-start | bytes 3145732
  2.6 4.5 %collective-permute-start = (f32[128,1,128]{0,1,2:T(1,128)S(1)}, f32[128,1,128]{0,1,2:T(1,128)S(1)}, u32[]{:S(2)}, u32[]{:S(2)}) collective-permute-start(f32[128,1,128]{0,1,2:T(1,128)S(1)} %get-tuple-element.13), channel_id=1, source_target_pairs={{4,0},{8,4},{12,8},{16,12},{20,16},{24,20},{28,24},{5,1},{9,5},{13... | collective-permute-start | bytes 196616 | tf_op jit(solution)/shard_map/ppermute | solution.py:22
  4.0 3.9 %collective-permute-start.1 = (f32[128,1,128]{0,1,2:T(1,128)S(1)}, f32[128,1,128]{0,1,2:T(1,128)S(1)}, u32[]{:S(2)}, u32[]{:S(2)}) collective-permute-start(f32[128,1,128]{0,1,2:T(1,128)S(1)} %get-tuple-element.12), channel_id=1, source_target_pairs={{0,4},{4,8},{8,12},{12,16},{16,20},{20,24},{24,28},{1,5},{5,9},{9,... | collective-permute-start | bytes 196616 | tf_op jit(solution)/shard_map/ppermute | solution.py:19
  8.0 7.6 %collective-permute-start.2 = (f32[128,18,1]{0,1,2:T(8,128)S(1)}, f32[128,18,1]{0,1,2:T(8,128)S(1)}, u32[]{:S(2)}, u32[]{:S(2)}) collective-permute-start(f32[128,18,1]{0,1,2:T(8,128)S(1)} %get-tuple-element.8), channel_id=1, source_target_pairs={{1,0},{2,1},{3,2},{5,4},{6,5},{7,6},{9,8},{10,9},{11,10},{13,12},{... | collective-permute-start | bytes 27656 | tf_op jit(solution)/shard_map/ppermute | solution.py:22
  9.2 7.0 %collective-permute-start.3 = (f32[128,18,1]{0,1,2:T(8,128)S(1)}, f32[128,18,1]{0,1,2:T(8,128)S(1)}, u32[]{:S(2)}, u32[]{:S(2)}) collective-permute-start(f32[128,18,1]{0,1,2:T(8,128)S(1)} %get-tuple-element.9), channel_id=1, source_target_pairs={{0,1},{1,2},{2,3},{4,5},{5,6},{6,7},{8,9},{9,10},{10,11},{12,13},{... | collective-permute-start | bytes 27656 | tf_op jit(solution)/shard_map/ppermute | solution.py:19
  16.9 4.7 %collective-permute-start.4 = (f32[128,1,128]{0,1,2:T(1,128)S(1)}, f32[128,1,128]{0,1,2:T(1,128)S(1)}, u32[]{:S(2)}, u32[]{:S(2)}) collective-permute-start(f32[128,1,128]{0,1,2:T(1,128)S(1)} %get-tuple-element.11), channel_id=1, source_target_pairs={{4,0},{8,4},{12,8},{16,12},{20,16},{24,20},{28,24},{5,1},{9,5},{13... | collective-permute-start | bytes 196616 | tf_op jit(solution)/shard_map/ppermute | solution.py:22
  18.2 4.3 %collective-permute-start.5 = (f32[128,1,128]{0,1,2:T(1,128)S(1)}, f32[128,1,128]{0,1,2:T(1,128)S(1)}, u32[]{:S(2)}, u32[]{:S(2)}) collective-permute-start(f32[128,1,128]{0,1,2:T(1,128)S(1)} %get-tuple-element.10), channel_id=1, source_target_pairs={{0,4},{4,8},{8,12},{12,16},{16,20},{20,24},{24,28},{1,5},{5,9},{9,... | collective-permute-start | bytes 196616 | tf_op jit(solution)/shard_map/ppermute | solution.py:19
  22.5 5.9 %copy-start.4 = (s32[1024]{0:T(1024)S(1)}, s32[1024]{0:T(1024)}, u32[]{:S(2)}) copy-start(s32[1024]{0:T(1024)} %param.9) | copy-start | bytes 12292
  22.5 5.9 %collective-permute-start.6 = (f32[128,18,1]{0,1,2:T(8,128)S(1)}, f32[128,18,1]{0,1,2:T(8,128)S(1)}, u32[]{:S(2)}, u32[]{:S(2)}) collective-permute-start(f32[128,18,1]{0,1,2:T(8,128)S(1)} %get-tuple-element.6), channel_id=1, source_target_pairs={{1,0},{2,1},{3,2},{5,4},{6,5},{7,6},{9,8},{10,9},{11,10},{13,12},{... | collective-permute-start | bytes 27656 | tf_op jit(solution)/shard_map/ppermute | solution.py:22
  23.8 5.9 %collective-permute-start.7 = (f32[128,18,1]{0,1,2:T(8,128)S(1)}, f32[128,18,1]{0,1,2:T(8,128)S(1)}, u32[]{:S(2)}, u32[]{:S(2)}) collective-permute-start(f32[128,18,1]{0,1,2:T(8,128)S(1)} %get-tuple-element.7), channel_id=1, source_target_pairs={{0,1},{1,2},{2,3},{4,5},{5,6},{6,7},{8,9},{9,10},{10,11},{12,13},{... | collective-permute-start | bytes 27656 | tf_op jit(solution)/shard_map/ppermute | solution.py:19
  31.1 1.0 copy-start.1
  41.1 2.8 %copy-start.5 = (f32[1024]{0:T(1024)S(1)}, f32[1024]{0:T(1024)}, u32[]{:S(2)}) copy-start(f32[1024]{0:T(1024)} %param.7) | copy-start | bytes 12292
  41.2 2.8 %copy-start.6 = (f32[1024]{0:T(1024)S(1)}, f32[1024]{0:T(1024)}, u32[]{:S(2)}) copy-start(f32[1024]{0:T(1024)} %param.8) | copy-start | bytes 12292
  46.3 8.9 %collective-permute-start.10 = (f32[129,128]{1,0:T(8,128)S(1)}, f32[129,128]{1,0:T(8,128)S(1)}, u32[]{:S(2)}, u32[]{:S(2)}) collective-permute-start(f32[129,128]{1,0:T(8,128)S(1)} %pad_maximum_fusion.16), channel_id=1, source_target_pairs={{0,12},{4,8},{8,4},{12,0},{16,28},{20,24},{24,20},{28,16},{1,13},{... | collective-permute-start | bytes 198152 | tf_op jit(solution)/shard_map/ppermute | solution.py:51
  52.6 2.6 %collective-permute-start.8 = (f32[129,128]{1,0:T(8,128)S(1)}, f32[129,128]{1,0:T(8,128)S(1)}, u32[]{:S(2)}, u32[]{:S(2)}) collective-permute-start(f32[129,128]{1,0:T(8,128)S(1)} %pad_maximum_fusion.16), channel_id=1, source_target_pairs={{0,4},{4,0},{8,12},{12,8},{16,20},{20,16},{24,28},{28,24},{1,5},{5... | collective-permute-start | bytes 198152 | tf_op jit(solution)/shard_map/ppermute | solution.py:51
  52.9 4.3 %collective-permute-start.9 = (f32[129,128]{1,0:T(8,128)S(1)}, f32[129,128]{1,0:T(8,128)S(1)}, u32[]{:S(2)}, u32[]{:S(2)}) collective-permute-start(f32[129,128]{1,0:T(8,128)S(1)} %pad_maximum_fusion.16), channel_id=1, source_target_pairs={{0,8},{4,12},{8,0},{12,4},{16,24},{20,28},{24,16},{28,20},{1,9},{5... | collective-permute-start | bytes 198152 | tf_op jit(solution)/shard_map/ppermute | solution.py:51
  57.3 35.6 %copy-start.2 = (f32[128,16,128]{2,1,0:T(8,128)S(1)}, f32[128,16,128]{2,1,0:T(8,128)}, u32[]{:S(2)}) copy-start(f32[128,16,128]{2,1,0:T(8,128)} %copy-done.1) | copy-start | bytes 3145732
  57.3 6.0 %collective-permute-start.11 = (f32[129,128]{1,0:T(8,128)S(1)}, f32[129,128]{1,0:T(8,128)S(1)}, u32[]{:S(2)}, u32[]{:S(2)}) collective-permute-start(f32[129,128]{1,0:T(8,128)S(1)} %add_add_fusion.1), channel_id=1, source_target_pairs={{0,16},{4,20},{8,24},{12,28},{16,0},{20,4},{24,8},{28,12},{1,17},{... | collective-permute-start | bytes 198152 | tf_op jit(solution)/shard_map/ppermute | solution.py:51
  63.3 5.4 %collective-permute-start.12 = (f32[129,128]{1,0:T(8,128)S(1)}, f32[129,128]{1,0:T(8,128)S(1)}, u32[]{:S(2)}, u32[]{:S(2)}) collective-permute-start(f32[129,128]{1,0:T(8,128)S(1)} %add.106), channel_id=1, source_target_pairs={{0,1},{1,0},{2,3},{3,2},{4,5},{5,4},{6,7},{7,6},{8,9},{9,8},{10,11... | collective-permute-start | bytes 198152 | tf_op jit(solution)/shard_map/ppermute | solution.py:51
  65.6 7.7 %collective-permute-start.13 = (f32[129,128]{1,0:T(8,128)S(1)}, f32[129,128]{1,0:T(8,128)S(1)}, u32[]{:S(2)}, u32[]{:S(2)}) collective-permute-start(f32[129,128]{1,0:T(8,128)S(1)} %add.106), channel_id=1, source_target_pairs={{0,2},{1,3},{2,0},{3,1},{4,6},{5,7},{6,4},{7,5},{8,10},{9,11},{10,... | collective-permute-start | bytes 198152 | tf_op jit(solution)/shard_map/ppermute | solution.py:51
  68.6 6.1 %collective-permute-start.14 = (f32[129,128]{1,0:T(8,128)S(1)}, f32[129,128]{1,0:T(8,128)S(1)}, u32[]{:S(2)}, u32[]{:S(2)}) collective-permute-start(f32[129,128]{1,0:T(8,128)S(1)} %add.106), channel_id=1, source_target_pairs={{0,3},{1,2},{2,1},{3,0},{4,7},{5,6},{6,5},{7,4},{8,11},{9,10},{10,... | collective-permute-start | bytes 198152 | tf_op jit(solution)/shard_map/ppermute | solution.py:51
  91.6 1.1 %copy-start.3 = (f32[128,128]{1,0:T(8,128)S(1)}, f32[128,128]{1,0:T(8,128)}, u32[]{:S(2)}) copy-start(f32[128,128]{1,0:T(8,128)} %shard_map.68) | copy-start | bytes 196612

commit v5 on v4

--- a/solution.py
+++ b/solution.py
@@ -112,22 +112,42 @@
     for section in range(2):
         bordered_vector = with_halo(predicted_vector, (("gx", 1), ("gy", 2)), 1)
         predicted_vector = propagate_model(bordered_vector, fire_power_output)
-    grid_points_number = block_height_number * block_width_number
-    warmth_vectorised = predicted_vector.reshape(sample_number, grid_points_number)
-    heat_flat = fire_power_output.reshape(sample_number, grid_points_number)
-    average_gas_warmth = jnp.mean(warmth_vectorised, axis=0)
-    mean_heat = jnp.mean(heat_flat, axis=0)
-    sample_deviation_matrix = warmth_vectorised - average_gas_warmth
-    heat_anomaly = heat_flat - mean_heat
-    picked = jnp.take(sample_deviation_matrix, reading_local_location, axis=1)
+    average_gas_warmth = jnp.mean(predicted_vector, axis=0)
+    mean_heat = jnp.mean(fire_power_output, axis=0)
+    sample_deviation_matrix = predicted_vector - average_gas_warmth
+    heat_anomaly = fire_power_output - mean_heat
     coefficient_line = 1.0 / (reading_noise_spread * math.sqrt(sample_number - 1))
-    s_matrix = picked * coefficient_line
-    measurement_residual = (
-        measured_warmth - jnp.take(average_gas_warmth, reading_local_location)
-    ) * coefficient_line
+    weight_line = coefficient_line * coefficient_line
+    row_hot = (
+        (reading_local_location // block_width_number)[:, None]
+        == lax.broadcasted_iota(jnp.int32, (1, block_height_number), 1)
+    ).astype(jnp.float32)
+    col_hot = (
+        (reading_local_location % block_width_number)[:, None]
+        == lax.broadcasted_iota(jnp.int32, (1, block_width_number), 1)
+    ).astype(jnp.float32)
+    weighted_rows = jnp.concatenate(
+        [row_hot * weight_line[:, None], row_hot * (weight_line * measured_warmth)[:, None]],
+        axis=1,
+    )
+    cell_sums = lax.dot_general(
+        weighted_rows, col_hot, (((0,), (0,)), ((), ())), precision=lax.Precision.HIGHEST
+    )
+    cell_weight = cell_sums[:block_height_number]
+    cell_residual = cell_sums[block_height_number:] - average_gas_warmth * cell_weight
+    gram_local = lax.dot_general(
+        sample_deviation_matrix * cell_weight,
+        sample_deviation_matrix,
+        (((1, 2), (1, 2)), ((), ())),
+        precision=lax.Precision.HIGHEST,
+    )
+    projected = lax.dot_general(
+        sample_deviation_matrix,
+        cell_residual,
+        (((1, 2), (0, 1)), ((), ())),
+        precision=lax.Precision.HIGHEST,
+    )
     identity = jnp.eye(sample_number, dtype=jnp.float32)
-    gram_local = jnp.dot(s_matrix, s_matrix.T, precision=lax.Precision.HIGHEST)
-    projected = jnp.dot(s_matrix, measurement_residual, precision=lax.Precision.HIGHEST)
     stacked = butterfly_sum(
         jnp.concatenate([gram_local, projected[None, :]], axis=0), ("gx", "gy")
     )
@@ -137,16 +157,14 @@
     whitened = jnp.dot(lower_inverse, projected_sum, precision=lax.Precision.HIGHEST)
     mean_weights = jnp.dot(lower_inverse.T, whitened, precision=lax.Precision.HIGHEST)
     combination_transposed = lower_inverse + mean_weights[None, :]
-    updated_warmth = average_gas_warmth + jnp.dot(
-        combination_transposed, sample_deviation_matrix, precision=lax.Precision.HIGHEST
+    contract = (((1,), (0,)), ((), ()))
+    updated_warmth = average_gas_warmth + lax.dot_general(
+        combination_transposed, sample_deviation_matrix, contract, precision=lax.Precision.HIGHEST
     )
-    heat_out = mean_heat + jnp.dot(
-        combination_transposed, heat_anomaly, precision=lax.Precision.HIGHEST
+    heat_out = mean_heat + lax.dot_general(
+        combination_transposed, heat_anomaly, contract, precision=lax.Precision.HIGHEST
     )
-    return (
-        updated_warmth.reshape(sample_number, block_height_number, block_width_number),
-        heat_out.reshape(sample_number, block_height_number, block_width_number),
-    )
+    return (updated_warmth, heat_out)
 
 
 def solution(mesh):

time: 98.4 us -> 100 us (1.016)
  other arithmetic: 3.52 us -> 6.47 us
  starting transfers between devices: 37.4 us -> 34.6 us
  matrix products: 6.16 us -> 7.68 us
    gather x2 -> x0, local copies, waits for them, and re-layouts: 8.96 us -> none  [the longest x1 6.15 us: shards(): jnp.take(average_gas_warmth, reading_local_location)]
    ppermute x0 -> x4, local copies, waits for them, and re-layouts: none -> 5.8 us  [the longest x2 2.92 us: with_halo(): lax.ppermute(lax.slice_in_dim(block, block.shape[dim] - width, None, axis...]
    slice x0 -> x5, local copies, waits for them, and re-layouts: none -> 4.25 us  [with_halo(): lax.slice_in_dim(block, 0, width, axis=dim)]
    ppermute x4, waiting for transfers between devices: 0.01 us -> 3.58 us  [with_halo(): lax.ppermute(lax.slice_in_dim(block, 0, width, axis=dim), axis, backward)]
    ppermute x4, waiting for transfers between devices: 3.76 us -> 0.23 us  [with_halo(): lax.ppermute(lax.slice_in_dim(block, block.shape[dim] - width, None, axis...]
    ppermute x7, starting transfers between devices: 15.6 us -> 12.8 us  [butterfly_sum(): received[offset] = lax.ppermute(value, axis, pairs)]
    slice x2 -> x3, local copies, waits for them, and re-layouts: 0.19 us -> 2.01 us  [with_halo(): lax.slice_in_dim(block, block.shape[dim] - width, None, axis=dim)]
    add x1, other arithmetic: 0.6 us -> 2.42 us  [propagate_model(): padded_field[:, 1:-1, 1:-1] + diffusion * laplacian + heating * source_term]
  transfers between devices with their start and end apart: 15 -> 15, of which waited for: 9 -> 7; matrix products, arithmetic and copies ran while one was open for 1% -> 6% of each run, Pallas kernels for 0% -> 0%
where the time goes in v5:
time: 100 us; the launch traced here: 99.4 us
  starting transfers between devices  34.6 us (35%)
  local copies, waits for them, and re-layouts  17.2 us (17%)
  waiting for transfers between devices  16.2 us (16%)
  Pallas kernels  16.2 us (16%)
  matrix products  7.68 us (8%)
  other arithmetic  6.47 us (6%)
    ppermute x4, starting transfers between devices, with_halo(): lax.ppermute(lax.slice_in_dim(block, block.shape[dim] - width, None, axis...  16.5 us
    pallas_call x1, Pallas kernels, inverse_factor(): pl.pallas_call(inverse_factor_kernel, out_shape=jax.ShapeDtypeStruct((siz...  16.2 us
    ppermute x7, starting transfers between devices, butterfly_sum(): received[offset] = lax.ppermute(value, axis, pairs)  12.8 us
    ppermute x7, waiting for transfers between devices, butterfly_sum(): received[offset] = lax.ppermute(value, axis, pairs)  12.4 us
    ppermute x4, starting transfers between devices, with_halo(): lax.ppermute(lax.slice_in_dim(block, 0, width, axis=dim), axis, backward)  5.3 us
    unnamed x25, local copies, waits for them, and re-layouts  5.17 us
    slice x5, local copies, waits for them, and re-layouts, with_halo(): lax.slice_in_dim(block, 0, width, axis=dim)  4.25 us
    ppermute x4, waiting for transfers between devices, with_halo(): lax.ppermute(lax.slice_in_dim(block, 0, width, axis=dim), axis, backward)  3.58 us
  transfers between devices with their start and end apart: 15, of which 7 were waited for; matrix products, arithmetic and copies ran while one was open for 6% of the time, Pallas kernels for 0%

profile of v5, /device:TPU:0, one launch (start us, length us, event | category | flops | bytes accessed | tf_op | source)
XLA Modules:
  0.0 99.4 jit_solution(6791543211752121543)
XLA Ops:
  0.6 0.0 copy-start.3
  0.6 0.0 copy-start.9
  0.6 0.0 copy-start.8
  0.7 1.6 %copy.28 = f32[128,16,128]{2,0,1:T(8,128)S(1)} copy(f32[128,16,128]{2,1,0:T(8,128)} %param.5) | data formatting | bytes 2097152 | tf_op args[0]
  2.3 2.4 %collective-permute-start.1 = (f32[128,1,128]{2,0,1:T(8,128)S(1)}, f32[128,1,128]{2,0,1:T(8,128)S(1)}, u32[]{:S(2)}, u32[]{:S(2)}) collective-permute-start(f32[128,1,128]{2,0,1:T(8,128)S(1)} %get-tuple-element.15), channel_id=1, source_target_pairs={{0,4},{4,8},{8,12},{12,16},{16,20},{20,24},{24,28},{1,5},{5,9},{9,... | collective-permute-start | bytes 196616 | tf_op jit(solution)/shard_map/ppermute | solution.py:19
  4.7 1.3 %collective-permute-start = (f32[128,1,128]{2,0,1:T(8,128)S(1)}, f32[128,1,128]{2,0,1:T(8,128)S(1)}, u32[]{:S(2)}, u32[]{:S(2)}) collective-permute-start(f32[128,1,128]{2,0,1:T(8,128)S(1)} %get-tuple-element.14), channel_id=1, source_target_pairs={{4,0},{8,4},{12,8},{16,12},{20,16},{24,20},{28,24},{5,1},{9,5},{13... | collective-permute-start | bytes 196616 | tf_op jit(solution)/shard_map/ppermute | solution.py:22
  6.0 0.0 collective-permute-done.1
  6.1 0.3 constant_dynamic-update-slice_fusion.1
  6.4 3.6 %collective-permute-done = f32[128,1,128]{2,0,1:T(8,128)S(1)} collective-permute-done((f32[128,1,128]{2,0,1:T(8,128)S(1)}, f32[128,1,128]{2,0,1:T(8,128)S(1)}, u32[]{:S(2)}, u32[]{:S(2)}) %collective-permute-start) | collective-permute-done | bytes 65568 | tf_op jit(solution)/shard_map/ppermute | solution.py:22
  10.0 1.8 %fusion.50 = (f32[128,18,1]{2,0,1:T(8,128)}, f32[128,18,1]{2,0,1:T(8,128)}) fusion(f32[128,18,128]{2,0,1:T(8,128)S(1)} %constant_dynamic-update-slice_fusion), kind=kLoop, calls=%fused_computation.87 | loop fusion | bytes 36864 | tf_op jit(solution)/shard_map/slice | solution.py:22
  11.8 1.6 %copy.23 = f32[128,18,1]{0,2,1:T(1,128)S(1)} copy(f32[128,18,1]{2,0,1:T(8,128)} %get-tuple-element.10) | data formatting | bytes 18432 | tf_op jit(solution)/shard_map/slice | solution.py:22
  13.4 1.3 %collective-permute-start.2 = (f32[128,18,1]{0,2,1:T(1,128)S(1)}, f32[128,18,1]{0,2,1:T(1,128)S(1)}, u32[]{:S(2)}, u32[]{:S(2)}) collective-permute-start(f32[128,18,1]{0,2,1:T(1,128)S(1)} %copy.23), channel_id=1, source_target_pairs={{1,0},{2,1},{3,2},{5,4},{6,5},{7,6},{9,8},{10,9},{11,10},{13,12},{... | collective-permute-start | bytes 27656 | tf_op jit(solution)/shard_map/ppermute | solution.py:22
  14.7 1.6 %copy.25 = f32[128,18,1]{0,2,1:T(1,128)S(1)} copy(f32[128,18,1]{2,0,1:T(8,128)} %get-tuple-element.11) | data formatting | bytes 18432 | tf_op jit(solution)/shard_map/slice | solution.py:20
  16.4 4.5 %collective-permute-start.3 = (f32[128,18,1]{0,2,1:T(1,128)S(1)}, f32[128,18,1]{0,2,1:T(1,128)S(1)}, u32[]{:S(2)}, u32[]{:S(2)}) collective-permute-start(f32[128,18,1]{0,2,1:T(1,128)S(1)} %copy.25), channel_id=1, source_target_pairs={{0,1},{1,2},{2,3},{4,5},{5,6},{6,7},{8,9},{9,10},{10,11},{12,13},{... | collective-permute-start | bytes 27656 | tf_op jit(solution)/shard_map/ppermute | solution.py:19
  20.9 0.0 copy-start
  21.0 0.0 collective-permute-done.2
  21.0 1.4 %copy.24 = f32[128,18,1]{2,0,1:T(8,128)} copy(f32[128,18,1]{0,2,1:T(1,128)S(1)} %collective-permute-done.2) | data formatting | bytes 18432 | tf_op jit(solution)/shard_map/ppermute | solution.py:22
  22.4 0.0 collective-permute-done.3
  22.4 1.5 %copy.26 = f32[128,18,1]{2,0,1:T(8,128)} copy(f32[128,18,1]{0,2,1:T(1,128)S(1)} %collective-permute-done.3) | data formatting | bytes 18432 | tf_op jit(solution)/shard_map/ppermute | solution.py:19
  23.9 2.4 %fusion.16 = f32[128,16,128]{2,0,1:T(8,128)S(1)} fusion(f32[128,16,128]{2,0,1:T(8,128)S(1)} %copy.28, f32[128,18,128]{2,0,1:T(8,128)S(1)} %constant_dynamic-update-slice_fusion, f32[128,18,1]{2,0,1:T(8,128)} %copy.26, f32[128,18,1]{2,0,1:T(8,128)} %copy.24, f32[128,1,128]{2,0,1:T(8,128)S(1)} %collective-permute-done.1, ...), kind=kLoop, calls=%fused_computation.29 | loop fusion | flops 3407872 | bytes 4474880 | tf_op jit(solution)/shard_map/add | solution.py:100
  26.3 0.0 copy-start.1
  26.3 1.3 %collective-permute-start.4 = (f32[128,1,128]{2,0,1:T(8,128)S(1)}, f32[128,1,128]{2,0,1:T(8,128)S(1)}, u32[]{:S(2)}, u32[]{:S(2)}) collective-permute-start(f32[128,1,128]{2,0,1:T(8,128)S(1)} %get-tuple-element.13), channel_id=1, source_target_pairs={{4,0},{8,4},{12,8},{16,12},{20,16},{24,20},{28,24},{5,1},{9,5},{13... | collective-permute-start | bytes 196616 | tf_op jit(solution)/shard_map/ppermute | solution.py:22
  27.6 4.9 %collective-permute-start.5 = (f32[128,1,128]{2,0,1:T(8,128)S(1)}, f32[128,1,128]{2,0,1:T(8,128)S(1)}, u32[]{:S(2)}, u32[]{:S(2)}) collective-permute-start(f32[128,1,128]{2,0,1:T(8,128)S(1)} %get-tuple-element.12), channel_id=1, source_target_pairs={{0,4},{4,8},{8,12},{12,16},{16,20},{20,24},{24,28},{1,5},{5,9},{9,... | collective-permute-start | bytes 196616 | tf_op jit(solution)/shard_map/ppermute | solution.py:19
  32.6 0.7 fusion.38
  33.2 0.0 collective-permute-done.4
  33.2 0.2 collective-permute-done.5
  33.4 0.1 pad_maximum_fusion
  33.5 0.4 fusion.49
  33.9 0.4 copy.30
  34.3 1.4 %collective-permute-start.6 = (f32[128,18,1]{0,2,1:T(1,128)S(1)}, f32[128,18,1]{0,2,1:T(1,128)S(1)}, u32[]{:S(2)}, u32[]{:S(2)}) collective-permute-start(f32[128,18,1]{0,2,1:T(1,128)S(1)} %copy.30), channel_id=1, source_target_pairs={{1,0},{2,1},{3,2},{5,4},{6,5},{7,6},{9,8},{10,9},{11,10},{13,12},{... | collective-permute-start | bytes 27656 | tf_op jit(solution)/shard_map/ppermute | solution.py:22
  35.7 0.4 copy.32
  36.1 4.7 %collective-permute-start.7 = (f32[128,18,1]{0,2,1:T(1,128)S(1)}, f32[128,18,1]{0,2,1:T(1,128)S(1)}, u32[]{:S(2)}, u32[]{:S(2)}) collective-permute-start(f32[128,18,1]{0,2,1:T(1,128)S(1)} %copy.32), channel_id=1, source_target_pairs={{0,1},{1,2},{2,3},{4,5},{5,6},{6,7},{8,9},{9,10},{10,11},{12,13},{... | collective-permute-start | bytes 27656 | tf_op jit(solution)/shard_map/ppermute | solution.py:19
  40.9 0.4 fusion.29
  41.3 0.0 copy-start.2
  41.3 0.0 collective-permute-done.6
  41.3 1.4 %copy.31 = f32[128,18,1]{2,0,1:T(8,128)} copy(f32[128,18,1]{0,2,1:T(1,128)S(1)} %collective-permute-done.6) | data formatting | bytes 18432 | tf_op jit(solution)/shard_map/ppermute | solution.py:22
  42.7 0.0 collective-permute-done.7
  42.7 1.5 %copy.33 = f32[128,18,1]{2,0,1:T(8,128)} copy(f32[128,18,1]{0,2,1:T(1,128)S(1)} %collective-permute-done.7) | data formatting | bytes 18432 | tf_op jit(solution)/shard_map/ppermute | solution.py:19
  44.2 2.4 %fusion.47 = (f32[16,128]{1,0:T(8,128)S(1)}, f32[128,16,128]{2,0,1:T(8,128)S(1)}) fusion(f32[128,16,128]{2,1,0:T(8,128)S(1)} %copy-done, f32[128,16,128]{2,0,1:T(8,128)S(1)} %copy-done.2, f32[128,1,128]{2,0,1:T(8,128)S(1)} %collective-permute-done.4, f32[128,1,128]{2,0,1:T(8,128)S(1)} %collective-permute-done.5, f32[128,18,1]{2,0,1:T(8,128)} %copy.33, ...), kind=kLoop, calls=%fused_computation.85 | loop fusion | flops 4716544 | bytes 3303424 | tf_op jit(solution)/shard_map/reduce_sum | solution.py:115
  46.7 1.1 %fusion.2 = f32[128,128]{1,0:T(8,128)S(1)} fusion(f32[128,16,128]{2,0,1:T(8,128)S(1)} %get-tuple-element.7, f32[16,128]{1,0:T(8,128)S(1)} %get-tuple-element.16, f32[16,128]{1,0:T(8,128)S(1)} %get-tuple-element.18), kind=kOutput, calls=%fused_computation.5 | convolution fusion | flops 403439616 | bytes 1130496 | tf_op jit(solution)/shard_map/dot_general | solution.py:138
  47.7 0.9 convolution_bitcast_fusion
  48.7 4.6 %collective-permute-start.10 = (f32[129,128]{1,0:T(8,128)S(1)}, f32[129,128]{1,0:T(8,128)S(1)}, u32[]{:S(2)}, u32[]{:S(2)}) collective-permute-start(f32[129,128]{1,0:T(8,128)S(1)} %pad_maximum_fusion.13), channel_id=1, source_target_pairs={{0,12},{4,8},{8,4},{12,0},{16,28},{20,24},{24,20},{28,16},{1,13},{... | collective-permute-start | bytes 198152 | tf_op jit(solution)/shard_map/ppermute | solution.py:51
  53.2 0.0 collective-permute-start.8
  53.3 0.4 collective-permute-start.9
  53.7 2.1 %collective-permute-done.10 = f32[129,128]{1,0:T(8,128)S(1)} collective-permute-done((f32[129,128]{1,0:T(8,128)S(1)}, f32[129,128]{1,0:T(8,128)S(1)}, u32[]{:S(2)}, u32[]{:S(2)}) %collective-permute-start.10) | collective-permute-done | bytes 66080 | tf_op jit(solution)/shard_map/ppermute | solution.py:51
  55.8 0.0 collective-permute-done.8
  55.8 2.1 %collective-permute-done.9 = f32[129,128]{1,0:T(8,128)S(1)} collective-permute-done((f32[129,128]{1,0:T(8,128)S(1)}, f32[129,128]{1,0:T(8,128)S(1)}, u32[]{:S(2)}, u32[]{:S(2)}) %collective-permute-start.9) | collective-permute-done | bytes 66080 | tf_op jit(solution)/shard_map/ppermute | solution.py:51
  57.9 3.3 %collective-permute-start.11 = (f32[129,128]{1,0:T(8,128)S(1)}, f32[129,128]{1,0:T(8,128)S(1)}, u32[]{:S(2)}, u32[]{:S(2)}) collective-permute-start(f32[129,128]{1,0:T(8,128)S(1)} %add_add_fusion.1), channel_id=1, source_target_pairs={{0,16},{4,20},{8,24},{12,28},{16,0},{20,4},{24,8},{28,12},{1,17},{... | collective-permute-start | bytes 198152 | tf_op jit(solution)/shard_map/ppermute | solution.py:51
  61.1 0.1 reduce_sum.19
  61.3 2.3 %collective-permute-done.11 = f32[129,128]{1,0:T(8,128)S(1)} collective-permute-done((f32[129,128]{1,0:T(8,128)S(1)}, f32[129,128]{1,0:T(8,128)S(1)}, u32[]{:S(2)}, u32[]{:S(2)}) %collective-permute-start.11) | collective-permute-done | bytes 66080 | tf_op jit(solution)/shard_map/ppermute | solution.py:51
  63.6 1.6 %collective-permute-start.12 = (f32[129,128]{1,0:T(8,128)S(1)}, f32[129,128]{1,0:T(8,128)S(1)}, u32[]{:S(2)}, u32[]{:S(2)}) collective-permute-start(f32[129,128]{1,0:T(8,128)S(1)} %add.100), channel_id=1, source_target_pairs={{0,1},{1,0},{2,3},{3,2},{4,5},{5,4},{6,7},{7,6},{8,9},{9,8},{10,11... | collective-permute-start | bytes 198152 | tf_op jit(solution)/shard_map/ppermute | solution.py:51
  65.3 2.6 %collective-permute-start.13 = (f32[129,128]{1,0:T(8,128)S(1)}, f32[129,128]{1,0:T(8,128)S(1)}, u32[]{:S(2)}, u32[]{:S(2)}) collective-permute-start(f32[129,128]{1,0:T(8,128)S(1)} %add.100), channel_id=1, source_target_pairs={{0,2},{1,3},{2,0},{3,1},{4,6},{5,7},{6,4},{7,5},{8,10},{9,11},{10,... | collective-permute-start | bytes 198152 | tf_op jit(solution)/shard_map/ppermute | solution.py:51
  67.8 0.2 collective-permute-start.14
  68.1 0.0 collective-permute-done.12
  68.1 4.5 %collective-permute-done.13 = f32[129,128]{1,0:T(8,128)S(1)} collective-permute-done((f32[129,128]{1,0:T(8,128)S(1)}, f32[129,128]{1,0:T(8,128)S(1)}, u32[]{:S(2)}, u32[]{:S(2)}) %collective-permute-start.13) | collective-permute-done | bytes 66080 | tf_op jit(solution)/shard_map/ppermute | solution.py:51
  72.6 1.5 %collective-permute-done.14 = f32[129,128]{1,0:T(8,128)S(1)} collective-permute-done((f32[129,128]{1,0:T(8,128)S(1)}, f32[129,128]{1,0:T(8,128)S(1)}, u32[]{:S(2)}, u32[]{:S(2)}) %collective-permute-start.14) | collective-permute-done | bytes 66080 | tf_op jit(solution)/shard_map/ppermute | solution.py:51
  74.1 0.6 slice_add_fusion.gram_ref
  74.7 16.2 %shard_map.68 = f32[128,128]{1,0:T(8,128)} custom-call(f32[128,128]{1,0:T(8,128)} %slice_add_fusion.gram_ref), custom_call_target="tpu_custom_call" | custom-call | tf_op jit(solution)/shard_map/pallas_call | solution.py:84
  90.9 1.1 %convolution_bitcast_fusion.2 = f32[128,1]{0,1:T(1,128)S(1)} fusion(f32[128,128]{1,0:T(8,128)} %shard_map.68, f32[129,128]{1,0:T(8,128)S(1)} %add_add_fusion), kind=kOutput, calls=%fused_computation.8 | convolution fusion | flops 196608 | bytes 66560 | tf_op jit(solution)/shard_map/dot_general | solution.py:157
  92.0 1.0 %convolution_bitcast_fusion.1 = f32[128]{0:T(128)S(1)} fusion(f32[128,1]{0,1:T(1,128)S(1)} %convolution_bitcast_fusion.2, f32[128,128]{1,0:T(8,128)} %shard_map.68), kind=kOutput, calls=%fused_computation.7 | convolution fusion | flops 196608 | bytes 66560 | tf_op jit(solution)/shard_map/dot_general | solution.py:158
  93.0 1.9 %convolution_add_fusion.1 = f32[128,16,128]{2,0,1:T(8,128)S(1)} fusion(f32[128,16,128]{2,0,1:T(8,128)S(1)} %get-tuple-element.7, f32[16,128]{1,0:T(8,128)S(1)} %get-tuple-element.18, f32[128,128]{1,0:T(8,128)} %shard_map.68, f32[128]{0:T(128)S(1)} %convolution_bitcast_fusion.1), kind=kOutput, calls=%fused_computation.3 | convolution fusion | flops 403193856 | bytes 2171392 | tf_op jit(solution)/shard_map/dot_general | solution.py:161
  94.9 1.3 %convolution_add_fusion = f32[128,16,128]{2,0,1:T(8,128)S(1)} fusion(f32[128,16,128]{2,1,0:T(8,128)S(1)} %copy-done, f32[16,128]{1,0:T(8,128)S(1)} %broadcast_multiply_fusion, f32[128,128]{1,0:T(8,128)S(1)} %copy-done.4, f32[128]{0:T(128)S(1)} %convolution_bitcast_fusion.1), kind=kOutput, calls=%fused_computation.2 | convolution fusion | flops 403193856 | bytes 2171392 | tf_op jit(solution)/shard_map/dot_general | solution.py:164
  96.2 1.6 %copy.36 = f32[128,16,128]{2,1,0:T(8,128)} copy(f32[128,16,128]{2,0,1:T(8,128)S(1)} %convolution_add_fusion) | data formatting | bytes 2097152
  97.8 1.6 %copy.35 = f32[128,16,128]{2,1,0:T(8,128)} copy(f32[128,16,128]{2,0,1:T(8,128)S(1)} %convolution_add_fusion.1) | data formatting | bytes 2097152
  (26 shorter events, 0.2 us)
Async XLA Ops:
  0.6 5.4 %copy-start.3 = (f32[128,16,128]{2,1,0:T(8,128)S(1)}, f32[128,16,128]{2,1,0:T(8,128)}, u32[]{:S(2)}) copy-start(f32[128,16,128]{2,1,0:T(8,128)} %param.5) | copy-start | bytes 3145732
  0.6 5.4 %copy-start.9 = (f32[1024]{0:T(1024)S(1)}, f32[1024]{0:T(1024)}, u32[]{:S(2)}) copy-start(f32[1024]{0:T(1024)} %param.7) | copy-start | bytes 12292
  0.6 5.4 %copy-start.8 = (f32[1024]{0:T(1024)S(1)}, f32[1024]{0:T(1024)}, u32[]{:S(2)}) copy-start(f32[1024]{0:T(1024)} %param.8) | copy-start | bytes 12292
  2.3 3.7 %collective-permute-start.1 = (f32[128,1,128]{2,0,1:T(8,128)S(1)}, f32[128,1,128]{2,0,1:T(8,128)S(1)}, u32[]{:S(2)}, u32[]{:S(2)}) collective-permute-start(f32[128,1,128]{2,0,1:T(8,128)S(1)} %get-tuple-element.15), channel_id=1, source_target_pairs={{0,4},{4,8},{8,12},{12,16},{16,20},{20,24},{24,28},{1,5},{5,9},{9,... | collective-permute-start | bytes 196616 | tf_op jit(solution)/shard_map/ppermute | solution.py:19
  4.7 5.3 %collective-permute-start = (f32[128,1,128]{2,0,1:T(8,128)S(1)}, f32[128,1,128]{2,0,1:T(8,128)S(1)}, u32[]{:S(2)}, u32[]{:S(2)}) collective-permute-start(f32[128,1,128]{2,0,1:T(8,128)S(1)} %get-tuple-element.14), channel_id=1, source_target_pairs={{4,0},{8,4},{12,8},{16,12},{20,16},{24,20},{28,24},{5,1},{9,5},{13... | collective-permute-start | bytes 196616 | tf_op jit(solution)/shard_map/ppermute | solution.py:22
  11.8 9.1 %copy-start.7 = (s32[1024]{0:T(1024)S(1)}, s32[1024]{0:T(1024)}, u32[]{:S(2)}) copy-start(s32[1024]{0:T(1024)} %param.9) | copy-start | bytes 12292
  13.4 7.5 %collective-permute-start.2 = (f32[128,18,1]{0,2,1:T(1,128)S(1)}, f32[128,18,1]{0,2,1:T(1,128)S(1)}, u32[]{:S(2)}, u32[]{:S(2)}) collective-permute-start(f32[128,18,1]{0,2,1:T(1,128)S(1)} %copy.23), channel_id=1, source_target_pairs={{1,0},{2,1},{3,2},{5,4},{6,5},{7,6},{9,8},{10,9},{11,10},{13,12},{... | collective-permute-start | bytes 27656 | tf_op jit(solution)/shard_map/ppermute | solution.py:22
  16.4 6.0 %collective-permute-start.3 = (f32[128,18,1]{0,2,1:T(1,128)S(1)}, f32[128,18,1]{0,2,1:T(1,128)S(1)}, u32[]{:S(2)}, u32[]{:S(2)}) collective-permute-start(f32[128,18,1]{0,2,1:T(1,128)S(1)} %copy.25), channel_id=1, source_target_pairs={{0,1},{1,2},{2,3},{4,5},{5,6},{6,7},{8,9},{9,10},{10,11},{12,13},{... | collective-permute-start | bytes 27656 | tf_op jit(solution)/shard_map/ppermute | solution.py:19
  20.9 2.9 %copy-start = (f32[128,16,128]{2,1,0:T(8,128)S(1)}, f32[128,16,128]{2,1,0:T(8,128)}, u32[]{:S(2)}) copy-start(f32[128,16,128]{2,1,0:T(8,128)} %param.6) | copy-start | bytes 3145732
  26.3 7.2 %copy-start.1 = (f32[128,16,128]{2,0,1:T(8,128)}, f32[128,16,128]{2,0,1:T(8,128)S(1)}, u32[]{:S(2)}) copy-start(f32[128,16,128]{2,0,1:T(8,128)S(1)} %fusion.16) | copy-start | bytes 3145732
  26.3 6.9 %collective-permute-start.4 = (f32[128,1,128]{2,0,1:T(8,128)S(1)}, f32[128,1,128]{2,0,1:T(8,128)S(1)}, u32[]{:S(2)}, u32[]{:S(2)}) collective-permute-start(f32[128,1,128]{2,0,1:T(8,128)S(1)} %get-tuple-element.13), channel_id=1, source_target_pairs={{4,0},{8,4},{12,8},{16,12},{20,16},{24,20},{28,24},{5,1},{9,5},{13... | collective-permute-start | bytes 196616 | tf_op jit(solution)/shard_map/ppermute | solution.py:22
  27.6 5.8 %collective-permute-start.5 = (f32[128,1,128]{2,0,1:T(8,128)S(1)}, f32[128,1,128]{2,0,1:T(8,128)S(1)}, u32[]{:S(2)}, u32[]{:S(2)}) collective-permute-start(f32[128,1,128]{2,0,1:T(8,128)S(1)} %get-tuple-element.12), channel_id=1, source_target_pairs={{0,4},{4,8},{8,12},{12,16},{16,20},{20,24},{24,28},{1,5},{5,9},{9,... | collective-permute-start | bytes 196616 | tf_op jit(solution)/shard_map/ppermute | solution.py:19
  34.3 6.5 %copy-start.5 = (f32[1024,16]{0,1:T(8,128)S(1)}, f32[1024,16]{0,1:T(8,128)}, u32[]{:S(2)}) copy-start(f32[1024,16]{0,1:T(8,128)} %get-tuple-element.19) | copy-start | bytes 196612
  34.3 6.5 %copy-start.6 = (f32[1024,16]{0,1:T(8,128)S(1)}, f32[1024,16]{0,1:T(8,128)}, u32[]{:S(2)}) copy-start(f32[1024,16]{0,1:T(8,128)} %get-tuple-element.20) | copy-start | bytes 196612
  34.3 7.0 %collective-permute-start.6 = (f32[128,18,1]{0,2,1:T(1,128)S(1)}, f32[128,18,1]{0,2,1:T(1,128)S(1)}, u32[]{:S(2)}, u32[]{:S(2)}) collective-permute-start(f32[128,18,1]{0,2,1:T(1,128)S(1)} %copy.30), channel_id=1, source_target_pairs={{1,0},{2,1},{3,2},{5,4},{6,5},{7,6},{9,8},{10,9},{11,10},{13,12},{... | collective-permute-start | bytes 27656 | tf_op jit(solution)/shard_map/ppermute | solution.py:22
  36.1 6.6 %collective-permute-start.7 = (f32[128,18,1]{0,2,1:T(1,128)S(1)}, f32[128,18,1]{0,2,1:T(1,128)S(1)}, u32[]{:S(2)}, u32[]{:S(2)}) collective-permute-start(f32[128,18,1]{0,2,1:T(1,128)S(1)} %copy.32), channel_id=1, source_target_pairs={{0,1},{1,2},{2,3},{4,5},{5,6},{6,7},{8,9},{9,10},{10,11},{12,13},{... | collective-permute-start | bytes 27656 | tf_op jit(solution)/shard_map/ppermute | solution.py:19
  41.3 2.9 %copy-start.2 = (f32[128,16,128]{2,0,1:T(8,128)S(1)}, f32[128,16,128]{2,0,1:T(8,128)}, u32[]{:S(2)}) copy-start(f32[128,16,128]{2,0,1:T(8,128)} %copy-done.1) | copy-start | bytes 3145732
  48.7 7.1 %collective-permute-start.10 = (f32[129,128]{1,0:T(8,128)S(1)}, f32[129,128]{1,0:T(8,128)S(1)}, u32[]{:S(2)}, u32[]{:S(2)}) collective-permute-start(f32[129,128]{1,0:T(8,128)S(1)} %pad_maximum_fusion.13), channel_id=1, source_target_pairs={{0,12},{4,8},{8,4},{12,0},{16,28},{20,24},{24,20},{28,16},{1,13},{... | collective-permute-start | bytes 198152 | tf_op jit(solution)/shard_map/ppermute | solution.py:51
  53.2 2.5 %collective-permute-start.8 = (f32[129,128]{1,0:T(8,128)S(1)}, f32[129,128]{1,0:T(8,128)S(1)}, u32[]{:S(2)}, u32[]{:S(2)}) collective-permute-start(f32[129,128]{1,0:T(8,128)S(1)} %pad_maximum_fusion.13), channel_id=1, source_target_pairs={{0,4},{4,0},{8,12},{12,8},{16,20},{20,16},{24,28},{28,24},{1,5},{5... | collective-permute-start | bytes 198152 | tf_op jit(solution)/shard_map/ppermute | solution.py:51
  53.3 4.6 %collective-permute-start.9 = (f32[129,128]{1,0:T(8,128)S(1)}, f32[129,128]{1,0:T(8,128)S(1)}, u32[]{:S(2)}, u32[]{:S(2)}) collective-permute-start(f32[129,128]{1,0:T(8,128)S(1)} %pad_maximum_fusion.13), channel_id=1, source_target_pairs={{0,8},{4,12},{8,0},{12,4},{16,24},{20,28},{24,16},{28,20},{1,9},{5... | collective-permute-start | bytes 198152 | tf_op jit(solution)/shard_map/ppermute | solution.py:51
  57.9 5.7 %collective-permute-start.11 = (f32[129,128]{1,0:T(8,128)S(1)}, f32[129,128]{1,0:T(8,128)S(1)}, u32[]{:S(2)}, u32[]{:S(2)}) collective-permute-start(f32[129,128]{1,0:T(8,128)S(1)} %add_add_fusion.1), channel_id=1, source_target_pairs={{0,16},{4,20},{8,24},{12,28},{16,0},{20,4},{24,8},{28,12},{1,17},{... | collective-permute-start | bytes 198152 | tf_op jit(solution)/shard_map/ppermute | solution.py:51
  63.6 4.5 %collective-permute-start.12 = (f32[129,128]{1,0:T(8,128)S(1)}, f32[129,128]{1,0:T(8,128)S(1)}, u32[]{:S(2)}, u32[]{:S(2)}) collective-permute-start(f32[129,128]{1,0:T(8,128)S(1)} %add.100), channel_id=1, source_target_pairs={{0,1},{1,0},{2,3},{3,2},{4,5},{5,4},{6,7},{7,6},{8,9},{9,8},{10,11... | collective-permute-start | bytes 198152 | tf_op jit(solution)/shard_map/ppermute | solution.py:51
  65.3 7.3 %collective-permute-start.13 = (f32[129,128]{1,0:T(8,128)S(1)}, f32[129,128]{1,0:T(8,128)S(1)}, u32[]{:S(2)}, u32[]{:S(2)}) collective-permute-start(f32[129,128]{1,0:T(8,128)S(1)} %add.100), channel_id=1, source_target_pairs={{0,2},{1,3},{2,0},{3,1},{4,6},{5,7},{6,4},{7,5},{8,10},{9,11},{10,... | collective-permute-start | bytes 198152 | tf_op jit(solution)/shard_map/ppermute | solution.py:51
  67.8 6.2 %collective-permute-start.14 = (f32[129,128]{1,0:T(8,128)S(1)}, f32[129,128]{1,0:T(8,128)S(1)}, u32[]{:S(2)}, u32[]{:S(2)}) collective-permute-start(f32[129,128]{1,0:T(8,128)S(1)} %add.100), channel_id=1, source_target_pairs={{0,3},{1,2},{2,1},{3,0},{4,7},{5,6},{6,5},{7,4},{8,11},{9,10},{10,... | collective-permute-start | bytes 198152 | tf_op jit(solution)/shard_map/ppermute | solution.py:51
  90.9 4.0 %copy-start.4 = (f32[128,128]{1,0:T(8,128)S(1)}, f32[128,128]{1,0:T(8,128)}, u32[]{:S(2)}) copy-start(f32[128,128]{1,0:T(8,128)} %shard_map.68) | copy-start | bytes 196612

commit v6 on v5

--- a/solution.py
+++ b/solution.py
@@ -100,6 +100,17 @@
     return padded_field[:, 1:-1, 1:-1] + diffusion * laplacian + heating * source_term
 
 
+def propagate_members_last(padded_field, source_term):
+    laplacian = (
+        padded_field[1:-1, 2:]
+        + padded_field[1:-1, :-2]
+        + padded_field[2:, 1:-1]
+        + padded_field[:-2, 1:-1]
+        - 4.0 * padded_field[1:-1, 1:-1]
+    )
+    return padded_field[1:-1, 1:-1] + diffusion * laplacian + heating * source_term
+
+
 def shards(
     prior_gas_warmth,
     fire_power_output,
@@ -108,14 +119,16 @@
     reading_local_location,
 ):
     sample_number, block_height_number, block_width_number = prior_gas_warmth.shape
-    predicted_vector = prior_gas_warmth
+    warmth_t = jnp.transpose(prior_gas_warmth, (2, 1, 0))
+    heat_t = jnp.transpose(fire_power_output, (2, 1, 0))
+    predicted_t = warmth_t
     for section in range(2):
-        bordered_vector = with_halo(predicted_vector, (("gx", 1), ("gy", 2)), 1)
-        predicted_vector = propagate_model(bordered_vector, fire_power_output)
-    average_gas_warmth = jnp.mean(predicted_vector, axis=0)
-    mean_heat = jnp.mean(fire_power_output, axis=0)
-    sample_deviation_matrix = predicted_vector - average_gas_warmth
-    heat_anomaly = fire_power_output - mean_heat
+        bordered = with_halo(predicted_t, (("gx", 1), ("gy", 0)), 1)
+        predicted_t = propagate_members_last(bordered, heat_t)
+    average_t = jnp.mean(predicted_t, axis=2)
+    mean_heat_t = jnp.mean(heat_t, axis=2)
+    deviation_t = predicted_t - average_t[:, :, None]
+    heat_anomaly_t = heat_t - mean_heat_t[:, :, None]
     coefficient_line = 1.0 / (reading_noise_spread * math.sqrt(sample_number - 1))
     weight_line = coefficient_line * coefficient_line
     row_hot = (
@@ -131,20 +144,20 @@
         axis=1,
     )
     cell_sums = lax.dot_general(
-        weighted_rows, col_hot, (((0,), (0,)), ((), ())), precision=lax.Precision.HIGHEST
+        col_hot, weighted_rows, (((0,), (0,)), ((), ())), precision=lax.Precision.HIGHEST
     )
-    cell_weight = cell_sums[:block_height_number]
-    cell_residual = cell_sums[block_height_number:] - average_gas_warmth * cell_weight
+    cell_weight = cell_sums[:, :block_height_number]
+    cell_residual = cell_sums[:, block_height_number:] - average_t * cell_weight
     gram_local = lax.dot_general(
-        sample_deviation_matrix * cell_weight,
-        sample_deviation_matrix,
-        (((1, 2), (1, 2)), ((), ())),
+        deviation_t * cell_weight[:, :, None],
+        deviation_t,
+        (((0, 1), (0, 1)), ((), ())),
         precision=lax.Precision.HIGHEST,
     )
     projected = lax.dot_general(
-        sample_deviation_matrix,
+        deviation_t,
         cell_residual,
-        (((1, 2), (0, 1)), ((), ())),
+        (((0, 1), (0, 1)), ((), ())),
         precision=lax.Precision.HIGHEST,
     )
     identity = jnp.eye(sample_number, dtype=jnp.float32)
@@ -157,14 +170,14 @@
     whitened = jnp.dot(lower_inverse, projected_sum, precision=lax.Precision.HIGHEST)
     mean_weights = jnp.dot(lower_inverse.T, whitened, precision=lax.Precision.HIGHEST)
     combination_transposed = lower_inverse + mean_weights[None, :]
-    contract = (((1,), (0,)), ((), ()))
-    updated_warmth = average_gas_warmth + lax.dot_general(
-        combination_transposed, sample_deviation_matrix, contract, precision=lax.Precision.HIGHEST
+    contract = (((2,), (1,)), ((), ()))
+    updated_t = average_t[:, :, None] + lax.dot_general(
+        deviation_t, combination_transposed, contract, precision=lax.Precision.HIGHEST
     )
-    heat_out = mean_heat + lax.dot_general(
-        combination_transposed, heat_anomaly, contract, precision=lax.Precision.HIGHEST
+    heat_out_t = mean_heat_t[:, :, None] + lax.dot_general(
+        heat_anomaly_t, combination_transposed, contract, precision=lax.Precision.HIGHEST
     )
-    return (updated_warmth, heat_out)
+    return (jnp.transpose(updated_t, (2, 1, 0)), jnp.transpose(heat_out_t, (2, 1, 0)))
 
 
 def solution(mesh):

time: 100 us -> 85.4 us (0.85)
  local copies, waits for them, and re-layouts: 17.2 us -> 4.81 us
  other arithmetic: 6.47 us -> 2.08 us
  starting transfers between devices: 34.6 us -> 37.4 us
    ppermute x4 -> x0, local copies, waits for them, and re-layouts: 5.8 us -> none  [the longest x2 2.92 us: with_halo(): lax.ppermute(lax.slice_in_dim(block, block.shape[dim] - width, None, axis...]
    slice x5 -> x0, local copies, waits for them, and re-layouts: 4.25 us -> none  [with_halo(): lax.slice_in_dim(block, 0, width, axis=dim)]
    ppermute x4, waiting for transfers between devices: 3.58 us -> 0.01 us  [with_halo(): lax.ppermute(lax.slice_in_dim(block, 0, width, axis=dim), axis, backward)]
    ppermute x4, waiting for transfers between devices: 0.23 us -> 3.52 us  [with_halo(): lax.ppermute(lax.slice_in_dim(block, block.shape[dim] - width, None, axis...]
    ppermute x7, starting transfers between devices: 12.8 us -> 15.6 us  [butterfly_sum(): received[offset] = lax.ppermute(value, axis, pairs)]
    slice x3 -> x2, local copies, waits for them, and re-layouts: 2.01 us -> 0.02 us  [with_halo(): lax.slice_in_dim(block, block.shape[dim] - width, None, axis=dim)]
    add x1, other arithmetic: 2.42 us -> 0.46 us  [propagate_members_last(): padded_field[1:-1, 1:-1] + diffusion * laplacian + heating * source_term]
    reduce_sum x2 -> x1, other arithmetic: 2.58 us -> 0.83 us  [shards(): average_t = jnp.mean(predicted_t, axis=2)]
  transfers between devices with their start and end apart: 15 -> 15, of which waited for: 7 -> 9; matrix products, arithmetic and copies ran while one was open for 6% -> 1% of each run, Pallas kernels for 0% -> 0%
where the time goes in v6:
time: 85.4 us; the launch traced here: 85 us
  starting transfers between devices  37.4 us (44%)
  waiting for transfers between devices  16.3 us (19%)
  Pallas kernels  16.2 us (19%)
  matrix products  7.25 us (8%)
  local copies, waits for them, and re-layouts  4.81 us (6%)
  other arithmetic  2.08 us (2%)
  between operations  0.9 us (1%)
    ppermute x4, starting transfers between devices, with_halo(): lax.ppermute(lax.slice_in_dim(block, block.shape[dim] - width, None, axis...  16.5 us
    pallas_call x1, Pallas kernels, inverse_factor(): pl.pallas_call(inverse_factor_kernel, out_shape=jax.ShapeDtypeStruct((siz...  16.2 us
    ppermute x7, starting transfers between devices, butterfly_sum(): received[offset] = lax.ppermute(value, axis, pairs)  15.6 us
    ppermute x7, waiting for transfers between devices, butterfly_sum(): received[offset] = lax.ppermute(value, axis, pairs)  12.8 us
    ppermute x4, starting transfers between devices, with_halo(): lax.ppermute(lax.slice_in_dim(block, 0, width, axis=dim), axis, backward)  5.3 us
    unnamed x14, local copies, waits for them, and re-layouts  4.79 us
    ppermute x4, waiting for transfers between devices, with_halo(): lax.ppermute(lax.slice_in_dim(block, block.shape[dim] - width, None, axis...  3.52 us
    dot_general x1, matrix products, shards(): lax.dot_general(deviation_t * cell_weight[:, :, None], deviation_t, (((0,...  2.7 us
  transfers between devices with their start and end apart: 15, of which 9 were waited for; matrix products, arithmetic and copies ran while one was open for 1% of the time, Pallas kernels for 0%

profile of v6, /device:TPU:0, one launch (start us, length us, event | category | flops | bytes accessed | tf_op | source)
XLA Modules:
  0.0 85.0 jit_solution(1552750392134596772)
XLA Ops:
  0.6 0.0 copy-start.3
  0.6 0.0 copy-start.4
  0.6 1.6 %copy.13 = f32[128,16,128]{0,2,1:T(8,128)S(1)} copy(f32[128,16,128]{2,1,0:T(8,128)} %param.5) | data formatting | bytes 2097152 | tf_op args[0]
  2.2 0.0 copy-start.1
  2.3 1.4 %collective-permute-start = (f32[128,1,128]{2,0,1:T(8,128)S(1)}, f32[128,1,128]{2,0,1:T(8,128)S(1)}, u32[]{:S(2)}, u32[]{:S(2)}) collective-permute-start(f32[128,1,128]{2,0,1:T(8,128)S(1)} %get-tuple-element.16), channel_id=1, source_target_pairs={{4,0},{8,4},{12,8},{16,12},{20,16},{24,20},{28,24},{5,1},{9,5},{13... | collective-permute-start | bytes 196616 | tf_op jit(solution)/shard_map/ppermute | solution.py:22
  3.7 3.0 %collective-permute-start.1 = (f32[128,1,128]{2,0,1:T(8,128)S(1)}, f32[128,1,128]{2,0,1:T(8,128)S(1)}, u32[]{:S(2)}, u32[]{:S(2)}) collective-permute-start(f32[128,1,128]{2,0,1:T(8,128)S(1)} %get-tuple-element.15), channel_id=1, source_target_pairs={{0,4},{4,8},{8,12},{12,16},{16,20},{20,24},{24,28},{1,5},{5,9},{9,... | collective-permute-start | bytes 196616 | tf_op jit(solution)/shard_map/ppermute | solution.py:19
  6.8 0.0 copy-done.3
  6.8 0.0 copy-done.4
  6.8 0.0 collective-permute-done
  6.8 0.8 collective-permute-done.1
  7.6 0.0 copy-start.2
  7.7 1.3 %collective-permute-start.2 = (f32[1,18,128]{2,0,1:T(1,128)S(1)}, f32[1,18,128]{2,0,1:T(1,128)S(1)}, u32[]{:S(2)}, u32[]{:S(2)}) collective-permute-start(f32[1,18,128]{2,0,1:T(1,128)S(1)} %get-tuple-element.10), channel_id=1, source_target_pairs={{1,0},{2,1},{3,2},{5,4},{6,5},{7,6},{9,8},{10,9},{11,10},{13,12},{... | collective-permute-start | bytes 27656 | tf_op jit(solution)/shard_map/ppermute | solution.py:22
  9.0 5.6 %collective-permute-start.3 = (f32[1,18,128]{2,0,1:T(1,128)S(1)}, f32[1,18,128]{2,0,1:T(1,128)S(1)}, u32[]{:S(2)}, u32[]{:S(2)}) collective-permute-start(f32[1,18,128]{2,0,1:T(1,128)S(1)} %get-tuple-element.11), channel_id=1, source_target_pairs={{0,1},{1,2},{2,3},{4,5},{5,6},{6,7},{8,9},{9,10},{10,11},{12,13},{... | collective-permute-start | bytes 27656 | tf_op jit(solution)/shard_map/ppermute | solution.py:19
  14.5 0.0 copy-done.2
  14.5 0.0 copy-done.1
  14.6 0.4 copy.14
  15.0 0.0 collective-permute-done.2
  15.0 0.9 %collective-permute-done.3 = f32[1,18,128]{2,0,1:T(1,128)S(1)} collective-permute-done((f32[1,18,128]{2,0,1:T(1,128)S(1)}, f32[1,18,128]{2,0,1:T(1,128)S(1)}, u32[]{:S(2)}, u32[]{:S(2)}) %collective-permute-start.3) | collective-permute-done | bytes 9248 | tf_op jit(solution)/shard_map/ppermute | solution.py:19
  15.9 0.5 fusion.18
  16.4 1.3 %collective-permute-start.4 = (f32[128,1,128]{2,0,1:T(8,128)S(1)}, f32[128,1,128]{2,0,1:T(8,128)S(1)}, u32[]{:S(2)}, u32[]{:S(2)}) collective-permute-start(f32[128,1,128]{2,0,1:T(8,128)S(1)} %get-tuple-element.14), channel_id=1, source_target_pairs={{4,0},{8,4},{12,8},{16,12},{20,16},{24,20},{28,24},{5,1},{9,5},{13... | collective-permute-start | bytes 196616 | tf_op jit(solution)/shard_map/ppermute | solution.py:22
  17.7 3.4 %collective-permute-start.5 = (f32[128,1,128]{2,0,1:T(8,128)S(1)}, f32[128,1,128]{2,0,1:T(8,128)S(1)}, u32[]{:S(2)}, u32[]{:S(2)}) collective-permute-start(f32[128,1,128]{2,0,1:T(8,128)S(1)} %get-tuple-element.13), channel_id=1, source_target_pairs={{0,4},{4,8},{8,12},{12,16},{16,20},{20,24},{24,28},{1,5},{5,9},{9,... | collective-permute-start | bytes 196616 | tf_op jit(solution)/shard_map/ppermute | solution.py:19
  21.1 0.0 collective-permute-done.4
  21.1 0.8 collective-permute-done.5
  21.9 1.3 %collective-permute-start.6 = (f32[1,18,128]{2,0,1:T(1,128)S(1)}, f32[1,18,128]{2,0,1:T(1,128)S(1)}, u32[]{:S(2)}, u32[]{:S(2)}) collective-permute-start(f32[1,18,128]{2,0,1:T(1,128)S(1)} %get-tuple-element.8), channel_id=1, source_target_pairs={{1,0},{2,1},{3,2},{5,4},{6,5},{7,6},{9,8},{10,9},{11,10},{13,12},{... | collective-permute-start | bytes 27656 | tf_op jit(solution)/shard_map/ppermute | solution.py:22
  23.2 4.5 %collective-permute-start.7 = (f32[1,18,128]{2,0,1:T(1,128)S(1)}, f32[1,18,128]{2,0,1:T(1,128)S(1)}, u32[]{:S(2)}, u32[]{:S(2)}) collective-permute-start(f32[1,18,128]{2,0,1:T(1,128)S(1)} %get-tuple-element.9), channel_id=1, source_target_pairs={{0,1},{1,2},{2,3},{4,5},{5,6},{6,7},{8,9},{9,10},{10,11},{12,13},{... | collective-permute-start | bytes 27656 | tf_op jit(solution)/shard_map/ppermute | solution.py:19
  27.8 0.4 fusion.29
  28.2 0.0 collective-permute-done.6
  28.2 1.0 %collective-permute-done.7 = f32[1,18,128]{2,0,1:T(1,128)S(1)} collective-permute-done((f32[1,18,128]{2,0,1:T(1,128)S(1)}, f32[1,18,128]{2,0,1:T(1,128)S(1)}, u32[]{:S(2)}, u32[]{:S(2)}) %collective-permute-start.7) | collective-permute-done | bytes 9248 | tf_op jit(solution)/shard_map/ppermute | solution.py:19
  29.2 0.8 fusion.49
  30.0 2.7 %fusion.4 = f32[128,128]{1,0:T(8,128)S(1)} fusion(f32[128,16,128]{2,0,1:T(8,128)S(1)} %get-tuple-element.7, f32[128,16]{0,1:T(8,128)S(1)} %get-tuple-element.17, f32[128,16]{0,1:T(8,128)S(1)} %get-tuple-element.20), kind=kOutput, calls=%fused_computation.6 | convolution fusion | flops 403439616 | bytes 1130496 | tf_op jit(solution)/shard_map/dot_general | solution.py:151
  32.7 0.8 convolution_bitcast_fusion.2
  33.5 6.3 %collective-permute-start.10 = (f32[129,128]{1,0:T(8,128)S(1)}, f32[129,128]{1,0:T(8,128)S(1)}, u32[]{:S(2)}, u32[]{:S(2)}) collective-permute-start(f32[129,128]{1,0:T(8,128)S(1)} %pad_maximum_fusion.16), channel_id=1, source_target_pairs={{0,12},{4,8},{8,4},{12,0},{16,28},{20,24},{24,20},{28,16},{1,13},{... | collective-permute-start | bytes 198152 | tf_op jit(solution)/shard_map/ppermute | solution.py:51
  39.8 0.4 collective-permute-start.8
  40.1 0.1 collective-permute-start.9
  40.3 2.1 %collective-permute-done.10 = f32[129,128]{1,0:T(8,128)S(1)} collective-permute-done((f32[129,128]{1,0:T(8,128)S(1)}, f32[129,128]{1,0:T(8,128)S(1)}, u32[]{:S(2)}, u32[]{:S(2)}) %collective-permute-start.10) | collective-permute-done | bytes 66080 | tf_op jit(solution)/shard_map/ppermute | solution.py:51
  42.4 0.0 collective-permute-done.8
  42.4 2.1 %collective-permute-done.9 = f32[129,128]{1,0:T(8,128)S(1)} collective-permute-done((f32[129,128]{1,0:T(8,128)S(1)}, f32[129,128]{1,0:T(8,128)S(1)}, u32[]{:S(2)}, u32[]{:S(2)}) %collective-permute-start.9) | collective-permute-done | bytes 66080 | tf_op jit(solution)/shard_map/ppermute | solution.py:51
  44.5 3.5 %collective-permute-start.11 = (f32[129,128]{1,0:T(8,128)S(1)}, f32[129,128]{1,0:T(8,128)S(1)}, u32[]{:S(2)}, u32[]{:S(2)}) collective-permute-start(f32[129,128]{1,0:T(8,128)S(1)} %add_add_fusion.1), channel_id=1, source_target_pairs={{0,16},{4,20},{8,24},{12,28},{16,0},{20,4},{24,8},{28,12},{1,17},{... | collective-permute-start | bytes 198152 | tf_op jit(solution)/shard_map/ppermute | solution.py:51
  48.0 2.5 %collective-permute-done.11 = f32[129,128]{1,0:T(8,128)S(1)} collective-permute-done((f32[129,128]{1,0:T(8,128)S(1)}, f32[129,128]{1,0:T(8,128)S(1)}, u32[]{:S(2)}, u32[]{:S(2)}) %collective-permute-start.11) | collective-permute-done | bytes 66080 | tf_op jit(solution)/shard_map/ppermute | solution.py:51
  50.5 2.4 %collective-permute-start.12 = (f32[129,128]{1,0:T(8,128)S(1)}, f32[129,128]{1,0:T(8,128)S(1)}, u32[]{:S(2)}, u32[]{:S(2)}) collective-permute-start(f32[129,128]{1,0:T(8,128)S(1)} %add.107), channel_id=1, source_target_pairs={{0,1},{1,0},{2,3},{3,2},{4,5},{5,4},{6,7},{7,6},{8,9},{9,8},{10,11... | collective-permute-start | bytes 198152 | tf_op jit(solution)/shard_map/ppermute | solution.py:51
  52.8 3.0 %collective-permute-start.13 = (f32[129,128]{1,0:T(8,128)S(1)}, f32[129,128]{1,0:T(8,128)S(1)}, u32[]{:S(2)}, u32[]{:S(2)}) collective-permute-start(f32[129,128]{1,0:T(8,128)S(1)} %add.107), channel_id=1, source_target_pairs={{0,2},{1,3},{2,0},{3,1},{4,6},{5,7},{6,4},{7,5},{8,10},{9,11},{10,... | collective-permute-start | bytes 198152 | tf_op jit(solution)/shard_map/ppermute | solution.py:51
  55.8 0.0 collective-permute-start.14
  55.8 0.0 collective-permute-done.12
  55.8 4.6 %collective-permute-done.13 = f32[129,128]{1,0:T(8,128)S(1)} collective-permute-done((f32[129,128]{1,0:T(8,128)S(1)}, f32[129,128]{1,0:T(8,128)S(1)}, u32[]{:S(2)}, u32[]{:S(2)}) %collective-permute-start.13) | collective-permute-done | bytes 66080 | tf_op jit(solution)/shard_map/ppermute | solution.py:51
  60.5 1.5 %collective-permute-done.14 = f32[129,128]{1,0:T(8,128)S(1)} collective-permute-done((f32[129,128]{1,0:T(8,128)S(1)}, f32[129,128]{1,0:T(8,128)S(1)}, u32[]{:S(2)}, u32[]{:S(2)}) %collective-permute-start.14) | collective-permute-done | bytes 66080 | tf_op jit(solution)/shard_map/ppermute | solution.py:51
  62.0 0.6 slice_add_fusion.gram_ref
  62.6 16.2 %shard_map.68 = f32[128,128]{1,0:T(8,128)} custom-call(f32[128,128]{1,0:T(8,128)} %slice_add_fusion.gram_ref), custom_call_target="tpu_custom_call" | custom-call | tf_op jit(solution)/shard_map/pallas_call | solution.py:84
  78.8 0.0 copy-start
  78.8 1.1 %convolution_bitcast_fusion.4 = f32[128,1]{0,1:T(1,128)S(1)} fusion(f32[128,128]{1,0:T(8,128)} %shard_map.68, f32[129,128]{1,0:T(8,128)S(1)} %add_add_fusion), kind=kOutput, calls=%fused_computation.9 | convolution fusion | flops 196608 | bytes 66560 | tf_op jit(solution)/shard_map/dot_general | solution.py:170
  79.9 0.0 copy-done
  79.9 0.2 convolution_bitcast_fusion.3
  80.1 1.1 %fusion.2 = f32[128,16,128]{0,2,1:T(8,128)S(1)} fusion(f32[128,16,128]{0,2,1:T(8,128)S(1)} %copy.14, f32[128,16]{0,1:T(8,128)S(1)} %get-tuple-element.22, f32[16,128]{1,0:T(8,128)S(1)} %get-tuple-element.21, f32[128,128]{1,0:T(8,128)S(1)} %copy-done, f32[128]{0:T(128)S(1)} %convolution_bitcast_fusion.3), kind=kOutput, calls=%fused_computation.3 | convolution fusion | flops 403193856 | bytes 2179584 | tf_op jit(solution)/shard_map/dot_general | solution.py:177
  81.2 1.4 %copy.17 = f32[128,16,128]{2,1,0:T(8,128)} copy(f32[128,16,128]{0,2,1:T(8,128)S(1)} %fusion.2) | data formatting | bytes 2097152
  82.5 1.0 %fusion.3 = f32[128,16,128]{0,2,1:T(8,128)S(1)} fusion(f32[128,16,128]{2,0,1:T(8,128)S(1)} %get-tuple-element.7, f32[128,16]{0,1:T(8,128)S(1)} %get-tuple-element.20, f32[16,128]{1,0:T(8,128)S(1)} %get-tuple-element.19, f32[128,128]{1,0:T(8,128)S(1)} %copy-done, f32[128]{0:T(128)S(1)} %convolution_bitcast_fusion.3), kind=kOutput, calls=%fused_computation.5 | convolution fusion | flops 403193856 | bytes 2179584 | tf_op jit(solution)/shard_map/dot_general | solution.py:174
  83.6 1.4 %copy.16 = f32[128,16,128]{2,1,0:T(8,128)} copy(f32[128,16,128]{0,2,1:T(8,128)S(1)} %fusion.3) | data formatting | bytes 2097152
  (13 shorter events, 0.2 us)
Async XLA Ops:
  0.6 6.1 %copy-start.3 = (f32[1024]{0:T(1024)S(1)}, f32[1024]{0:T(1024)}, u32[]{:S(2)}) copy-start(f32[1024]{0:T(1024)} %param.8) | copy-start | bytes 12292
  0.6 6.1 %copy-start.4 = (f32[1024]{0:T(1024)S(1)}, f32[1024]{0:T(1024)}, u32[]{:S(2)}) copy-start(f32[1024]{0:T(1024)} %param.7) | copy-start | bytes 12292
  2.2 12.3 %copy-start.1 = (f32[128,16,128]{2,1,0:T(8,128)S(1)}, f32[128,16,128]{2,1,0:T(8,128)}, u32[]{:S(2)}) copy-start(f32[128,16,128]{2,1,0:T(8,128)} %param.6) | copy-start | bytes 3145732
  2.3 4.5 %collective-permute-start = (f32[128,1,128]{2,0,1:T(8,128)S(1)}, f32[128,1,128]{2,0,1:T(8,128)S(1)}, u32[]{:S(2)}, u32[]{:S(2)}) collective-permute-start(f32[128,1,128]{2,0,1:T(8,128)S(1)} %get-tuple-element.16), channel_id=1, source_target_pairs={{4,0},{8,4},{12,8},{16,12},{20,16},{24,20},{28,24},{5,1},{9,5},{13... | collective-permute-start | bytes 196616 | tf_op jit(solution)/shard_map/ppermute | solution.py:22
  3.7 3.9 %collective-permute-start.1 = (f32[128,1,128]{2,0,1:T(8,128)S(1)}, f32[128,1,128]{2,0,1:T(8,128)S(1)}, u32[]{:S(2)}, u32[]{:S(2)}) collective-permute-start(f32[128,1,128]{2,0,1:T(8,128)S(1)} %get-tuple-element.15), channel_id=1, source_target_pairs={{0,4},{4,8},{8,12},{12,16},{16,20},{20,24},{24,28},{1,5},{5,9},{9,... | collective-permute-start | bytes 196616 | tf_op jit(solution)/shard_map/ppermute | solution.py:19
  7.6 6.9 %copy-start.2 = (s32[1024]{0:T(1024)S(1)}, s32[1024]{0:T(1024)}, u32[]{:S(2)}) copy-start(s32[1024]{0:T(1024)} %param.9) | copy-start | bytes 12292
  7.7 7.3 %collective-permute-start.2 = (f32[1,18,128]{2,0,1:T(1,128)S(1)}, f32[1,18,128]{2,0,1:T(1,128)S(1)}, u32[]{:S(2)}, u32[]{:S(2)}) collective-permute-start(f32[1,18,128]{2,0,1:T(1,128)S(1)} %get-tuple-element.10), channel_id=1, source_target_pairs={{1,0},{2,1},{3,2},{5,4},{6,5},{7,6},{9,8},{10,9},{11,10},{13,12},{... | collective-permute-start | bytes 27656 | tf_op jit(solution)/shard_map/ppermute | solution.py:22
  9.0 6.9 %collective-permute-start.3 = (f32[1,18,128]{2,0,1:T(1,128)S(1)}, f32[1,18,128]{2,0,1:T(1,128)S(1)}, u32[]{:S(2)}, u32[]{:S(2)}) collective-permute-start(f32[1,18,128]{2,0,1:T(1,128)S(1)} %get-tuple-element.11), channel_id=1, source_target_pairs={{0,1},{1,2},{2,3},{4,5},{5,6},{6,7},{8,9},{9,10},{10,11},{12,13},{... | collective-permute-start | bytes 27656 | tf_op jit(solution)/shard_map/ppermute | solution.py:19
  16.4 4.7 %collective-permute-start.4 = (f32[128,1,128]{2,0,1:T(8,128)S(1)}, f32[128,1,128]{2,0,1:T(8,128)S(1)}, u32[]{:S(2)}, u32[]{:S(2)}) collective-permute-start(f32[128,1,128]{2,0,1:T(8,128)S(1)} %get-tuple-element.14), channel_id=1, source_target_pairs={{4,0},{8,4},{12,8},{16,12},{20,16},{24,20},{28,24},{5,1},{9,5},{13... | collective-permute-start | bytes 196616 | tf_op jit(solution)/shard_map/ppermute | solution.py:22
  17.7 4.3 %collective-permute-start.5 = (f32[128,1,128]{2,0,1:T(8,128)S(1)}, f32[128,1,128]{2,0,1:T(8,128)S(1)}, u32[]{:S(2)}, u32[]{:S(2)}) collective-permute-start(f32[128,1,128]{2,0,1:T(8,128)S(1)} %get-tuple-element.13), channel_id=1, source_target_pairs={{0,4},{4,8},{8,12},{12,16},{16,20},{20,24},{24,28},{1,5},{5,9},{9,... | collective-permute-start | bytes 196616 | tf_op jit(solution)/shard_map/ppermute | solution.py:19
  21.9 6.3 %collective-permute-start.6 = (f32[1,18,128]{2,0,1:T(1,128)S(1)}, f32[1,18,128]{2,0,1:T(1,128)S(1)}, u32[]{:S(2)}, u32[]{:S(2)}) collective-permute-start(f32[1,18,128]{2,0,1:T(1,128)S(1)} %get-tuple-element.8), channel_id=1, source_target_pairs={{1,0},{2,1},{3,2},{5,4},{6,5},{7,6},{9,8},{10,9},{11,10},{13,12},{... | collective-permute-start | bytes 27656 | tf_op jit(solution)/shard_map/ppermute | solution.py:22
  23.2 5.9 %collective-permute-start.7 = (f32[1,18,128]{2,0,1:T(1,128)S(1)}, f32[1,18,128]{2,0,1:T(1,128)S(1)}, u32[]{:S(2)}, u32[]{:S(2)}) collective-permute-start(f32[1,18,128]{2,0,1:T(1,128)S(1)} %get-tuple-element.9), channel_id=1, source_target_pairs={{0,1},{1,2},{2,3},{4,5},{5,6},{6,7},{8,9},{9,10},{10,11},{12,13},{... | collective-permute-start | bytes 27656 | tf_op jit(solution)/shard_map/ppermute | solution.py:19
  33.5 8.8 %collective-permute-start.10 = (f32[129,128]{1,0:T(8,128)S(1)}, f32[129,128]{1,0:T(8,128)S(1)}, u32[]{:S(2)}, u32[]{:S(2)}) collective-permute-start(f32[129,128]{1,0:T(8,128)S(1)} %pad_maximum_fusion.16), channel_id=1, source_target_pairs={{0,12},{4,8},{8,4},{12,0},{16,28},{20,24},{24,20},{28,16},{1,13},{... | collective-permute-start | bytes 198152 | tf_op jit(solution)/shard_map/ppermute | solution.py:51
  39.8 2.6 %collective-permute-start.8 = (f32[129,128]{1,0:T(8,128)S(1)}, f32[129,128]{1,0:T(8,128)S(1)}, u32[]{:S(2)}, u32[]{:S(2)}) collective-permute-start(f32[129,128]{1,0:T(8,128)S(1)} %pad_maximum_fusion.16), channel_id=1, source_target_pairs={{0,4},{4,0},{8,12},{12,8},{16,20},{20,16},{24,28},{28,24},{1,5},{5... | collective-permute-start | bytes 198152 | tf_op jit(solution)/shard_map/ppermute | solution.py:51
  40.1 4.3 %collective-permute-start.9 = (f32[129,128]{1,0:T(8,128)S(1)}, f32[129,128]{1,0:T(8,128)S(1)}, u32[]{:S(2)}, u32[]{:S(2)}) collective-permute-start(f32[129,128]{1,0:T(8,128)S(1)} %pad_maximum_fusion.16), channel_id=1, source_target_pairs={{0,8},{4,12},{8,0},{12,4},{16,24},{20,28},{24,16},{28,20},{1,9},{5... | collective-permute-start | bytes 198152 | tf_op jit(solution)/shard_map/ppermute | solution.py:51
  44.5 6.0 %collective-permute-start.11 = (f32[129,128]{1,0:T(8,128)S(1)}, f32[129,128]{1,0:T(8,128)S(1)}, u32[]{:S(2)}, u32[]{:S(2)}) collective-permute-start(f32[129,128]{1,0:T(8,128)S(1)} %add_add_fusion.1), channel_id=1, source_target_pairs={{0,16},{4,20},{8,24},{12,28},{16,0},{20,4},{24,8},{28,12},{1,17},{... | collective-permute-start | bytes 198152 | tf_op jit(solution)/shard_map/ppermute | solution.py:51
  50.5 5.4 %collective-permute-start.12 = (f32[129,128]{1,0:T(8,128)S(1)}, f32[129,128]{1,0:T(8,128)S(1)}, u32[]{:S(2)}, u32[]{:S(2)}) collective-permute-start(f32[129,128]{1,0:T(8,128)S(1)} %add.107), channel_id=1, source_target_pairs={{0,1},{1,0},{2,3},{3,2},{4,5},{5,4},{6,7},{7,6},{8,9},{9,8},{10,11... | collective-permute-start | bytes 198152 | tf_op jit(solution)/shard_map/ppermute | solution.py:51
  52.8 7.7 %collective-permute-start.13 = (f32[129,128]{1,0:T(8,128)S(1)}, f32[129,128]{1,0:T(8,128)S(1)}, u32[]{:S(2)}, u32[]{:S(2)}) collective-permute-start(f32[129,128]{1,0:T(8,128)S(1)} %add.107), channel_id=1, source_target_pairs={{0,2},{1,3},{2,0},{3,1},{4,6},{5,7},{6,4},{7,5},{8,10},{9,11},{10,... | collective-permute-start | bytes 198152 | tf_op jit(solution)/shard_map/ppermute | solution.py:51
  55.8 6.1 %collective-permute-start.14 = (f32[129,128]{1,0:T(8,128)S(1)}, f32[129,128]{1,0:T(8,128)S(1)}, u32[]{:S(2)}, u32[]{:S(2)}) collective-permute-start(f32[129,128]{1,0:T(8,128)S(1)} %add.107), channel_id=1, source_target_pairs={{0,3},{1,2},{2,1},{3,0},{4,7},{5,6},{6,5},{7,4},{8,11},{9,10},{10,... | collective-permute-start | bytes 198152 | tf_op jit(solution)/shard_map/ppermute | solution.py:51
  78.8 1.1 %copy-start = (f32[128,128]{1,0:T(8,128)S(1)}, f32[128,128]{1,0:T(8,128)}, u32[]{:S(2)}) copy-start(f32[128,128]{1,0:T(8,128)} %shard_map.68) | copy-start | bytes 196612

commit v7 on v6

--- a/solution.py
+++ b/solution.py
@@ -9,19 +9,6 @@
 
 diffusion = 0.2
 heating = 0.5
-
-
-def with_halo(block, sides, width):
-    for axis, dim in sides:
-        count = lax.axis_size(axis)
-        forward = [(i, i + 1) for i in range(count - 1)]
-        backward = [(target, source) for source, target in forward]
-        low = lax.ppermute(
-            lax.slice_in_dim(block, block.shape[dim] - width, None, axis=dim), axis, forward
-        )
-        high = lax.ppermute(lax.slice_in_dim(block, 0, width, axis=dim), axis, backward)
-        block = jnp.concatenate([low, block, high], axis=dim)
-    return block
 
 
 def xor_tree(received, base, strides):
@@ -111,6 +98,70 @@
     return padded_field[1:-1, 1:-1] + diffusion * laplacian + heating * source_term
 
 
+def from_neighbour(block, axis, step):
+    count = lax.axis_size(axis)
+    if step > 0:
+        pairs = [(i, i + 1) for i in range(count - 1)]
+    else:
+        pairs = [(i + 1, i) for i in range(count - 1)]
+    return lax.ppermute(block, axis, pairs)
+
+
+def from_diagonal(block, step_x, step_y):
+    rows, cols = lax.axis_size("gx"), lax.axis_size("gy")
+    pairs = []
+    for a in range(rows):
+        for b in range(cols):
+            if 0 <= a + step_x < rows and 0 <= b + step_y < cols:
+                pairs.append((a * cols + b, (a + step_x) * cols + b + step_y))
+    return lax.ppermute(block, ("gx", "gy"), pairs)
+
+
+def forecast_two_steps(warmth, heat):
+    width, height = warmth.shape[0], warmth.shape[1]
+    top = from_neighbour(
+        jnp.concatenate([warmth[:, -2:], heat[:, -1:]], axis=1), "gx", 1
+    )
+    bottom = from_neighbour(
+        jnp.concatenate([warmth[:, :2], heat[:, :1]], axis=1), "gx", -1
+    )
+    left = from_neighbour(jnp.concatenate([warmth[-2:], heat[-1:]], axis=0), "gy", 1)
+    right = from_neighbour(jnp.concatenate([warmth[:2], heat[:1]], axis=0), "gy", -1)
+    top_left = from_diagonal(warmth[-2:, -2:], 1, 1)
+    top_right = from_diagonal(warmth[:2, -2:], 1, -1)
+    bottom_left = from_diagonal(warmth[-2:, :2], -1, 1)
+    bottom_right = from_diagonal(warmth[:2, :2], -1, -1)
+    warmth_wide = jnp.concatenate(
+        [
+            jnp.concatenate([top_left, left[:2], bottom_left], axis=1),
+            jnp.concatenate([top[:, :2], warmth, bottom[:, :2]], axis=1),
+            jnp.concatenate([top_right, right[:2], bottom_right], axis=1),
+        ],
+        axis=0,
+    )
+    corner = jnp.zeros_like(heat[:1, :1])
+    heat_wide = jnp.concatenate(
+        [
+            jnp.concatenate([corner, left[2:], corner], axis=1),
+            jnp.concatenate([top[:, 2:], heat, bottom[:, 2:]], axis=1),
+            jnp.concatenate([corner, right[2:], corner], axis=1),
+        ],
+        axis=0,
+    )
+    first = propagate_members_last(warmth_wide, heat_wide)
+    col = lax.broadcasted_iota(jnp.int32, (width + 2, height + 2), 0)
+    row = lax.broadcasted_iota(jnp.int32, (width + 2, height + 2), 1)
+    at_x, at_y = lax.axis_index("gx"), lax.axis_index("gy")
+    outside = (
+        ((row == 0) & (at_x == 0))
+        | ((row == height + 1) & (at_x == lax.axis_size("gx") - 1))
+        | ((col == 0) & (at_y == 0))
+        | ((col == width + 1) & (at_y == lax.axis_size("gy") - 1))
+    )
+    first = jnp.where(outside[:, :, None], 0.0, first)
+    return propagate_members_last(first, heat)
+
+
 def shards(
     prior_gas_warmth,
     fire_power_output,
@@ -121,10 +172,7 @@
     sample_number, block_height_number, block_width_number = prior_gas_warmth.shape
     warmth_t = jnp.transpose(prior_gas_warmth, (2, 1, 0))
     heat_t = jnp.transpose(fire_power_output, (2, 1, 0))
-    predicted_t = warmth_t
-    for section in range(2):
-        bordered = with_halo(predicted_t, (("gx", 1), ("gy", 0)), 1)
-        predicted_t = propagate_members_last(bordered, heat_t)
+    predicted_t = forecast_two_steps(warmth_t, heat_t)
     average_t = jnp.mean(predicted_t, axis=2)
     mean_heat_t = jnp.mean(heat_t, axis=2)
     deviation_t = predicted_t - average_t[:, :, None]

time: 85.4 us -> 91.2 us (1.068)
  starting transfers between devices: 37.4 us -> 27.9 us
  waiting for transfers between devices: 16.3 us -> 22.9 us
  other arithmetic: 2.08 us -> 7.29 us
  matrix products: 7.25 us -> 8.91 us
  local copies, waits for them, and re-layouts: 4.81 us -> 6.36 us
    ppermute x8, waiting for transfers between devices: 3.53 us -> 9.6 us  [the longest x4 9.59 us: from_diagonal(): return lax.ppermute(block, ('gx', 'gy'), pairs)]
    ppermute x7, starting transfers between devices: 15.6 us -> 9.83 us  [butterfly_sum(): received[offset] = lax.ppermute(value, axis, pairs)]
    select_n x0 -> x1, other arithmetic: none -> 4.35 us  [forecast_two_steps(): first = jnp.where(outside[:, :, None], 0.0, first)]
    ppermute x8, starting transfers between devices: 21.8 us -> 18 us  [the longest x4 9.27 us: from_neighbour(): return lax.ppermute(block, axis, pairs)]
    dot_general x1, matrix products: 1.06 us -> 2.13 us  [shards(): lax.dot_general(heat_anomaly_t, combination_transposed, contract, precisi...]
  transfers between devices with their start and end apart: 15 -> 15, of which waited for: 9 -> 7; matrix products, arithmetic and copies ran while one was open for 1% -> 2% of each run, Pallas kernels for 0% -> 0%
where the time goes in v7:
time: 91.2 us; the launch traced here: 90.7 us
  starting transfers between devices  27.9 us (31%)
  waiting for transfers between devices  22.9 us (25%)
  Pallas kernels  16.2 us (18%)
  matrix products  8.91 us (10%)
  other arithmetic  7.29 us (8%)
  local copies, waits for them, and re-layouts  6.36 us (7%)
  between operations  1.1 us (1%)
    pallas_call x1, Pallas kernels, inverse_factor(): pl.pallas_call(inverse_factor_kernel, out_shape=jax.ShapeDtypeStruct((siz...  16.2 us
    ppermute x7, waiting for transfers between devices, butterfly_sum(): received[offset] = lax.ppermute(value, axis, pairs)  13.3 us
    ppermute x7, starting transfers between devices, butterfly_sum(): received[offset] = lax.ppermute(value, axis, pairs)  9.83 us
    ppermute x4, waiting for transfers between devices, from_diagonal(): return lax.ppermute(block, ('gx', 'gy'), pairs)  9.59 us
    ppermute x4, starting transfers between devices, from_neighbour(): return lax.ppermute(block, axis, pairs)  9.27 us
    ppermute x4, starting transfers between devices, from_diagonal(): return lax.ppermute(block, ('gx', 'gy'), pairs)  8.78 us
    unnamed x14, local copies, waits for them, and re-layouts  5.4 us
    select_n x1, other arithmetic, forecast_two_steps(): first = jnp.where(outside[:, :, None], 0.0, first)  4.35 us
  transfers between devices with their start and end apart: 15, of which 7 were waited for; matrix products, arithmetic and copies ran while one was open for 2% of the time, Pallas kernels for 0%

profile of v7, /device:TPU:0, one launch (start us, length us, event | category | flops | bytes accessed | tf_op | source)
XLA Modules:
  0.0 90.7 jit_solution(15487480376777204829)
XLA Ops:
  0.6 1.9 %copy.96 = f32[128,16,128]{0,1,2:T(8,128)S(1)} copy(f32[128,16,128]{2,1,0:T(8,128)} %param.5) | data formatting | bytes 2097152 | tf_op args[0]
  2.6 0.1 fusion.49
  2.7 0.7 copy.97
  3.4 0.0 copy-start.2
  3.4 0.0 copy-start.3
  3.4 0.0 copy-start.4
  3.4 0.1 fusion.50
  3.5 0.1 pad_maximum_fusion.8
  3.7 2.4 %collective-permute-start.3 = (f32[128,3,128]{2,1,0:T(4,128)S(1)}, f32[128,3,128]{2,1,0:T(4,128)S(1)}, u32[]{:S(2)}, u32[]{:S(2)}) collective-permute-start(f32[128,3,128]{2,1,0:T(4,128)S(1)} %pad_maximum_fusion.8), channel_id=1, source_target_pairs={{0,4},{4,8},{8,12},{12,16},{16,20},{20,24},{24,28},{1,5},{5,9},{9,... | collective-permute-start | bytes 589832 | tf_op jit(solution)/shard_map/ppermute | solution.py:107
  6.0 0.1 pad_maximum_fusion.9
  6.2 1.3 %collective-permute-start.4 = (f32[128,3,128]{2,1,0:T(4,128)S(1)}, f32[128,3,128]{2,1,0:T(4,128)S(1)}, u32[]{:S(2)}, u32[]{:S(2)}) collective-permute-start(f32[128,3,128]{2,1,0:T(4,128)S(1)} %pad_maximum_fusion.9), channel_id=1, source_target_pairs={{4,0},{8,4},{12,8},{16,12},{20,16},{24,20},{28,24},{5,1},{9,5},{13... | collective-permute-start | bytes 589832 | tf_op jit(solution)/shard_map/ppermute | solution.py:107
  7.5 4.3 %collective-permute-start.1 = (f32[3,16,128]{2,1,0:T(8,128)S(1)}, f32[3,16,128]{2,1,0:T(8,128)S(1)}, u32[]{:S(2)}, u32[]{:S(2)}) collective-permute-start(f32[3,16,128]{2,1,0:T(8,128)S(1)} %pad_maximum_fusion.11), channel_id=1, source_target_pairs={{0,1},{1,2},{2,3},{4,5},{5,6},{6,7},{8,9},{9,10},{10,11},{12,13},{... | collective-permute-start | bytes 73736 | tf_op jit(solution)/shard_map/ppermute | solution.py:107
  11.8 1.3 %collective-permute-start.6 = (f32[3,16,128]{2,1,0:T(8,128)S(1)}, f32[3,16,128]{2,1,0:T(8,128)S(1)}, u32[]{:S(2)}, u32[]{:S(2)}) collective-permute-start(f32[3,16,128]{2,1,0:T(8,128)S(1)} %pad_maximum_fusion.12), channel_id=1, source_target_pairs={{1,0},{2,1},{3,2},{5,4},{6,5},{7,6},{9,8},{10,9},{11,10},{13,12},{... | collective-permute-start | bytes 73736 | tf_op jit(solution)/shard_map/ppermute | solution.py:107
  13.1 6.0 %collective-permute-start = (f32[2,2,128]{2,1,0:T(2,128)S(1)}, f32[2,2,128]{2,1,0:T(2,128)S(1)}, u32[]{:S(2)}, u32[]{:S(2)}) collective-permute-start(f32[2,2,128]{2,1,0:T(2,128)S(1)} %get-tuple-element.18), channel_id=1, source_target_pairs={{0,5},{1,6},{2,7},{4,9},{5,10},{6,11},{8,13},{9,14},{10,15},{12,17... | collective-permute-start | bytes 6152 | tf_op jit(solution)/shard_map/ppermute | solution.py:117
  19.1 0.3 bitcast_reduce_fusion
  19.5 0.1 copy.102
  19.6 0.4 fusion.23
  20.1 0.0 collective-permute-done.1
  20.1 0.7 collective-permute-start.2
  20.8 0.0 collective-permute-done.6
  20.8 0.7 collective-permute-start.5
  21.4 0.0 collective-permute-done.3
  21.4 1.5 %collective-permute-start.7 = (f32[2,2,128]{2,1,0:T(2,128)S(1)}, f32[2,2,128]{2,1,0:T(2,128)S(1)}, u32[]{:S(2)}, u32[]{:S(2)}) collective-permute-start(f32[2,2,128]{2,1,0:T(2,128)S(1)} %get-tuple-element.16), channel_id=1, source_target_pairs={{5,0},{6,1},{7,2},{9,4},{10,5},{11,6},{13,8},{14,9},{15,10},{17,12... | collective-permute-start | bytes 6152 | tf_op jit(solution)/shard_map/ppermute | solution.py:117
  22.9 0.1 or_or_fusion
  23.0 0.1 copy.103
  23.2 0.1 slice.160
  23.3 0.0 collective-permute-done.4
  23.4 0.1 slice.161
  23.4 0.0 collective-permute-done
  23.5 0.0 collective-permute-done.2
  23.5 0.0 collective-permute-done.5
  23.5 9.6 %collective-permute-done.7 = f32[2,2,128]{2,1,0:T(2,128)S(1)} collective-permute-done((f32[2,2,128]{2,1,0:T(2,128)S(1)}, f32[2,2,128]{2,1,0:T(2,128)S(1)}, u32[]{:S(2)}, u32[]{:S(2)}) %collective-permute-start.7) | collective-permute-done | bytes 2080 | tf_op jit(solution)/shard_map/ppermute | solution.py:117
  33.1 0.3 maximum_maximum_fusion
  33.3 4.3 %fusion.6 = f32[130,18,128]{2,1,0:T(8,128)S(1)} fusion(f32[128,2,128]{2,1,0:T(2,128)S(1)} %slice.150, f32[2,2,128]{2,1,0:T(2,128)S(1)} %collective-permute-done.2, f32[128,16,128]{2,1,0:T(8,128)S(1)} %bitcast.55, f32[128,2,128]{2,1,0:T(2,128)S(1)} %slice.147, f32[2,16,128]{2,1,0:T(8,128)S(1)} %slice.143, f32[2,2,128]{2,1,0:T(2,128)S(1)} %collective-permute-done, ...), kind=kLoop, calls=%fused_computation.8 | loop fusion | flops 8386560 | bytes 7342884 | tf_op jit(solution)/shard_map/jit(_where)/select_n | solution.py:161
  37.7 0.8 fusion.44
  38.6 0.1 copy.98
  38.6 0.1 copy.99
  38.7 0.1 copy.100
  38.8 0.1 copy.107
  38.9 0.3 broadcast_subtract_fusion.1
  39.3 2.2 %fusion.13 = f32[128,128]{1,0:T(8,128)S(1)} fusion(f32[128,16,128]{2,1,0:T(8,128)S(1)} %broadcast_subtract_fusion.1, f32[128,16]{1,0:T(8,128)S(1)} %copy.100), kind=kOutput, calls=%fused_computation.26 | convolution fusion | flops 402915328 | bytes 1122304 | tf_op jit(solution)/shard_map/dot_general | solution.py:199
  41.5 0.9 %convolution_bitcast_fusion.2 = f32[1,128]{1,0:T(1,128)S(1)} fusion(f32[128,16,128]{2,1,0:T(8,128)S(1)} %broadcast_subtract_fusion.1, f32[128,16,1]{1,2,0:T(1,128)S(1)} %copy.107), kind=kOutput, calls=%fused_computation.27 | convolution fusion | flops 3145728 | bytes 1057280 | tf_op jit(solution)/shard_map/dot_general | solution.py:205
  42.4 2.9 %collective-permute-start.10 = (f32[129,128]{1,0:T(8,128)S(1)}, f32[129,128]{1,0:T(8,128)S(1)}, u32[]{:S(2)}, u32[]{:S(2)}) collective-permute-start(f32[129,128]{1,0:T(8,128)S(1)} %pad_maximum_fusion.10), channel_id=1, source_target_pairs={{0,12},{4,8},{8,4},{12,0},{16,28},{20,24},{24,20},{28,16},{1,13},{... | collective-permute-start | bytes 198152 | tf_op jit(solution)/shard_map/ppermute | solution.py:38
  45.3 0.6 collective-permute-start.8
  45.9 0.0 collective-permute-start.9
  45.9 2.0 %collective-permute-done.10 = f32[129,128]{1,0:T(8,128)S(1)} collective-permute-done((f32[129,128]{1,0:T(8,128)S(1)}, f32[129,128]{1,0:T(8,128)S(1)}, u32[]{:S(2)}, u32[]{:S(2)}) %collective-permute-start.10) | collective-permute-done | bytes 66080 | tf_op jit(solution)/shard_map/ppermute | solution.py:38
  47.9 0.0 collective-permute-done.8
  47.9 2.3 %collective-permute-done.9 = f32[129,128]{1,0:T(8,128)S(1)} collective-permute-done((f32[129,128]{1,0:T(8,128)S(1)}, f32[129,128]{1,0:T(8,128)S(1)}, u32[]{:S(2)}, u32[]{:S(2)}) %collective-permute-start.9) | collective-permute-done | bytes 66080 | tf_op jit(solution)/shard_map/ppermute | solution.py:38
  50.2 0.1 collective-permute-start.11
  50.3 4.3 %collective-permute-done.11 = f32[129,128]{1,0:T(8,128)S(1)} collective-permute-done((f32[129,128]{1,0:T(8,128)S(1)}, f32[129,128]{1,0:T(8,128)S(1)}, u32[]{:S(2)}, u32[]{:S(2)}) %collective-permute-start.11) | collective-permute-done | bytes 66080 | tf_op jit(solution)/shard_map/ppermute | solution.py:38
  54.6 3.8 %collective-permute-start.12 = (f32[129,128]{1,0:T(8,128)S(1)}, f32[129,128]{1,0:T(8,128)S(1)}, u32[]{:S(2)}, u32[]{:S(2)}) collective-permute-start(f32[129,128]{1,0:T(8,128)S(1)} %add.107), channel_id=1, source_target_pairs={{0,1},{1,0},{2,3},{3,2},{4,5},{5,4},{6,7},{7,6},{8,9},{9,8},{10,11... | collective-permute-start | bytes 198152 | tf_op jit(solution)/shard_map/ppermute | solution.py:38
  58.4 1.1 %collective-permute-start.13 = (f32[129,128]{1,0:T(8,128)S(1)}, f32[129,128]{1,0:T(8,128)S(1)}, u32[]{:S(2)}, u32[]{:S(2)}) collective-permute-start(f32[129,128]{1,0:T(8,128)S(1)} %add.107), channel_id=1, source_target_pairs={{0,2},{1,3},{2,0},{3,1},{4,6},{5,7},{6,4},{7,5},{8,10},{9,11},{10,... | collective-permute-start | bytes 198152 | tf_op jit(solution)/shard_map/ppermute | solution.py:38
  59.5 1.4 %collective-permute-start.14 = (f32[129,128]{1,0:T(8,128)S(1)}, f32[129,128]{1,0:T(8,128)S(1)}, u32[]{:S(2)}, u32[]{:S(2)}) collective-permute-start(f32[129,128]{1,0:T(8,128)S(1)} %add.107), channel_id=1, source_target_pairs={{0,3},{1,2},{2,1},{3,0},{4,7},{5,6},{6,5},{7,4},{8,11},{9,10},{10,... | collective-permute-start | bytes 198152 | tf_op jit(solution)/shard_map/ppermute | solution.py:38
  60.9 0.5 collective-permute-done.12
  61.4 3.3 %collective-permute-done.13 = f32[129,128]{1,0:T(8,128)S(1)} collective-permute-done((f32[129,128]{1,0:T(8,128)S(1)}, f32[129,128]{1,0:T(8,128)S(1)}, u32[]{:S(2)}, u32[]{:S(2)}) %collective-permute-start.13) | collective-permute-done | bytes 66080 | tf_op jit(solution)/shard_map/ppermute | solution.py:38
  64.7 1.0 %collective-permute-done.14 = f32[129,128]{1,0:T(8,128)S(1)} collective-permute-done((f32[129,128]{1,0:T(8,128)S(1)}, f32[129,128]{1,0:T(8,128)S(1)}, u32[]{:S(2)}, u32[]{:S(2)}) %collective-permute-start.14) | collective-permute-done | bytes 66080 | tf_op jit(solution)/shard_map/ppermute | solution.py:38
  65.7 0.6 slice_add_fusion.4.gram_ref
  66.3 16.2 %shard_map.68 = f32[128,128]{1,0:T(8,128)} custom-call(f32[128,128]{1,0:T(8,128)} %slice_add_fusion.4.gram_ref), custom_call_target="tpu_custom_call" | custom-call | tf_op jit(solution)/shard_map/pallas_call | solution.py:71
  82.5 1.0 %convolution_bitcast_fusion.4 = f32[128,1]{0,1:T(1,128)S(1)} fusion(f32[128,128]{1,0:T(8,128)} %shard_map.68, f32[129,128]{1,0:T(8,128)S(1)} %add_add_fusion), kind=kOutput, calls=%fused_computation.29 | convolution fusion | flops 196608 | bytes 66560 | tf_op jit(solution)/shard_map/dot_general | solution.py:218
  83.5 1.0 %convolution_bitcast_fusion.3 = f32[128]{0:T(128)S(1)} fusion(f32[128,1]{0,1:T(1,128)S(1)} %convolution_bitcast_fusion.4, f32[128,128]{1,0:T(8,128)} %shard_map.68), kind=kOutput, calls=%fused_computation.28 | convolution fusion | flops 196608 | bytes 66560 | tf_op jit(solution)/shard_map/dot_general | solution.py:219
  84.6 2.1 %fusion.11 = f32[128,16,128]{0,2,1:T(8,128)S(1)} fusion(f32[128,16,128]{2,1,0:T(8,128)S(1)} %get-tuple-element.14, f32[16,128]{1,0:T(8,128)S(1)} %get-tuple-element.31, f32[128,128]{1,0:T(8,128)} %shard_map.68, f32[128]{0:T(128)S(1)} %convolution_bitcast_fusion.3), kind=kOutput, calls=%fused_computation.23 | convolution fusion | flops 402931712 | bytes 2171392 | tf_op jit(solution)/shard_map/dot_general | solution.py:225
  86.7 1.4 %copy.106 = f32[128,16,128]{2,1,0:T(8,128)} copy(f32[128,16,128]{0,2,1:T(8,128)S(1)} %fusion.11) | data formatting | bytes 2097152
  88.1 1.2 %fusion.12 = f32[128,16,128]{0,2,1:T(8,128)S(1)} fusion(f32[128,16,128]{2,1,0:T(8,128)S(1)} %broadcast_subtract_fusion.1, f32[16,128]{1,0:T(8,128)S(1)} %get-tuple-element.29, f32[128,128]{1,0:T(8,128)S(1)} %copy-done, f32[128]{0:T(128)S(1)} %convolution_bitcast_fusion.3), kind=kOutput, calls=%fused_computation.25 | convolution fusion | flops 402931712 | bytes 2171392 | tf_op jit(solution)/shard_map/dot_general | solution.py:222
  89.3 1.4 %copy.105 = f32[128,16,128]{2,1,0:T(8,128)} copy(f32[128,16,128]{0,2,1:T(8,128)S(1)} %fusion.12) | data formatting | bytes 2097152
  (30 shorter events, 0.3 us)
Async XLA Ops:
  0.6 2.1 %copy-start.1 = (f32[128,16,128]{2,1,0:T(8,128)S(1)}, f32[128,16,128]{2,1,0:T(8,128)}, u32[]{:S(2)}) copy-start(f32[128,16,128]{2,1,0:T(8,128)} %param.6) | copy-start | bytes 3145732
  3.4 16.2 %copy-start.2 = (s32[1024]{0:T(1024)S(1)}, s32[1024]{0:T(1024)}, u32[]{:S(2)}) copy-start(s32[1024]{0:T(1024)} %param.9) | copy-start | bytes 12292
  3.4 16.2 %copy-start.3 = (f32[1024]{0:T(1024)S(1)}, f32[1024]{0:T(1024)}, u32[]{:S(2)}) copy-start(f32[1024]{0:T(1024)} %param.8) | copy-start | bytes 12292
  3.4 16.2 %copy-start.4 = (f32[1024]{0:T(1024)S(1)}, f32[1024]{0:T(1024)}, u32[]{:S(2)}) copy-start(f32[1024]{0:T(1024)} %param.7) | copy-start | bytes 12292
  3.7 17.8 %collective-permute-start.3 = (f32[128,3,128]{2,1,0:T(4,128)S(1)}, f32[128,3,128]{2,1,0:T(4,128)S(1)}, u32[]{:S(2)}, u32[]{:S(2)}) collective-permute-start(f32[128,3,128]{2,1,0:T(4,128)S(1)} %pad_maximum_fusion.8), channel_id=1, source_target_pairs={{0,4},{4,8},{8,12},{12,16},{16,20},{20,24},{24,28},{1,5},{5,9},{9,... | collective-permute-start | bytes 589832 | tf_op jit(solution)/shard_map/ppermute | solution.py:107
  6.2 17.1 %collective-permute-start.4 = (f32[128,3,128]{2,1,0:T(4,128)S(1)}, f32[128,3,128]{2,1,0:T(4,128)S(1)}, u32[]{:S(2)}, u32[]{:S(2)}) collective-permute-start(f32[128,3,128]{2,1,0:T(4,128)S(1)} %pad_maximum_fusion.9), channel_id=1, source_target_pairs={{4,0},{8,4},{12,8},{16,12},{20,16},{24,20},{28,24},{5,1},{9,5},{13... | collective-permute-start | bytes 589832 | tf_op jit(solution)/shard_map/ppermute | solution.py:107
  7.5 12.6 %collective-permute-start.1 = (f32[3,16,128]{2,1,0:T(8,128)S(1)}, f32[3,16,128]{2,1,0:T(8,128)S(1)}, u32[]{:S(2)}, u32[]{:S(2)}) collective-permute-start(f32[3,16,128]{2,1,0:T(8,128)S(1)} %pad_maximum_fusion.11), channel_id=1, source_target_pairs={{0,1},{1,2},{2,3},{4,5},{5,6},{6,7},{8,9},{9,10},{10,11},{12,13},{... | collective-permute-start | bytes 73736 | tf_op jit(solution)/shard_map/ppermute | solution.py:107
  11.8 8.9 %collective-permute-start.6 = (f32[3,16,128]{2,1,0:T(8,128)S(1)}, f32[3,16,128]{2,1,0:T(8,128)S(1)}, u32[]{:S(2)}, u32[]{:S(2)}) collective-permute-start(f32[3,16,128]{2,1,0:T(8,128)S(1)} %pad_maximum_fusion.12), channel_id=1, source_target_pairs={{1,0},{2,1},{3,2},{5,4},{6,5},{7,6},{9,8},{10,9},{11,10},{13,12},{... | collective-permute-start | bytes 73736 | tf_op jit(solution)/shard_map/ppermute | solution.py:107
  13.1 10.3 %collective-permute-start = (f32[2,2,128]{2,1,0:T(2,128)S(1)}, f32[2,2,128]{2,1,0:T(2,128)S(1)}, u32[]{:S(2)}, u32[]{:S(2)}) collective-permute-start(f32[2,2,128]{2,1,0:T(2,128)S(1)} %get-tuple-element.18), channel_id=1, source_target_pairs={{0,5},{1,6},{2,7},{4,9},{5,10},{6,11},{8,13},{9,14},{10,15},{12,17... | collective-permute-start | bytes 6152 | tf_op jit(solution)/shard_map/ppermute | solution.py:117
  20.1 3.4 %collective-permute-start.2 = (f32[2,2,128]{2,1,0:T(2,128)S(1)}, f32[2,2,128]{2,1,0:T(2,128)S(1)}, u32[]{:S(2)}, u32[]{:S(2)}) collective-permute-start(f32[2,2,128]{2,1,0:T(2,128)S(1)} %get-tuple-element.17), channel_id=1, source_target_pairs={{4,1},{5,2},{6,3},{8,5},{9,6},{10,7},{12,9},{13,10},{14,11},{16,13... | collective-permute-start | bytes 6152 | tf_op jit(solution)/shard_map/ppermute | solution.py:117
  20.8 2.7 %collective-permute-start.5 = (f32[2,2,128]{2,1,0:T(2,128)S(1)}, f32[2,2,128]{2,1,0:T(2,128)S(1)}, u32[]{:S(2)}, u32[]{:S(2)}) collective-permute-start(f32[2,2,128]{2,1,0:T(2,128)S(1)} %get-tuple-element.15), channel_id=1, source_target_pairs={{1,4},{2,5},{3,6},{5,8},{6,9},{7,10},{9,12},{10,13},{11,14},{13,16... | collective-permute-start | bytes 6152 | tf_op jit(solution)/shard_map/ppermute | solution.py:117
  21.4 11.6 %collective-permute-start.7 = (f32[2,2,128]{2,1,0:T(2,128)S(1)}, f32[2,2,128]{2,1,0:T(2,128)S(1)}, u32[]{:S(2)}, u32[]{:S(2)}) collective-permute-start(f32[2,2,128]{2,1,0:T(2,128)S(1)} %get-tuple-element.16), channel_id=1, source_target_pairs={{5,0},{6,1},{7,2},{9,4},{10,5},{11,6},{13,8},{14,9},{15,10},{17,12... | collective-permute-start | bytes 6152 | tf_op jit(solution)/shard_map/ppermute | solution.py:117
  42.4 5.5 %collective-permute-start.10 = (f32[129,128]{1,0:T(8,128)S(1)}, f32[129,128]{1,0:T(8,128)S(1)}, u32[]{:S(2)}, u32[]{:S(2)}) collective-permute-start(f32[129,128]{1,0:T(8,128)S(1)} %pad_maximum_fusion.10), channel_id=1, source_target_pairs={{0,12},{4,8},{8,4},{12,0},{16,28},{20,24},{24,20},{28,16},{1,13},{... | collective-permute-start | bytes 198152 | tf_op jit(solution)/shard_map/ppermute | solution.py:38
  45.3 2.6 %collective-permute-start.8 = (f32[129,128]{1,0:T(8,128)S(1)}, f32[129,128]{1,0:T(8,128)S(1)}, u32[]{:S(2)}, u32[]{:S(2)}) collective-permute-start(f32[129,128]{1,0:T(8,128)S(1)} %pad_maximum_fusion.10), channel_id=1, source_target_pairs={{0,4},{4,0},{8,12},{12,8},{16,20},{20,16},{24,28},{28,24},{1,5},{5... | collective-permute-start | bytes 198152 | tf_op jit(solution)/shard_map/ppermute | solution.py:38
  45.9 4.3 %collective-permute-start.9 = (f32[129,128]{1,0:T(8,128)S(1)}, f32[129,128]{1,0:T(8,128)S(1)}, u32[]{:S(2)}, u32[]{:S(2)}) collective-permute-start(f32[129,128]{1,0:T(8,128)S(1)} %pad_maximum_fusion.10), channel_id=1, source_target_pairs={{0,8},{4,12},{8,0},{12,4},{16,24},{20,28},{24,16},{28,20},{1,9},{5... | collective-permute-start | bytes 198152 | tf_op jit(solution)/shard_map/ppermute | solution.py:38
  50.2 4.4 %collective-permute-start.11 = (f32[129,128]{1,0:T(8,128)S(1)}, f32[129,128]{1,0:T(8,128)S(1)}, u32[]{:S(2)}, u32[]{:S(2)}) collective-permute-start(f32[129,128]{1,0:T(8,128)S(1)} %add_add_fusion.1), channel_id=1, source_target_pairs={{0,16},{4,20},{8,24},{12,28},{16,0},{20,4},{24,8},{28,12},{1,17},{... | collective-permute-start | bytes 198152 | tf_op jit(solution)/shard_map/ppermute | solution.py:38
  54.6 6.7 %collective-permute-start.12 = (f32[129,128]{1,0:T(8,128)S(1)}, f32[129,128]{1,0:T(8,128)S(1)}, u32[]{:S(2)}, u32[]{:S(2)}) collective-permute-start(f32[129,128]{1,0:T(8,128)S(1)} %add.107), channel_id=1, source_target_pairs={{0,1},{1,0},{2,3},{3,2},{4,5},{5,4},{6,7},{7,6},{8,9},{9,8},{10,11... | collective-permute-start | bytes 198152 | tf_op jit(solution)/shard_map/ppermute | solution.py:38
  58.4 6.3 %collective-permute-start.13 = (f32[129,128]{1,0:T(8,128)S(1)}, f32[129,128]{1,0:T(8,128)S(1)}, u32[]{:S(2)}, u32[]{:S(2)}) collective-permute-start(f32[129,128]{1,0:T(8,128)S(1)} %add.107), channel_id=1, source_target_pairs={{0,2},{1,3},{2,0},{3,1},{4,6},{5,7},{6,4},{7,5},{8,10},{9,11},{10,... | collective-permute-start | bytes 198152 | tf_op jit(solution)/shard_map/ppermute | solution.py:38
  59.5 6.2 %collective-permute-start.14 = (f32[129,128]{1,0:T(8,128)S(1)}, f32[129,128]{1,0:T(8,128)S(1)}, u32[]{:S(2)}, u32[]{:S(2)}) collective-permute-start(f32[129,128]{1,0:T(8,128)S(1)} %add.107), channel_id=1, source_target_pairs={{0,3},{1,2},{2,1},{3,0},{4,7},{5,6},{6,5},{7,4},{8,11},{9,10},{10,... | collective-permute-start | bytes 198152 | tf_op jit(solution)/shard_map/ppermute | solution.py:38
  84.6 3.5 %copy-start = (f32[128,128]{1,0:T(8,128)S(1)}, f32[128,128]{1,0:T(8,128)}, u32[]{:S(2)}) copy-start(f32[128,128]{1,0:T(8,128)} %shard_map.68) | copy-start | bytes 196612

commit v8 on v7

--- a/solution.py
+++ b/solution.py
@@ -107,16 +107,6 @@
     return lax.ppermute(block, axis, pairs)
 
 
-def from_diagonal(block, step_x, step_y):
-    rows, cols = lax.axis_size("gx"), lax.axis_size("gy")
-    pairs = []
-    for a in range(rows):
-        for b in range(cols):
-            if 0 <= a + step_x < rows and 0 <= b + step_y < cols:
-                pairs.append((a * cols + b, (a + step_x) * cols + b + step_y))
-    return lax.ppermute(block, ("gx", "gy"), pairs)
-
-
 def forecast_two_steps(warmth, heat):
     width, height = warmth.shape[0], warmth.shape[1]
     top = from_neighbour(
@@ -125,29 +115,27 @@
     bottom = from_neighbour(
         jnp.concatenate([warmth[:, :2], heat[:, :1]], axis=1), "gx", -1
     )
-    left = from_neighbour(jnp.concatenate([warmth[-2:], heat[-1:]], axis=0), "gy", 1)
-    right = from_neighbour(jnp.concatenate([warmth[:2], heat[:1]], axis=0), "gy", -1)
-    top_left = from_diagonal(warmth[-2:, -2:], 1, 1)
-    top_right = from_diagonal(warmth[:2, -2:], 1, -1)
-    bottom_left = from_diagonal(warmth[-2:, :2], -1, 1)
-    bottom_right = from_diagonal(warmth[:2, :2], -1, -1)
-    warmth_wide = jnp.concatenate(
-        [
-            jnp.concatenate([top_left, left[:2], bottom_left], axis=1),
-            jnp.concatenate([top[:, :2], warmth, bottom[:, :2]], axis=1),
-            jnp.concatenate([top_right, right[:2], bottom_right], axis=1),
-        ],
-        axis=0,
-    )
-    corner = jnp.zeros_like(heat[:1, :1])
-    heat_wide = jnp.concatenate(
-        [
-            jnp.concatenate([corner, left[2:], corner], axis=1),
-            jnp.concatenate([top[:, 2:], heat, bottom[:, 2:]], axis=1),
-            jnp.concatenate([corner, right[2:], corner], axis=1),
-        ],
-        axis=0,
-    )
+    warmth_tall = jnp.concatenate([top[:, :2], warmth, bottom[:, :2]], axis=1)
+    heat_tall = jnp.concatenate([top[:, 2:], heat, bottom[:, 2:]], axis=1)
+    edge = jnp.zeros_like(heat_tall[:1, :1])
+    left = from_neighbour(
+        jnp.concatenate(
+            [warmth_tall[-2:], jnp.concatenate([edge, heat_tall[-1:], edge], axis=1)],
+            axis=0,
+        ),
+        "gy",
+        1,
+    )
+    right = from_neighbour(
+        jnp.concatenate(
+            [warmth_tall[:2], jnp.concatenate([edge, heat_tall[:1], edge], axis=1)],
+            axis=0,
+        ),
+        "gy",
+        -1,
+    )
+    warmth_wide = jnp.concatenate([left[:2], warmth_tall, right[:2]], axis=0)
+    heat_wide = jnp.concatenate([left[2:, 1:-1], heat_tall, right[2:, 1:-1]], axis=0)
     first = propagate_members_last(warmth_wide, heat_wide)
     col = lax.broadcasted_iota(jnp.int32, (width + 2, height + 2), 0)
     row = lax.broadcasted_iota(jnp.int32, (width + 2, height + 2), 1)

time: 91.2 us -> 73.8 us (0.81)
  starting transfers between devices: 27.9 us -> 20.4 us
  waiting for transfers between devices: 22.9 us -> 17.8 us
  other arithmetic: 7.29 us -> 4.06 us
  local copies, waits for them, and re-layouts: 6.36 us -> 5.01 us
    ppermute x4 -> x0, waiting for transfers between devices: 9.59 us -> none  [from_diagonal(): return lax.ppermute(block, ('gx', 'gy'), pairs)]
    ppermute x4 -> x0, starting transfers between devices: 8.78 us -> none  [from_diagonal(): return lax.ppermute(block, ('gx', 'gy'), pairs)]
    ppermute x4, waiting for transfers between devices: 0.01 us -> 5.09 us  [from_neighbour(): return lax.ppermute(block, axis, pairs)]
    select_n x1, other arithmetic: 4.35 us -> 2.12 us  [forecast_two_steps(): first = jnp.where(outside[:, :, None], 0.0, first)]
    ppermute x7, starting transfers between devices: 9.83 us -> 10.9 us  [butterfly_sum(): received[offset] = lax.ppermute(value, axis, pairs)]
  transfers between devices with their start and end apart: 15 -> 11, of which waited for: 7 -> 8; matrix products, arithmetic and copies ran while one was open for 2% -> 1% of each run, Pallas kernels for 0% -> 0%
where the time goes in v8:
time: 73.8 us; the launch traced here: 73.4 us
  starting transfers between devices  20.4 us (28%)
  waiting for transfers between devices  17.8 us (24%)
  Pallas kernels  16.2 us (22%)
  matrix products  8.85 us (12%)
  local copies, waits for them, and re-layouts  5.01 us (7%)
  other arithmetic  4.06 us (6%)
  between operations  1.04 us (1%)
    pallas_call x1, Pallas kernels, inverse_factor(): pl.pallas_call(inverse_factor_kernel, out_shape=jax.ShapeDtypeStruct((siz...  16.2 us
    ppermute x7, waiting for transfers between devices, butterfly_sum(): received[offset] = lax.ppermute(value, axis, pairs)  12.7 us
    ppermute x7, starting transfers between devices, butterfly_sum(): received[offset] = lax.ppermute(value, axis, pairs)  10.9 us
    ppermute x4, starting transfers between devices, from_neighbour(): return lax.ppermute(block, axis, pairs)  9.5 us
    ppermute x4, waiting for transfers between devices, from_neighbour(): return lax.ppermute(block, axis, pairs)  5.09 us
    unnamed x14, local copies, waits for them, and re-layouts  4.87 us
    dot_general x1, matrix products, shards(): lax.dot_general(deviation_t * cell_weight[:, :, None], deviation_t, (((0,...  2.7 us
    select_n x1, other arithmetic, forecast_two_steps(): first = jnp.where(outside[:, :, None], 0.0, first)  2.12 us
  transfers between devices with their start and end apart: 11, of which 8 were waited for; matrix products, arithmetic and copies ran while one was open for 1% of the time, Pallas kernels for 0%

profile of v8, /device:TPU:0, one launch (start us, length us, event | category | flops | bytes accessed | tf_op | source)
XLA Modules:
  0.0 73.4 jit_solution(12812782718934290058)
XLA Ops:
  0.6 0.0 copy-start.1
  0.6 1.7 %copy.14 = f32[128,16,128]{0,2,1:T(8,128)S(1)} copy(f32[128,16,128]{2,1,0:T(8,128)} %param.6) | data formatting | bytes 2097152 | tf_op args[1]
  2.3 0.0 copy-done.1
  2.3 0.0 copy-start.2
  2.4 0.0 copy-start.3
  2.4 0.0 copy-start.4
  2.4 0.4 copy.13
  2.9 2.4 %collective-permute-start = (f32[128,3,128]{2,0,1:T(8,128)S(1)}, f32[128,3,128]{2,0,1:T(8,128)S(1)}, u32[]{:S(2)}, u32[]{:S(2)}) collective-permute-start(f32[128,3,128]{2,0,1:T(8,128)S(1)} %pad_maximum_fusion.7), channel_id=1, source_target_pairs={{0,4},{4,8},{8,12},{12,16},{16,20},{20,24},{24,28},{1,5},{5,9},{9,... | collective-permute-start | bytes 589832 | tf_op jit(solution)/shard_map/ppermute | solution.py:107
  5.3 1.3 %collective-permute-start.1 = (f32[128,3,128]{2,0,1:T(8,128)S(1)}, f32[128,3,128]{2,0,1:T(8,128)S(1)}, u32[]{:S(2)}, u32[]{:S(2)}) collective-permute-start(f32[128,3,128]{2,0,1:T(8,128)S(1)} %pad_maximum_fusion.8), channel_id=1, source_target_pairs={{4,0},{8,4},{12,8},{16,12},{20,16},{24,20},{28,24},{5,1},{9,5},{13... | collective-permute-start | bytes 589832 | tf_op jit(solution)/shard_map/ppermute | solution.py:107
  6.6 0.0 copy-done.2
  6.6 0.0 copy-done.3
  6.6 0.0 copy-done.4
  6.7 0.4 fusion.27
  7.1 0.0 collective-permute-done
  7.1 3.6 %collective-permute-done.1 = f32[128,3,128]{2,0,1:T(8,128)S(1)} collective-permute-done((f32[128,3,128]{2,0,1:T(8,128)S(1)}, f32[128,3,128]{2,0,1:T(8,128)S(1)}, u32[]{:S(2)}, u32[]{:S(2)}) %collective-permute-start.1) | collective-permute-done | bytes 196640 | tf_op jit(solution)/shard_map/ppermute | solution.py:107
  10.8 1.3 %collective-permute-start.3 = (f32[3,20,128]{2,1,0:T(8,128)S(1)}, f32[3,20,128]{2,1,0:T(8,128)S(1)}, u32[]{:S(2)}, u32[]{:S(2)}) collective-permute-start(f32[3,20,128]{2,1,0:T(8,128)S(1)} %pad_maximum_fusion.11), channel_id=1, source_target_pairs={{1,0},{2,1},{3,2},{5,4},{6,5},{7,6},{9,8},{10,9},{11,10},{13,12},{... | collective-permute-start | bytes 92168 | tf_op jit(solution)/shard_map/ppermute | solution.py:107
  12.2 4.5 %collective-permute-start.2 = (f32[3,20,128]{2,1,0:T(8,128)S(1)}, f32[3,20,128]{2,1,0:T(8,128)S(1)}, u32[]{:S(2)}, u32[]{:S(2)}) collective-permute-start(f32[3,20,128]{2,1,0:T(8,128)S(1)} %pad_maximum_fusion.10), channel_id=1, source_target_pairs={{0,1},{1,2},{2,3},{4,5},{5,6},{6,7},{8,9},{9,10},{10,11},{12,13},{... | collective-permute-start | bytes 92168 | tf_op jit(solution)/shard_map/ppermute | solution.py:107
  16.7 0.1 or_or_fusion
  16.8 0.0 collective-permute-done.3
  16.8 1.5 %collective-permute-done.2 = f32[3,20,128]{2,1,0:T(8,128)S(1)} collective-permute-done((f32[3,20,128]{2,1,0:T(8,128)S(1)}, f32[3,20,128]{2,1,0:T(8,128)S(1)}, u32[]{:S(2)}, u32[]{:S(2)}) %collective-permute-start.2) | collective-permute-done | bytes 30752 | tf_op jit(solution)/shard_map/ppermute | solution.py:107
  18.4 0.1 pad_maximum_fusion
  18.5 2.1 %fusion.9 = f32[130,18,128]{2,0,1:T(8,128)S(1)} fusion(f32[2,20,128]{2,0,1:T(2,128)S(1)} %copy.19, f32[128,2,128]{2,0,1:T(8,128)S(1)} %slice.129, f32[128,16,128]{2,0,1:T(8,128)S(1)} %bitcast.56, f32[128,2,128]{2,0,1:T(8,128)S(1)} %slice.126, f32[2,20,128]{2,0,1:T(2,128)S(1)} %copy.20, f32[132,20,128]{2,0,1:T(8,128)S(1)} %pad_maximum_fusion, ...), kind=kLoop, calls=%fused_computation.13 | loop fusion | flops 5990400 | bytes 7344420 | tf_op jit(solution)/shard_map/jit(_where)/select_n | solution.py:149
  20.7 0.9 %fusion.48 = (f32[128,16]{0,1:T(8,128)S(1)}, f32[128,16,128]{2,0,1:T(8,128)S(1)}, f32[128,16]{0,1:T(8,128)S(1)}) fusion(f32[128,16,128]{0,2,1:T(8,128)S(1)} %copy.14, f32[130,18,128]{2,0,1:T(8,128)S(1)} %fusion.9), kind=kLoop, calls=%fused_computation.101 | loop fusion | flops 2879488 | bytes 7356416 | tf_op jit(solution)/shard_map/reduce_sum | solution.py:164
  21.6 2.7 %fusion.11 = f32[128,128]{1,0:T(8,128)S(1)} fusion(f32[128,16,128]{2,0,1:T(8,128)S(1)} %get-tuple-element.7, f32[128,16]{0,1:T(8,128)S(1)} %get-tuple-element.17, f32[128,16]{0,1:T(8,128)S(1)} %get-tuple-element.20), kind=kOutput, calls=%fused_computation.22 | convolution fusion | flops 403439616 | bytes 1130496 | tf_op jit(solution)/shard_map/dot_general | solution.py:187
  24.3 0.8 %convolution_bitcast_fusion.2 = f32[1,128]{1,0:T(1,128)S(1)} fusion(f32[128,16,1]{0,2,1:T(1,128)S(1)} %bitcast.57, f32[128,16,128]{2,0,1:T(8,128)S(1)} %get-tuple-element.7, f32[128,16]{0,1:T(8,128)S(1)} %get-tuple-element.20), kind=kOutput, calls=%fused_computation.23 | convolution fusion | flops 3407872 | bytes 1065472 | tf_op jit(solution)/shard_map/dot_general | solution.py:193
  25.1 3.1 %collective-permute-start.4 = (f32[129,128]{1,0:T(8,128)S(1)}, f32[129,128]{1,0:T(8,128)S(1)}, u32[]{:S(2)}, u32[]{:S(2)}) collective-permute-start(f32[129,128]{1,0:T(8,128)S(1)} %pad_maximum_fusion.9), channel_id=1, source_target_pairs={{0,4},{4,0},{8,12},{12,8},{16,20},{20,16},{24,28},{28,24},{1,5},{5... | collective-permute-start | bytes 198152 | tf_op jit(solution)/shard_map/ppermute | solution.py:38
  28.2 2.4 %collective-permute-start.5 = (f32[129,128]{1,0:T(8,128)S(1)}, f32[129,128]{1,0:T(8,128)S(1)}, u32[]{:S(2)}, u32[]{:S(2)}) collective-permute-start(f32[129,128]{1,0:T(8,128)S(1)} %pad_maximum_fusion.9), channel_id=1, source_target_pairs={{0,8},{4,12},{8,0},{12,4},{16,24},{20,28},{24,16},{28,20},{1,9},{5... | collective-permute-start | bytes 198152 | tf_op jit(solution)/shard_map/ppermute | solution.py:38
  30.6 0.0 collective-permute-start.6
  30.6 0.0 collective-permute-done.4
  30.6 2.4 %collective-permute-done.5 = f32[129,128]{1,0:T(8,128)S(1)} collective-permute-done((f32[129,128]{1,0:T(8,128)S(1)}, f32[129,128]{1,0:T(8,128)S(1)}, u32[]{:S(2)}, u32[]{:S(2)}) %collective-permute-start.5) | collective-permute-done | bytes 66080 | tf_op jit(solution)/shard_map/ppermute | solution.py:38
  33.0 2.0 %collective-permute-done.6 = f32[129,128]{1,0:T(8,128)S(1)} collective-permute-done((f32[129,128]{1,0:T(8,128)S(1)}, f32[129,128]{1,0:T(8,128)S(1)}, u32[]{:S(2)}, u32[]{:S(2)}) %collective-permute-start.6) | collective-permute-done | bytes 66080 | tf_op jit(solution)/shard_map/ppermute | solution.py:38
  35.0 0.6 collective-permute-start.7
  35.7 3.7 %collective-permute-done.7 = f32[129,128]{1,0:T(8,128)S(1)} collective-permute-done((f32[129,128]{1,0:T(8,128)S(1)}, f32[129,128]{1,0:T(8,128)S(1)}, u32[]{:S(2)}, u32[]{:S(2)}) %collective-permute-start.7) | collective-permute-done | bytes 66080 | tf_op jit(solution)/shard_map/ppermute | solution.py:38
  39.4 4.1 %collective-permute-start.10 = (f32[129,128]{1,0:T(8,128)S(1)}, f32[129,128]{1,0:T(8,128)S(1)}, u32[]{:S(2)}, u32[]{:S(2)}) collective-permute-start(f32[129,128]{1,0:T(8,128)S(1)} %add.107), channel_id=1, source_target_pairs={{0,3},{1,2},{2,1},{3,0},{4,7},{5,6},{6,5},{7,4},{8,11},{9,10},{10,... | collective-permute-start | bytes 198152 | tf_op jit(solution)/shard_map/ppermute | solution.py:38
  43.5 0.0 collective-permute-start.8
  43.5 0.6 collective-permute-start.9
  44.2 1.8 %collective-permute-done.10 = f32[129,128]{1,0:T(8,128)S(1)} collective-permute-done((f32[129,128]{1,0:T(8,128)S(1)}, f32[129,128]{1,0:T(8,128)S(1)}, u32[]{:S(2)}, u32[]{:S(2)}) %collective-permute-start.10) | collective-permute-done | bytes 66080 | tf_op jit(solution)/shard_map/ppermute | solution.py:38
  46.0 1.9 %collective-permute-done.8 = f32[129,128]{1,0:T(8,128)S(1)} collective-permute-done((f32[129,128]{1,0:T(8,128)S(1)}, f32[129,128]{1,0:T(8,128)S(1)}, u32[]{:S(2)}, u32[]{:S(2)}) %collective-permute-start.8) | collective-permute-done | bytes 66080 | tf_op jit(solution)/shard_map/ppermute | solution.py:38
  47.9 0.9 %collective-permute-done.9 = f32[129,128]{1,0:T(8,128)S(1)} collective-permute-done((f32[129,128]{1,0:T(8,128)S(1)}, f32[129,128]{1,0:T(8,128)S(1)}, u32[]{:S(2)}, u32[]{:S(2)}) %collective-permute-start.9) | collective-permute-done | bytes 66080 | tf_op jit(solution)/shard_map/ppermute | solution.py:38
  48.8 0.6 slice_add_fusion.4.gram_ref
  49.4 16.2 %shard_map.68 = f32[128,128]{1,0:T(8,128)} custom-call(f32[128,128]{1,0:T(8,128)} %slice_add_fusion.4.gram_ref), custom_call_target="tpu_custom_call" | custom-call | tf_op jit(solution)/shard_map/pallas_call | solution.py:71
  65.6 1.0 %convolution_bitcast_fusion.4 = f32[128,1]{0,1:T(1,128)S(1)} fusion(f32[128,128]{1,0:T(8,128)} %shard_map.68, f32[129,128]{1,0:T(8,128)S(1)} %add_add_fusion), kind=kOutput, calls=%fused_computation.25 | convolution fusion | flops 196608 | bytes 66560 | tf_op jit(solution)/shard_map/dot_general | solution.py:206
  66.6 1.0 %convolution_bitcast_fusion.3 = f32[128]{0:T(128)S(1)} fusion(f32[128,1]{0,1:T(1,128)S(1)} %convolution_bitcast_fusion.4, f32[128,128]{1,0:T(8,128)} %shard_map.68), kind=kOutput, calls=%fused_computation.24 | convolution fusion | flops 196608 | bytes 66560 | tf_op jit(solution)/shard_map/dot_general | solution.py:207
  67.7 1.9 %fusion.2 = f32[128,16,128]{0,2,1:T(8,128)S(1)} fusion(f32[128,16]{0,1:T(8,128)S(1)} %get-tuple-element.22, f32[16,128]{1,0:T(8,128)S(1)} %get-tuple-element.21, f32[128,128]{1,0:T(8,128)} %shard_map.68, f32[128]{0:T(128)S(1)} %convolution_bitcast_fusion.3, f32[128,16,128]{0,2,1:T(8,128)S(1)} %copy.14), kind=kOutput, calls=%fused_computation.4 | convolution fusion | flops 403193856 | bytes 2179584 | tf_op jit(solution)/shard_map/dot_general | solution.py:213
  69.6 0.0 copy-start
  69.6 1.4 %copy.27 = f32[128,16,128]{2,1,0:T(8,128)} copy(f32[128,16,128]{0,2,1:T(8,128)S(1)} %fusion.2) | data formatting | bytes 2097152
  70.9 0.0 copy-done
  71.0 1.0 %fusion.3 = f32[128,16,128]{0,2,1:T(8,128)S(1)} fusion(f32[128,16,128]{2,0,1:T(8,128)S(1)} %get-tuple-element.7, f32[128,16]{0,1:T(8,128)S(1)} %get-tuple-element.20, f32[16,128]{1,0:T(8,128)S(1)} %get-tuple-element.19, f32[128,128]{1,0:T(8,128)S(1)} %copy-done, f32[128]{0:T(128)S(1)} %convolution_bitcast_fusion.3), kind=kOutput, calls=%fused_computation.6 | convolution fusion | flops 403193856 | bytes 2179584 | tf_op jit(solution)/shard_map/dot_general | solution.py:210
  72.0 1.4 %copy.26 = f32[128,16,128]{2,1,0:T(8,128)} copy(f32[128,16,128]{0,2,1:T(8,128)S(1)} %fusion.3) | data formatting | bytes 2097152
  (36 shorter events, 0.4 us)
Async XLA Ops:
  0.6 1.7 %copy-start.1 = (f32[128,16,128]{2,1,0:T(8,128)S(1)}, f32[128,16,128]{2,1,0:T(8,128)}, u32[]{:S(2)}) copy-start(f32[128,16,128]{2,1,0:T(8,128)} %param.5) | copy-start | bytes 3145732
  2.3 4.2 %copy-start.2 = (s32[1024]{0:T(1024)S(1)}, s32[1024]{0:T(1024)}, u32[]{:S(2)}) copy-start(s32[1024]{0:T(1024)} %param.9) | copy-start | bytes 12292
  2.4 4.3 %copy-start.3 = (f32[1024]{0:T(1024)S(1)}, f32[1024]{0:T(1024)}, u32[]{:S(2)}) copy-start(f32[1024]{0:T(1024)} %param.8) | copy-start | bytes 12292
  2.4 4.3 %copy-start.4 = (f32[1024]{0:T(1024)S(1)}, f32[1024]{0:T(1024)}, u32[]{:S(2)}) copy-start(f32[1024]{0:T(1024)} %param.7) | copy-start | bytes 12292
  2.9 4.2 %collective-permute-start = (f32[128,3,128]{2,0,1:T(8,128)S(1)}, f32[128,3,128]{2,0,1:T(8,128)S(1)}, u32[]{:S(2)}, u32[]{:S(2)}) collective-permute-start(f32[128,3,128]{2,0,1:T(8,128)S(1)} %pad_maximum_fusion.7), channel_id=1, source_target_pairs={{0,4},{4,8},{8,12},{12,16},{16,20},{20,24},{24,28},{1,5},{5,9},{9,... | collective-permute-start | bytes 589832 | tf_op jit(solution)/shard_map/ppermute | solution.py:107
  5.3 5.4 %collective-permute-start.1 = (f32[128,3,128]{2,0,1:T(8,128)S(1)}, f32[128,3,128]{2,0,1:T(8,128)S(1)}, u32[]{:S(2)}, u32[]{:S(2)}) collective-permute-start(f32[128,3,128]{2,0,1:T(8,128)S(1)} %pad_maximum_fusion.8), channel_id=1, source_target_pairs={{4,0},{8,4},{12,8},{16,12},{20,16},{24,20},{28,24},{5,1},{9,5},{13... | collective-permute-start | bytes 589832 | tf_op jit(solution)/shard_map/ppermute | solution.py:107
  10.8 6.0 %collective-permute-start.3 = (f32[3,20,128]{2,1,0:T(8,128)S(1)}, f32[3,20,128]{2,1,0:T(8,128)S(1)}, u32[]{:S(2)}, u32[]{:S(2)}) collective-permute-start(f32[3,20,128]{2,1,0:T(8,128)S(1)} %pad_maximum_fusion.11), channel_id=1, source_target_pairs={{1,0},{2,1},{3,2},{5,4},{6,5},{7,6},{9,8},{10,9},{11,10},{13,12},{... | collective-permute-start | bytes 92168 | tf_op jit(solution)/shard_map/ppermute | solution.py:107
  12.2 6.2 %collective-permute-start.2 = (f32[3,20,128]{2,1,0:T(8,128)S(1)}, f32[3,20,128]{2,1,0:T(8,128)S(1)}, u32[]{:S(2)}, u32[]{:S(2)}) collective-permute-start(f32[3,20,128]{2,1,0:T(8,128)S(1)} %pad_maximum_fusion.10), channel_id=1, source_target_pairs={{0,1},{1,2},{2,3},{4,5},{5,6},{6,7},{8,9},{9,10},{10,11},{12,13},{... | collective-permute-start | bytes 92168 | tf_op jit(solution)/shard_map/ppermute | solution.py:107
  25.1 5.5 %collective-permute-start.4 = (f32[129,128]{1,0:T(8,128)S(1)}, f32[129,128]{1,0:T(8,128)S(1)}, u32[]{:S(2)}, u32[]{:S(2)}) collective-permute-start(f32[129,128]{1,0:T(8,128)S(1)} %pad_maximum_fusion.9), channel_id=1, source_target_pairs={{0,4},{4,0},{8,12},{12,8},{16,20},{20,16},{24,28},{28,24},{1,5},{5... | collective-permute-start | bytes 198152 | tf_op jit(solution)/shard_map/ppermute | solution.py:38
  28.2 4.8 %collective-permute-start.5 = (f32[129,128]{1,0:T(8,128)S(1)}, f32[129,128]{1,0:T(8,128)S(1)}, u32[]{:S(2)}, u32[]{:S(2)}) collective-permute-start(f32[129,128]{1,0:T(8,128)S(1)} %pad_maximum_fusion.9), channel_id=1, source_target_pairs={{0,8},{4,12},{8,0},{12,4},{16,24},{20,28},{24,16},{28,20},{1,9},{5... | collective-permute-start | bytes 198152 | tf_op jit(solution)/shard_map/ppermute | solution.py:38
  30.6 4.5 %collective-permute-start.6 = (f32[129,128]{1,0:T(8,128)S(1)}, f32[129,128]{1,0:T(8,128)S(1)}, u32[]{:S(2)}, u32[]{:S(2)}) collective-permute-start(f32[129,128]{1,0:T(8,128)S(1)} %pad_maximum_fusion.9), channel_id=1, source_target_pairs={{0,12},{4,8},{8,4},{12,0},{16,28},{20,24},{24,20},{28,16},{1,13},{... | collective-permute-start | bytes 198152 | tf_op jit(solution)/shard_map/ppermute | solution.py:38
  35.0 4.4 %collective-permute-start.7 = (f32[129,128]{1,0:T(8,128)S(1)}, f32[129,128]{1,0:T(8,128)S(1)}, u32[]{:S(2)}, u32[]{:S(2)}) collective-permute-start(f32[129,128]{1,0:T(8,128)S(1)} %add_add_fusion.1), channel_id=1, source_target_pairs={{0,16},{4,20},{8,24},{12,28},{16,0},{20,4},{24,8},{28,12},{1,17},{... | collective-permute-start | bytes 198152 | tf_op jit(solution)/shard_map/ppermute | solution.py:38
  39.4 6.6 %collective-permute-start.10 = (f32[129,128]{1,0:T(8,128)S(1)}, f32[129,128]{1,0:T(8,128)S(1)}, u32[]{:S(2)}, u32[]{:S(2)}) collective-permute-start(f32[129,128]{1,0:T(8,128)S(1)} %add.107), channel_id=1, source_target_pairs={{0,3},{1,2},{2,1},{3,0},{4,7},{5,6},{6,5},{7,4},{8,11},{9,10},{10,... | collective-permute-start | bytes 198152 | tf_op jit(solution)/shard_map/ppermute | solution.py:38
  43.5 4.3 %collective-permute-start.8 = (f32[129,128]{1,0:T(8,128)S(1)}, f32[129,128]{1,0:T(8,128)S(1)}, u32[]{:S(2)}, u32[]{:S(2)}) collective-permute-start(f32[129,128]{1,0:T(8,128)S(1)} %add.107), channel_id=1, source_target_pairs={{0,1},{1,0},{2,3},{3,2},{4,5},{5,4},{6,7},{7,6},{8,9},{9,8},{10,11... | collective-permute-start | bytes 198152 | tf_op jit(solution)/shard_map/ppermute | solution.py:38
  43.5 5.2 %collective-permute-start.9 = (f32[129,128]{1,0:T(8,128)S(1)}, f32[129,128]{1,0:T(8,128)S(1)}, u32[]{:S(2)}, u32[]{:S(2)}) collective-permute-start(f32[129,128]{1,0:T(8,128)S(1)} %add.107), channel_id=1, source_target_pairs={{0,2},{1,3},{2,0},{3,1},{4,6},{5,7},{6,4},{7,5},{8,10},{9,11},{10,... | collective-permute-start | bytes 198152 | tf_op jit(solution)/shard_map/ppermute | solution.py:38
  69.6 1.4 %copy-start = (f32[128,128]{1,0:T(8,128)S(1)}, f32[128,128]{1,0:T(8,128)}, u32[]{:S(2)}) copy-start(f32[128,128]{1,0:T(8,128)} %shard_map.68) | copy-start | bytes 196612

commit v9 on v8

--- a/solution.py
+++ b/solution.py
@@ -47,23 +47,27 @@
     square_col = lax.broadcasted_iota(jnp.int32, (size, size), 1)
     inverse_ref[...] = jnp.where(square_row == square_col, 1.0, 0.0).astype(jnp.float32)
     lane = lax.broadcasted_iota(jnp.int32, (1, size), 1)
-    sublane = lax.broadcasted_iota(jnp.int32, (size, 1), 0)
-
-    def step(k, carry):
-        row = work_ref[pl.ds(k, 1), :]
-        column = jnp.sum(jnp.where(square_col == k, work_ref[...], 0.0), axis=1, keepdims=True)
-        pivot = jnp.sum(jnp.where(lane == k, row, 0.0), axis=1, keepdims=True)
-        root = jnp.sqrt(pivot)
-        factor_row = jnp.where(lane >= k, row / root, 0.0)
-        factor_col = jnp.where(sublane >= k, column / root, 0.0)
-        work_ref[...] = work_ref[...] - factor_col * factor_row
-        inverse_row = inverse_ref[pl.ds(k, 1), :] / root
-        below = jnp.where(sublane > k, factor_col, 0.0)
-        inverse_ref[...] = inverse_ref[...] - below * inverse_row
-        inverse_ref[pl.ds(k, 1), :] = inverse_row
-        return carry
-
-    lax.fori_loop(0, size, step, 0)
+    for first in range(0, size, 8):
+        span = size - first
+        sublane = lax.broadcasted_iota(jnp.int32, (span, 1), 0) + first
+        band_col = lax.broadcasted_iota(jnp.int32, (span, size), 1)
+
+        def step(k, carry, first=first, sublane=sublane, band_col=band_col):
+            row = work_ref[pl.ds(k, 1), :]
+            band = work_ref[first:, :]
+            column = jnp.sum(jnp.where(band_col == k, band, 0.0), axis=1, keepdims=True)
+            pivot = jnp.sum(jnp.where(lane == k, row, 0.0), axis=1, keepdims=True)
+            root = jnp.sqrt(pivot)
+            factor_row = jnp.where(lane >= k, row / root, 0.0)
+            factor_col = jnp.where(sublane >= k, column / root, 0.0)
+            work_ref[first:, :] = band - factor_col * factor_row
+            inverse_row = inverse_ref[pl.ds(k, 1), :] / root
+            below = jnp.where(sublane > k, factor_col, 0.0)
+            inverse_ref[first:, :] = inverse_ref[first:, :] - below * inverse_row
+            inverse_ref[pl.ds(k, 1), :] = inverse_row
+            return carry
+
+        lax.fori_loop(first, min(first + 8, size), step, 0)
 
 
 def inverse_factor(gram):

time: 73.8 us -> 72.7 us (0.985)
  Pallas kernels: 16.2 us -> 15.1 us
    pallas_call x1, Pallas kernels: 16.2 us -> 15.1 us  [inverse_factor(): pl.pallas_call(inverse_factor_kernel, out_shape=jax.ShapeDtypeStruct((siz...]
where the time goes in v9:
time: 72.7 us; the launch traced here: 72.3 us
  starting transfers between devices  20.4 us (28%)
  waiting for transfers between devices  17.8 us (24%)
  Pallas kernels  15.1 us (21%)
  matrix products  8.86 us (12%)
  local copies, waits for them, and re-layouts  5.01 us (7%)
  other arithmetic  4.06 us (6%)
  between operations  1.04 us (1%)
    pallas_call x1, Pallas kernels, inverse_factor(): pl.pallas_call(inverse_factor_kernel, out_shape=jax.ShapeDtypeStruct((siz...  15.1 us
    ppermute x7, waiting for transfers between devices, butterfly_sum(): received[offset] = lax.ppermute(value, axis, pairs)  12.7 us
    ppermute x7, starting transfers between devices, butterfly_sum(): received[offset] = lax.ppermute(value, axis, pairs)  10.9 us
    ppermute x4, starting transfers between devices, from_neighbour(): return lax.ppermute(block, axis, pairs)  9.5 us
    ppermute x4, waiting for transfers between devices, from_neighbour(): return lax.ppermute(block, axis, pairs)  5.09 us
    unnamed x14, local copies, waits for them, and re-layouts  4.87 us
    dot_general x1, matrix products, shards(): lax.dot_general(deviation_t * cell_weight[:, :, None], deviation_t, (((0,...  2.7 us
    select_n x1, other arithmetic, forecast_two_steps(): first = jnp.where(outside[:, :, None], 0.0, first)  2.12 us
  transfers between devices with their start and end apart: 11, of which 8 were waited for; matrix products, arithmetic and copies ran while one was open for 1% of the time, Pallas kernels for 0%

profile of v9, /device:TPU:0, one launch (start us, length us, event | category | flops | bytes accessed | tf_op | source)
XLA Modules:
  0.0 72.3 jit_solution(14146151497724598481)
XLA Ops:
  0.6 0.0 copy-start.1
  0.6 1.7 %copy.14 = f32[128,16,128]{0,2,1:T(8,128)S(1)} copy(f32[128,16,128]{2,1,0:T(8,128)} %param.6) | data formatting | bytes 2097152 | tf_op args[1]
  2.3 0.0 copy-done.1
  2.3 0.0 copy-start.2
  2.4 0.0 copy-start.3
  2.4 0.0 copy-start.4
  2.4 0.4 copy.13
  2.9 2.4 %collective-permute-start = (f32[128,3,128]{2,0,1:T(8,128)S(1)}, f32[128,3,128]{2,0,1:T(8,128)S(1)}, u32[]{:S(2)}, u32[]{:S(2)}) collective-permute-start(f32[128,3,128]{2,0,1:T(8,128)S(1)} %pad_maximum_fusion.7), channel_id=1, source_target_pairs={{0,4},{4,8},{8,12},{12,16},{16,20},{20,24},{24,28},{1,5},{5,9},{9,... | collective-permute-start | bytes 589832 | tf_op jit(solution)/shard_map/ppermute | solution.py:111
  5.3 1.3 %collective-permute-start.1 = (f32[128,3,128]{2,0,1:T(8,128)S(1)}, f32[128,3,128]{2,0,1:T(8,128)S(1)}, u32[]{:S(2)}, u32[]{:S(2)}) collective-permute-start(f32[128,3,128]{2,0,1:T(8,128)S(1)} %pad_maximum_fusion.8), channel_id=1, source_target_pairs={{4,0},{8,4},{12,8},{16,12},{20,16},{24,20},{28,24},{5,1},{9,5},{13... | collective-permute-start | bytes 589832 | tf_op jit(solution)/shard_map/ppermute | solution.py:111
  6.6 0.0 copy-done.2
  6.6 0.0 copy-done.3
  6.6 0.0 copy-done.4
  6.7 0.4 fusion.27
  7.1 0.0 collective-permute-done
  7.1 3.6 %collective-permute-done.1 = f32[128,3,128]{2,0,1:T(8,128)S(1)} collective-permute-done((f32[128,3,128]{2,0,1:T(8,128)S(1)}, f32[128,3,128]{2,0,1:T(8,128)S(1)}, u32[]{:S(2)}, u32[]{:S(2)}) %collective-permute-start.1) | collective-permute-done | bytes 196640 | tf_op jit(solution)/shard_map/ppermute | solution.py:111
  10.8 1.3 %collective-permute-start.3 = (f32[3,20,128]{2,1,0:T(8,128)S(1)}, f32[3,20,128]{2,1,0:T(8,128)S(1)}, u32[]{:S(2)}, u32[]{:S(2)}) collective-permute-start(f32[3,20,128]{2,1,0:T(8,128)S(1)} %pad_maximum_fusion.11), channel_id=1, source_target_pairs={{1,0},{2,1},{3,2},{5,4},{6,5},{7,6},{9,8},{10,9},{11,10},{13,12},{... | collective-permute-start | bytes 92168 | tf_op jit(solution)/shard_map/ppermute | solution.py:111
  12.2 4.5 %collective-permute-start.2 = (f32[3,20,128]{2,1,0:T(8,128)S(1)}, f32[3,20,128]{2,1,0:T(8,128)S(1)}, u32[]{:S(2)}, u32[]{:S(2)}) collective-permute-start(f32[3,20,128]{2,1,0:T(8,128)S(1)} %pad_maximum_fusion.10), channel_id=1, source_target_pairs={{0,1},{1,2},{2,3},{4,5},{5,6},{6,7},{8,9},{9,10},{10,11},{12,13},{... | collective-permute-start | bytes 92168 | tf_op jit(solution)/shard_map/ppermute | solution.py:111
  16.7 0.1 or_or_fusion
  16.8 0.0 collective-permute-done.3
  16.8 1.5 %collective-permute-done.2 = f32[3,20,128]{2,1,0:T(8,128)S(1)} collective-permute-done((f32[3,20,128]{2,1,0:T(8,128)S(1)}, f32[3,20,128]{2,1,0:T(8,128)S(1)}, u32[]{:S(2)}, u32[]{:S(2)}) %collective-permute-start.2) | collective-permute-done | bytes 30752 | tf_op jit(solution)/shard_map/ppermute | solution.py:111
  18.4 0.1 pad_maximum_fusion
  18.5 2.1 %fusion.9 = f32[130,18,128]{2,0,1:T(8,128)S(1)} fusion(f32[2,20,128]{2,0,1:T(2,128)S(1)} %copy.19, f32[128,2,128]{2,0,1:T(8,128)S(1)} %slice.129, f32[128,16,128]{2,0,1:T(8,128)S(1)} %bitcast.56, f32[128,2,128]{2,0,1:T(8,128)S(1)} %slice.126, f32[2,20,128]{2,0,1:T(2,128)S(1)} %copy.20, f32[132,20,128]{2,0,1:T(8,128)S(1)} %pad_maximum_fusion, ...), kind=kLoop, calls=%fused_computation.13 | loop fusion | flops 5990400 | bytes 7344420 | tf_op jit(solution)/shard_map/jit(_where)/select_n | solution.py:153
  20.7 0.9 %fusion.48 = (f32[128,16]{0,1:T(8,128)S(1)}, f32[128,16,128]{2,0,1:T(8,128)S(1)}, f32[128,16]{0,1:T(8,128)S(1)}) fusion(f32[128,16,128]{0,2,1:T(8,128)S(1)} %copy.14, f32[130,18,128]{2,0,1:T(8,128)S(1)} %fusion.9), kind=kLoop, calls=%fused_computation.101 | loop fusion | flops 2879488 | bytes 7356416 | tf_op jit(solution)/shard_map/reduce_sum | solution.py:168
  21.6 2.7 %fusion.11 = f32[128,128]{1,0:T(8,128)S(1)} fusion(f32[128,16,128]{2,0,1:T(8,128)S(1)} %get-tuple-element.7, f32[128,16]{0,1:T(8,128)S(1)} %get-tuple-element.17, f32[128,16]{0,1:T(8,128)S(1)} %get-tuple-element.20), kind=kOutput, calls=%fused_computation.22 | convolution fusion | flops 403439616 | bytes 1130496 | tf_op jit(solution)/shard_map/dot_general | solution.py:191
  24.3 0.8 %convolution_bitcast_fusion.2 = f32[1,128]{1,0:T(1,128)S(1)} fusion(f32[128,16,1]{0,2,1:T(1,128)S(1)} %bitcast.57, f32[128,16,128]{2,0,1:T(8,128)S(1)} %get-tuple-element.7, f32[128,16]{0,1:T(8,128)S(1)} %get-tuple-element.20), kind=kOutput, calls=%fused_computation.23 | convolution fusion | flops 3407872 | bytes 1065472 | tf_op jit(solution)/shard_map/dot_general | solution.py:197
  25.1 3.1 %collective-permute-start.4 = (f32[129,128]{1,0:T(8,128)S(1)}, f32[129,128]{1,0:T(8,128)S(1)}, u32[]{:S(2)}, u32[]{:S(2)}) collective-permute-start(f32[129,128]{1,0:T(8,128)S(1)} %pad_maximum_fusion.9), channel_id=1, source_target_pairs={{0,4},{4,0},{8,12},{12,8},{16,20},{20,16},{24,28},{28,24},{1,5},{5... | collective-permute-start | bytes 198152 | tf_op jit(solution)/shard_map/ppermute | solution.py:38
  28.2 2.4 %collective-permute-start.5 = (f32[129,128]{1,0:T(8,128)S(1)}, f32[129,128]{1,0:T(8,128)S(1)}, u32[]{:S(2)}, u32[]{:S(2)}) collective-permute-start(f32[129,128]{1,0:T(8,128)S(1)} %pad_maximum_fusion.9), channel_id=1, source_target_pairs={{0,8},{4,12},{8,0},{12,4},{16,24},{20,28},{24,16},{28,20},{1,9},{5... | collective-permute-start | bytes 198152 | tf_op jit(solution)/shard_map/ppermute | solution.py:38
  30.6 0.0 collective-permute-start.6
  30.6 0.0 collective-permute-done.4
  30.6 2.4 %collective-permute-done.5 = f32[129,128]{1,0:T(8,128)S(1)} collective-permute-done((f32[129,128]{1,0:T(8,128)S(1)}, f32[129,128]{1,0:T(8,128)S(1)}, u32[]{:S(2)}, u32[]{:S(2)}) %collective-permute-start.5) | collective-permute-done | bytes 66080 | tf_op jit(solution)/shard_map/ppermute | solution.py:38
  33.0 2.0 %collective-permute-done.6 = f32[129,128]{1,0:T(8,128)S(1)} collective-permute-done((f32[129,128]{1,0:T(8,128)S(1)}, f32[129,128]{1,0:T(8,128)S(1)}, u32[]{:S(2)}, u32[]{:S(2)}) %collective-permute-start.6) | collective-permute-done | bytes 66080 | tf_op jit(solution)/shard_map/ppermute | solution.py:38
  35.0 0.6 collective-permute-start.7
  35.7 3.7 %collective-permute-done.7 = f32[129,128]{1,0:T(8,128)S(1)} collective-permute-done((f32[129,128]{1,0:T(8,128)S(1)}, f32[129,128]{1,0:T(8,128)S(1)}, u32[]{:S(2)}, u32[]{:S(2)}) %collective-permute-start.7) | collective-permute-done | bytes 66080 | tf_op jit(solution)/shard_map/ppermute | solution.py:38
  39.4 4.1 %collective-permute-start.10 = (f32[129,128]{1,0:T(8,128)S(1)}, f32[129,128]{1,0:T(8,128)S(1)}, u32[]{:S(2)}, u32[]{:S(2)}) collective-permute-start(f32[129,128]{1,0:T(8,128)S(1)} %add.107), channel_id=1, source_target_pairs={{0,3},{1,2},{2,1},{3,0},{4,7},{5,6},{6,5},{7,4},{8,11},{9,10},{10,... | collective-permute-start | bytes 198152 | tf_op jit(solution)/shard_map/ppermute | solution.py:38
  43.5 0.0 collective-permute-start.8
  43.5 0.6 collective-permute-start.9
  44.2 1.8 %collective-permute-done.10 = f32[129,128]{1,0:T(8,128)S(1)} collective-permute-done((f32[129,128]{1,0:T(8,128)S(1)}, f32[129,128]{1,0:T(8,128)S(1)}, u32[]{:S(2)}, u32[]{:S(2)}) %collective-permute-start.10) | collective-permute-done | bytes 66080 | tf_op jit(solution)/shard_map/ppermute | solution.py:38
  46.0 1.9 %collective-permute-done.8 = f32[129,128]{1,0:T(8,128)S(1)} collective-permute-done((f32[129,128]{1,0:T(8,128)S(1)}, f32[129,128]{1,0:T(8,128)S(1)}, u32[]{:S(2)}, u32[]{:S(2)}) %collective-permute-start.8) | collective-permute-done | bytes 66080 | tf_op jit(solution)/shard_map/ppermute | solution.py:38
  47.9 0.9 %collective-permute-done.9 = f32[129,128]{1,0:T(8,128)S(1)} collective-permute-done((f32[129,128]{1,0:T(8,128)S(1)}, f32[129,128]{1,0:T(8,128)S(1)}, u32[]{:S(2)}, u32[]{:S(2)}) %collective-permute-start.9) | collective-permute-done | bytes 66080 | tf_op jit(solution)/shard_map/ppermute | solution.py:38
  48.8 0.6 slice_add_fusion.4.gram_ref
  49.4 15.1 %shard_map.68 = f32[128,128]{1,0:T(8,128)} custom-call(f32[128,128]{1,0:T(8,128)} %slice_add_fusion.4.gram_ref), custom_call_target="tpu_custom_call" | custom-call | tf_op jit(solution)/shard_map/pallas_call | solution.py:75
  64.5 1.0 %convolution_bitcast_fusion.4 = f32[128,1]{0,1:T(1,128)S(1)} fusion(f32[128,128]{1,0:T(8,128)} %shard_map.68, f32[129,128]{1,0:T(8,128)S(1)} %add_add_fusion), kind=kOutput, calls=%fused_computation.25 | convolution fusion | flops 196608 | bytes 66560 | tf_op jit(solution)/shard_map/dot_general | solution.py:210
  65.5 1.0 %convolution_bitcast_fusion.3 = f32[128]{0:T(128)S(1)} fusion(f32[128,1]{0,1:T(1,128)S(1)} %convolution_bitcast_fusion.4, f32[128,128]{1,0:T(8,128)} %shard_map.68), kind=kOutput, calls=%fused_computation.24 | convolution fusion | flops 196608 | bytes 66560 | tf_op jit(solution)/shard_map/dot_general | solution.py:211
  66.5 1.9 %fusion.2 = f32[128,16,128]{0,2,1:T(8,128)S(1)} fusion(f32[128,16]{0,1:T(8,128)S(1)} %get-tuple-element.22, f32[16,128]{1,0:T(8,128)S(1)} %get-tuple-element.21, f32[128,128]{1,0:T(8,128)} %shard_map.68, f32[128]{0:T(128)S(1)} %convolution_bitcast_fusion.3, f32[128,16,128]{0,2,1:T(8,128)S(1)} %copy.14), kind=kOutput, calls=%fused_computation.4 | convolution fusion | flops 403193856 | bytes 2179584 | tf_op jit(solution)/shard_map/dot_general | solution.py:217
  68.4 0.0 copy-start
  68.5 1.4 %copy.27 = f32[128,16,128]{2,1,0:T(8,128)} copy(f32[128,16,128]{0,2,1:T(8,128)S(1)} %fusion.2) | data formatting | bytes 2097152
  69.8 0.0 copy-done
  69.8 1.0 %fusion.3 = f32[128,16,128]{0,2,1:T(8,128)S(1)} fusion(f32[128,16,128]{2,0,1:T(8,128)S(1)} %get-tuple-element.7, f32[128,16]{0,1:T(8,128)S(1)} %get-tuple-element.20, f32[16,128]{1,0:T(8,128)S(1)} %get-tuple-element.19, f32[128,128]{1,0:T(8,128)S(1)} %copy-done, f32[128]{0:T(128)S(1)} %convolution_bitcast_fusion.3), kind=kOutput, calls=%fused_computation.6 | convolution fusion | flops 403193856 | bytes 2179584 | tf_op jit(solution)/shard_map/dot_general | solution.py:214
  70.9 1.4 %copy.26 = f32[128,16,128]{2,1,0:T(8,128)} copy(f32[128,16,128]{0,2,1:T(8,128)S(1)} %fusion.3) | data formatting | bytes 2097152
  (36 shorter events, 0.4 us)
Async XLA Ops:
  0.6 1.7 %copy-start.1 = (f32[128,16,128]{2,1,0:T(8,128)S(1)}, f32[128,16,128]{2,1,0:T(8,128)}, u32[]{:S(2)}) copy-start(f32[128,16,128]{2,1,0:T(8,128)} %param.5) | copy-start | bytes 3145732
  2.3 4.2 %copy-start.2 = (s32[1024]{0:T(1024)S(1)}, s32[1024]{0:T(1024)}, u32[]{:S(2)}) copy-start(s32[1024]{0:T(1024)} %param.9) | copy-start | bytes 12292
  2.4 4.3 %copy-start.3 = (f32[1024]{0:T(1024)S(1)}, f32[1024]{0:T(1024)}, u32[]{:S(2)}) copy-start(f32[1024]{0:T(1024)} %param.8) | copy-start | bytes 12292
  2.4 4.3 %copy-start.4 = (f32[1024]{0:T(1024)S(1)}, f32[1024]{0:T(1024)}, u32[]{:S(2)}) copy-start(f32[1024]{0:T(1024)} %param.7) | copy-start | bytes 12292
  2.9 4.2 %collective-permute-start = (f32[128,3,128]{2,0,1:T(8,128)S(1)}, f32[128,3,128]{2,0,1:T(8,128)S(1)}, u32[]{:S(2)}, u32[]{:S(2)}) collective-permute-start(f32[128,3,128]{2,0,1:T(8,128)S(1)} %pad_maximum_fusion.7), channel_id=1, source_target_pairs={{0,4},{4,8},{8,12},{12,16},{16,20},{20,24},{24,28},{1,5},{5,9},{9,... | collective-permute-start | bytes 589832 | tf_op jit(solution)/shard_map/ppermute | solution.py:111
  5.3 5.4 %collective-permute-start.1 = (f32[128,3,128]{2,0,1:T(8,128)S(1)}, f32[128,3,128]{2,0,1:T(8,128)S(1)}, u32[]{:S(2)}, u32[]{:S(2)}) collective-permute-start(f32[128,3,128]{2,0,1:T(8,128)S(1)} %pad_maximum_fusion.8), channel_id=1, source_target_pairs={{4,0},{8,4},{12,8},{16,12},{20,16},{24,20},{28,24},{5,1},{9,5},{13... | collective-permute-start | bytes 589832 | tf_op jit(solution)/shard_map/ppermute | solution.py:111
  10.8 6.0 %collective-permute-start.3 = (f32[3,20,128]{2,1,0:T(8,128)S(1)}, f32[3,20,128]{2,1,0:T(8,128)S(1)}, u32[]{:S(2)}, u32[]{:S(2)}) collective-permute-start(f32[3,20,128]{2,1,0:T(8,128)S(1)} %pad_maximum_fusion.11), channel_id=1, source_target_pairs={{1,0},{2,1},{3,2},{5,4},{6,5},{7,6},{9,8},{10,9},{11,10},{13,12},{... | collective-permute-start | bytes 92168 | tf_op jit(solution)/shard_map/ppermute | solution.py:111
  12.2 6.2 %collective-permute-start.2 = (f32[3,20,128]{2,1,0:T(8,128)S(1)}, f32[3,20,128]{2,1,0:T(8,128)S(1)}, u32[]{:S(2)}, u32[]{:S(2)}) collective-permute-start(f32[3,20,128]{2,1,0:T(8,128)S(1)} %pad_maximum_fusion.10), channel_id=1, source_target_pairs={{0,1},{1,2},{2,3},{4,5},{5,6},{6,7},{8,9},{9,10},{10,11},{12,13},{... | collective-permute-start | bytes 92168 | tf_op jit(solution)/shard_map/ppermute | solution.py:111
  25.1 5.5 %collective-permute-start.4 = (f32[129,128]{1,0:T(8,128)S(1)}, f32[129,128]{1,0:T(8,128)S(1)}, u32[]{:S(2)}, u32[]{:S(2)}) collective-permute-start(f32[129,128]{1,0:T(8,128)S(1)} %pad_maximum_fusion.9), channel_id=1, source_target_pairs={{0,4},{4,0},{8,12},{12,8},{16,20},{20,16},{24,28},{28,24},{1,5},{5... | collective-permute-start | bytes 198152 | tf_op jit(solution)/shard_map/ppermute | solution.py:38
  28.2 4.8 %collective-permute-start.5 = (f32[129,128]{1,0:T(8,128)S(1)}, f32[129,128]{1,0:T(8,128)S(1)}, u32[]{:S(2)}, u32[]{:S(2)}) collective-permute-start(f32[129,128]{1,0:T(8,128)S(1)} %pad_maximum_fusion.9), channel_id=1, source_target_pairs={{0,8},{4,12},{8,0},{12,4},{16,24},{20,28},{24,16},{28,20},{1,9},{5... | collective-permute-start | bytes 198152 | tf_op jit(solution)/shard_map/ppermute | solution.py:38
  30.6 4.5 %collective-permute-start.6 = (f32[129,128]{1,0:T(8,128)S(1)}, f32[129,128]{1,0:T(8,128)S(1)}, u32[]{:S(2)}, u32[]{:S(2)}) collective-permute-start(f32[129,128]{1,0:T(8,128)S(1)} %pad_maximum_fusion.9), channel_id=1, source_target_pairs={{0,12},{4,8},{8,4},{12,0},{16,28},{20,24},{24,20},{28,16},{1,13},{... | collective-permute-start | bytes 198152 | tf_op jit(solution)/shard_map/ppermute | solution.py:38
  35.0 4.4 %collective-permute-start.7 = (f32[129,128]{1,0:T(8,128)S(1)}, f32[129,128]{1,0:T(8,128)S(1)}, u32[]{:S(2)}, u32[]{:S(2)}) collective-permute-start(f32[129,128]{1,0:T(8,128)S(1)} %add_add_fusion.1), channel_id=1, source_target_pairs={{0,16},{4,20},{8,24},{12,28},{16,0},{20,4},{24,8},{28,12},{1,17},{... | collective-permute-start | bytes 198152 | tf_op jit(solution)/shard_map/ppermute | solution.py:38
  39.4 6.6 %collective-permute-start.10 = (f32[129,128]{1,0:T(8,128)S(1)}, f32[129,128]{1,0:T(8,128)S(1)}, u32[]{:S(2)}, u32[]{:S(2)}) collective-permute-start(f32[129,128]{1,0:T(8,128)S(1)} %add.107), channel_id=1, source_target_pairs={{0,3},{1,2},{2,1},{3,0},{4,7},{5,6},{6,5},{7,4},{8,11},{9,10},{10,... | collective-permute-start | bytes 198152 | tf_op jit(solution)/shard_map/ppermute | solution.py:38
  43.5 4.3 %collective-permute-start.8 = (f32[129,128]{1,0:T(8,128)S(1)}, f32[129,128]{1,0:T(8,128)S(1)}, u32[]{:S(2)}, u32[]{:S(2)}) collective-permute-start(f32[129,128]{1,0:T(8,128)S(1)} %add.107), channel_id=1, source_target_pairs={{0,1},{1,0},{2,3},{3,2},{4,5},{5,4},{6,7},{7,6},{8,9},{9,8},{10,11... | collective-permute-start | bytes 198152 | tf_op jit(solution)/shard_map/ppermute | solution.py:38
  43.5 5.2 %collective-permute-start.9 = (f32[129,128]{1,0:T(8,128)S(1)}, f32[129,128]{1,0:T(8,128)S(1)}, u32[]{:S(2)}, u32[]{:S(2)}) collective-permute-start(f32[129,128]{1,0:T(8,128)S(1)} %add.107), channel_id=1, source_target_pairs={{0,2},{1,3},{2,0},{3,1},{4,6},{5,7},{6,4},{7,5},{8,10},{9,11},{10,... | collective-permute-start | bytes 198152 | tf_op jit(solution)/shard_map/ppermute | solution.py:38
  68.4 1.4 %copy-start = (f32[128,128]{1,0:T(8,128)S(1)}, f32[128,128]{1,0:T(8,128)}, u32[]{:S(2)}) copy-start(f32[128,128]{1,0:T(8,128)} %shard_map.68) | copy-start | bytes 196612

commit v10 on v9

--- a/solution.py
+++ b/solution.py
@@ -40,12 +40,13 @@
     return value
 
 
-def inverse_factor_kernel(gram_ref, inverse_ref, work_ref):
-    size = gram_ref.shape[0]
-    work_ref[...] = gram_ref[...]
+def combination_kernel(stacked_ref, combination_ref, work_ref, inverse_ref):
+    size = stacked_ref.shape[1]
     square_row = lax.broadcasted_iota(jnp.int32, (size, size), 0)
     square_col = lax.broadcasted_iota(jnp.int32, (size, size), 1)
-    inverse_ref[...] = jnp.where(square_row == square_col, 1.0, 0.0).astype(jnp.float32)
+    unit = jnp.where(square_row == square_col, 1.0, 0.0).astype(jnp.float32)
+    work_ref[...] = stacked_ref[:size, :] + unit
+    inverse_ref[...] = unit
     lane = lax.broadcasted_iota(jnp.int32, (1, size), 1)
     for first in range(0, size, 8):
         span = size - first
@@ -57,28 +58,33 @@
             band = work_ref[first:, :]
             column = jnp.sum(jnp.where(band_col == k, band, 0.0), axis=1, keepdims=True)
             pivot = jnp.sum(jnp.where(lane == k, row, 0.0), axis=1, keepdims=True)
-            root = jnp.sqrt(pivot)
-            factor_row = jnp.where(lane >= k, row / root, 0.0)
-            factor_col = jnp.where(sublane >= k, column / root, 0.0)
+            scale = 1.0 / jnp.sqrt(pivot)
+            factor_row = jnp.where(lane >= k, row * scale, 0.0)
+            factor_col = jnp.where(sublane >= k, column * scale, 0.0)
             work_ref[first:, :] = band - factor_col * factor_row
-            inverse_row = inverse_ref[pl.ds(k, 1), :] / root
+            inverse_row = inverse_ref[pl.ds(k, 1), :] * scale
             below = jnp.where(sublane > k, factor_col, 0.0)
             inverse_ref[first:, :] = inverse_ref[first:, :] - below * inverse_row
             inverse_ref[pl.ds(k, 1), :] = inverse_row
             return carry
 
         lax.fori_loop(first, min(first + 8, size), step, 0)
-
-
-def inverse_factor(gram):
-    size = gram.shape[0]
+    lower_inverse = inverse_ref[...]
+    projected_row = stacked_ref[size : size + 1, :]
+    whitened = jnp.sum(lower_inverse * projected_row, axis=1, keepdims=True)
+    mean_weights = jnp.sum(lower_inverse * whitened, axis=0, keepdims=True)
+    combination_ref[...] = lower_inverse + mean_weights
+
+
+def combination_transposed_of(stacked):
+    size = stacked.shape[1]
     return pl.pallas_call(
-        inverse_factor_kernel,
+        combination_kernel,
         out_shape=jax.ShapeDtypeStruct((size, size), jnp.float32),
         in_specs=[pl.BlockSpec(memory_space=pltpu.VMEM)],
         out_specs=pl.BlockSpec(memory_space=pltpu.VMEM),
-        scratch_shapes=[pltpu.VMEM((size, size), jnp.float32)],
-    )(gram)
+        scratch_shapes=[pltpu.VMEM((size, size), jnp.float32)] * 2,
+    )(stacked)
 
 def propagate_model(padded_field, source_term):
     laplacian = (
@@ -200,16 +206,9 @@
         (((0, 1), (0, 1)), ((), ())),
         precision=lax.Precision.HIGHEST,
     )
-    identity = jnp.eye(sample_number, dtype=jnp.float32)
-    stacked = butterfly_sum(
-        jnp.concatenate([gram_local, projected[None, :]], axis=0), ("gx", "gy")
-    )
-    gram_sum = stacked[:sample_number] + identity
-    projected_sum = stacked[sample_number]
-    lower_inverse = inverse_factor(gram_sum)
-    whitened = jnp.dot(lower_inverse, projected_sum, precision=lax.Precision.HIGHEST)
-    mean_weights = jnp.dot(lower_inverse.T, whitened, precision=lax.Precision.HIGHEST)
-    combination_transposed = lower_inverse + mean_weights[None, :]
+    combination_transposed = combination_transposed_of(
+        butterfly_sum(jnp.concatenate([gram_local, projected[None, :]], axis=0), ("gx", "gy"))
+    )
     contract = (((2,), (1,)), ((), ()))
     updated_t = average_t[:, :, None] + lax.dot_general(
         deviation_t, combination_transposed, contract, precision=lax.Precision.HIGHEST

time: 72.7 us -> 70.6 us (0.971)
  matrix products: 8.86 us -> 6.76 us
    dot_general x2 -> x0, matrix products: 2.05 us -> none  [the longest x1 1.04 us: shards(): jnp.dot(lower_inverse.T, whitened, precision=lax.Precision.HIGHEST)]
where the time goes in v10:
time: 70.6 us; the launch traced here: 70.3 us
  starting transfers between devices  20.4 us (29%)
  waiting for transfers between devices  17.8 us (25%)
  Pallas kernels  15.2 us (22%)
  matrix products  6.76 us (10%)
  local copies, waits for them, and re-layouts  5.02 us (7%)
  other arithmetic  4.05 us (6%)
  between operations  1.03 us (1%)
    pallas_call x1, Pallas kernels, combination_transposed_of(): pl.pallas_call(combination_kernel, out_shape=jax.ShapeDtypeStruct((size,...  15.2 us
    ppermute x7, waiting for transfers between devices, butterfly_sum(): received[offset] = lax.ppermute(value, axis, pairs)  12.7 us
    ppermute x7, starting transfers between devices, butterfly_sum(): received[offset] = lax.ppermute(value, axis, pairs)  10.9 us
    ppermute x4, starting transfers between devices, from_neighbour(): return lax.ppermute(block, axis, pairs)  9.5 us
    ppermute x4, waiting for transfers between devices, from_neighbour(): return lax.ppermute(block, axis, pairs)  5.09 us
    unnamed x14, local copies, waits for them, and re-layouts  4.87 us
    dot_general x1, matrix products, shards(): lax.dot_general(deviation_t * cell_weight[:, :, None], deviation_t, (((0,...  2.7 us
    select_n x1, other arithmetic, forecast_two_steps(): first = jnp.where(outside[:, :, None], 0.0, first)  2.12 us
  transfers between devices with their start and end apart: 11, of which 8 were waited for; matrix products, arithmetic and copies ran while one was open for 1% of the time, Pallas kernels for 0%

profile of v10, /device:TPU:0, one launch (start us, length us, event | category | flops | bytes accessed | tf_op | source)
XLA Modules:
  0.0 70.3 jit_solution(10142584848191122413)
XLA Ops:
  0.6 0.0 copy-start
  0.6 1.7 %copy.14 = f32[128,16,128]{0,2,1:T(8,128)S(1)} copy(f32[128,16,128]{2,1,0:T(8,128)} %param.6) | data formatting | bytes 2097152 | tf_op args[1]
  2.3 0.0 copy-done
  2.3 0.0 copy-start.2
  2.4 0.0 copy-start.3
  2.4 0.0 copy-start.4
  2.4 0.4 copy.13
  2.9 2.4 %collective-permute-start = (f32[128,3,128]{2,0,1:T(8,128)S(1)}, f32[128,3,128]{2,0,1:T(8,128)S(1)}, u32[]{:S(2)}, u32[]{:S(2)}) collective-permute-start(f32[128,3,128]{2,0,1:T(8,128)S(1)} %pad_maximum_fusion.7), channel_id=1, source_target_pairs={{0,4},{4,8},{8,12},{12,16},{16,20},{20,24},{24,28},{1,5},{5,9},{9,... | collective-permute-start | bytes 589832 | tf_op jit(solution)/shard_map/ppermute | solution.py:117
  5.3 1.3 %collective-permute-start.1 = (f32[128,3,128]{2,0,1:T(8,128)S(1)}, f32[128,3,128]{2,0,1:T(8,128)S(1)}, u32[]{:S(2)}, u32[]{:S(2)}) collective-permute-start(f32[128,3,128]{2,0,1:T(8,128)S(1)} %pad_maximum_fusion.8), channel_id=1, source_target_pairs={{4,0},{8,4},{12,8},{16,12},{20,16},{24,20},{28,24},{5,1},{9,5},{13... | collective-permute-start | bytes 589832 | tf_op jit(solution)/shard_map/ppermute | solution.py:117
  6.6 0.0 copy-done.2
  6.6 0.0 copy-done.3
  6.6 0.0 copy-done.4
  6.7 0.4 fusion.27
  7.1 0.0 collective-permute-done
  7.1 3.6 %collective-permute-done.1 = f32[128,3,128]{2,0,1:T(8,128)S(1)} collective-permute-done((f32[128,3,128]{2,0,1:T(8,128)S(1)}, f32[128,3,128]{2,0,1:T(8,128)S(1)}, u32[]{:S(2)}, u32[]{:S(2)}) %collective-permute-start.1) | collective-permute-done | bytes 196640 | tf_op jit(solution)/shard_map/ppermute | solution.py:117
  10.8 1.3 %collective-permute-start.3 = (f32[3,20,128]{2,1,0:T(8,128)S(1)}, f32[3,20,128]{2,1,0:T(8,128)S(1)}, u32[]{:S(2)}, u32[]{:S(2)}) collective-permute-start(f32[3,20,128]{2,1,0:T(8,128)S(1)} %pad_maximum_fusion.11), channel_id=1, source_target_pairs={{1,0},{2,1},{3,2},{5,4},{6,5},{7,6},{9,8},{10,9},{11,10},{13,12},{... | collective-permute-start | bytes 92168 | tf_op jit(solution)/shard_map/ppermute | solution.py:117
  12.2 4.5 %collective-permute-start.2 = (f32[3,20,128]{2,1,0:T(8,128)S(1)}, f32[3,20,128]{2,1,0:T(8,128)S(1)}, u32[]{:S(2)}, u32[]{:S(2)}) collective-permute-start(f32[3,20,128]{2,1,0:T(8,128)S(1)} %pad_maximum_fusion.10), channel_id=1, source_target_pairs={{0,1},{1,2},{2,3},{4,5},{5,6},{6,7},{8,9},{9,10},{10,11},{12,13},{... | collective-permute-start | bytes 92168 | tf_op jit(solution)/shard_map/ppermute | solution.py:117
  16.7 0.1 or_or_fusion
  16.8 0.0 collective-permute-done.3
  16.8 1.5 %collective-permute-done.2 = f32[3,20,128]{2,1,0:T(8,128)S(1)} collective-permute-done((f32[3,20,128]{2,1,0:T(8,128)S(1)}, f32[3,20,128]{2,1,0:T(8,128)S(1)}, u32[]{:S(2)}, u32[]{:S(2)}) %collective-permute-start.2) | collective-permute-done | bytes 30752 | tf_op jit(solution)/shard_map/ppermute | solution.py:117
  18.4 0.1 pad_maximum_fusion
  18.5 2.1 %fusion.9 = f32[130,18,128]{2,0,1:T(8,128)S(1)} fusion(f32[2,20,128]{2,0,1:T(2,128)S(1)} %copy.19, f32[128,2,128]{2,0,1:T(8,128)S(1)} %slice.121, f32[128,16,128]{2,0,1:T(8,128)S(1)} %bitcast.42, f32[128,2,128]{2,0,1:T(8,128)S(1)} %slice.118, f32[2,20,128]{2,0,1:T(2,128)S(1)} %copy.20, f32[132,20,128]{2,0,1:T(8,128)S(1)} %pad_maximum_fusion, ...), kind=kLoop, calls=%fused_computation.13 | loop fusion | flops 5990400 | bytes 7344420 | tf_op jit(solution)/shard_map/jit(_where)/select_n | solution.py:159
  20.7 0.9 %fusion.43 = (f32[128,16]{0,1:T(8,128)S(1)}, f32[128,16,128]{2,0,1:T(8,128)S(1)}, f32[128,16]{0,1:T(8,128)S(1)}) fusion(f32[128,16,128]{0,2,1:T(8,128)S(1)} %copy.14, f32[130,18,128]{2,0,1:T(8,128)S(1)} %fusion.9), kind=kLoop, calls=%fused_computation.91 | loop fusion | flops 2879488 | bytes 7356416 | tf_op jit(solution)/shard_map/reduce_sum | solution.py:174
  21.6 2.7 %fusion.11 = f32[128,128]{1,0:T(8,128)S(1)} fusion(f32[128,16,128]{2,0,1:T(8,128)S(1)} %get-tuple-element.7, f32[128,16]{0,1:T(8,128)S(1)} %get-tuple-element.17, f32[128,16]{0,1:T(8,128)S(1)} %get-tuple-element.20), kind=kOutput, calls=%fused_computation.22 | convolution fusion | flops 403439616 | bytes 1130496 | tf_op jit(solution)/shard_map/dot_general | solution.py:197
  24.3 0.8 %convolution_bitcast_fusion.2 = f32[1,128]{1,0:T(1,128)S(1)} fusion(f32[128,16,1]{0,2,1:T(1,128)S(1)} %bitcast.43, f32[128,16,128]{2,0,1:T(8,128)S(1)} %get-tuple-element.7, f32[128,16]{0,1:T(8,128)S(1)} %get-tuple-element.20), kind=kOutput, calls=%fused_computation.23 | convolution fusion | flops 3407872 | bytes 1065472 | tf_op jit(solution)/shard_map/dot_general | solution.py:203
  25.1 3.1 %collective-permute-start.4 = (f32[129,128]{1,0:T(8,128)S(1)}, f32[129,128]{1,0:T(8,128)S(1)}, u32[]{:S(2)}, u32[]{:S(2)}) collective-permute-start(f32[129,128]{1,0:T(8,128)S(1)} %pad_maximum_fusion.9), channel_id=1, source_target_pairs={{0,4},{4,0},{8,12},{12,8},{16,20},{20,16},{24,28},{28,24},{1,5},{5... | collective-permute-start | bytes 198152 | tf_op jit(solution)/shard_map/ppermute | solution.py:38
  28.2 2.4 %collective-permute-start.5 = (f32[129,128]{1,0:T(8,128)S(1)}, f32[129,128]{1,0:T(8,128)S(1)}, u32[]{:S(2)}, u32[]{:S(2)}) collective-permute-start(f32[129,128]{1,0:T(8,128)S(1)} %pad_maximum_fusion.9), channel_id=1, source_target_pairs={{0,8},{4,12},{8,0},{12,4},{16,24},{20,28},{24,16},{28,20},{1,9},{5... | collective-permute-start | bytes 198152 | tf_op jit(solution)/shard_map/ppermute | solution.py:38
  30.6 0.0 collective-permute-start.6
  30.6 0.0 collective-permute-done.4
  30.6 2.4 %collective-permute-done.5 = f32[129,128]{1,0:T(8,128)S(1)} collective-permute-done((f32[129,128]{1,0:T(8,128)S(1)}, f32[129,128]{1,0:T(8,128)S(1)}, u32[]{:S(2)}, u32[]{:S(2)}) %collective-permute-start.5) | collective-permute-done | bytes 66080 | tf_op jit(solution)/shard_map/ppermute | solution.py:38
  33.0 2.0 %collective-permute-done.6 = f32[129,128]{1,0:T(8,128)S(1)} collective-permute-done((f32[129,128]{1,0:T(8,128)S(1)}, f32[129,128]{1,0:T(8,128)S(1)}, u32[]{:S(2)}, u32[]{:S(2)}) %collective-permute-start.6) | collective-permute-done | bytes 66080 | tf_op jit(solution)/shard_map/ppermute | solution.py:38
  35.0 0.6 collective-permute-start.7
  35.7 3.7 %collective-permute-done.7 = f32[129,128]{1,0:T(8,128)S(1)} collective-permute-done((f32[129,128]{1,0:T(8,128)S(1)}, f32[129,128]{1,0:T(8,128)S(1)}, u32[]{:S(2)}, u32[]{:S(2)}) %collective-permute-start.7) | collective-permute-done | bytes 66080 | tf_op jit(solution)/shard_map/ppermute | solution.py:38
  39.4 4.1 %collective-permute-start.10 = (f32[129,128]{1,0:T(8,128)S(1)}, f32[129,128]{1,0:T(8,128)S(1)}, u32[]{:S(2)}, u32[]{:S(2)}) collective-permute-start(f32[129,128]{1,0:T(8,128)S(1)} %add.96), channel_id=1, source_target_pairs={{0,3},{1,2},{2,1},{3,0},{4,7},{5,6},{6,5},{7,4},{8,11},{9,10},{10,... | collective-permute-start | bytes 198152 | tf_op jit(solution)/shard_map/ppermute | solution.py:38
  43.5 0.0 collective-permute-start.8
  43.5 0.6 collective-permute-start.9
  44.2 1.8 %collective-permute-done.10 = f32[129,128]{1,0:T(8,128)S(1)} collective-permute-done((f32[129,128]{1,0:T(8,128)S(1)}, f32[129,128]{1,0:T(8,128)S(1)}, u32[]{:S(2)}, u32[]{:S(2)}) %collective-permute-start.10) | collective-permute-done | bytes 66080 | tf_op jit(solution)/shard_map/ppermute | solution.py:38
  46.0 1.9 %collective-permute-done.8 = f32[129,128]{1,0:T(8,128)S(1)} collective-permute-done((f32[129,128]{1,0:T(8,128)S(1)}, f32[129,128]{1,0:T(8,128)S(1)}, u32[]{:S(2)}, u32[]{:S(2)}) %collective-permute-start.8) | collective-permute-done | bytes 66080 | tf_op jit(solution)/shard_map/ppermute | solution.py:38
  47.9 0.9 %collective-permute-done.9 = f32[129,128]{1,0:T(8,128)S(1)} collective-permute-done((f32[129,128]{1,0:T(8,128)S(1)}, f32[129,128]{1,0:T(8,128)S(1)}, u32[]{:S(2)}, u32[]{:S(2)}) %collective-permute-start.9) | collective-permute-done | bytes 66080 | tf_op jit(solution)/shard_map/ppermute | solution.py:38
  48.8 0.6 add_add_fusion.stacked_ref
  49.4 15.2 %shard_map.68 = f32[128,128]{1,0:T(8,128)} custom-call(f32[129,128]{1,0:T(8,128)} %add_add_fusion.stacked_ref), custom_call_target="tpu_custom_call" | custom-call | tf_op jit(solution)/shard_map/pallas_call | solution.py:81
  64.6 1.9 %fusion.2 = f32[128,16,128]{0,2,1:T(8,128)S(1)} fusion(f32[128,16]{0,1:T(8,128)S(1)} %get-tuple-element.22, f32[16,128]{1,0:T(8,128)S(1)} %get-tuple-element.21, f32[128,128]{1,0:T(8,128)} %shard_map.68, f32[128,16,128]{0,2,1:T(8,128)S(1)} %copy.14), kind=kOutput, calls=%fused_computation.4 | convolution fusion | flops 403177472 | bytes 2179072 | tf_op jit(solution)/shard_map/dot_general | solution.py:216
  66.5 0.0 copy-start.1
  66.5 1.4 %copy.27 = f32[128,16,128]{2,1,0:T(8,128)} copy(f32[128,16,128]{0,2,1:T(8,128)S(1)} %fusion.2) | data formatting | bytes 2097152
  67.9 0.0 copy-done.1
  67.9 1.0 %fusion.3 = f32[128,16,128]{0,2,1:T(8,128)S(1)} fusion(f32[128,16,128]{2,0,1:T(8,128)S(1)} %get-tuple-element.7, f32[128,16]{0,1:T(8,128)S(1)} %get-tuple-element.20, f32[16,128]{1,0:T(8,128)S(1)} %get-tuple-element.19, f32[128,128]{1,0:T(8,128)S(1)} %copy-done.1), kind=kOutput, calls=%fused_computation.6 | convolution fusion | flops 403177472 | bytes 2179072 | tf_op jit(solution)/shard_map/dot_general | solution.py:213
  68.9 1.4 %copy.26 = f32[128,16,128]{2,1,0:T(8,128)} copy(f32[128,16,128]{0,2,1:T(8,128)S(1)} %fusion.3) | data formatting | bytes 2097152
  (35 shorter events, 0.3 us)
Async XLA Ops:
  0.6 1.7 %copy-start = (f32[128,16,128]{2,1,0:T(8,128)S(1)}, f32[128,16,128]{2,1,0:T(8,128)}, u32[]{:S(2)}) copy-start(f32[128,16,128]{2,1,0:T(8,128)} %param.5) | copy-start | bytes 3145732
  2.3 4.2 %copy-start.2 = (s32[1024]{0:T(1024)S(1)}, s32[1024]{0:T(1024)}, u32[]{:S(2)}) copy-start(s32[1024]{0:T(1024)} %param.9) | copy-start | bytes 12292
  2.4 4.3 %copy-start.3 = (f32[1024]{0:T(1024)S(1)}, f32[1024]{0:T(1024)}, u32[]{:S(2)}) copy-start(f32[1024]{0:T(1024)} %param.8) | copy-start | bytes 12292
  2.4 4.3 %copy-start.4 = (f32[1024]{0:T(1024)S(1)}, f32[1024]{0:T(1024)}, u32[]{:S(2)}) copy-start(f32[1024]{0:T(1024)} %param.7) | copy-start | bytes 12292
  2.9 4.2 %collective-permute-start = (f32[128,3,128]{2,0,1:T(8,128)S(1)}, f32[128,3,128]{2,0,1:T(8,128)S(1)}, u32[]{:S(2)}, u32[]{:S(2)}) collective-permute-start(f32[128,3,128]{2,0,1:T(8,128)S(1)} %pad_maximum_fusion.7), channel_id=1, source_target_pairs={{0,4},{4,8},{8,12},{12,16},{16,20},{20,24},{24,28},{1,5},{5,9},{9,... | collective-permute-start | bytes 589832 | tf_op jit(solution)/shard_map/ppermute | solution.py:117
  5.3 5.4 %collective-permute-start.1 = (f32[128,3,128]{2,0,1:T(8,128)S(1)}, f32[128,3,128]{2,0,1:T(8,128)S(1)}, u32[]{:S(2)}, u32[]{:S(2)}) collective-permute-start(f32[128,3,128]{2,0,1:T(8,128)S(1)} %pad_maximum_fusion.8), channel_id=1, source_target_pairs={{4,0},{8,4},{12,8},{16,12},{20,16},{24,20},{28,24},{5,1},{9,5},{13... | collective-permute-start | bytes 589832 | tf_op jit(solution)/shard_map/ppermute | solution.py:117
  10.8 6.0 %collective-permute-start.3 = (f32[3,20,128]{2,1,0:T(8,128)S(1)}, f32[3,20,128]{2,1,0:T(8,128)S(1)}, u32[]{:S(2)}, u32[]{:S(2)}) collective-permute-start(f32[3,20,128]{2,1,0:T(8,128)S(1)} %pad_maximum_fusion.11), channel_id=1, source_target_pairs={{1,0},{2,1},{3,2},{5,4},{6,5},{7,6},{9,8},{10,9},{11,10},{13,12},{... | collective-permute-start | bytes 92168 | tf_op jit(solution)/shard_map/ppermute | solution.py:117
  12.2 6.2 %collective-permute-start.2 = (f32[3,20,128]{2,1,0:T(8,128)S(1)}, f32[3,20,128]{2,1,0:T(8,128)S(1)}, u32[]{:S(2)}, u32[]{:S(2)}) collective-permute-start(f32[3,20,128]{2,1,0:T(8,128)S(1)} %pad_maximum_fusion.10), channel_id=1, source_target_pairs={{0,1},{1,2},{2,3},{4,5},{5,6},{6,7},{8,9},{9,10},{10,11},{12,13},{... | collective-permute-start | bytes 92168 | tf_op jit(solution)/shard_map/ppermute | solution.py:117
  25.1 5.5 %collective-permute-start.4 = (f32[129,128]{1,0:T(8,128)S(1)}, f32[129,128]{1,0:T(8,128)S(1)}, u32[]{:S(2)}, u32[]{:S(2)}) collective-permute-start(f32[129,128]{1,0:T(8,128)S(1)} %pad_maximum_fusion.9), channel_id=1, source_target_pairs={{0,4},{4,0},{8,12},{12,8},{16,20},{20,16},{24,28},{28,24},{1,5},{5... | collective-permute-start | bytes 198152 | tf_op jit(solution)/shard_map/ppermute | solution.py:38
  28.2 4.8 %collective-permute-start.5 = (f32[129,128]{1,0:T(8,128)S(1)}, f32[129,128]{1,0:T(8,128)S(1)}, u32[]{:S(2)}, u32[]{:S(2)}) collective-permute-start(f32[129,128]{1,0:T(8,128)S(1)} %pad_maximum_fusion.9), channel_id=1, source_target_pairs={{0,8},{4,12},{8,0},{12,4},{16,24},{20,28},{24,16},{28,20},{1,9},{5... | collective-permute-start | bytes 198152 | tf_op jit(solution)/shard_map/ppermute | solution.py:38
  30.6 4.5 %collective-permute-start.6 = (f32[129,128]{1,0:T(8,128)S(1)}, f32[129,128]{1,0:T(8,128)S(1)}, u32[]{:S(2)}, u32[]{:S(2)}) collective-permute-start(f32[129,128]{1,0:T(8,128)S(1)} %pad_maximum_fusion.9), channel_id=1, source_target_pairs={{0,12},{4,8},{8,4},{12,0},{16,28},{20,24},{24,20},{28,16},{1,13},{... | collective-permute-start | bytes 198152 | tf_op jit(solution)/shard_map/ppermute | solution.py:38
  35.0 4.4 %collective-permute-start.7 = (f32[129,128]{1,0:T(8,128)S(1)}, f32[129,128]{1,0:T(8,128)S(1)}, u32[]{:S(2)}, u32[]{:S(2)}) collective-permute-start(f32[129,128]{1,0:T(8,128)S(1)} %add_add_fusion.1), channel_id=1, source_target_pairs={{0,16},{4,20},{8,24},{12,28},{16,0},{20,4},{24,8},{28,12},{1,17},{... | collective-permute-start | bytes 198152 | tf_op jit(solution)/shard_map/ppermute | solution.py:38
  39.4 6.6 %collective-permute-start.10 = (f32[129,128]{1,0:T(8,128)S(1)}, f32[129,128]{1,0:T(8,128)S(1)}, u32[]{:S(2)}, u32[]{:S(2)}) collective-permute-start(f32[129,128]{1,0:T(8,128)S(1)} %add.96), channel_id=1, source_target_pairs={{0,3},{1,2},{2,1},{3,0},{4,7},{5,6},{6,5},{7,4},{8,11},{9,10},{10,... | collective-permute-start | bytes 198152 | tf_op jit(solution)/shard_map/ppermute | solution.py:38
  43.5 4.3 %collective-permute-start.8 = (f32[129,128]{1,0:T(8,128)S(1)}, f32[129,128]{1,0:T(8,128)S(1)}, u32[]{:S(2)}, u32[]{:S(2)}) collective-permute-start(f32[129,128]{1,0:T(8,128)S(1)} %add.96), channel_id=1, source_target_pairs={{0,1},{1,0},{2,3},{3,2},{4,5},{5,4},{6,7},{7,6},{8,9},{9,8},{10,11... | collective-permute-start | bytes 198152 | tf_op jit(solution)/shard_map/ppermute | solution.py:38
  43.5 5.2 %collective-permute-start.9 = (f32[129,128]{1,0:T(8,128)S(1)}, f32[129,128]{1,0:T(8,128)S(1)}, u32[]{:S(2)}, u32[]{:S(2)}) collective-permute-start(f32[129,128]{1,0:T(8,128)S(1)} %add.96), channel_id=1, source_target_pairs={{0,2},{1,3},{2,0},{3,1},{4,6},{5,7},{6,4},{7,5},{8,10},{9,11},{10,... | collective-permute-start | bytes 198152 | tf_op jit(solution)/shard_map/ppermute | solution.py:38
  66.5 1.4 %copy-start.1 = (f32[128,128]{1,0:T(8,128)S(1)}, f32[128,128]{1,0:T(8,128)}, u32[]{:S(2)}) copy-start(f32[128,128]{1,0:T(8,128)} %shard_map.68) | copy-start | bytes 196612

commit v11 on v10

--- a/solution.py
+++ b/solution.py
@@ -26,8 +26,8 @@
             value = lax.psum(value, axis)
             continue
         bits = [1 << b for b in range(count.bit_length() - 1)]
-        for first in range(0, len(bits), 2):
-            strides = bits[first : first + 2]
+        for first in range(len(bits)):
+            strides = bits[first : first + 1]
             received = {0: value}
             for mask in range(1, 1 << len(strides)):
                 offset = 0

time: 70.6 us -> 70.5 us (level)
  waiting for transfers between devices: 17.8 us -> 16.2 us
  starting transfers between devices: 20.4 us -> 21.7 us
    ppermute x7 -> x5, waiting for transfers between devices: 12.7 us -> 11.1 us  [butterfly_sum(): received[offset] = lax.ppermute(value, axis, pairs)]
    ppermute x7 -> x5, starting transfers between devices: 10.9 us -> 12.1 us  [butterfly_sum(): received[offset] = lax.ppermute(value, axis, pairs)]
  transfers between devices with their start and end apart: 11 -> 9, of which waited for: 8 -> 7; matrix products, arithmetic and copies ran while one was open for 1% -> 1% of each run, Pallas kernels for 0% -> 0%
where the time goes in v11:
time: 70.5 us; the launch traced here: 70 us
  starting transfers between devices  21.7 us (31%)
  waiting for transfers between devices  16.2 us (23%)
  Pallas kernels  15.2 us (22%)
  matrix products  6.77 us (10%)
  local copies, waits for them, and re-layouts  5.02 us (7%)
  other arithmetic  4.04 us (6%)
  between operations  1.04 us (1%)
    pallas_call x1, Pallas kernels, combination_transposed_of(): pl.pallas_call(combination_kernel, out_shape=jax.ShapeDtypeStruct((size,...  15.2 us
    ppermute x5, starting transfers between devices, butterfly_sum(): received[offset] = lax.ppermute(value, axis, pairs)  12.1 us
    ppermute x5, waiting for transfers between devices, butterfly_sum(): received[offset] = lax.ppermute(value, axis, pairs)  11.1 us
    ppermute x4, starting transfers between devices, from_neighbour(): return lax.ppermute(block, axis, pairs)  9.5 us
    ppermute x4, waiting for transfers between devices, from_neighbour(): return lax.ppermute(block, axis, pairs)  5.09 us
    unnamed x14, local copies, waits for them, and re-layouts  4.87 us
    dot_general x1, matrix products, shards(): lax.dot_general(deviation_t * cell_weight[:, :, None], deviation_t, (((0,...  2.7 us
    select_n x1, other arithmetic, forecast_two_steps(): first = jnp.where(outside[:, :, None], 0.0, first)  2.12 us
  transfers between devices with their start and end apart: 9, of which 7 were waited for; matrix products, arithmetic and copies ran while one was open for 1% of the time, Pallas kernels for 0%

profile of v11, /device:TPU:0, one launch (start us, length us, event | category | flops | bytes accessed | tf_op | source)
XLA Modules:
  0.0 70.0 jit_solution(18077509673397837743)
XLA Ops:
  0.6 0.0 copy-start
  0.6 1.7 %copy.14 = f32[128,16,128]{0,2,1:T(8,128)S(1)} copy(f32[128,16,128]{2,1,0:T(8,128)} %param.6) | data formatting | bytes 2097152 | tf_op args[1]
  2.3 0.0 copy-done
  2.3 0.0 copy-start.2
  2.4 0.0 copy-start.3
  2.4 0.0 copy-start.4
  2.4 0.4 copy.13
  2.9 2.4 %collective-permute-start = (f32[128,3,128]{2,0,1:T(8,128)S(1)}, f32[128,3,128]{2,0,1:T(8,128)S(1)}, u32[]{:S(2)}, u32[]{:S(2)}) collective-permute-start(f32[128,3,128]{2,0,1:T(8,128)S(1)} %pad_maximum_fusion.7), channel_id=1, source_target_pairs={{0,4},{4,8},{8,12},{12,16},{16,20},{20,24},{24,28},{1,5},{5,9},{9,... | collective-permute-start | bytes 589832 | tf_op jit(solution)/shard_map/ppermute | solution.py:117
  5.3 1.3 %collective-permute-start.1 = (f32[128,3,128]{2,0,1:T(8,128)S(1)}, f32[128,3,128]{2,0,1:T(8,128)S(1)}, u32[]{:S(2)}, u32[]{:S(2)}) collective-permute-start(f32[128,3,128]{2,0,1:T(8,128)S(1)} %pad_maximum_fusion.8), channel_id=1, source_target_pairs={{4,0},{8,4},{12,8},{16,12},{20,16},{24,20},{28,24},{5,1},{9,5},{13... | collective-permute-start | bytes 589832 | tf_op jit(solution)/shard_map/ppermute | solution.py:117
  6.6 0.0 copy-done.2
  6.6 0.0 copy-done.3
  6.6 0.0 copy-done.4
  6.7 0.4 fusion.27
  7.1 0.0 collective-permute-done
  7.1 3.6 %collective-permute-done.1 = f32[128,3,128]{2,0,1:T(8,128)S(1)} collective-permute-done((f32[128,3,128]{2,0,1:T(8,128)S(1)}, f32[128,3,128]{2,0,1:T(8,128)S(1)}, u32[]{:S(2)}, u32[]{:S(2)}) %collective-permute-start.1) | collective-permute-done | bytes 196640 | tf_op jit(solution)/shard_map/ppermute | solution.py:117
  10.8 1.3 %collective-permute-start.3 = (f32[3,20,128]{2,1,0:T(8,128)S(1)}, f32[3,20,128]{2,1,0:T(8,128)S(1)}, u32[]{:S(2)}, u32[]{:S(2)}) collective-permute-start(f32[3,20,128]{2,1,0:T(8,128)S(1)} %pad_maximum_fusion.11), channel_id=1, source_target_pairs={{1,0},{2,1},{3,2},{5,4},{6,5},{7,6},{9,8},{10,9},{11,10},{13,12},{... | collective-permute-start | bytes 92168 | tf_op jit(solution)/shard_map/ppermute | solution.py:117
  12.2 4.5 %collective-permute-start.2 = (f32[3,20,128]{2,1,0:T(8,128)S(1)}, f32[3,20,128]{2,1,0:T(8,128)S(1)}, u32[]{:S(2)}, u32[]{:S(2)}) collective-permute-start(f32[3,20,128]{2,1,0:T(8,128)S(1)} %pad_maximum_fusion.10), channel_id=1, source_target_pairs={{0,1},{1,2},{2,3},{4,5},{5,6},{6,7},{8,9},{9,10},{10,11},{12,13},{... | collective-permute-start | bytes 92168 | tf_op jit(solution)/shard_map/ppermute | solution.py:117
  16.7 0.1 or_or_fusion
  16.8 0.0 collective-permute-done.3
  16.8 1.5 %collective-permute-done.2 = f32[3,20,128]{2,1,0:T(8,128)S(1)} collective-permute-done((f32[3,20,128]{2,1,0:T(8,128)S(1)}, f32[3,20,128]{2,1,0:T(8,128)S(1)}, u32[]{:S(2)}, u32[]{:S(2)}) %collective-permute-start.2) | collective-permute-done | bytes 30752 | tf_op jit(solution)/shard_map/ppermute | solution.py:117
  18.4 0.1 pad_maximum_fusion
  18.5 2.1 %fusion.9 = f32[130,18,128]{2,0,1:T(8,128)S(1)} fusion(f32[2,20,128]{2,0,1:T(2,128)S(1)} %copy.19, f32[128,2,128]{2,0,1:T(8,128)S(1)} %slice.121, f32[128,16,128]{2,0,1:T(8,128)S(1)} %bitcast.42, f32[128,2,128]{2,0,1:T(8,128)S(1)} %slice.118, f32[2,20,128]{2,0,1:T(2,128)S(1)} %copy.20, f32[132,20,128]{2,0,1:T(8,128)S(1)} %pad_maximum_fusion, ...), kind=kLoop, calls=%fused_computation.13 | loop fusion | flops 5990400 | bytes 7344420 | tf_op jit(solution)/shard_map/jit(_where)/select_n | solution.py:159
  20.7 0.9 %fusion.44 = (f32[128,16]{0,1:T(8,128)S(1)}, f32[128,16,128]{2,0,1:T(8,128)S(1)}, f32[128,16]{0,1:T(8,128)S(1)}) fusion(f32[128,16,128]{0,2,1:T(8,128)S(1)} %copy.14, f32[130,18,128]{2,0,1:T(8,128)S(1)} %fusion.9), kind=kLoop, calls=%fused_computation.90 | loop fusion | flops 2879488 | bytes 7356416 | tf_op jit(solution)/shard_map/reduce_sum | solution.py:174
  21.6 2.7 %fusion.11 = f32[128,128]{1,0:T(8,128)S(1)} fusion(f32[128,16,128]{2,0,1:T(8,128)S(1)} %get-tuple-element.7, f32[128,16]{0,1:T(8,128)S(1)} %get-tuple-element.17, f32[128,16]{0,1:T(8,128)S(1)} %get-tuple-element.20), kind=kOutput, calls=%fused_computation.22 | convolution fusion | flops 403439616 | bytes 1130496 | tf_op jit(solution)/shard_map/dot_general | solution.py:197
  24.3 0.8 %convolution_bitcast_fusion.2 = f32[1,128]{1,0:T(1,128)S(1)} fusion(f32[128,16,1]{0,2,1:T(1,128)S(1)} %bitcast.43, f32[128,16,128]{2,0,1:T(8,128)S(1)} %get-tuple-element.7, f32[128,16]{0,1:T(8,128)S(1)} %get-tuple-element.20), kind=kOutput, calls=%fused_computation.23 | convolution fusion | flops 3407872 | bytes 1065472 | tf_op jit(solution)/shard_map/dot_general | solution.py:203
  25.1 3.1 %collective-permute-start.4 = (f32[129,128]{1,0:T(8,128)S(1)}, f32[129,128]{1,0:T(8,128)S(1)}, u32[]{:S(2)}, u32[]{:S(2)}) collective-permute-start(f32[129,128]{1,0:T(8,128)S(1)} %pad_maximum_fusion.9), channel_id=1, source_target_pairs={{0,4},{4,0},{8,12},{12,8},{16,20},{20,16},{24,28},{28,24},{1,5},{5... | collective-permute-start | bytes 198152 | tf_op jit(solution)/shard_map/ppermute | solution.py:38
  28.2 0.9 %collective-permute-done.4 = f32[129,128]{1,0:T(8,128)S(1)} collective-permute-done((f32[129,128]{1,0:T(8,128)S(1)}, f32[129,128]{1,0:T(8,128)S(1)}, u32[]{:S(2)}, u32[]{:S(2)}) %collective-permute-start.4) | collective-permute-done | bytes 66080 | tf_op jit(solution)/shard_map/ppermute | solution.py:38
  29.1 2.5 %collective-permute-start.5 = (f32[129,128]{1,0:T(8,128)S(1)}, f32[129,128]{1,0:T(8,128)S(1)}, u32[]{:S(2)}, u32[]{:S(2)}) collective-permute-start(f32[129,128]{1,0:T(8,128)S(1)} %fusion.43), channel_id=1, source_target_pairs={{0,8},{4,12},{8,0},{12,4},{16,24},{20,28},{24,16},{28,20},{1,9},{5... | collective-permute-start | bytes 198152 | tf_op jit(solution)/shard_map/ppermute | solution.py:38
  31.5 2.7 %collective-permute-done.5 = f32[129,128]{1,0:T(8,128)S(1)} collective-permute-done((f32[129,128]{1,0:T(8,128)S(1)}, f32[129,128]{1,0:T(8,128)S(1)}, u32[]{:S(2)}, u32[]{:S(2)}) %collective-permute-start.5) | collective-permute-done | bytes 66080 | tf_op jit(solution)/shard_map/ppermute | solution.py:38
  34.3 1.4 %collective-permute-start.6 = (f32[129,128]{1,0:T(8,128)S(1)}, f32[129,128]{1,0:T(8,128)S(1)}, u32[]{:S(2)}, u32[]{:S(2)}) collective-permute-start(f32[129,128]{1,0:T(8,128)S(1)} %add.88), channel_id=1, source_target_pairs={{0,16},{4,20},{8,24},{12,28},{16,0},{20,4},{24,8},{28,12},{1,17},{... | collective-permute-start | bytes 198152 | tf_op jit(solution)/shard_map/ppermute | solution.py:38
  35.7 3.0 %collective-permute-done.6 = f32[129,128]{1,0:T(8,128)S(1)} collective-permute-done((f32[129,128]{1,0:T(8,128)S(1)}, f32[129,128]{1,0:T(8,128)S(1)}, u32[]{:S(2)}, u32[]{:S(2)}) %collective-permute-start.6) | collective-permute-done | bytes 66080 | tf_op jit(solution)/shard_map/ppermute | solution.py:38
  38.6 2.1 %collective-permute-start.7 = (f32[129,128]{1,0:T(8,128)S(1)}, f32[129,128]{1,0:T(8,128)S(1)}, u32[]{:S(2)}, u32[]{:S(2)}) collective-permute-start(f32[129,128]{1,0:T(8,128)S(1)} %add.89), channel_id=1, source_target_pairs={{0,1},{1,0},{2,3},{3,2},{4,5},{5,4},{6,7},{7,6},{8,9},{9,8},{10,11... | collective-permute-start | bytes 198152 | tf_op jit(solution)/shard_map/ppermute | solution.py:38
  40.7 2.3 %collective-permute-done.7 = f32[129,128]{1,0:T(8,128)S(1)} collective-permute-done((f32[129,128]{1,0:T(8,128)S(1)}, f32[129,128]{1,0:T(8,128)S(1)}, u32[]{:S(2)}, u32[]{:S(2)}) %collective-permute-start.7) | collective-permute-done | bytes 66080 | tf_op jit(solution)/shard_map/ppermute | solution.py:38
  43.0 3.1 %collective-permute-start.8 = (f32[129,128]{1,0:T(8,128)S(1)}, f32[129,128]{1,0:T(8,128)S(1)}, u32[]{:S(2)}, u32[]{:S(2)}) collective-permute-start(f32[129,128]{1,0:T(8,128)S(1)} %add.90), channel_id=1, source_target_pairs={{0,2},{1,3},{2,0},{3,1},{4,6},{5,7},{6,4},{7,5},{8,10},{9,11},{10,... | collective-permute-start | bytes 198152 | tf_op jit(solution)/shard_map/ppermute | solution.py:38
  46.1 2.3 %collective-permute-done.8 = f32[129,128]{1,0:T(8,128)S(1)} collective-permute-done((f32[129,128]{1,0:T(8,128)S(1)}, f32[129,128]{1,0:T(8,128)S(1)}, u32[]{:S(2)}, u32[]{:S(2)}) %collective-permute-start.8) | collective-permute-done | bytes 66080 | tf_op jit(solution)/shard_map/ppermute | solution.py:38
  48.4 0.6 add.91.stacked_ref
  49.1 15.2 %shard_map.68 = f32[128,128]{1,0:T(8,128)} custom-call(f32[129,128]{1,0:T(8,128)} %add.91.stacked_ref), custom_call_target="tpu_custom_call" | custom-call | tf_op jit(solution)/shard_map/pallas_call | solution.py:81
  64.3 1.9 %fusion.2 = f32[128,16,128]{0,2,1:T(8,128)S(1)} fusion(f32[128,16]{0,1:T(8,128)S(1)} %get-tuple-element.22, f32[16,128]{1,0:T(8,128)S(1)} %get-tuple-element.21, f32[128,128]{1,0:T(8,128)} %shard_map.68, f32[128,16,128]{0,2,1:T(8,128)S(1)} %copy.14), kind=kOutput, calls=%fused_computation.4 | convolution fusion | flops 403177472 | bytes 2179072 | tf_op jit(solution)/shard_map/dot_general | solution.py:216
  66.2 0.0 copy-start.1
  66.2 1.4 %copy.27 = f32[128,16,128]{2,1,0:T(8,128)} copy(f32[128,16,128]{0,2,1:T(8,128)S(1)} %fusion.2) | data formatting | bytes 2097152
  67.6 0.0 copy-done.1
  67.6 1.0 %fusion.3 = f32[128,16,128]{0,2,1:T(8,128)S(1)} fusion(f32[128,16,128]{2,0,1:T(8,128)S(1)} %get-tuple-element.7, f32[128,16]{0,1:T(8,128)S(1)} %get-tuple-element.20, f32[16,128]{1,0:T(8,128)S(1)} %get-tuple-element.19, f32[128,128]{1,0:T(8,128)S(1)} %copy-done.1), kind=kOutput, calls=%fused_computation.6 | convolution fusion | flops 403177472 | bytes 2179072 | tf_op jit(solution)/shard_map/dot_general | solution.py:213
  68.6 1.4 %copy.26 = f32[128,16,128]{2,1,0:T(8,128)} copy(f32[128,16,128]{0,2,1:T(8,128)S(1)} %fusion.3) | data formatting | bytes 2097152
  (37 shorter events, 0.4 us)
Async XLA Ops:
  0.6 1.7 %copy-start = (f32[128,16,128]{2,1,0:T(8,128)S(1)}, f32[128,16,128]{2,1,0:T(8,128)}, u32[]{:S(2)}) copy-start(f32[128,16,128]{2,1,0:T(8,128)} %param.5) | copy-start | bytes 3145732
  2.3 4.2 %copy-start.2 = (s32[1024]{0:T(1024)S(1)}, s32[1024]{0:T(1024)}, u32[]{:S(2)}) copy-start(s32[1024]{0:T(1024)} %param.9) | copy-start | bytes 12292
  2.4 4.3 %copy-start.3 = (f32[1024]{0:T(1024)S(1)}, f32[1024]{0:T(1024)}, u32[]{:S(2)}) copy-start(f32[1024]{0:T(1024)} %param.8) | copy-start | bytes 12292
  2.4 4.3 %copy-start.4 = (f32[1024]{0:T(1024)S(1)}, f32[1024]{0:T(1024)}, u32[]{:S(2)}) copy-start(f32[1024]{0:T(1024)} %param.7) | copy-start | bytes 12292
  2.9 4.2 %collective-permute-start = (f32[128,3,128]{2,0,1:T(8,128)S(1)}, f32[128,3,128]{2,0,1:T(8,128)S(1)}, u32[]{:S(2)}, u32[]{:S(2)}) collective-permute-start(f32[128,3,128]{2,0,1:T(8,128)S(1)} %pad_maximum_fusion.7), channel_id=1, source_target_pairs={{0,4},{4,8},{8,12},{12,16},{16,20},{20,24},{24,28},{1,5},{5,9},{9,... | collective-permute-start | bytes 589832 | tf_op jit(solution)/shard_map/ppermute | solution.py:117
  5.3 5.4 %collective-permute-start.1 = (f32[128,3,128]{2,0,1:T(8,128)S(1)}, f32[128,3,128]{2,0,1:T(8,128)S(1)}, u32[]{:S(2)}, u32[]{:S(2)}) collective-permute-start(f32[128,3,128]{2,0,1:T(8,128)S(1)} %pad_maximum_fusion.8), channel_id=1, source_target_pairs={{4,0},{8,4},{12,8},{16,12},{20,16},{24,20},{28,24},{5,1},{9,5},{13... | collective-permute-start | bytes 589832 | tf_op jit(solution)/shard_map/ppermute | solution.py:117
  10.8 6.0 %collective-permute-start.3 = (f32[3,20,128]{2,1,0:T(8,128)S(1)}, f32[3,20,128]{2,1,0:T(8,128)S(1)}, u32[]{:S(2)}, u32[]{:S(2)}) collective-permute-start(f32[3,20,128]{2,1,0:T(8,128)S(1)} %pad_maximum_fusion.11), channel_id=1, source_target_pairs={{1,0},{2,1},{3,2},{5,4},{6,5},{7,6},{9,8},{10,9},{11,10},{13,12},{... | collective-permute-start | bytes 92168 | tf_op jit(solution)/shard_map/ppermute | solution.py:117
  12.2 6.2 %collective-permute-start.2 = (f32[3,20,128]{2,1,0:T(8,128)S(1)}, f32[3,20,128]{2,1,0:T(8,128)S(1)}, u32[]{:S(2)}, u32[]{:S(2)}) collective-permute-start(f32[3,20,128]{2,1,0:T(8,128)S(1)} %pad_maximum_fusion.10), channel_id=1, source_target_pairs={{0,1},{1,2},{2,3},{4,5},{5,6},{6,7},{8,9},{9,10},{10,11},{12,13},{... | collective-permute-start | bytes 92168 | tf_op jit(solution)/shard_map/ppermute | solution.py:117
  25.1 4.0 %collective-permute-start.4 = (f32[129,128]{1,0:T(8,128)S(1)}, f32[129,128]{1,0:T(8,128)S(1)}, u32[]{:S(2)}, u32[]{:S(2)}) collective-permute-start(f32[129,128]{1,0:T(8,128)S(1)} %pad_maximum_fusion.9), channel_id=1, source_target_pairs={{0,4},{4,0},{8,12},{12,8},{16,20},{20,16},{24,28},{28,24},{1,5},{5... | collective-permute-start | bytes 198152 | tf_op jit(solution)/shard_map/ppermute | solution.py:38
  29.1 5.2 %collective-permute-start.5 = (f32[129,128]{1,0:T(8,128)S(1)}, f32[129,128]{1,0:T(8,128)S(1)}, u32[]{:S(2)}, u32[]{:S(2)}) collective-permute-start(f32[129,128]{1,0:T(8,128)S(1)} %fusion.43), channel_id=1, source_target_pairs={{0,8},{4,12},{8,0},{12,4},{16,24},{20,28},{24,16},{28,20},{1,9},{5... | collective-permute-start | bytes 198152 | tf_op jit(solution)/shard_map/ppermute | solution.py:38
  34.3 4.4 %collective-permute-start.6 = (f32[129,128]{1,0:T(8,128)S(1)}, f32[129,128]{1,0:T(8,128)S(1)}, u32[]{:S(2)}, u32[]{:S(2)}) collective-permute-start(f32[129,128]{1,0:T(8,128)S(1)} %add.88), channel_id=1, source_target_pairs={{0,16},{4,20},{8,24},{12,28},{16,0},{20,4},{24,8},{28,12},{1,17},{... | collective-permute-start | bytes 198152 | tf_op jit(solution)/shard_map/ppermute | solution.py:38
  38.6 4.4 %collective-permute-start.7 = (f32[129,128]{1,0:T(8,128)S(1)}, f32[129,128]{1,0:T(8,128)S(1)}, u32[]{:S(2)}, u32[]{:S(2)}) collective-permute-start(f32[129,128]{1,0:T(8,128)S(1)} %add.89), channel_id=1, source_target_pairs={{0,1},{1,0},{2,3},{3,2},{4,5},{5,4},{6,7},{7,6},{8,9},{9,8},{10,11... | collective-permute-start | bytes 198152 | tf_op jit(solution)/shard_map/ppermute | solution.py:38
  43.0 5.4 %collective-permute-start.8 = (f32[129,128]{1,0:T(8,128)S(1)}, f32[129,128]{1,0:T(8,128)S(1)}, u32[]{:S(2)}, u32[]{:S(2)}) collective-permute-start(f32[129,128]{1,0:T(8,128)S(1)} %add.90), channel_id=1, source_target_pairs={{0,2},{1,3},{2,0},{3,1},{4,6},{5,7},{6,4},{7,5},{8,10},{9,11},{10,... | collective-permute-start | bytes 198152 | tf_op jit(solution)/shard_map/ppermute | solution.py:38
  66.2 1.4 %copy-start.1 = (f32[128,128]{1,0:T(8,128)S(1)}, f32[128,128]{1,0:T(8,128)}, u32[]{:S(2)}) copy-start(f32[128,128]{1,0:T(8,128)} %shard_map.68) | copy-start | bytes 196612

commit v12 on v11

--- a/solution.py
+++ b/solution.py
@@ -68,7 +68,7 @@
             inverse_ref[pl.ds(k, 1), :] = inverse_row
             return carry
 
-        lax.fori_loop(first, min(first + 8, size), step, 0)
+        lax.fori_loop(first, min(first + 8, size), step, 0, unroll=True)
     lower_inverse = inverse_ref[...]
     projected_row = stacked_ref[size : size + 1, :]
     whitened = jnp.sum(lower_inverse * projected_row, axis=1, keepdims=True)

time: 70.5 us -> 70.5 us (level)
  no operation moved by 1% of the time
where the time goes in v12:
time: 70.5 us; the launch traced here: 70 us
  starting transfers between devices  21.7 us (31%)
  waiting for transfers between devices  16.2 us (23%)
  Pallas kernels  15 us (21%)
  matrix products  6.76 us (10%)
  local copies, waits for them, and re-layouts  5.02 us (7%)
  other arithmetic  4.22 us (6%)
  between operations  1.04 us (1%)
    pallas_call x1, Pallas kernels, combination_transposed_of(): pl.pallas_call(combination_kernel, out_shape=jax.ShapeDtypeStruct((size,...  15 us
    ppermute x5, starting transfers between devices, butterfly_sum(): received[offset] = lax.ppermute(value, axis, pairs)  12.2 us
    ppermute x5, waiting for transfers between devices, butterfly_sum(): received[offset] = lax.ppermute(value, axis, pairs)  11.1 us
    ppermute x4, starting transfers between devices, from_neighbour(): return lax.ppermute(block, axis, pairs)  9.5 us
    ppermute x4, waiting for transfers between devices, from_neighbour(): return lax.ppermute(block, axis, pairs)  5.09 us
    unnamed x14, local copies, waits for them, and re-layouts  4.87 us
    dot_general x1, matrix products, shards(): lax.dot_general(deviation_t * cell_weight[:, :, None], deviation_t, (((0,...  2.7 us
    select_n x1, other arithmetic, forecast_two_steps(): first = jnp.where(outside[:, :, None], 0.0, first)  2.3 us
  transfers between devices with their start and end apart: 9, of which 7 were waited for; matrix products, arithmetic and copies ran while one was open for 1% of the time, Pallas kernels for 0%

profile of v12, /device:TPU:0, one launch (start us, length us, event | category | flops | bytes accessed | tf_op | source)
XLA Modules:
  0.0 70.0 jit_solution(16380030886406220604)
XLA Ops:
  0.6 0.0 copy-start
  0.6 1.7 %copy.14 = f32[128,16,128]{0,2,1:T(8,128)S(1)} copy(f32[128,16,128]{2,1,0:T(8,128)} %param.6) | data formatting | bytes 2097152 | tf_op args[1]
  2.3 0.0 copy-done
  2.3 0.0 copy-start.2
  2.4 0.0 copy-start.3
  2.4 0.0 copy-start.4
  2.4 0.4 copy.13
  2.9 2.4 %collective-permute-start = (f32[128,3,128]{2,0,1:T(8,128)S(1)}, f32[128,3,128]{2,0,1:T(8,128)S(1)}, u32[]{:S(2)}, u32[]{:S(2)}) collective-permute-start(f32[128,3,128]{2,0,1:T(8,128)S(1)} %pad_maximum_fusion.7), channel_id=1, source_target_pairs={{0,4},{4,8},{8,12},{12,16},{16,20},{20,24},{24,28},{1,5},{5,9},{9,... | collective-permute-start | bytes 589832 | tf_op jit(solution)/shard_map/ppermute | solution.py:117
  5.3 1.3 %collective-permute-start.1 = (f32[128,3,128]{2,0,1:T(8,128)S(1)}, f32[128,3,128]{2,0,1:T(8,128)S(1)}, u32[]{:S(2)}, u32[]{:S(2)}) collective-permute-start(f32[128,3,128]{2,0,1:T(8,128)S(1)} %pad_maximum_fusion.8), channel_id=1, source_target_pairs={{4,0},{8,4},{12,8},{16,12},{20,16},{24,20},{28,24},{5,1},{9,5},{13... | collective-permute-start | bytes 589832 | tf_op jit(solution)/shard_map/ppermute | solution.py:117
  6.6 0.0 copy-done.2
  6.6 0.0 copy-done.3
  6.6 0.0 copy-done.4
  6.7 0.4 fusion.27
  7.1 0.0 collective-permute-done
  7.1 3.6 %collective-permute-done.1 = f32[128,3,128]{2,0,1:T(8,128)S(1)} collective-permute-done((f32[128,3,128]{2,0,1:T(8,128)S(1)}, f32[128,3,128]{2,0,1:T(8,128)S(1)}, u32[]{:S(2)}, u32[]{:S(2)}) %collective-permute-start.1) | collective-permute-done | bytes 196640 | tf_op jit(solution)/shard_map/ppermute | solution.py:117
  10.8 1.3 %collective-permute-start.3 = (f32[3,20,128]{2,1,0:T(8,128)S(1)}, f32[3,20,128]{2,1,0:T(8,128)S(1)}, u32[]{:S(2)}, u32[]{:S(2)}) collective-permute-start(f32[3,20,128]{2,1,0:T(8,128)S(1)} %pad_maximum_fusion.11), channel_id=1, source_target_pairs={{1,0},{2,1},{3,2},{5,4},{6,5},{7,6},{9,8},{10,9},{11,10},{13,12},{... | collective-permute-start | bytes 92168 | tf_op jit(solution)/shard_map/ppermute | solution.py:117
  12.2 4.5 %collective-permute-start.2 = (f32[3,20,128]{2,1,0:T(8,128)S(1)}, f32[3,20,128]{2,1,0:T(8,128)S(1)}, u32[]{:S(2)}, u32[]{:S(2)}) collective-permute-start(f32[3,20,128]{2,1,0:T(8,128)S(1)} %pad_maximum_fusion.10), channel_id=1, source_target_pairs={{0,1},{1,2},{2,3},{4,5},{5,6},{6,7},{8,9},{9,10},{10,11},{12,13},{... | collective-permute-start | bytes 92168 | tf_op jit(solution)/shard_map/ppermute | solution.py:117
  16.7 0.1 or_or_fusion
  16.8 0.0 collective-permute-done.3
  16.8 1.5 %collective-permute-done.2 = f32[3,20,128]{2,1,0:T(8,128)S(1)} collective-permute-done((f32[3,20,128]{2,1,0:T(8,128)S(1)}, f32[3,20,128]{2,1,0:T(8,128)S(1)}, u32[]{:S(2)}, u32[]{:S(2)}) %collective-permute-start.2) | collective-permute-done | bytes 30752 | tf_op jit(solution)/shard_map/ppermute | solution.py:117
  18.4 0.1 pad_maximum_fusion
  18.5 2.3 %fusion.9 = f32[130,18,128]{2,0,1:T(8,128)S(1)} fusion(f32[2,20,128]{2,0,1:T(2,128)S(1)} %copy.19, f32[128,2,128]{2,0,1:T(8,128)S(1)} %slice.121, f32[128,16,128]{2,0,1:T(8,128)S(1)} %bitcast.42, f32[128,2,128]{2,0,1:T(8,128)S(1)} %slice.118, f32[2,20,128]{2,0,1:T(2,128)S(1)} %copy.20, f32[132,20,128]{2,0,1:T(8,128)S(1)} %pad_maximum_fusion, ...), kind=kLoop, calls=%fused_computation.13 | loop fusion | flops 5990400 | bytes 7344420 | tf_op jit(solution)/shard_map/jit(_where)/select_n | solution.py:159
  20.8 0.9 %fusion.44 = (f32[128,16]{0,1:T(8,128)S(1)}, f32[128,16,128]{2,0,1:T(8,128)S(1)}, f32[128,16]{0,1:T(8,128)S(1)}) fusion(f32[128,16,128]{0,2,1:T(8,128)S(1)} %copy.14, f32[130,18,128]{2,0,1:T(8,128)S(1)} %fusion.9), kind=kLoop, calls=%fused_computation.90 | loop fusion | flops 2879488 | bytes 7356416 | tf_op jit(solution)/shard_map/reduce_sum | solution.py:174
  21.7 2.7 %fusion.11 = f32[128,128]{1,0:T(8,128)S(1)} fusion(f32[128,16,128]{2,0,1:T(8,128)S(1)} %get-tuple-element.7, f32[128,16]{0,1:T(8,128)S(1)} %get-tuple-element.17, f32[128,16]{0,1:T(8,128)S(1)} %get-tuple-element.20), kind=kOutput, calls=%fused_computation.22 | convolution fusion | flops 403439616 | bytes 1130496 | tf_op jit(solution)/shard_map/dot_general | solution.py:197
  24.5 0.8 %convolution_bitcast_fusion.2 = f32[1,128]{1,0:T(1,128)S(1)} fusion(f32[128,16,1]{0,2,1:T(1,128)S(1)} %bitcast.43, f32[128,16,128]{2,0,1:T(8,128)S(1)} %get-tuple-element.7, f32[128,16]{0,1:T(8,128)S(1)} %get-tuple-element.20), kind=kOutput, calls=%fused_computation.23 | convolution fusion | flops 3407872 | bytes 1065472 | tf_op jit(solution)/shard_map/dot_general | solution.py:203
  25.3 3.1 %collective-permute-start.4 = (f32[129,128]{1,0:T(8,128)S(1)}, f32[129,128]{1,0:T(8,128)S(1)}, u32[]{:S(2)}, u32[]{:S(2)}) collective-permute-start(f32[129,128]{1,0:T(8,128)S(1)} %pad_maximum_fusion.9), channel_id=1, source_target_pairs={{0,4},{4,0},{8,12},{12,8},{16,20},{20,16},{24,28},{28,24},{1,5},{5... | collective-permute-start | bytes 198152 | tf_op jit(solution)/shard_map/ppermute | solution.py:38
  28.4 0.9 %collective-permute-done.4 = f32[129,128]{1,0:T(8,128)S(1)} collective-permute-done((f32[129,128]{1,0:T(8,128)S(1)}, f32[129,128]{1,0:T(8,128)S(1)}, u32[]{:S(2)}, u32[]{:S(2)}) %collective-permute-start.4) | collective-permute-done | bytes 66080 | tf_op jit(solution)/shard_map/ppermute | solution.py:38
  29.3 2.5 %collective-permute-start.5 = (f32[129,128]{1,0:T(8,128)S(1)}, f32[129,128]{1,0:T(8,128)S(1)}, u32[]{:S(2)}, u32[]{:S(2)}) collective-permute-start(f32[129,128]{1,0:T(8,128)S(1)} %fusion.43), channel_id=1, source_target_pairs={{0,8},{4,12},{8,0},{12,4},{16,24},{20,28},{24,16},{28,20},{1,9},{5... | collective-permute-start | bytes 198152 | tf_op jit(solution)/shard_map/ppermute | solution.py:38
  31.7 2.7 %collective-permute-done.5 = f32[129,128]{1,0:T(8,128)S(1)} collective-permute-done((f32[129,128]{1,0:T(8,128)S(1)}, f32[129,128]{1,0:T(8,128)S(1)}, u32[]{:S(2)}, u32[]{:S(2)}) %collective-permute-start.5) | collective-permute-done | bytes 66080 | tf_op jit(solution)/shard_map/ppermute | solution.py:38
  34.4 1.4 %collective-permute-start.6 = (f32[129,128]{1,0:T(8,128)S(1)}, f32[129,128]{1,0:T(8,128)S(1)}, u32[]{:S(2)}, u32[]{:S(2)}) collective-permute-start(f32[129,128]{1,0:T(8,128)S(1)} %add.88), channel_id=1, source_target_pairs={{0,16},{4,20},{8,24},{12,28},{16,0},{20,4},{24,8},{28,12},{1,17},{... | collective-permute-start | bytes 198152 | tf_op jit(solution)/shard_map/ppermute | solution.py:38
  35.9 3.0 %collective-permute-done.6 = f32[129,128]{1,0:T(8,128)S(1)} collective-permute-done((f32[129,128]{1,0:T(8,128)S(1)}, f32[129,128]{1,0:T(8,128)S(1)}, u32[]{:S(2)}, u32[]{:S(2)}) %collective-permute-start.6) | collective-permute-done | bytes 66080 | tf_op jit(solution)/shard_map/ppermute | solution.py:38
  38.8 2.1 %collective-permute-start.7 = (f32[129,128]{1,0:T(8,128)S(1)}, f32[129,128]{1,0:T(8,128)S(1)}, u32[]{:S(2)}, u32[]{:S(2)}) collective-permute-start(f32[129,128]{1,0:T(8,128)S(1)} %add.89), channel_id=1, source_target_pairs={{0,1},{1,0},{2,3},{3,2},{4,5},{5,4},{6,7},{7,6},{8,9},{9,8},{10,11... | collective-permute-start | bytes 198152 | tf_op jit(solution)/shard_map/ppermute | solution.py:38
  40.9 2.3 %collective-permute-done.7 = f32[129,128]{1,0:T(8,128)S(1)} collective-permute-done((f32[129,128]{1,0:T(8,128)S(1)}, f32[129,128]{1,0:T(8,128)S(1)}, u32[]{:S(2)}, u32[]{:S(2)}) %collective-permute-start.7) | collective-permute-done | bytes 66080 | tf_op jit(solution)/shard_map/ppermute | solution.py:38
  43.2 3.1 %collective-permute-start.8 = (f32[129,128]{1,0:T(8,128)S(1)}, f32[129,128]{1,0:T(8,128)S(1)}, u32[]{:S(2)}, u32[]{:S(2)}) collective-permute-start(f32[129,128]{1,0:T(8,128)S(1)} %add.90), channel_id=1, source_target_pairs={{0,2},{1,3},{2,0},{3,1},{4,6},{5,7},{6,4},{7,5},{8,10},{9,11},{10,... | collective-permute-start | bytes 198152 | tf_op jit(solution)/shard_map/ppermute | solution.py:38
  46.3 2.3 %collective-permute-done.8 = f32[129,128]{1,0:T(8,128)S(1)} collective-permute-done((f32[129,128]{1,0:T(8,128)S(1)}, f32[129,128]{1,0:T(8,128)S(1)}, u32[]{:S(2)}, u32[]{:S(2)}) %collective-permute-start.8) | collective-permute-done | bytes 66080 | tf_op jit(solution)/shard_map/ppermute | solution.py:38
  48.6 0.6 add.91.stacked_ref
  49.2 15.0 %shard_map.68 = f32[128,128]{1,0:T(8,128)} custom-call(f32[129,128]{1,0:T(8,128)} %add.91.stacked_ref), custom_call_target="tpu_custom_call" | custom-call | tf_op jit(solution)/shard_map/pallas_call | solution.py:81
  64.3 1.9 %fusion.2 = f32[128,16,128]{0,2,1:T(8,128)S(1)} fusion(f32[128,16]{0,1:T(8,128)S(1)} %get-tuple-element.22, f32[16,128]{1,0:T(8,128)S(1)} %get-tuple-element.21, f32[128,128]{1,0:T(8,128)} %shard_map.68, f32[128,16,128]{0,2,1:T(8,128)S(1)} %copy.14), kind=kOutput, calls=%fused_computation.4 | convolution fusion | flops 403177472 | bytes 2179072 | tf_op jit(solution)/shard_map/dot_general | solution.py:216
  66.2 0.0 copy-start.1
  66.2 1.4 %copy.27 = f32[128,16,128]{2,1,0:T(8,128)} copy(f32[128,16,128]{0,2,1:T(8,128)S(1)} %fusion.2) | data formatting | bytes 2097152
  67.6 0.0 copy-done.1
  67.6 1.0 %fusion.3 = f32[128,16,128]{0,2,1:T(8,128)S(1)} fusion(f32[128,16,128]{2,0,1:T(8,128)S(1)} %get-tuple-element.7, f32[128,16]{0,1:T(8,128)S(1)} %get-tuple-element.20, f32[16,128]{1,0:T(8,128)S(1)} %get-tuple-element.19, f32[128,128]{1,0:T(8,128)S(1)} %copy-done.1), kind=kOutput, calls=%fused_computation.6 | convolution fusion | flops 403177472 | bytes 2179072 | tf_op jit(solution)/shard_map/dot_general | solution.py:213
  68.6 1.4 %copy.26 = f32[128,16,128]{2,1,0:T(8,128)} copy(f32[128,16,128]{0,2,1:T(8,128)S(1)} %fusion.3) | data formatting | bytes 2097152
  (37 shorter events, 0.4 us)
Async XLA Ops:
  0.6 1.7 %copy-start = (f32[128,16,128]{2,1,0:T(8,128)S(1)}, f32[128,16,128]{2,1,0:T(8,128)}, u32[]{:S(2)}) copy-start(f32[128,16,128]{2,1,0:T(8,128)} %param.5) | copy-start | bytes 3145732
  2.3 4.2 %copy-start.2 = (s32[1024]{0:T(1024)S(1)}, s32[1024]{0:T(1024)}, u32[]{:S(2)}) copy-start(s32[1024]{0:T(1024)} %param.9) | copy-start | bytes 12292
  2.4 4.3 %copy-start.3 = (f32[1024]{0:T(1024)S(1)}, f32[1024]{0:T(1024)}, u32[]{:S(2)}) copy-start(f32[1024]{0:T(1024)} %param.8) | copy-start | bytes 12292
  2.4 4.3 %copy-start.4 = (f32[1024]{0:T(1024)S(1)}, f32[1024]{0:T(1024)}, u32[]{:S(2)}) copy-start(f32[1024]{0:T(1024)} %param.7) | copy-start | bytes 12292
  2.9 4.2 %collective-permute-start = (f32[128,3,128]{2,0,1:T(8,128)S(1)}, f32[128,3,128]{2,0,1:T(8,128)S(1)}, u32[]{:S(2)}, u32[]{:S(2)}) collective-permute-start(f32[128,3,128]{2,0,1:T(8,128)S(1)} %pad_maximum_fusion.7), channel_id=1, source_target_pairs={{0,4},{4,8},{8,12},{12,16},{16,20},{20,24},{24,28},{1,5},{5,9},{9,... | collective-permute-start | bytes 589832 | tf_op jit(solution)/shard_map/ppermute | solution.py:117
  5.3 5.4 %collective-permute-start.1 = (f32[128,3,128]{2,0,1:T(8,128)S(1)}, f32[128,3,128]{2,0,1:T(8,128)S(1)}, u32[]{:S(2)}, u32[]{:S(2)}) collective-permute-start(f32[128,3,128]{2,0,1:T(8,128)S(1)} %pad_maximum_fusion.8), channel_id=1, source_target_pairs={{4,0},{8,4},{12,8},{16,12},{20,16},{24,20},{28,24},{5,1},{9,5},{13... | collective-permute-start | bytes 589832 | tf_op jit(solution)/shard_map/ppermute | solution.py:117
  10.8 6.0 %collective-permute-start.3 = (f32[3,20,128]{2,1,0:T(8,128)S(1)}, f32[3,20,128]{2,1,0:T(8,128)S(1)}, u32[]{:S(2)}, u32[]{:S(2)}) collective-permute-start(f32[3,20,128]{2,1,0:T(8,128)S(1)} %pad_maximum_fusion.11), channel_id=1, source_target_pairs={{1,0},{2,1},{3,2},{5,4},{6,5},{7,6},{9,8},{10,9},{11,10},{13,12},{... | collective-permute-start | bytes 92168 | tf_op jit(solution)/shard_map/ppermute | solution.py:117
  12.2 6.2 %collective-permute-start.2 = (f32[3,20,128]{2,1,0:T(8,128)S(1)}, f32[3,20,128]{2,1,0:T(8,128)S(1)}, u32[]{:S(2)}, u32[]{:S(2)}) collective-permute-start(f32[3,20,128]{2,1,0:T(8,128)S(1)} %pad_maximum_fusion.10), channel_id=1, source_target_pairs={{0,1},{1,2},{2,3},{4,5},{5,6},{6,7},{8,9},{9,10},{10,11},{12,13},{... | collective-permute-start | bytes 92168 | tf_op jit(solution)/shard_map/ppermute | solution.py:117
  25.3 4.0 %collective-permute-start.4 = (f32[129,128]{1,0:T(8,128)S(1)}, f32[129,128]{1,0:T(8,128)S(1)}, u32[]{:S(2)}, u32[]{:S(2)}) collective-permute-start(f32[129,128]{1,0:T(8,128)S(1)} %pad_maximum_fusion.9), channel_id=1, source_target_pairs={{0,4},{4,0},{8,12},{12,8},{16,20},{20,16},{24,28},{28,24},{1,5},{5... | collective-permute-start | bytes 198152 | tf_op jit(solution)/shard_map/ppermute | solution.py:38
  29.3 5.2 %collective-permute-start.5 = (f32[129,128]{1,0:T(8,128)S(1)}, f32[129,128]{1,0:T(8,128)S(1)}, u32[]{:S(2)}, u32[]{:S(2)}) collective-permute-start(f32[129,128]{1,0:T(8,128)S(1)} %fusion.43), channel_id=1, source_target_pairs={{0,8},{4,12},{8,0},{12,4},{16,24},{20,28},{24,16},{28,20},{1,9},{5... | collective-permute-start | bytes 198152 | tf_op jit(solution)/shard_map/ppermute | solution.py:38
  34.4 4.4 %collective-permute-start.6 = (f32[129,128]{1,0:T(8,128)S(1)}, f32[129,128]{1,0:T(8,128)S(1)}, u32[]{:S(2)}, u32[]{:S(2)}) collective-permute-start(f32[129,128]{1,0:T(8,128)S(1)} %add.88), channel_id=1, source_target_pairs={{0,16},{4,20},{8,24},{12,28},{16,0},{20,4},{24,8},{28,12},{1,17},{... | collective-permute-start | bytes 198152 | tf_op jit(solution)/shard_map/ppermute | solution.py:38
  38.8 4.4 %collective-permute-start.7 = (f32[129,128]{1,0:T(8,128)S(1)}, f32[129,128]{1,0:T(8,128)S(1)}, u32[]{:S(2)}, u32[]{:S(2)}) collective-permute-start(f32[129,128]{1,0:T(8,128)S(1)} %add.89), channel_id=1, source_target_pairs={{0,1},{1,0},{2,3},{3,2},{4,5},{5,4},{6,7},{7,6},{8,9},{9,8},{10,11... | collective-permute-start | bytes 198152 | tf_op jit(solution)/shard_map/ppermute | solution.py:38
  43.2 5.4 %collective-permute-start.8 = (f32[129,128]{1,0:T(8,128)S(1)}, f32[129,128]{1,0:T(8,128)S(1)}, u32[]{:S(2)}, u32[]{:S(2)}) collective-permute-start(f32[129,128]{1,0:T(8,128)S(1)} %add.90), channel_id=1, source_target_pairs={{0,2},{1,3},{2,0},{3,1},{4,6},{5,7},{6,4},{7,5},{8,10},{9,11},{10,... | collective-permute-start | bytes 198152 | tf_op jit(solution)/shard_map/ppermute | solution.py:38
  66.2 1.4 %copy-start.1 = (f32[128,128]{1,0:T(8,128)S(1)}, f32[128,128]{1,0:T(8,128)}, u32[]{:S(2)}) copy-start(f32[128,128]{1,0:T(8,128)} %shard_map.68) | copy-start | bytes 196612

commit v13 on v12

--- a/solution.py
+++ b/solution.py
@@ -48,15 +48,21 @@
     work_ref[...] = stacked_ref[:size, :] + unit
     inverse_ref[...] = unit
     lane = lax.broadcasted_iota(jnp.int32, (1, size), 1)
+    row = work_ref[0:1, :]
+    column = jnp.sum(jnp.where(square_col == 0, work_ref[...], 0.0), axis=1, keepdims=True)
     for first in range(0, size, 8):
         span = size - first
+        column = column[column.shape[0] - span :]
         sublane = lax.broadcasted_iota(jnp.int32, (span, 1), 0) + first
         band_col = lax.broadcasted_iota(jnp.int32, (span, size), 1)
 
         def step(k, carry, first=first, sublane=sublane, band_col=band_col):
-            row = work_ref[pl.ds(k, 1), :]
+            row, column = carry
             band = work_ref[first:, :]
-            column = jnp.sum(jnp.where(band_col == k, band, 0.0), axis=1, keepdims=True)
+            old_next_row = work_ref[pl.ds(jnp.minimum(k + 1, size - 1), 1), :]
+            old_next_col = jnp.sum(
+                jnp.where(band_col == k + 1, band, 0.0), axis=1, keepdims=True
+            )
             pivot = jnp.sum(jnp.where(lane == k, row, 0.0), axis=1, keepdims=True)
             scale = 1.0 / jnp.sqrt(pivot)
             factor_row = jnp.where(lane >= k, row * scale, 0.0)
@@ -66,9 +72,15 @@
             below = jnp.where(sublane > k, factor_col, 0.0)
             inverse_ref[first:, :] = inverse_ref[first:, :] - below * inverse_row
             inverse_ref[pl.ds(k, 1), :] = inverse_row
-            return carry
-
-        lax.fori_loop(first, min(first + 8, size), step, 0, unroll=True)
+            col_at_next = jnp.sum(
+                jnp.where(sublane == k + 1, factor_col, 0.0), axis=0, keepdims=True
+            )
+            row_at_next = jnp.sum(
+                jnp.where(lane == k + 1, factor_row, 0.0), axis=1, keepdims=True
+            )
+            return (old_next_row - col_at_next * factor_row, old_next_col - factor_col * row_at_next)
+
+        row, column = lax.fori_loop(first, min(first + 8, size), step, (row, column), unroll=True)
     lower_inverse = inverse_ref[...]
     projected_row = stacked_ref[size : size + 1, :]
     whitened = jnp.sum(lower_inverse * projected_row, axis=1, keepdims=True)

time: 70.5 us -> 70.7 us (level)
  no operation moved by 1% of the time
where the time goes in v13:
time: 70.7 us; the launch traced here: 70.2 us
  starting transfers between devices  21.7 us (31%)
  waiting for transfers between devices  16.2 us (23%)
  Pallas kernels  15.3 us (22%)
  matrix products  6.77 us (10%)
  local copies, waits for them, and re-layouts  5.02 us (7%)
  other arithmetic  4.22 us (6%)
  between operations  1.04 us (1%)
    pallas_call x1, Pallas kernels, combination_transposed_of(): pl.pallas_call(combination_kernel, out_shape=jax.ShapeDtypeStruct((size,...  15.3 us
    ppermute x5, starting transfers between devices, butterfly_sum(): received[offset] = lax.ppermute(value, axis, pairs)  12.2 us
    ppermute x5, waiting for transfers between devices, butterfly_sum(): received[offset] = lax.ppermute(value, axis, pairs)  11.1 us
    ppermute x4, starting transfers between devices, from_neighbour(): return lax.ppermute(block, axis, pairs)  9.5 us
    ppermute x4, waiting for transfers between devices, from_neighbour(): return lax.ppermute(block, axis, pairs)  5.09 us
    unnamed x14, local copies, waits for them, and re-layouts  4.87 us
    dot_general x1, matrix products, shards(): lax.dot_general(deviation_t * cell_weight[:, :, None], deviation_t, (((0,...  2.7 us
    select_n x1, other arithmetic, forecast_two_steps(): first = jnp.where(outside[:, :, None], 0.0, first)  2.3 us
  transfers between devices with their start and end apart: 9, of which 7 were waited for; matrix products, arithmetic and copies ran while one was open for 1% of the time, Pallas kernels for 0%

profile of v13, /device:TPU:0, one launch (start us, length us, event | category | flops | bytes accessed | tf_op | source)
XLA Modules:
  0.0 70.2 jit_solution(4757390086562162331)
XLA Ops:
  0.6 0.0 copy-start
  0.6 1.7 %copy.14 = f32[128,16,128]{0,2,1:T(8,128)S(1)} copy(f32[128,16,128]{2,1,0:T(8,128)} %param.6) | data formatting | bytes 2097152 | tf_op args[1]
  2.3 0.0 copy-done
  2.3 0.0 copy-start.2
  2.4 0.0 copy-start.3
  2.4 0.0 copy-start.4
  2.4 0.4 copy.13
  2.9 2.4 %collective-permute-start = (f32[128,3,128]{2,0,1:T(8,128)S(1)}, f32[128,3,128]{2,0,1:T(8,128)S(1)}, u32[]{:S(2)}, u32[]{:S(2)}) collective-permute-start(f32[128,3,128]{2,0,1:T(8,128)S(1)} %pad_maximum_fusion.7), channel_id=1, source_target_pairs={{0,4},{4,8},{8,12},{12,16},{16,20},{20,24},{24,28},{1,5},{5,9},{9,... | collective-permute-start | bytes 589832 | tf_op jit(solution)/shard_map/ppermute | solution.py:129
  5.3 1.3 %collective-permute-start.1 = (f32[128,3,128]{2,0,1:T(8,128)S(1)}, f32[128,3,128]{2,0,1:T(8,128)S(1)}, u32[]{:S(2)}, u32[]{:S(2)}) collective-permute-start(f32[128,3,128]{2,0,1:T(8,128)S(1)} %pad_maximum_fusion.8), channel_id=1, source_target_pairs={{4,0},{8,4},{12,8},{16,12},{20,16},{24,20},{28,24},{5,1},{9,5},{13... | collective-permute-start | bytes 589832 | tf_op jit(solution)/shard_map/ppermute | solution.py:129
  6.6 0.0 copy-done.2
  6.6 0.0 copy-done.3
  6.6 0.0 copy-done.4
  6.7 0.4 fusion.27
  7.1 0.0 collective-permute-done
  7.1 3.6 %collective-permute-done.1 = f32[128,3,128]{2,0,1:T(8,128)S(1)} collective-permute-done((f32[128,3,128]{2,0,1:T(8,128)S(1)}, f32[128,3,128]{2,0,1:T(8,128)S(1)}, u32[]{:S(2)}, u32[]{:S(2)}) %collective-permute-start.1) | collective-permute-done | bytes 196640 | tf_op jit(solution)/shard_map/ppermute | solution.py:129
  10.8 1.3 %collective-permute-start.3 = (f32[3,20,128]{2,1,0:T(8,128)S(1)}, f32[3,20,128]{2,1,0:T(8,128)S(1)}, u32[]{:S(2)}, u32[]{:S(2)}) collective-permute-start(f32[3,20,128]{2,1,0:T(8,128)S(1)} %pad_maximum_fusion.11), channel_id=1, source_target_pairs={{1,0},{2,1},{3,2},{5,4},{6,5},{7,6},{9,8},{10,9},{11,10},{13,12},{... | collective-permute-start | bytes 92168 | tf_op jit(solution)/shard_map/ppermute | solution.py:129
  12.2 4.5 %collective-permute-start.2 = (f32[3,20,128]{2,1,0:T(8,128)S(1)}, f32[3,20,128]{2,1,0:T(8,128)S(1)}, u32[]{:S(2)}, u32[]{:S(2)}) collective-permute-start(f32[3,20,128]{2,1,0:T(8,128)S(1)} %pad_maximum_fusion.10), channel_id=1, source_target_pairs={{0,1},{1,2},{2,3},{4,5},{5,6},{6,7},{8,9},{9,10},{10,11},{12,13},{... | collective-permute-start | bytes 92168 | tf_op jit(solution)/shard_map/ppermute | solution.py:129
  16.7 0.1 or_or_fusion
  16.8 0.0 collective-permute-done.3
  16.8 1.5 %collective-permute-done.2 = f32[3,20,128]{2,1,0:T(8,128)S(1)} collective-permute-done((f32[3,20,128]{2,1,0:T(8,128)S(1)}, f32[3,20,128]{2,1,0:T(8,128)S(1)}, u32[]{:S(2)}, u32[]{:S(2)}) %collective-permute-start.2) | collective-permute-done | bytes 30752 | tf_op jit(solution)/shard_map/ppermute | solution.py:129
  18.4 0.1 pad_maximum_fusion
  18.5 2.3 %fusion.9 = f32[130,18,128]{2,0,1:T(8,128)S(1)} fusion(f32[2,20,128]{2,0,1:T(2,128)S(1)} %copy.19, f32[128,2,128]{2,0,1:T(8,128)S(1)} %slice.121, f32[128,16,128]{2,0,1:T(8,128)S(1)} %bitcast.42, f32[128,2,128]{2,0,1:T(8,128)S(1)} %slice.118, f32[2,20,128]{2,0,1:T(2,128)S(1)} %copy.20, f32[132,20,128]{2,0,1:T(8,128)S(1)} %pad_maximum_fusion, ...), kind=kLoop, calls=%fused_computation.13 | loop fusion | flops 5990400 | bytes 7344420 | tf_op jit(solution)/shard_map/jit(_where)/select_n | solution.py:171
  20.8 0.9 %fusion.44 = (f32[128,16]{0,1:T(8,128)S(1)}, f32[128,16,128]{2,0,1:T(8,128)S(1)}, f32[128,16]{0,1:T(8,128)S(1)}) fusion(f32[128,16,128]{0,2,1:T(8,128)S(1)} %copy.14, f32[130,18,128]{2,0,1:T(8,128)S(1)} %fusion.9), kind=kLoop, calls=%fused_computation.90 | loop fusion | flops 2879488 | bytes 7356416 | tf_op jit(solution)/shard_map/reduce_sum | solution.py:186
  21.7 2.7 %fusion.11 = f32[128,128]{1,0:T(8,128)S(1)} fusion(f32[128,16,128]{2,0,1:T(8,128)S(1)} %get-tuple-element.7, f32[128,16]{0,1:T(8,128)S(1)} %get-tuple-element.17, f32[128,16]{0,1:T(8,128)S(1)} %get-tuple-element.20), kind=kOutput, calls=%fused_computation.22 | convolution fusion | flops 403439616 | bytes 1130496 | tf_op jit(solution)/shard_map/dot_general | solution.py:209
  24.5 0.8 %convolution_bitcast_fusion.2 = f32[1,128]{1,0:T(1,128)S(1)} fusion(f32[128,16,1]{0,2,1:T(1,128)S(1)} %bitcast.43, f32[128,16,128]{2,0,1:T(8,128)S(1)} %get-tuple-element.7, f32[128,16]{0,1:T(8,128)S(1)} %get-tuple-element.20), kind=kOutput, calls=%fused_computation.23 | convolution fusion | flops 3407872 | bytes 1065472 | tf_op jit(solution)/shard_map/dot_general | solution.py:215
  25.3 3.1 %collective-permute-start.4 = (f32[129,128]{1,0:T(8,128)S(1)}, f32[129,128]{1,0:T(8,128)S(1)}, u32[]{:S(2)}, u32[]{:S(2)}) collective-permute-start(f32[129,128]{1,0:T(8,128)S(1)} %pad_maximum_fusion.9), channel_id=1, source_target_pairs={{0,4},{4,0},{8,12},{12,8},{16,20},{20,16},{24,28},{28,24},{1,5},{5... | collective-permute-start | bytes 198152 | tf_op jit(solution)/shard_map/ppermute | solution.py:38
  28.4 0.9 %collective-permute-done.4 = f32[129,128]{1,0:T(8,128)S(1)} collective-permute-done((f32[129,128]{1,0:T(8,128)S(1)}, f32[129,128]{1,0:T(8,128)S(1)}, u32[]{:S(2)}, u32[]{:S(2)}) %collective-permute-start.4) | collective-permute-done | bytes 66080 | tf_op jit(solution)/shard_map/ppermute | solution.py:38
  29.3 2.5 %collective-permute-start.5 = (f32[129,128]{1,0:T(8,128)S(1)}, f32[129,128]{1,0:T(8,128)S(1)}, u32[]{:S(2)}, u32[]{:S(2)}) collective-permute-start(f32[129,128]{1,0:T(8,128)S(1)} %fusion.43), channel_id=1, source_target_pairs={{0,8},{4,12},{8,0},{12,4},{16,24},{20,28},{24,16},{28,20},{1,9},{5... | collective-permute-start | bytes 198152 | tf_op jit(solution)/shard_map/ppermute | solution.py:38
  31.7 2.7 %collective-permute-done.5 = f32[129,128]{1,0:T(8,128)S(1)} collective-permute-done((f32[129,128]{1,0:T(8,128)S(1)}, f32[129,128]{1,0:T(8,128)S(1)}, u32[]{:S(2)}, u32[]{:S(2)}) %collective-permute-start.5) | collective-permute-done | bytes 66080 | tf_op jit(solution)/shard_map/ppermute | solution.py:38
  34.4 1.4 %collective-permute-start.6 = (f32[129,128]{1,0:T(8,128)S(1)}, f32[129,128]{1,0:T(8,128)S(1)}, u32[]{:S(2)}, u32[]{:S(2)}) collective-permute-start(f32[129,128]{1,0:T(8,128)S(1)} %add.88), channel_id=1, source_target_pairs={{0,16},{4,20},{8,24},{12,28},{16,0},{20,4},{24,8},{28,12},{1,17},{... | collective-permute-start | bytes 198152 | tf_op jit(solution)/shard_map/ppermute | solution.py:38
  35.9 3.0 %collective-permute-done.6 = f32[129,128]{1,0:T(8,128)S(1)} collective-permute-done((f32[129,128]{1,0:T(8,128)S(1)}, f32[129,128]{1,0:T(8,128)S(1)}, u32[]{:S(2)}, u32[]{:S(2)}) %collective-permute-start.6) | collective-permute-done | bytes 66080 | tf_op jit(solution)/shard_map/ppermute | solution.py:38
  38.8 2.1 %collective-permute-start.7 = (f32[129,128]{1,0:T(8,128)S(1)}, f32[129,128]{1,0:T(8,128)S(1)}, u32[]{:S(2)}, u32[]{:S(2)}) collective-permute-start(f32[129,128]{1,0:T(8,128)S(1)} %add.89), channel_id=1, source_target_pairs={{0,1},{1,0},{2,3},{3,2},{4,5},{5,4},{6,7},{7,6},{8,9},{9,8},{10,11... | collective-permute-start | bytes 198152 | tf_op jit(solution)/shard_map/ppermute | solution.py:38
  40.9 2.3 %collective-permute-done.7 = f32[129,128]{1,0:T(8,128)S(1)} collective-permute-done((f32[129,128]{1,0:T(8,128)S(1)}, f32[129,128]{1,0:T(8,128)S(1)}, u32[]{:S(2)}, u32[]{:S(2)}) %collective-permute-start.7) | collective-permute-done | bytes 66080 | tf_op jit(solution)/shard_map/ppermute | solution.py:38
  43.2 3.1 %collective-permute-start.8 = (f32[129,128]{1,0:T(8,128)S(1)}, f32[129,128]{1,0:T(8,128)S(1)}, u32[]{:S(2)}, u32[]{:S(2)}) collective-permute-start(f32[129,128]{1,0:T(8,128)S(1)} %add.90), channel_id=1, source_target_pairs={{0,2},{1,3},{2,0},{3,1},{4,6},{5,7},{6,4},{7,5},{8,10},{9,11},{10,... | collective-permute-start | bytes 198152 | tf_op jit(solution)/shard_map/ppermute | solution.py:38
  46.3 2.3 %collective-permute-done.8 = f32[129,128]{1,0:T(8,128)S(1)} collective-permute-done((f32[129,128]{1,0:T(8,128)S(1)}, f32[129,128]{1,0:T(8,128)S(1)}, u32[]{:S(2)}, u32[]{:S(2)}) %collective-permute-start.8) | collective-permute-done | bytes 66080 | tf_op jit(solution)/shard_map/ppermute | solution.py:38
  48.6 0.6 add.91.stacked_ref
  49.2 15.3 %shard_map.68 = f32[128,128]{1,0:T(8,128)} custom-call(f32[129,128]{1,0:T(8,128)} %add.91.stacked_ref), custom_call_target="tpu_custom_call" | custom-call | tf_op jit(solution)/shard_map/pallas_call | solution.py:93
  64.6 1.9 %fusion.2 = f32[128,16,128]{0,2,1:T(8,128)S(1)} fusion(f32[128,16]{0,1:T(8,128)S(1)} %get-tuple-element.22, f32[16,128]{1,0:T(8,128)S(1)} %get-tuple-element.21, f32[128,128]{1,0:T(8,128)} %shard_map.68, f32[128,16,128]{0,2,1:T(8,128)S(1)} %copy.14), kind=kOutput, calls=%fused_computation.4 | convolution fusion | flops 403177472 | bytes 2179072 | tf_op jit(solution)/shard_map/dot_general | solution.py:228
  66.4 0.0 copy-start.1
  66.4 1.4 %copy.27 = f32[128,16,128]{2,1,0:T(8,128)} copy(f32[128,16,128]{0,2,1:T(8,128)S(1)} %fusion.2) | data formatting | bytes 2097152
  67.8 0.0 copy-done.1
  67.8 1.0 %fusion.3 = f32[128,16,128]{0,2,1:T(8,128)S(1)} fusion(f32[128,16,128]{2,0,1:T(8,128)S(1)} %get-tuple-element.7, f32[128,16]{0,1:T(8,128)S(1)} %get-tuple-element.20, f32[16,128]{1,0:T(8,128)S(1)} %get-tuple-element.19, f32[128,128]{1,0:T(8,128)S(1)} %copy-done.1), kind=kOutput, calls=%fused_computation.6 | convolution fusion | flops 403177472 | bytes 2179072 | tf_op jit(solution)/shard_map/dot_general | solution.py:225
  68.9 1.4 %copy.26 = f32[128,16,128]{2,1,0:T(8,128)} copy(f32[128,16,128]{0,2,1:T(8,128)S(1)} %fusion.3) | data formatting | bytes 2097152
  (37 shorter events, 0.4 us)
Async XLA Ops:
  0.6 1.7 %copy-start = (f32[128,16,128]{2,1,0:T(8,128)S(1)}, f32[128,16,128]{2,1,0:T(8,128)}, u32[]{:S(2)}) copy-start(f32[128,16,128]{2,1,0:T(8,128)} %param.5) | copy-start | bytes 3145732
  2.3 4.2 %copy-start.2 = (s32[1024]{0:T(1024)S(1)}, s32[1024]{0:T(1024)}, u32[]{:S(2)}) copy-start(s32[1024]{0:T(1024)} %param.9) | copy-start | bytes 12292
  2.4 4.3 %copy-start.3 = (f32[1024]{0:T(1024)S(1)}, f32[1024]{0:T(1024)}, u32[]{:S(2)}) copy-start(f32[1024]{0:T(1024)} %param.8) | copy-start | bytes 12292
  2.4 4.3 %copy-start.4 = (f32[1024]{0:T(1024)S(1)}, f32[1024]{0:T(1024)}, u32[]{:S(2)}) copy-start(f32[1024]{0:T(1024)} %param.7) | copy-start | bytes 12292
  2.9 4.2 %collective-permute-start = (f32[128,3,128]{2,0,1:T(8,128)S(1)}, f32[128,3,128]{2,0,1:T(8,128)S(1)}, u32[]{:S(2)}, u32[]{:S(2)}) collective-permute-start(f32[128,3,128]{2,0,1:T(8,128)S(1)} %pad_maximum_fusion.7), channel_id=1, source_target_pairs={{0,4},{4,8},{8,12},{12,16},{16,20},{20,24},{24,28},{1,5},{5,9},{9,... | collective-permute-start | bytes 589832 | tf_op jit(solution)/shard_map/ppermute | solution.py:129
  5.3 5.4 %collective-permute-start.1 = (f32[128,3,128]{2,0,1:T(8,128)S(1)}, f32[128,3,128]{2,0,1:T(8,128)S(1)}, u32[]{:S(2)}, u32[]{:S(2)}) collective-permute-start(f32[128,3,128]{2,0,1:T(8,128)S(1)} %pad_maximum_fusion.8), channel_id=1, source_target_pairs={{4,0},{8,4},{12,8},{16,12},{20,16},{24,20},{28,24},{5,1},{9,5},{13... | collective-permute-start | bytes 589832 | tf_op jit(solution)/shard_map/ppermute | solution.py:129
  10.8 6.0 %collective-permute-start.3 = (f32[3,20,128]{2,1,0:T(8,128)S(1)}, f32[3,20,128]{2,1,0:T(8,128)S(1)}, u32[]{:S(2)}, u32[]{:S(2)}) collective-permute-start(f32[3,20,128]{2,1,0:T(8,128)S(1)} %pad_maximum_fusion.11), channel_id=1, source_target_pairs={{1,0},{2,1},{3,2},{5,4},{6,5},{7,6},{9,8},{10,9},{11,10},{13,12},{... | collective-permute-start | bytes 92168 | tf_op jit(solution)/shard_map/ppermute | solution.py:129
  12.2 6.2 %collective-permute-start.2 = (f32[3,20,128]{2,1,0:T(8,128)S(1)}, f32[3,20,128]{2,1,0:T(8,128)S(1)}, u32[]{:S(2)}, u32[]{:S(2)}) collective-permute-start(f32[3,20,128]{2,1,0:T(8,128)S(1)} %pad_maximum_fusion.10), channel_id=1, source_target_pairs={{0,1},{1,2},{2,3},{4,5},{5,6},{6,7},{8,9},{9,10},{10,11},{12,13},{... | collective-permute-start | bytes 92168 | tf_op jit(solution)/shard_map/ppermute | solution.py:129
  25.3 4.0 %collective-permute-start.4 = (f32[129,128]{1,0:T(8,128)S(1)}, f32[129,128]{1,0:T(8,128)S(1)}, u32[]{:S(2)}, u32[]{:S(2)}) collective-permute-start(f32[129,128]{1,0:T(8,128)S(1)} %pad_maximum_fusion.9), channel_id=1, source_target_pairs={{0,4},{4,0},{8,12},{12,8},{16,20},{20,16},{24,28},{28,24},{1,5},{5... | collective-permute-start | bytes 198152 | tf_op jit(solution)/shard_map/ppermute | solution.py:38
  29.3 5.2 %collective-permute-start.5 = (f32[129,128]{1,0:T(8,128)S(1)}, f32[129,128]{1,0:T(8,128)S(1)}, u32[]{:S(2)}, u32[]{:S(2)}) collective-permute-start(f32[129,128]{1,0:T(8,128)S(1)} %fusion.43), channel_id=1, source_target_pairs={{0,8},{4,12},{8,0},{12,4},{16,24},{20,28},{24,16},{28,20},{1,9},{5... | collective-permute-start | bytes 198152 | tf_op jit(solution)/shard_map/ppermute | solution.py:38
  34.4 4.4 %collective-permute-start.6 = (f32[129,128]{1,0:T(8,128)S(1)}, f32[129,128]{1,0:T(8,128)S(1)}, u32[]{:S(2)}, u32[]{:S(2)}) collective-permute-start(f32[129,128]{1,0:T(8,128)S(1)} %add.88), channel_id=1, source_target_pairs={{0,16},{4,20},{8,24},{12,28},{16,0},{20,4},{24,8},{28,12},{1,17},{... | collective-permute-start | bytes 198152 | tf_op jit(solution)/shard_map/ppermute | solution.py:38
  38.8 4.4 %collective-permute-start.7 = (f32[129,128]{1,0:T(8,128)S(1)}, f32[129,128]{1,0:T(8,128)S(1)}, u32[]{:S(2)}, u32[]{:S(2)}) collective-permute-start(f32[129,128]{1,0:T(8,128)S(1)} %add.89), channel_id=1, source_target_pairs={{0,1},{1,0},{2,3},{3,2},{4,5},{5,4},{6,7},{7,6},{8,9},{9,8},{10,11... | collective-permute-start | bytes 198152 | tf_op jit(solution)/shard_map/ppermute | solution.py:38
  43.2 5.4 %collective-permute-start.8 = (f32[129,128]{1,0:T(8,128)S(1)}, f32[129,128]{1,0:T(8,128)S(1)}, u32[]{:S(2)}, u32[]{:S(2)}) collective-permute-start(f32[129,128]{1,0:T(8,128)S(1)} %add.90), channel_id=1, source_target_pairs={{0,2},{1,3},{2,0},{3,1},{4,6},{5,7},{6,4},{7,5},{8,10},{9,11},{10,... | collective-permute-start | bytes 198152 | tf_op jit(solution)/shard_map/ppermute | solution.py:38
  66.4 1.4 %copy-start.1 = (f32[128,128]{1,0:T(8,128)S(1)}, f32[128,128]{1,0:T(8,128)}, u32[]{:S(2)}) copy-start(f32[128,128]{1,0:T(8,128)} %shard_map.68) | copy-start | bytes 196612

commit v14 on v11

--- a/solution.py
+++ b/solution.py
@@ -51,17 +51,14 @@
     for first in range(0, size, 8):
         span = size - first
         sublane = lax.broadcasted_iota(jnp.int32, (span, 1), 0) + first
-        band_col = lax.broadcasted_iota(jnp.int32, (span, size), 1)
-
-        def step(k, carry, first=first, sublane=sublane, band_col=band_col):
+
+        def step(k, carry, first=first, sublane=sublane):
             row = work_ref[pl.ds(k, 1), :]
-            band = work_ref[first:, :]
-            column = jnp.sum(jnp.where(band_col == k, band, 0.0), axis=1, keepdims=True)
             pivot = jnp.sum(jnp.where(lane == k, row, 0.0), axis=1, keepdims=True)
             scale = 1.0 / jnp.sqrt(pivot)
             factor_row = jnp.where(lane >= k, row * scale, 0.0)
-            factor_col = jnp.where(sublane >= k, column * scale, 0.0)
-            work_ref[first:, :] = band - factor_col * factor_row
+            factor_col = jnp.transpose(jnp.broadcast_to(factor_row, (8, size)))[first:, :1]
+            work_ref[first:, :] = work_ref[first:, :] - factor_col * factor_row
             inverse_row = inverse_ref[pl.ds(k, 1), :] * scale
             below = jnp.where(sublane > k, factor_col, 0.0)
             inverse_ref[first:, :] = inverse_ref[first:, :] - below * inverse_row

time: 70.5 us -> 92.9 us (1.32)
  Pallas kernels: 15.2 us -> 37.7 us
    pallas_call x1, Pallas kernels: 15.2 us -> 37.7 us  [combination_transposed_of(): pl.pallas_call(combination_kernel, out_shape=jax.ShapeDtypeStruct((size,...]
where the time goes in v14:
time: 92.9 us; the launch traced here: 92.4 us
  Pallas kernels  37.7 us (41%)
  starting transfers between devices  21.7 us (23%)
  waiting for transfers between devices  16.2 us (17%)
  matrix products  6.76 us (7%)
  local copies, waits for them, and re-layouts  5.02 us (5%)
  other arithmetic  4.04 us (4%)
  between operations  1.04 us (1%)
    pallas_call x1, Pallas kernels, combination_transposed_of(): pl.pallas_call(combination_kernel, out_shape=jax.ShapeDtypeStruct((size,...  37.7 us
    ppermute x5, starting transfers between devices, butterfly_sum(): received[offset] = lax.ppermute(value, axis, pairs)  12.2 us
    ppermute x5, waiting for transfers between devices, butterfly_sum(): received[offset] = lax.ppermute(value, axis, pairs)  11.1 us
    ppermute x4, starting transfers between devices, from_neighbour(): return lax.ppermute(block, axis, pairs)  9.5 us
    ppermute x4, waiting for transfers between devices, from_neighbour(): return lax.ppermute(block, axis, pairs)  5.09 us
    unnamed x14, local copies, waits for them, and re-layouts  4.87 us
    dot_general x1, matrix products, shards(): lax.dot_general(deviation_t * cell_weight[:, :, None], deviation_t, (((0,...  2.7 us
    select_n x1, other arithmetic, forecast_two_steps(): first = jnp.where(outside[:, :, None], 0.0, first)  2.12 us
  transfers between devices with their start and end apart: 9, of which 7 were waited for; matrix products, arithmetic and copies ran while one was open for 1% of the time, Pallas kernels for 0%

profile of v14, /device:TPU:0, one launch (start us, length us, event | category | flops | bytes accessed | tf_op | source)
XLA Modules:
  0.0 92.4 jit_solution(1986877032375791651)
XLA Ops:
  0.6 0.0 copy-start
  0.6 1.7 %copy.14 = f32[128,16,128]{0,2,1:T(8,128)S(1)} copy(f32[128,16,128]{2,1,0:T(8,128)} %param.6) | data formatting | bytes 2097152 | tf_op args[1]
  2.3 0.0 copy-done
  2.3 0.0 copy-start.2
  2.4 0.0 copy-start.3
  2.4 0.0 copy-start.4
  2.4 0.4 copy.13
  2.9 2.4 %collective-permute-start = (f32[128,3,128]{2,0,1:T(8,128)S(1)}, f32[128,3,128]{2,0,1:T(8,128)S(1)}, u32[]{:S(2)}, u32[]{:S(2)}) collective-permute-start(f32[128,3,128]{2,0,1:T(8,128)S(1)} %pad_maximum_fusion.7), channel_id=1, source_target_pairs={{0,4},{4,8},{8,12},{12,16},{16,20},{20,24},{24,28},{1,5},{5,9},{9,... | collective-permute-start | bytes 589832 | tf_op jit(solution)/shard_map/ppermute | solution.py:114
  5.3 1.3 %collective-permute-start.1 = (f32[128,3,128]{2,0,1:T(8,128)S(1)}, f32[128,3,128]{2,0,1:T(8,128)S(1)}, u32[]{:S(2)}, u32[]{:S(2)}) collective-permute-start(f32[128,3,128]{2,0,1:T(8,128)S(1)} %pad_maximum_fusion.8), channel_id=1, source_target_pairs={{4,0},{8,4},{12,8},{16,12},{20,16},{24,20},{28,24},{5,1},{9,5},{13... | collective-permute-start | bytes 589832 | tf_op jit(solution)/shard_map/ppermute | solution.py:114
  6.6 0.0 copy-done.2
  6.6 0.0 copy-done.3
  6.6 0.0 copy-done.4
  6.7 0.4 fusion.27
  7.1 0.0 collective-permute-done
  7.1 3.6 %collective-permute-done.1 = f32[128,3,128]{2,0,1:T(8,128)S(1)} collective-permute-done((f32[128,3,128]{2,0,1:T(8,128)S(1)}, f32[128,3,128]{2,0,1:T(8,128)S(1)}, u32[]{:S(2)}, u32[]{:S(2)}) %collective-permute-start.1) | collective-permute-done | bytes 196640 | tf_op jit(solution)/shard_map/ppermute | solution.py:114
  10.8 1.3 %collective-permute-start.3 = (f32[3,20,128]{2,1,0:T(8,128)S(1)}, f32[3,20,128]{2,1,0:T(8,128)S(1)}, u32[]{:S(2)}, u32[]{:S(2)}) collective-permute-start(f32[3,20,128]{2,1,0:T(8,128)S(1)} %pad_maximum_fusion.11), channel_id=1, source_target_pairs={{1,0},{2,1},{3,2},{5,4},{6,5},{7,6},{9,8},{10,9},{11,10},{13,12},{... | collective-permute-start | bytes 92168 | tf_op jit(solution)/shard_map/ppermute | solution.py:114
  12.2 4.5 %collective-permute-start.2 = (f32[3,20,128]{2,1,0:T(8,128)S(1)}, f32[3,20,128]{2,1,0:T(8,128)S(1)}, u32[]{:S(2)}, u32[]{:S(2)}) collective-permute-start(f32[3,20,128]{2,1,0:T(8,128)S(1)} %pad_maximum_fusion.10), channel_id=1, source_target_pairs={{0,1},{1,2},{2,3},{4,5},{5,6},{6,7},{8,9},{9,10},{10,11},{12,13},{... | collective-permute-start | bytes 92168 | tf_op jit(solution)/shard_map/ppermute | solution.py:114
  16.7 0.1 or_or_fusion
  16.8 0.0 collective-permute-done.3
  16.8 1.5 %collective-permute-done.2 = f32[3,20,128]{2,1,0:T(8,128)S(1)} collective-permute-done((f32[3,20,128]{2,1,0:T(8,128)S(1)}, f32[3,20,128]{2,1,0:T(8,128)S(1)}, u32[]{:S(2)}, u32[]{:S(2)}) %collective-permute-start.2) | collective-permute-done | bytes 30752 | tf_op jit(solution)/shard_map/ppermute | solution.py:114
  18.4 0.1 pad_maximum_fusion
  18.5 2.1 %fusion.9 = f32[130,18,128]{2,0,1:T(8,128)S(1)} fusion(f32[2,20,128]{2,0,1:T(2,128)S(1)} %copy.19, f32[128,2,128]{2,0,1:T(8,128)S(1)} %slice.121, f32[128,16,128]{2,0,1:T(8,128)S(1)} %bitcast.42, f32[128,2,128]{2,0,1:T(8,128)S(1)} %slice.118, f32[2,20,128]{2,0,1:T(2,128)S(1)} %copy.20, f32[132,20,128]{2,0,1:T(8,128)S(1)} %pad_maximum_fusion, ...), kind=kLoop, calls=%fused_computation.13 | loop fusion | flops 5990400 | bytes 7344420 | tf_op jit(solution)/shard_map/jit(_where)/select_n | solution.py:156
  20.7 0.9 fusion.44
  21.6 2.7 %fusion.11 = f32[128,128]{1,0:T(8,128)S(1)} fusion(f32[128,16,128]{2,0,1:T(8,128)S(1)} %get-tuple-element.7, f32[128,16]{0,1:T(8,128)S(1)} %get-tuple-element.17, f32[128,16]{0,1:T(8,128)S(1)} %get-tuple-element.20), kind=kOutput, calls=%fused_computation.22 | convolution fusion | flops 403439616 | bytes 1130496 | tf_op jit(solution)/shard_map/dot_general | solution.py:194
  24.3 0.8 convolution_bitcast_fusion.2
  25.1 3.1 %collective-permute-start.4 = (f32[129,128]{1,0:T(8,128)S(1)}, f32[129,128]{1,0:T(8,128)S(1)}, u32[]{:S(2)}, u32[]{:S(2)}) collective-permute-start(f32[129,128]{1,0:T(8,128)S(1)} %pad_maximum_fusion.9), channel_id=1, source_target_pairs={{0,4},{4,0},{8,12},{12,8},{16,20},{20,16},{24,28},{28,24},{1,5},{5... | collective-permute-start | bytes 198152 | tf_op jit(solution)/shard_map/ppermute | solution.py:38
  28.2 0.9 collective-permute-done.4
  29.1 2.5 %collective-permute-start.5 = (f32[129,128]{1,0:T(8,128)S(1)}, f32[129,128]{1,0:T(8,128)S(1)}, u32[]{:S(2)}, u32[]{:S(2)}) collective-permute-start(f32[129,128]{1,0:T(8,128)S(1)} %fusion.43), channel_id=1, source_target_pairs={{0,8},{4,12},{8,0},{12,4},{16,24},{20,28},{24,16},{28,20},{1,9},{5... | collective-permute-start | bytes 198152 | tf_op jit(solution)/shard_map/ppermute | solution.py:38
  31.5 2.7 %collective-permute-done.5 = f32[129,128]{1,0:T(8,128)S(1)} collective-permute-done((f32[129,128]{1,0:T(8,128)S(1)}, f32[129,128]{1,0:T(8,128)S(1)}, u32[]{:S(2)}, u32[]{:S(2)}) %collective-permute-start.5) | collective-permute-done | bytes 66080 | tf_op jit(solution)/shard_map/ppermute | solution.py:38
  34.3 1.4 %collective-permute-start.6 = (f32[129,128]{1,0:T(8,128)S(1)}, f32[129,128]{1,0:T(8,128)S(1)}, u32[]{:S(2)}, u32[]{:S(2)}) collective-permute-start(f32[129,128]{1,0:T(8,128)S(1)} %add.88), channel_id=1, source_target_pairs={{0,16},{4,20},{8,24},{12,28},{16,0},{20,4},{24,8},{28,12},{1,17},{... | collective-permute-start | bytes 198152 | tf_op jit(solution)/shard_map/ppermute | solution.py:38
  35.7 3.0 %collective-permute-done.6 = f32[129,128]{1,0:T(8,128)S(1)} collective-permute-done((f32[129,128]{1,0:T(8,128)S(1)}, f32[129,128]{1,0:T(8,128)S(1)}, u32[]{:S(2)}, u32[]{:S(2)}) %collective-permute-start.6) | collective-permute-done | bytes 66080 | tf_op jit(solution)/shard_map/ppermute | solution.py:38
  38.6 2.1 %collective-permute-start.7 = (f32[129,128]{1,0:T(8,128)S(1)}, f32[129,128]{1,0:T(8,128)S(1)}, u32[]{:S(2)}, u32[]{:S(2)}) collective-permute-start(f32[129,128]{1,0:T(8,128)S(1)} %add.89), channel_id=1, source_target_pairs={{0,1},{1,0},{2,3},{3,2},{4,5},{5,4},{6,7},{7,6},{8,9},{9,8},{10,11... | collective-permute-start | bytes 198152 | tf_op jit(solution)/shard_map/ppermute | solution.py:38
  40.7 2.3 %collective-permute-done.7 = f32[129,128]{1,0:T(8,128)S(1)} collective-permute-done((f32[129,128]{1,0:T(8,128)S(1)}, f32[129,128]{1,0:T(8,128)S(1)}, u32[]{:S(2)}, u32[]{:S(2)}) %collective-permute-start.7) | collective-permute-done | bytes 66080 | tf_op jit(solution)/shard_map/ppermute | solution.py:38
  43.0 3.1 %collective-permute-start.8 = (f32[129,128]{1,0:T(8,128)S(1)}, f32[129,128]{1,0:T(8,128)S(1)}, u32[]{:S(2)}, u32[]{:S(2)}) collective-permute-start(f32[129,128]{1,0:T(8,128)S(1)} %add.90), channel_id=1, source_target_pairs={{0,2},{1,3},{2,0},{3,1},{4,6},{5,7},{6,4},{7,5},{8,10},{9,11},{10,... | collective-permute-start | bytes 198152 | tf_op jit(solution)/shard_map/ppermute | solution.py:38
  46.1 2.3 %collective-permute-done.8 = f32[129,128]{1,0:T(8,128)S(1)} collective-permute-done((f32[129,128]{1,0:T(8,128)S(1)}, f32[129,128]{1,0:T(8,128)S(1)}, u32[]{:S(2)}, u32[]{:S(2)}) %collective-permute-start.8) | collective-permute-done | bytes 66080 | tf_op jit(solution)/shard_map/ppermute | solution.py:38
  48.4 0.6 add.91.stacked_ref
  49.1 37.7 %shard_map.68 = f32[128,128]{1,0:T(8,128)} custom-call(f32[129,128]{1,0:T(8,128)} %add.91.stacked_ref), custom_call_target="tpu_custom_call" | custom-call | tf_op jit(solution)/shard_map/pallas_call | solution.py:78
  86.8 1.9 %fusion.2 = f32[128,16,128]{0,2,1:T(8,128)S(1)} fusion(f32[128,16]{0,1:T(8,128)S(1)} %get-tuple-element.22, f32[16,128]{1,0:T(8,128)S(1)} %get-tuple-element.21, f32[128,128]{1,0:T(8,128)} %shard_map.68, f32[128,16,128]{0,2,1:T(8,128)S(1)} %copy.14), kind=kOutput, calls=%fused_computation.4 | convolution fusion | flops 403177472 | bytes 2179072 | tf_op jit(solution)/shard_map/dot_general | solution.py:213
  88.6 0.0 copy-start.1
  88.6 1.4 %copy.27 = f32[128,16,128]{2,1,0:T(8,128)} copy(f32[128,16,128]{0,2,1:T(8,128)S(1)} %fusion.2) | data formatting | bytes 2097152
  90.0 0.0 copy-done.1
  90.0 1.0 %fusion.3 = f32[128,16,128]{0,2,1:T(8,128)S(1)} fusion(f32[128,16,128]{2,0,1:T(8,128)S(1)} %get-tuple-element.7, f32[128,16]{0,1:T(8,128)S(1)} %get-tuple-element.20, f32[16,128]{1,0:T(8,128)S(1)} %get-tuple-element.19, f32[128,128]{1,0:T(8,128)S(1)} %copy-done.1), kind=kOutput, calls=%fused_computation.6 | convolution fusion | flops 403177472 | bytes 2179072 | tf_op jit(solution)/shard_map/dot_general | solution.py:210
  91.1 1.4 %copy.26 = f32[128,16,128]{2,1,0:T(8,128)} copy(f32[128,16,128]{0,2,1:T(8,128)S(1)} %fusion.3) | data formatting | bytes 2097152
  (37 shorter events, 0.4 us)
Async XLA Ops:
  0.6 1.7 %copy-start = (f32[128,16,128]{2,1,0:T(8,128)S(1)}, f32[128,16,128]{2,1,0:T(8,128)}, u32[]{:S(2)}) copy-start(f32[128,16,128]{2,1,0:T(8,128)} %param.5) | copy-start | bytes 3145732
  2.3 4.2 %copy-start.2 = (s32[1024]{0:T(1024)S(1)}, s32[1024]{0:T(1024)}, u32[]{:S(2)}) copy-start(s32[1024]{0:T(1024)} %param.9) | copy-start | bytes 12292
  2.4 4.3 %copy-start.3 = (f32[1024]{0:T(1024)S(1)}, f32[1024]{0:T(1024)}, u32[]{:S(2)}) copy-start(f32[1024]{0:T(1024)} %param.8) | copy-start | bytes 12292
  2.4 4.3 %copy-start.4 = (f32[1024]{0:T(1024)S(1)}, f32[1024]{0:T(1024)}, u32[]{:S(2)}) copy-start(f32[1024]{0:T(1024)} %param.7) | copy-start | bytes 12292
  2.9 4.2 %collective-permute-start = (f32[128,3,128]{2,0,1:T(8,128)S(1)}, f32[128,3,128]{2,0,1:T(8,128)S(1)}, u32[]{:S(2)}, u32[]{:S(2)}) collective-permute-start(f32[128,3,128]{2,0,1:T(8,128)S(1)} %pad_maximum_fusion.7), channel_id=1, source_target_pairs={{0,4},{4,8},{8,12},{12,16},{16,20},{20,24},{24,28},{1,5},{5,9},{9,... | collective-permute-start | bytes 589832 | tf_op jit(solution)/shard_map/ppermute | solution.py:114
  5.3 5.4 %collective-permute-start.1 = (f32[128,3,128]{2,0,1:T(8,128)S(1)}, f32[128,3,128]{2,0,1:T(8,128)S(1)}, u32[]{:S(2)}, u32[]{:S(2)}) collective-permute-start(f32[128,3,128]{2,0,1:T(8,128)S(1)} %pad_maximum_fusion.8), channel_id=1, source_target_pairs={{4,0},{8,4},{12,8},{16,12},{20,16},{24,20},{28,24},{5,1},{9,5},{13... | collective-permute-start | bytes 589832 | tf_op jit(solution)/shard_map/ppermute | solution.py:114
  10.8 6.0 %collective-permute-start.3 = (f32[3,20,128]{2,1,0:T(8,128)S(1)}, f32[3,20,128]{2,1,0:T(8,128)S(1)}, u32[]{:S(2)}, u32[]{:S(2)}) collective-permute-start(f32[3,20,128]{2,1,0:T(8,128)S(1)} %pad_maximum_fusion.11), channel_id=1, source_target_pairs={{1,0},{2,1},{3,2},{5,4},{6,5},{7,6},{9,8},{10,9},{11,10},{13,12},{... | collective-permute-start | bytes 92168 | tf_op jit(solution)/shard_map/ppermute | solution.py:114
  12.2 6.2 %collective-permute-start.2 = (f32[3,20,128]{2,1,0:T(8,128)S(1)}, f32[3,20,128]{2,1,0:T(8,128)S(1)}, u32[]{:S(2)}, u32[]{:S(2)}) collective-permute-start(f32[3,20,128]{2,1,0:T(8,128)S(1)} %pad_maximum_fusion.10), channel_id=1, source_target_pairs={{0,1},{1,2},{2,3},{4,5},{5,6},{6,7},{8,9},{9,10},{10,11},{12,13},{... | collective-permute-start | bytes 92168 | tf_op jit(solution)/shard_map/ppermute | solution.py:114
  25.1 4.0 %collective-permute-start.4 = (f32[129,128]{1,0:T(8,128)S(1)}, f32[129,128]{1,0:T(8,128)S(1)}, u32[]{:S(2)}, u32[]{:S(2)}) collective-permute-start(f32[129,128]{1,0:T(8,128)S(1)} %pad_maximum_fusion.9), channel_id=1, source_target_pairs={{0,4},{4,0},{8,12},{12,8},{16,20},{20,16},{24,28},{28,24},{1,5},{5... | collective-permute-start | bytes 198152 | tf_op jit(solution)/shard_map/ppermute | solution.py:38
  29.1 5.2 %collective-permute-start.5 = (f32[129,128]{1,0:T(8,128)S(1)}, f32[129,128]{1,0:T(8,128)S(1)}, u32[]{:S(2)}, u32[]{:S(2)}) collective-permute-start(f32[129,128]{1,0:T(8,128)S(1)} %fusion.43), channel_id=1, source_target_pairs={{0,8},{4,12},{8,0},{12,4},{16,24},{20,28},{24,16},{28,20},{1,9},{5... | collective-permute-start | bytes 198152 | tf_op jit(solution)/shard_map/ppermute | solution.py:38
  34.3 4.4 %collective-permute-start.6 = (f32[129,128]{1,0:T(8,128)S(1)}, f32[129,128]{1,0:T(8,128)S(1)}, u32[]{:S(2)}, u32[]{:S(2)}) collective-permute-start(f32[129,128]{1,0:T(8,128)S(1)} %add.88), channel_id=1, source_target_pairs={{0,16},{4,20},{8,24},{12,28},{16,0},{20,4},{24,8},{28,12},{1,17},{... | collective-permute-start | bytes 198152 | tf_op jit(solution)/shard_map/ppermute | solution.py:38
  38.6 4.4 %collective-permute-start.7 = (f32[129,128]{1,0:T(8,128)S(1)}, f32[129,128]{1,0:T(8,128)S(1)}, u32[]{:S(2)}, u32[]{:S(2)}) collective-permute-start(f32[129,128]{1,0:T(8,128)S(1)} %add.89), channel_id=1, source_target_pairs={{0,1},{1,0},{2,3},{3,2},{4,5},{5,4},{6,7},{7,6},{8,9},{9,8},{10,11... | collective-permute-start | bytes 198152 | tf_op jit(solution)/shard_map/ppermute | solution.py:38
  43.0 5.4 %collective-permute-start.8 = (f32[129,128]{1,0:T(8,128)S(1)}, f32[129,128]{1,0:T(8,128)S(1)}, u32[]{:S(2)}, u32[]{:S(2)}) collective-permute-start(f32[129,128]{1,0:T(8,128)S(1)} %add.90), channel_id=1, source_target_pairs={{0,2},{1,3},{2,0},{3,1},{4,6},{5,7},{6,4},{7,5},{8,10},{9,11},{10,... | collective-permute-start | bytes 198152 | tf_op jit(solution)/shard_map/ppermute | solution.py:38
  88.6 1.4 %copy-start.1 = (f32[128,128]{1,0:T(8,128)S(1)}, f32[128,128]{1,0:T(8,128)}, u32[]{:S(2)}) copy-start(f32[128,128]{1,0:T(8,128)} %shard_map.68) | copy-start | bytes 196612

commit v15 on v12

--- a/solution.py
+++ b/solution.py
@@ -211,10 +211,10 @@
     )
     contract = (((2,), (1,)), ((), ()))
     updated_t = average_t[:, :, None] + lax.dot_general(
-        deviation_t, combination_transposed, contract, precision=lax.Precision.HIGHEST
+        deviation_t, combination_transposed, contract, precision=lax.Precision.HIGH
     )
     heat_out_t = mean_heat_t[:, :, None] + lax.dot_general(
-        heat_anomaly_t, combination_transposed, contract, precision=lax.Precision.HIGHEST
+        heat_anomaly_t, combination_transposed, contract, precision=lax.Precision.HIGH
     )
     return (jnp.transpose(updated_t, (2, 1, 0)), jnp.transpose(heat_out_t, (2, 1, 0)))
 

time: 70.5 us -> 69.9 us (level)
  no operation moved by 1% of the time
where the time goes in v15:
time: 69.9 us; the launch traced here: 69.4 us
  starting transfers between devices  21.7 us (31%)
  waiting for transfers between devices  16.2 us (23%)
  Pallas kernels  15 us (21%)
  matrix products  6.42 us (9%)
  local copies, waits for them, and re-layouts  5.02 us (7%)
  other arithmetic  4.04 us (6%)
  between operations  1.04 us (1%)
    pallas_call x1, Pallas kernels, combination_transposed_of(): pl.pallas_call(combination_kernel, out_shape=jax.ShapeDtypeStruct((size,...  15 us
    ppermute x5, starting transfers between devices, butterfly_sum(): received[offset] = lax.ppermute(value, axis, pairs)  12.1 us
    ppermute x5, waiting for transfers between devices, butterfly_sum(): received[offset] = lax.ppermute(value, axis, pairs)  11.1 us
    ppermute x4, starting transfers between devices, from_neighbour(): return lax.ppermute(block, axis, pairs)  9.5 us
    ppermute x4, waiting for transfers between devices, from_neighbour(): return lax.ppermute(block, axis, pairs)  5.09 us
    unnamed x14, local copies, waits for them, and re-layouts  4.87 us
    dot_general x1, matrix products, shards(): lax.dot_general(deviation_t * cell_weight[:, :, None], deviation_t, (((0,...  2.7 us
    select_n x1, other arithmetic, forecast_two_steps(): first = jnp.where(outside[:, :, None], 0.0, first)  2.12 us
  transfers between devices with their start and end apart: 9, of which 7 were waited for; matrix products, arithmetic and copies ran while one was open for 1% of the time, Pallas kernels for 0%

profile of v15, /device:TPU:0, one launch (start us, length us, event | category | flops | bytes accessed | tf_op | source)
XLA Modules:
  0.0 69.4 jit_solution(6110175371957223097)
XLA Ops:
  0.6 0.0 copy-start
  0.6 1.7 %copy.14 = f32[128,16,128]{0,2,1:T(8,128)S(1)} copy(f32[128,16,128]{2,1,0:T(8,128)} %param.6) | data formatting | bytes 2097152 | tf_op args[1]
  2.3 0.0 copy-done
  2.3 0.0 copy-start.2
  2.4 0.0 copy-start.3
  2.4 0.0 copy-start.4
  2.4 0.4 copy.13
  2.9 2.4 %collective-permute-start = (f32[128,3,128]{2,0,1:T(8,128)S(1)}, f32[128,3,128]{2,0,1:T(8,128)S(1)}, u32[]{:S(2)}, u32[]{:S(2)}) collective-permute-start(f32[128,3,128]{2,0,1:T(8,128)S(1)} %pad_maximum_fusion.7), channel_id=1, source_target_pairs={{0,4},{4,8},{8,12},{12,16},{16,20},{20,24},{24,28},{1,5},{5,9},{9,... | collective-permute-start | bytes 589832 | tf_op jit(solution)/shard_map/ppermute | solution.py:117
  5.3 1.3 %collective-permute-start.1 = (f32[128,3,128]{2,0,1:T(8,128)S(1)}, f32[128,3,128]{2,0,1:T(8,128)S(1)}, u32[]{:S(2)}, u32[]{:S(2)}) collective-permute-start(f32[128,3,128]{2,0,1:T(8,128)S(1)} %pad_maximum_fusion.8), channel_id=1, source_target_pairs={{4,0},{8,4},{12,8},{16,12},{20,16},{24,20},{28,24},{5,1},{9,5},{13... | collective-permute-start | bytes 589832 | tf_op jit(solution)/shard_map/ppermute | solution.py:117
  6.6 0.0 copy-done.2
  6.6 0.0 copy-done.3
  6.6 0.0 copy-done.4
  6.7 0.4 fusion.27
  7.1 0.0 collective-permute-done
  7.1 3.6 %collective-permute-done.1 = f32[128,3,128]{2,0,1:T(8,128)S(1)} collective-permute-done((f32[128,3,128]{2,0,1:T(8,128)S(1)}, f32[128,3,128]{2,0,1:T(8,128)S(1)}, u32[]{:S(2)}, u32[]{:S(2)}) %collective-permute-start.1) | collective-permute-done | bytes 196640 | tf_op jit(solution)/shard_map/ppermute | solution.py:117
  10.8 1.3 %collective-permute-start.3 = (f32[3,20,128]{2,1,0:T(8,128)S(1)}, f32[3,20,128]{2,1,0:T(8,128)S(1)}, u32[]{:S(2)}, u32[]{:S(2)}) collective-permute-start(f32[3,20,128]{2,1,0:T(8,128)S(1)} %pad_maximum_fusion.11), channel_id=1, source_target_pairs={{1,0},{2,1},{3,2},{5,4},{6,5},{7,6},{9,8},{10,9},{11,10},{13,12},{... | collective-permute-start | bytes 92168 | tf_op jit(solution)/shard_map/ppermute | solution.py:117
  12.2 4.5 %collective-permute-start.2 = (f32[3,20,128]{2,1,0:T(8,128)S(1)}, f32[3,20,128]{2,1,0:T(8,128)S(1)}, u32[]{:S(2)}, u32[]{:S(2)}) collective-permute-start(f32[3,20,128]{2,1,0:T(8,128)S(1)} %pad_maximum_fusion.10), channel_id=1, source_target_pairs={{0,1},{1,2},{2,3},{4,5},{5,6},{6,7},{8,9},{9,10},{10,11},{12,13},{... | collective-permute-start | bytes 92168 | tf_op jit(solution)/shard_map/ppermute | solution.py:117
  16.7 0.1 or_or_fusion
  16.8 0.0 collective-permute-done.3
  16.8 1.5 %collective-permute-done.2 = f32[3,20,128]{2,1,0:T(8,128)S(1)} collective-permute-done((f32[3,20,128]{2,1,0:T(8,128)S(1)}, f32[3,20,128]{2,1,0:T(8,128)S(1)}, u32[]{:S(2)}, u32[]{:S(2)}) %collective-permute-start.2) | collective-permute-done | bytes 30752 | tf_op jit(solution)/shard_map/ppermute | solution.py:117
  18.4 0.1 pad_maximum_fusion
  18.5 2.1 %fusion.9 = f32[130,18,128]{2,0,1:T(8,128)S(1)} fusion(f32[2,20,128]{2,0,1:T(2,128)S(1)} %copy.19, f32[128,2,128]{2,0,1:T(8,128)S(1)} %slice.121, f32[128,16,128]{2,0,1:T(8,128)S(1)} %bitcast.42, f32[128,2,128]{2,0,1:T(8,128)S(1)} %slice.118, f32[2,20,128]{2,0,1:T(2,128)S(1)} %copy.20, f32[132,20,128]{2,0,1:T(8,128)S(1)} %pad_maximum_fusion, ...), kind=kLoop, calls=%fused_computation.13 | loop fusion | flops 5990400 | bytes 7344420 | tf_op jit(solution)/shard_map/jit(_where)/select_n | solution.py:159
  20.7 0.9 %fusion.44 = (f32[128,16]{0,1:T(8,128)S(1)}, f32[128,16,128]{2,0,1:T(8,128)S(1)}, f32[128,16]{0,1:T(8,128)S(1)}) fusion(f32[128,16,128]{0,2,1:T(8,128)S(1)} %copy.14, f32[130,18,128]{2,0,1:T(8,128)S(1)} %fusion.9), kind=kLoop, calls=%fused_computation.90 | loop fusion | flops 2879488 | bytes 7356416 | tf_op jit(solution)/shard_map/reduce_sum | solution.py:174
  21.6 2.7 %fusion.11 = f32[128,128]{1,0:T(8,128)S(1)} fusion(f32[128,16,128]{2,0,1:T(8,128)S(1)} %get-tuple-element.7, f32[128,16]{0,1:T(8,128)S(1)} %get-tuple-element.17, f32[128,16]{0,1:T(8,128)S(1)} %get-tuple-element.20), kind=kOutput, calls=%fused_computation.22 | convolution fusion | flops 403439616 | bytes 1130496 | tf_op jit(solution)/shard_map/dot_general | solution.py:197
  24.3 0.8 %convolution_bitcast_fusion.2 = f32[1,128]{1,0:T(1,128)S(1)} fusion(f32[128,16,1]{0,2,1:T(1,128)S(1)} %bitcast.43, f32[128,16,128]{2,0,1:T(8,128)S(1)} %get-tuple-element.7, f32[128,16]{0,1:T(8,128)S(1)} %get-tuple-element.20), kind=kOutput, calls=%fused_computation.23 | convolution fusion | flops 3407872 | bytes 1065472 | tf_op jit(solution)/shard_map/dot_general | solution.py:203
  25.1 3.1 %collective-permute-start.4 = (f32[129,128]{1,0:T(8,128)S(1)}, f32[129,128]{1,0:T(8,128)S(1)}, u32[]{:S(2)}, u32[]{:S(2)}) collective-permute-start(f32[129,128]{1,0:T(8,128)S(1)} %pad_maximum_fusion.9), channel_id=1, source_target_pairs={{0,4},{4,0},{8,12},{12,8},{16,20},{20,16},{24,28},{28,24},{1,5},{5... | collective-permute-start | bytes 198152 | tf_op jit(solution)/shard_map/ppermute | solution.py:38
  28.2 0.9 %collective-permute-done.4 = f32[129,128]{1,0:T(8,128)S(1)} collective-permute-done((f32[129,128]{1,0:T(8,128)S(1)}, f32[129,128]{1,0:T(8,128)S(1)}, u32[]{:S(2)}, u32[]{:S(2)}) %collective-permute-start.4) | collective-permute-done | bytes 66080 | tf_op jit(solution)/shard_map/ppermute | solution.py:38
  29.1 2.5 %collective-permute-start.5 = (f32[129,128]{1,0:T(8,128)S(1)}, f32[129,128]{1,0:T(8,128)S(1)}, u32[]{:S(2)}, u32[]{:S(2)}) collective-permute-start(f32[129,128]{1,0:T(8,128)S(1)} %fusion.43), channel_id=1, source_target_pairs={{0,8},{4,12},{8,0},{12,4},{16,24},{20,28},{24,16},{28,20},{1,9},{5... | collective-permute-start | bytes 198152 | tf_op jit(solution)/shard_map/ppermute | solution.py:38
  31.5 2.7 %collective-permute-done.5 = f32[129,128]{1,0:T(8,128)S(1)} collective-permute-done((f32[129,128]{1,0:T(8,128)S(1)}, f32[129,128]{1,0:T(8,128)S(1)}, u32[]{:S(2)}, u32[]{:S(2)}) %collective-permute-start.5) | collective-permute-done | bytes 66080 | tf_op jit(solution)/shard_map/ppermute | solution.py:38
  34.3 1.4 %collective-permute-start.6 = (f32[129,128]{1,0:T(8,128)S(1)}, f32[129,128]{1,0:T(8,128)S(1)}, u32[]{:S(2)}, u32[]{:S(2)}) collective-permute-start(f32[129,128]{1,0:T(8,128)S(1)} %add.88), channel_id=1, source_target_pairs={{0,16},{4,20},{8,24},{12,28},{16,0},{20,4},{24,8},{28,12},{1,17},{... | collective-permute-start | bytes 198152 | tf_op jit(solution)/shard_map/ppermute | solution.py:38
  35.7 3.0 %collective-permute-done.6 = f32[129,128]{1,0:T(8,128)S(1)} collective-permute-done((f32[129,128]{1,0:T(8,128)S(1)}, f32[129,128]{1,0:T(8,128)S(1)}, u32[]{:S(2)}, u32[]{:S(2)}) %collective-permute-start.6) | collective-permute-done | bytes 66080 | tf_op jit(solution)/shard_map/ppermute | solution.py:38
  38.6 2.1 %collective-permute-start.7 = (f32[129,128]{1,0:T(8,128)S(1)}, f32[129,128]{1,0:T(8,128)S(1)}, u32[]{:S(2)}, u32[]{:S(2)}) collective-permute-start(f32[129,128]{1,0:T(8,128)S(1)} %add.89), channel_id=1, source_target_pairs={{0,1},{1,0},{2,3},{3,2},{4,5},{5,4},{6,7},{7,6},{8,9},{9,8},{10,11... | collective-permute-start | bytes 198152 | tf_op jit(solution)/shard_map/ppermute | solution.py:38
  40.7 2.3 %collective-permute-done.7 = f32[129,128]{1,0:T(8,128)S(1)} collective-permute-done((f32[129,128]{1,0:T(8,128)S(1)}, f32[129,128]{1,0:T(8,128)S(1)}, u32[]{:S(2)}, u32[]{:S(2)}) %collective-permute-start.7) | collective-permute-done | bytes 66080 | tf_op jit(solution)/shard_map/ppermute | solution.py:38
  43.0 3.1 %collective-permute-start.8 = (f32[129,128]{1,0:T(8,128)S(1)}, f32[129,128]{1,0:T(8,128)S(1)}, u32[]{:S(2)}, u32[]{:S(2)}) collective-permute-start(f32[129,128]{1,0:T(8,128)S(1)} %add.90), channel_id=1, source_target_pairs={{0,2},{1,3},{2,0},{3,1},{4,6},{5,7},{6,4},{7,5},{8,10},{9,11},{10,... | collective-permute-start | bytes 198152 | tf_op jit(solution)/shard_map/ppermute | solution.py:38
  46.1 2.3 %collective-permute-done.8 = f32[129,128]{1,0:T(8,128)S(1)} collective-permute-done((f32[129,128]{1,0:T(8,128)S(1)}, f32[129,128]{1,0:T(8,128)S(1)}, u32[]{:S(2)}, u32[]{:S(2)}) %collective-permute-start.8) | collective-permute-done | bytes 66080 | tf_op jit(solution)/shard_map/ppermute | solution.py:38
  48.4 0.6 add.91.stacked_ref
  49.1 15.0 %shard_map.68 = f32[128,128]{1,0:T(8,128)} custom-call(f32[129,128]{1,0:T(8,128)} %add.91.stacked_ref), custom_call_target="tpu_custom_call" | custom-call | tf_op jit(solution)/shard_map/pallas_call | solution.py:81
  64.1 1.6 %fusion.2 = f32[128,16,128]{0,2,1:T(8,128)S(1)} fusion(f32[128,16]{0,1:T(8,128)S(1)} %get-tuple-element.22, f32[16,128]{1,0:T(8,128)S(1)} %get-tuple-element.21, f32[128,128]{1,0:T(8,128)} %shard_map.68, f32[128,16,128]{0,2,1:T(8,128)S(1)} %copy.14), kind=kOutput, calls=%fused_computation.4 | convolution fusion | flops 201850880 | bytes 2179072 | tf_op jit(solution)/shard_map/dot_general | solution.py:216
  65.7 0.0 copy-start.1
  65.7 1.4 %copy.27 = f32[128,16,128]{2,1,0:T(8,128)} copy(f32[128,16,128]{0,2,1:T(8,128)S(1)} %fusion.2) | data formatting | bytes 2097152
  67.1 0.0 copy-done.1
  67.1 1.0 %fusion.3 = f32[128,16,128]{0,2,1:T(8,128)S(1)} fusion(f32[128,16,128]{2,0,1:T(8,128)S(1)} %get-tuple-element.7, f32[128,16]{0,1:T(8,128)S(1)} %get-tuple-element.20, f32[16,128]{1,0:T(8,128)S(1)} %get-tuple-element.19, f32[128,128]{1,0:T(8,128)S(1)} %copy-done.1), kind=kOutput, calls=%fused_computation.6 | convolution fusion | flops 201850880 | bytes 2179072 | tf_op jit(solution)/shard_map/dot_general | solution.py:213
  68.1 1.4 %copy.26 = f32[128,16,128]{2,1,0:T(8,128)} copy(f32[128,16,128]{0,2,1:T(8,128)S(1)} %fusion.3) | data formatting | bytes 2097152
  (37 shorter events, 0.4 us)
Async XLA Ops:
  0.6 1.7 %copy-start = (f32[128,16,128]{2,1,0:T(8,128)S(1)}, f32[128,16,128]{2,1,0:T(8,128)}, u32[]{:S(2)}) copy-start(f32[128,16,128]{2,1,0:T(8,128)} %param.5) | copy-start | bytes 3145732
  2.3 4.2 %copy-start.2 = (s32[1024]{0:T(1024)S(1)}, s32[1024]{0:T(1024)}, u32[]{:S(2)}) copy-start(s32[1024]{0:T(1024)} %param.9) | copy-start | bytes 12292
  2.4 4.3 %copy-start.3 = (f32[1024]{0:T(1024)S(1)}, f32[1024]{0:T(1024)}, u32[]{:S(2)}) copy-start(f32[1024]{0:T(1024)} %param.8) | copy-start | bytes 12292
  2.4 4.3 %copy-start.4 = (f32[1024]{0:T(1024)S(1)}, f32[1024]{0:T(1024)}, u32[]{:S(2)}) copy-start(f32[1024]{0:T(1024)} %param.7) | copy-start | bytes 12292
  2.9 4.2 %collective-permute-start = (f32[128,3,128]{2,0,1:T(8,128)S(1)}, f32[128,3,128]{2,0,1:T(8,128)S(1)}, u32[]{:S(2)}, u32[]{:S(2)}) collective-permute-start(f32[128,3,128]{2,0,1:T(8,128)S(1)} %pad_maximum_fusion.7), channel_id=1, source_target_pairs={{0,4},{4,8},{8,12},{12,16},{16,20},{20,24},{24,28},{1,5},{5,9},{9,... | collective-permute-start | bytes 589832 | tf_op jit(solution)/shard_map/ppermute | solution.py:117
  5.3 5.4 %collective-permute-start.1 = (f32[128,3,128]{2,0,1:T(8,128)S(1)}, f32[128,3,128]{2,0,1:T(8,128)S(1)}, u32[]{:S(2)}, u32[]{:S(2)}) collective-permute-start(f32[128,3,128]{2,0,1:T(8,128)S(1)} %pad_maximum_fusion.8), channel_id=1, source_target_pairs={{4,0},{8,4},{12,8},{16,12},{20,16},{24,20},{28,24},{5,1},{9,5},{13... | collective-permute-start | bytes 589832 | tf_op jit(solution)/shard_map/ppermute | solution.py:117
  10.8 6.0 %collective-permute-start.3 = (f32[3,20,128]{2,1,0:T(8,128)S(1)}, f32[3,20,128]{2,1,0:T(8,128)S(1)}, u32[]{:S(2)}, u32[]{:S(2)}) collective-permute-start(f32[3,20,128]{2,1,0:T(8,128)S(1)} %pad_maximum_fusion.11), channel_id=1, source_target_pairs={{1,0},{2,1},{3,2},{5,4},{6,5},{7,6},{9,8},{10,9},{11,10},{13,12},{... | collective-permute-start | bytes 92168 | tf_op jit(solution)/shard_map/ppermute | solution.py:117
  12.2 6.2 %collective-permute-start.2 = (f32[3,20,128]{2,1,0:T(8,128)S(1)}, f32[3,20,128]{2,1,0:T(8,128)S(1)}, u32[]{:S(2)}, u32[]{:S(2)}) collective-permute-start(f32[3,20,128]{2,1,0:T(8,128)S(1)} %pad_maximum_fusion.10), channel_id=1, source_target_pairs={{0,1},{1,2},{2,3},{4,5},{5,6},{6,7},{8,9},{9,10},{10,11},{12,13},{... | collective-permute-start | bytes 92168 | tf_op jit(solution)/shard_map/ppermute | solution.py:117
  25.1 4.0 %collective-permute-start.4 = (f32[129,128]{1,0:T(8,128)S(1)}, f32[129,128]{1,0:T(8,128)S(1)}, u32[]{:S(2)}, u32[]{:S(2)}) collective-permute-start(f32[129,128]{1,0:T(8,128)S(1)} %pad_maximum_fusion.9), channel_id=1, source_target_pairs={{0,4},{4,0},{8,12},{12,8},{16,20},{20,16},{24,28},{28,24},{1,5},{5... | collective-permute-start | bytes 198152 | tf_op jit(solution)/shard_map/ppermute | solution.py:38
  29.1 5.2 %collective-permute-start.5 = (f32[129,128]{1,0:T(8,128)S(1)}, f32[129,128]{1,0:T(8,128)S(1)}, u32[]{:S(2)}, u32[]{:S(2)}) collective-permute-start(f32[129,128]{1,0:T(8,128)S(1)} %fusion.43), channel_id=1, source_target_pairs={{0,8},{4,12},{8,0},{12,4},{16,24},{20,28},{24,16},{28,20},{1,9},{5... | collective-permute-start | bytes 198152 | tf_op jit(solution)/shard_map/ppermute | solution.py:38
  34.3 4.4 %collective-permute-start.6 = (f32[129,128]{1,0:T(8,128)S(1)}, f32[129,128]{1,0:T(8,128)S(1)}, u32[]{:S(2)}, u32[]{:S(2)}) collective-permute-start(f32[129,128]{1,0:T(8,128)S(1)} %add.88), channel_id=1, source_target_pairs={{0,16},{4,20},{8,24},{12,28},{16,0},{20,4},{24,8},{28,12},{1,17},{... | collective-permute-start | bytes 198152 | tf_op jit(solution)/shard_map/ppermute | solution.py:38
  38.6 4.4 %collective-permute-start.7 = (f32[129,128]{1,0:T(8,128)S(1)}, f32[129,128]{1,0:T(8,128)S(1)}, u32[]{:S(2)}, u32[]{:S(2)}) collective-permute-start(f32[129,128]{1,0:T(8,128)S(1)} %add.89), channel_id=1, source_target_pairs={{0,1},{1,0},{2,3},{3,2},{4,5},{5,4},{6,7},{7,6},{8,9},{9,8},{10,11... | collective-permute-start | bytes 198152 | tf_op jit(solution)/shard_map/ppermute | solution.py:38
  43.0 5.4 %collective-permute-start.8 = (f32[129,128]{1,0:T(8,128)S(1)}, f32[129,128]{1,0:T(8,128)S(1)}, u32[]{:S(2)}, u32[]{:S(2)}) collective-permute-start(f32[129,128]{1,0:T(8,128)S(1)} %add.90), channel_id=1, source_target_pairs={{0,2},{1,3},{2,0},{3,1},{4,6},{5,7},{6,4},{7,5},{8,10},{9,11},{10,... | collective-permute-start | bytes 198152 | tf_op jit(solution)/shard_map/ppermute | solution.py:38
  65.7 1.4 %copy-start.1 = (f32[128,128]{1,0:T(8,128)S(1)}, f32[128,128]{1,0:T(8,128)}, u32[]{:S(2)}) copy-start(f32[128,128]{1,0:T(8,128)} %shard_map.68) | copy-start | bytes 196612

commit v16 on v12

--- a/solution.py
+++ b/solution.py
@@ -48,27 +48,44 @@
     work_ref[...] = stacked_ref[:size, :] + unit
     inverse_ref[...] = unit
     lane = lax.broadcasted_iota(jnp.int32, (1, size), 1)
+
+    def pick(vector, where_true, axis):
+        return jnp.sum(jnp.where(where_true, vector, 0.0), axis=axis, keepdims=True)
+
     for first in range(0, size, 8):
         span = size - first
         sublane = lax.broadcasted_iota(jnp.int32, (span, 1), 0) + first
         band_col = lax.broadcasted_iota(jnp.int32, (span, size), 1)
 
-        def step(k, carry, first=first, sublane=sublane, band_col=band_col):
-            row = work_ref[pl.ds(k, 1), :]
+        def step(pair, carry, first=first, sublane=sublane, band_col=band_col):
+            k = 2 * pair
+            row0 = work_ref[pl.ds(k, 1), :]
+            row1 = work_ref[pl.ds(k + 1, 1), :]
             band = work_ref[first:, :]
-            column = jnp.sum(jnp.where(band_col == k, band, 0.0), axis=1, keepdims=True)
-            pivot = jnp.sum(jnp.where(lane == k, row, 0.0), axis=1, keepdims=True)
-            scale = 1.0 / jnp.sqrt(pivot)
-            factor_row = jnp.where(lane >= k, row * scale, 0.0)
-            factor_col = jnp.where(sublane >= k, column * scale, 0.0)
-            work_ref[first:, :] = band - factor_col * factor_row
-            inverse_row = inverse_ref[pl.ds(k, 1), :] * scale
-            below = jnp.where(sublane > k, factor_col, 0.0)
-            inverse_ref[first:, :] = inverse_ref[first:, :] - below * inverse_row
-            inverse_ref[pl.ds(k, 1), :] = inverse_row
+            col0 = pick(band, band_col == k, 1)
+            col1 = pick(band, band_col == k + 1, 1)
+            scale0 = 1.0 / jnp.sqrt(pick(row0, lane == k, 1))
+            coupling = pick(row0, lane == k + 1, 1) * scale0
+            scale1 = 1.0 / jnp.sqrt(pick(row1, lane == k + 1, 1) - coupling * coupling)
+            factor_row0 = jnp.where(lane >= k, row0 * scale0, 0.0)
+            factor_row1 = jnp.where(lane >= k + 1, (row1 - coupling * factor_row0) * scale1, 0.0)
+            factor_col0 = jnp.where(sublane >= k, col0 * scale0, 0.0)
+            factor_col1 = jnp.where(
+                sublane >= k + 1, (col1 - factor_col0 * coupling) * scale1, 0.0
+            )
+            work_ref[first:, :] = band - factor_col0 * factor_row0 - factor_col1 * factor_row1
+            inverse_row0 = inverse_ref[pl.ds(k, 1), :] * scale0
+            inverse_row1 = (inverse_ref[pl.ds(k + 1, 1), :] - coupling * inverse_row0) * scale1
+            below0 = jnp.where(sublane > k + 1, factor_col0, 0.0)
+            below1 = jnp.where(sublane > k + 1, factor_col1, 0.0)
+            inverse_ref[first:, :] = (
+                inverse_ref[first:, :] - below0 * inverse_row0 - below1 * inverse_row1
+            )
+            inverse_ref[pl.ds(k, 1), :] = inverse_row0
+            inverse_ref[pl.ds(k + 1, 1), :] = inverse_row1
             return carry
 
-        lax.fori_loop(first, min(first + 8, size), step, 0, unroll=True)
+        lax.fori_loop(first // 2, min(first + 8, size) // 2, step, 0)
     lower_inverse = inverse_ref[...]
     projected_row = stacked_ref[size : size + 1, :]
     whitened = jnp.sum(lower_inverse * projected_row, axis=1, keepdims=True)

time: 70.5 us -> 64.9 us (0.921)
  Pallas kernels: 15 us -> 9.64 us
    pallas_call x1, Pallas kernels: 15 us -> 9.64 us  [combination_transposed_of(): pl.pallas_call(combination_kernel, out_shape=jax.ShapeDtypeStruct((size,...]
where the time goes in v16:
time: 64.9 us; the launch traced here: 64.4 us
  starting transfers between devices  21.7 us (33%)
  waiting for transfers between devices  16.2 us (25%)
  Pallas kernels  9.64 us (15%)
  matrix products  6.77 us (10%)
  local copies, waits for them, and re-layouts  5.02 us (8%)
  other arithmetic  4.04 us (6%)
  between operations  1.04 us (2%)
    ppermute x5, starting transfers between devices, butterfly_sum(): received[offset] = lax.ppermute(value, axis, pairs)  12.1 us
    ppermute x5, waiting for transfers between devices, butterfly_sum(): received[offset] = lax.ppermute(value, axis, pairs)  11.1 us
    pallas_call x1, Pallas kernels, combination_transposed_of(): pl.pallas_call(combination_kernel, out_shape=jax.ShapeDtypeStruct((size,...  9.64 us
    ppermute x4, starting transfers between devices, from_neighbour(): return lax.ppermute(block, axis, pairs)  9.5 us
    ppermute x4, waiting for transfers between devices, from_neighbour(): return lax.ppermute(block, axis, pairs)  5.09 us
    unnamed x14, local copies, waits for them, and re-layouts  4.87 us
    dot_general x1, matrix products, shards(): lax.dot_general(deviation_t * cell_weight[:, :, None], deviation_t, (((0,...  2.7 us
    select_n x1, other arithmetic, forecast_two_steps(): first = jnp.where(outside[:, :, None], 0.0, first)  2.12 us
  transfers between devices with their start and end apart: 9, of which 7 were waited for; matrix products, arithmetic and copies ran while one was open for 1% of the time, Pallas kernels for 0%

profile of v16, /device:TPU:0, one launch (start us, length us, event | category | flops | bytes accessed | tf_op | source)
XLA Modules:
  0.0 64.4 jit_solution(1862537158486975317)
XLA Ops:
  0.6 0.0 copy-start
  0.6 1.7 %copy.14 = f32[128,16,128]{0,2,1:T(8,128)S(1)} copy(f32[128,16,128]{2,1,0:T(8,128)} %param.6) | data formatting | bytes 2097152 | tf_op args[1]
  2.3 0.0 copy-done
  2.3 0.0 copy-start.2
  2.4 0.0 copy-start.3
  2.4 0.0 copy-start.4
  2.4 0.4 copy.13
  2.9 2.4 %collective-permute-start = (f32[128,3,128]{2,0,1:T(8,128)S(1)}, f32[128,3,128]{2,0,1:T(8,128)S(1)}, u32[]{:S(2)}, u32[]{:S(2)}) collective-permute-start(f32[128,3,128]{2,0,1:T(8,128)S(1)} %pad_maximum_fusion.7), channel_id=1, source_target_pairs={{0,4},{4,8},{8,12},{12,16},{16,20},{20,24},{24,28},{1,5},{5,9},{9,... | collective-permute-start | bytes 589832 | tf_op jit(solution)/shard_map/ppermute | solution.py:134
  5.3 1.3 %collective-permute-start.1 = (f32[128,3,128]{2,0,1:T(8,128)S(1)}, f32[128,3,128]{2,0,1:T(8,128)S(1)}, u32[]{:S(2)}, u32[]{:S(2)}) collective-permute-start(f32[128,3,128]{2,0,1:T(8,128)S(1)} %pad_maximum_fusion.8), channel_id=1, source_target_pairs={{4,0},{8,4},{12,8},{16,12},{20,16},{24,20},{28,24},{5,1},{9,5},{13... | collective-permute-start | bytes 589832 | tf_op jit(solution)/shard_map/ppermute | solution.py:134
  6.6 0.0 copy-done.2
  6.6 0.0 copy-done.3
  6.6 0.0 copy-done.4
  6.7 0.4 fusion.27
  7.1 0.0 collective-permute-done
  7.1 3.6 %collective-permute-done.1 = f32[128,3,128]{2,0,1:T(8,128)S(1)} collective-permute-done((f32[128,3,128]{2,0,1:T(8,128)S(1)}, f32[128,3,128]{2,0,1:T(8,128)S(1)}, u32[]{:S(2)}, u32[]{:S(2)}) %collective-permute-start.1) | collective-permute-done | bytes 196640 | tf_op jit(solution)/shard_map/ppermute | solution.py:134
  10.8 1.3 %collective-permute-start.3 = (f32[3,20,128]{2,1,0:T(8,128)S(1)}, f32[3,20,128]{2,1,0:T(8,128)S(1)}, u32[]{:S(2)}, u32[]{:S(2)}) collective-permute-start(f32[3,20,128]{2,1,0:T(8,128)S(1)} %pad_maximum_fusion.11), channel_id=1, source_target_pairs={{1,0},{2,1},{3,2},{5,4},{6,5},{7,6},{9,8},{10,9},{11,10},{13,12},{... | collective-permute-start | bytes 92168 | tf_op jit(solution)/shard_map/ppermute | solution.py:134
  12.2 4.5 %collective-permute-start.2 = (f32[3,20,128]{2,1,0:T(8,128)S(1)}, f32[3,20,128]{2,1,0:T(8,128)S(1)}, u32[]{:S(2)}, u32[]{:S(2)}) collective-permute-start(f32[3,20,128]{2,1,0:T(8,128)S(1)} %pad_maximum_fusion.10), channel_id=1, source_target_pairs={{0,1},{1,2},{2,3},{4,5},{5,6},{6,7},{8,9},{9,10},{10,11},{12,13},{... | collective-permute-start | bytes 92168 | tf_op jit(solution)/shard_map/ppermute | solution.py:134
  16.7 0.1 or_or_fusion
  16.8 0.0 collective-permute-done.3
  16.8 1.5 %collective-permute-done.2 = f32[3,20,128]{2,1,0:T(8,128)S(1)} collective-permute-done((f32[3,20,128]{2,1,0:T(8,128)S(1)}, f32[3,20,128]{2,1,0:T(8,128)S(1)}, u32[]{:S(2)}, u32[]{:S(2)}) %collective-permute-start.2) | collective-permute-done | bytes 30752 | tf_op jit(solution)/shard_map/ppermute | solution.py:134
  18.4 0.1 pad_maximum_fusion
  18.5 2.1 %fusion.9 = f32[130,18,128]{2,0,1:T(8,128)S(1)} fusion(f32[2,20,128]{2,0,1:T(2,128)S(1)} %copy.19, f32[128,2,128]{2,0,1:T(8,128)S(1)} %slice.121, f32[128,16,128]{2,0,1:T(8,128)S(1)} %bitcast.42, f32[128,2,128]{2,0,1:T(8,128)S(1)} %slice.118, f32[2,20,128]{2,0,1:T(2,128)S(1)} %copy.20, f32[132,20,128]{2,0,1:T(8,128)S(1)} %pad_maximum_fusion, ...), kind=kLoop, calls=%fused_computation.13 | loop fusion | flops 5990400 | bytes 7344420 | tf_op jit(solution)/shard_map/jit(_where)/select_n | solution.py:176
  20.7 0.9 %fusion.44 = (f32[128,16]{0,1:T(8,128)S(1)}, f32[128,16,128]{2,0,1:T(8,128)S(1)}, f32[128,16]{0,1:T(8,128)S(1)}) fusion(f32[128,16,128]{0,2,1:T(8,128)S(1)} %copy.14, f32[130,18,128]{2,0,1:T(8,128)S(1)} %fusion.9), kind=kLoop, calls=%fused_computation.90 | loop fusion | flops 2879488 | bytes 7356416 | tf_op jit(solution)/shard_map/reduce_sum | solution.py:191
  21.6 2.7 %fusion.11 = f32[128,128]{1,0:T(8,128)S(1)} fusion(f32[128,16,128]{2,0,1:T(8,128)S(1)} %get-tuple-element.7, f32[128,16]{0,1:T(8,128)S(1)} %get-tuple-element.17, f32[128,16]{0,1:T(8,128)S(1)} %get-tuple-element.20), kind=kOutput, calls=%fused_computation.22 | convolution fusion | flops 403439616 | bytes 1130496 | tf_op jit(solution)/shard_map/dot_general | solution.py:214
  24.3 0.8 %convolution_bitcast_fusion.2 = f32[1,128]{1,0:T(1,128)S(1)} fusion(f32[128,16,1]{0,2,1:T(1,128)S(1)} %bitcast.43, f32[128,16,128]{2,0,1:T(8,128)S(1)} %get-tuple-element.7, f32[128,16]{0,1:T(8,128)S(1)} %get-tuple-element.20), kind=kOutput, calls=%fused_computation.23 | convolution fusion | flops 3407872 | bytes 1065472 | tf_op jit(solution)/shard_map/dot_general | solution.py:220
  25.1 3.1 %collective-permute-start.4 = (f32[129,128]{1,0:T(8,128)S(1)}, f32[129,128]{1,0:T(8,128)S(1)}, u32[]{:S(2)}, u32[]{:S(2)}) collective-permute-start(f32[129,128]{1,0:T(8,128)S(1)} %pad_maximum_fusion.9), channel_id=1, source_target_pairs={{0,4},{4,0},{8,12},{12,8},{16,20},{20,16},{24,28},{28,24},{1,5},{5... | collective-permute-start | bytes 198152 | tf_op jit(solution)/shard_map/ppermute | solution.py:38
  28.2 0.9 %collective-permute-done.4 = f32[129,128]{1,0:T(8,128)S(1)} collective-permute-done((f32[129,128]{1,0:T(8,128)S(1)}, f32[129,128]{1,0:T(8,128)S(1)}, u32[]{:S(2)}, u32[]{:S(2)}) %collective-permute-start.4) | collective-permute-done | bytes 66080 | tf_op jit(solution)/shard_map/ppermute | solution.py:38
  29.1 2.5 %collective-permute-start.5 = (f32[129,128]{1,0:T(8,128)S(1)}, f32[129,128]{1,0:T(8,128)S(1)}, u32[]{:S(2)}, u32[]{:S(2)}) collective-permute-start(f32[129,128]{1,0:T(8,128)S(1)} %fusion.43), channel_id=1, source_target_pairs={{0,8},{4,12},{8,0},{12,4},{16,24},{20,28},{24,16},{28,20},{1,9},{5... | collective-permute-start | bytes 198152 | tf_op jit(solution)/shard_map/ppermute | solution.py:38
  31.5 2.7 %collective-permute-done.5 = f32[129,128]{1,0:T(8,128)S(1)} collective-permute-done((f32[129,128]{1,0:T(8,128)S(1)}, f32[129,128]{1,0:T(8,128)S(1)}, u32[]{:S(2)}, u32[]{:S(2)}) %collective-permute-start.5) | collective-permute-done | bytes 66080 | tf_op jit(solution)/shard_map/ppermute | solution.py:38
  34.3 1.4 %collective-permute-start.6 = (f32[129,128]{1,0:T(8,128)S(1)}, f32[129,128]{1,0:T(8,128)S(1)}, u32[]{:S(2)}, u32[]{:S(2)}) collective-permute-start(f32[129,128]{1,0:T(8,128)S(1)} %add.88), channel_id=1, source_target_pairs={{0,16},{4,20},{8,24},{12,28},{16,0},{20,4},{24,8},{28,12},{1,17},{... | collective-permute-start | bytes 198152 | tf_op jit(solution)/shard_map/ppermute | solution.py:38
  35.7 3.0 %collective-permute-done.6 = f32[129,128]{1,0:T(8,128)S(1)} collective-permute-done((f32[129,128]{1,0:T(8,128)S(1)}, f32[129,128]{1,0:T(8,128)S(1)}, u32[]{:S(2)}, u32[]{:S(2)}) %collective-permute-start.6) | collective-permute-done | bytes 66080 | tf_op jit(solution)/shard_map/ppermute | solution.py:38
  38.6 2.1 %collective-permute-start.7 = (f32[129,128]{1,0:T(8,128)S(1)}, f32[129,128]{1,0:T(8,128)S(1)}, u32[]{:S(2)}, u32[]{:S(2)}) collective-permute-start(f32[129,128]{1,0:T(8,128)S(1)} %add.89), channel_id=1, source_target_pairs={{0,1},{1,0},{2,3},{3,2},{4,5},{5,4},{6,7},{7,6},{8,9},{9,8},{10,11... | collective-permute-start | bytes 198152 | tf_op jit(solution)/shard_map/ppermute | solution.py:38
  40.7 2.3 %collective-permute-done.7 = f32[129,128]{1,0:T(8,128)S(1)} collective-permute-done((f32[129,128]{1,0:T(8,128)S(1)}, f32[129,128]{1,0:T(8,128)S(1)}, u32[]{:S(2)}, u32[]{:S(2)}) %collective-permute-start.7) | collective-permute-done | bytes 66080 | tf_op jit(solution)/shard_map/ppermute | solution.py:38
  43.0 3.1 %collective-permute-start.8 = (f32[129,128]{1,0:T(8,128)S(1)}, f32[129,128]{1,0:T(8,128)S(1)}, u32[]{:S(2)}, u32[]{:S(2)}) collective-permute-start(f32[129,128]{1,0:T(8,128)S(1)} %add.90), channel_id=1, source_target_pairs={{0,2},{1,3},{2,0},{3,1},{4,6},{5,7},{6,4},{7,5},{8,10},{9,11},{10,... | collective-permute-start | bytes 198152 | tf_op jit(solution)/shard_map/ppermute | solution.py:38
  46.1 2.3 %collective-permute-done.8 = f32[129,128]{1,0:T(8,128)S(1)} collective-permute-done((f32[129,128]{1,0:T(8,128)S(1)}, f32[129,128]{1,0:T(8,128)S(1)}, u32[]{:S(2)}, u32[]{:S(2)}) %collective-permute-start.8) | collective-permute-done | bytes 66080 | tf_op jit(solution)/shard_map/ppermute | solution.py:38
  48.4 0.6 add.91.stacked_ref
  49.1 9.6 %shard_map.68 = f32[128,128]{1,0:T(8,128)} custom-call(f32[129,128]{1,0:T(8,128)} %add.91.stacked_ref), custom_call_target="tpu_custom_call" | custom-call | tf_op jit(solution)/shard_map/pallas_call | solution.py:98
  58.7 1.9 %fusion.2 = f32[128,16,128]{0,2,1:T(8,128)S(1)} fusion(f32[128,16]{0,1:T(8,128)S(1)} %get-tuple-element.22, f32[16,128]{1,0:T(8,128)S(1)} %get-tuple-element.21, f32[128,128]{1,0:T(8,128)} %shard_map.68, f32[128,16,128]{0,2,1:T(8,128)S(1)} %copy.14), kind=kOutput, calls=%fused_computation.4 | convolution fusion | flops 403177472 | bytes 2179072 | tf_op jit(solution)/shard_map/dot_general | solution.py:233
  60.6 0.0 copy-start.1
  60.6 1.4 %copy.27 = f32[128,16,128]{2,1,0:T(8,128)} copy(f32[128,16,128]{0,2,1:T(8,128)S(1)} %fusion.2) | data formatting | bytes 2097152
  62.0 0.0 copy-done.1
  62.0 1.0 %fusion.3 = f32[128,16,128]{0,2,1:T(8,128)S(1)} fusion(f32[128,16,128]{2,0,1:T(8,128)S(1)} %get-tuple-element.7, f32[128,16]{0,1:T(8,128)S(1)} %get-tuple-element.20, f32[16,128]{1,0:T(8,128)S(1)} %get-tuple-element.19, f32[128,128]{1,0:T(8,128)S(1)} %copy-done.1), kind=kOutput, calls=%fused_computation.6 | convolution fusion | flops 403177472 | bytes 2179072 | tf_op jit(solution)/shard_map/dot_general | solution.py:230
  63.0 1.4 %copy.26 = f32[128,16,128]{2,1,0:T(8,128)} copy(f32[128,16,128]{0,2,1:T(8,128)S(1)} %fusion.3) | data formatting | bytes 2097152
  (37 shorter events, 0.4 us)
Async XLA Ops:
  0.6 1.7 %copy-start = (f32[128,16,128]{2,1,0:T(8,128)S(1)}, f32[128,16,128]{2,1,0:T(8,128)}, u32[]{:S(2)}) copy-start(f32[128,16,128]{2,1,0:T(8,128)} %param.5) | copy-start | bytes 3145732
  2.3 4.2 %copy-start.2 = (s32[1024]{0:T(1024)S(1)}, s32[1024]{0:T(1024)}, u32[]{:S(2)}) copy-start(s32[1024]{0:T(1024)} %param.9) | copy-start | bytes 12292
  2.4 4.3 %copy-start.3 = (f32[1024]{0:T(1024)S(1)}, f32[1024]{0:T(1024)}, u32[]{:S(2)}) copy-start(f32[1024]{0:T(1024)} %param.8) | copy-start | bytes 12292
  2.4 4.3 %copy-start.4 = (f32[1024]{0:T(1024)S(1)}, f32[1024]{0:T(1024)}, u32[]{:S(2)}) copy-start(f32[1024]{0:T(1024)} %param.7) | copy-start | bytes 12292
  2.9 4.2 %collective-permute-start = (f32[128,3,128]{2,0,1:T(8,128)S(1)}, f32[128,3,128]{2,0,1:T(8,128)S(1)}, u32[]{:S(2)}, u32[]{:S(2)}) collective-permute-start(f32[128,3,128]{2,0,1:T(8,128)S(1)} %pad_maximum_fusion.7), channel_id=1, source_target_pairs={{0,4},{4,8},{8,12},{12,16},{16,20},{20,24},{24,28},{1,5},{5,9},{9,... | collective-permute-start | bytes 589832 | tf_op jit(solution)/shard_map/ppermute | solution.py:134
  5.3 5.4 %collective-permute-start.1 = (f32[128,3,128]{2,0,1:T(8,128)S(1)}, f32[128,3,128]{2,0,1:T(8,128)S(1)}, u32[]{:S(2)}, u32[]{:S(2)}) collective-permute-start(f32[128,3,128]{2,0,1:T(8,128)S(1)} %pad_maximum_fusion.8), channel_id=1, source_target_pairs={{4,0},{8,4},{12,8},{16,12},{20,16},{24,20},{28,24},{5,1},{9,5},{13... | collective-permute-start | bytes 589832 | tf_op jit(solution)/shard_map/ppermute | solution.py:134
  10.8 6.0 %collective-permute-start.3 = (f32[3,20,128]{2,1,0:T(8,128)S(1)}, f32[3,20,128]{2,1,0:T(8,128)S(1)}, u32[]{:S(2)}, u32[]{:S(2)}) collective-permute-start(f32[3,20,128]{2,1,0:T(8,128)S(1)} %pad_maximum_fusion.11), channel_id=1, source_target_pairs={{1,0},{2,1},{3,2},{5,4},{6,5},{7,6},{9,8},{10,9},{11,10},{13,12},{... | collective-permute-start | bytes 92168 | tf_op jit(solution)/shard_map/ppermute | solution.py:134
  12.2 6.2 %collective-permute-start.2 = (f32[3,20,128]{2,1,0:T(8,128)S(1)}, f32[3,20,128]{2,1,0:T(8,128)S(1)}, u32[]{:S(2)}, u32[]{:S(2)}) collective-permute-start(f32[3,20,128]{2,1,0:T(8,128)S(1)} %pad_maximum_fusion.10), channel_id=1, source_target_pairs={{0,1},{1,2},{2,3},{4,5},{5,6},{6,7},{8,9},{9,10},{10,11},{12,13},{... | collective-permute-start | bytes 92168 | tf_op jit(solution)/shard_map/ppermute | solution.py:134
  25.1 4.0 %collective-permute-start.4 = (f32[129,128]{1,0:T(8,128)S(1)}, f32[129,128]{1,0:T(8,128)S(1)}, u32[]{:S(2)}, u32[]{:S(2)}) collective-permute-start(f32[129,128]{1,0:T(8,128)S(1)} %pad_maximum_fusion.9), channel_id=1, source_target_pairs={{0,4},{4,0},{8,12},{12,8},{16,20},{20,16},{24,28},{28,24},{1,5},{5... | collective-permute-start | bytes 198152 | tf_op jit(solution)/shard_map/ppermute | solution.py:38
  29.1 5.2 %collective-permute-start.5 = (f32[129,128]{1,0:T(8,128)S(1)}, f32[129,128]{1,0:T(8,128)S(1)}, u32[]{:S(2)}, u32[]{:S(2)}) collective-permute-start(f32[129,128]{1,0:T(8,128)S(1)} %fusion.43), channel_id=1, source_target_pairs={{0,8},{4,12},{8,0},{12,4},{16,24},{20,28},{24,16},{28,20},{1,9},{5... | collective-permute-start | bytes 198152 | tf_op jit(solution)/shard_map/ppermute | solution.py:38
  34.3 4.4 %collective-permute-start.6 = (f32[129,128]{1,0:T(8,128)S(1)}, f32[129,128]{1,0:T(8,128)S(1)}, u32[]{:S(2)}, u32[]{:S(2)}) collective-permute-start(f32[129,128]{1,0:T(8,128)S(1)} %add.88), channel_id=1, source_target_pairs={{0,16},{4,20},{8,24},{12,28},{16,0},{20,4},{24,8},{28,12},{1,17},{... | collective-permute-start | bytes 198152 | tf_op jit(solution)/shard_map/ppermute | solution.py:38
  38.6 4.4 %collective-permute-start.7 = (f32[129,128]{1,0:T(8,128)S(1)}, f32[129,128]{1,0:T(8,128)S(1)}, u32[]{:S(2)}, u32[]{:S(2)}) collective-permute-start(f32[129,128]{1,0:T(8,128)S(1)} %add.89), channel_id=1, source_target_pairs={{0,1},{1,0},{2,3},{3,2},{4,5},{5,4},{6,7},{7,6},{8,9},{9,8},{10,11... | collective-permute-start | bytes 198152 | tf_op jit(solution)/shard_map/ppermute | solution.py:38
  43.0 5.4 %collective-permute-start.8 = (f32[129,128]{1,0:T(8,128)S(1)}, f32[129,128]{1,0:T(8,128)S(1)}, u32[]{:S(2)}, u32[]{:S(2)}) collective-permute-start(f32[129,128]{1,0:T(8,128)S(1)} %add.90), channel_id=1, source_target_pairs={{0,2},{1,3},{2,0},{3,1},{4,6},{5,7},{6,4},{7,5},{8,10},{9,11},{10,... | collective-permute-start | bytes 198152 | tf_op jit(solution)/shard_map/ppermute | solution.py:38
  60.6 1.4 %copy-start.1 = (f32[128,128]{1,0:T(8,128)S(1)}, f32[128,128]{1,0:T(8,128)}, u32[]{:S(2)}) copy-start(f32[128,128]{1,0:T(8,128)} %shard_map.68) | copy-start | bytes 196612

commit v17 on v12

--- a/solution.py
+++ b/solution.py
@@ -40,7 +40,7 @@
     return value
 
 
-def combination_kernel(stacked_ref, combination_ref, work_ref, inverse_ref):
+def combination_kernel(stacked_ref, combination_ref, work_ref, inverse_ref, block=4):
     size = stacked_ref.shape[1]
     square_row = lax.broadcasted_iota(jnp.int32, (size, size), 0)
     square_col = lax.broadcasted_iota(jnp.int32, (size, size), 1)
@@ -48,27 +48,45 @@
     work_ref[...] = stacked_ref[:size, :] + unit
     inverse_ref[...] = unit
     lane = lax.broadcasted_iota(jnp.int32, (1, size), 1)
+
+    def pick(vector, where_true, axis):
+        return jnp.sum(jnp.where(where_true, vector, 0.0), axis=axis, keepdims=True)
+
     for first in range(0, size, 8):
         span = size - first
         sublane = lax.broadcasted_iota(jnp.int32, (span, 1), 0) + first
         band_col = lax.broadcasted_iota(jnp.int32, (span, size), 1)
 
-        def step(k, carry, first=first, sublane=sublane, band_col=band_col):
-            row = work_ref[pl.ds(k, 1), :]
+        def step(group, carry, first=first, sublane=sublane, band_col=band_col):
+            k = block * group
             band = work_ref[first:, :]
-            column = jnp.sum(jnp.where(band_col == k, band, 0.0), axis=1, keepdims=True)
-            pivot = jnp.sum(jnp.where(lane == k, row, 0.0), axis=1, keepdims=True)
-            scale = 1.0 / jnp.sqrt(pivot)
-            factor_row = jnp.where(lane >= k, row * scale, 0.0)
-            factor_col = jnp.where(sublane >= k, column * scale, 0.0)
-            work_ref[first:, :] = band - factor_col * factor_row
-            inverse_row = inverse_ref[pl.ds(k, 1), :] * scale
-            below = jnp.where(sublane > k, factor_col, 0.0)
-            inverse_ref[first:, :] = inverse_ref[first:, :] - below * inverse_row
-            inverse_ref[pl.ds(k, 1), :] = inverse_row
+            factor_rows, factor_cols, inverse_rows = [], [], []
+            for j in range(block):
+                row = work_ref[pl.ds(k + j, 1), :]
+                col = pick(band, band_col == k + j, 1)
+                inverse_row = inverse_ref[pl.ds(k + j, 1), :]
+                for i in range(j):
+                    coupling = pick(factor_rows[i], lane == k + j, 1)
+                    row = row - coupling * factor_rows[i]
+                    col = col - factor_cols[i] * coupling
+                    inverse_row = inverse_row - coupling * inverse_rows[i]
+                scale = 1.0 / jnp.sqrt(pick(row, lane == k + j, 1))
+                factor_rows.append(jnp.where(lane >= k + j, row * scale, 0.0))
+                factor_cols.append(jnp.where(sublane >= k + j, col * scale, 0.0))
+                inverse_rows.append(inverse_row * scale)
+            update = band
+            inverse_band = inverse_ref[first:, :]
+            for j in range(block):
+                update = update - factor_cols[j] * factor_rows[j]
+                below = jnp.where(sublane >= k + block, factor_cols[j], 0.0)
+                inverse_band = inverse_band - below * inverse_rows[j]
+            work_ref[first:, :] = update
+            inverse_ref[first:, :] = inverse_band
+            for j in range(block):
+                inverse_ref[pl.ds(k + j, 1), :] = inverse_rows[j]
             return carry
 
-        lax.fori_loop(first, min(first + 8, size), step, 0, unroll=True)
+        lax.fori_loop(first // block, min(first + 8, size) // block, step, 0)
     lower_inverse = inverse_ref[...]
     projected_row = stacked_ref[size : size + 1, :]
     whitened = jnp.sum(lower_inverse * projected_row, axis=1, keepdims=True)

time: 70.5 us -> 76.5 us (1.085)
  Pallas kernels: 15 us -> 21.3 us
    pallas_call x1, Pallas kernels: 15 us -> 21.3 us  [combination_transposed_of(): pl.pallas_call(combination_kernel, out_shape=jax.ShapeDtypeStruct((size,...]
where the time goes in v17:
time: 76.5 us; the launch traced here: 76 us
  starting transfers between devices  21.7 us (28%)
  Pallas kernels  21.3 us (28%)
  waiting for transfers between devices  16.2 us (21%)
  matrix products  6.76 us (9%)
  local copies, waits for them, and re-layouts  5.02 us (7%)
  other arithmetic  4.04 us (5%)
  between operations  1.04 us (1%)
    pallas_call x1, Pallas kernels, combination_transposed_of(): pl.pallas_call(combination_kernel, out_shape=jax.ShapeDtypeStruct((size,...  21.3 us
    ppermute x5, starting transfers between devices, butterfly_sum(): received[offset] = lax.ppermute(value, axis, pairs)  12.1 us
    ppermute x5, waiting for transfers between devices, butterfly_sum(): received[offset] = lax.ppermute(value, axis, pairs)  11.1 us
    ppermute x4, starting transfers between devices, from_neighbour(): return lax.ppermute(block, axis, pairs)  9.5 us
    ppermute x4, waiting for transfers between devices, from_neighbour(): return lax.ppermute(block, axis, pairs)  5.09 us
    unnamed x14, local copies, waits for them, and re-layouts  4.87 us
    dot_general x1, matrix products, shards(): lax.dot_general(deviation_t * cell_weight[:, :, None], deviation_t, (((0,...  2.7 us
    select_n x1, other arithmetic, forecast_two_steps(): first = jnp.where(outside[:, :, None], 0.0, first)  2.12 us
  transfers between devices with their start and end apart: 9, of which 7 were waited for; matrix products, arithmetic and copies ran while one was open for 1% of the time, Pallas kernels for 0%

profile of v17, /device:TPU:0, one launch (start us, length us, event | category | flops | bytes accessed | tf_op | source)
XLA Modules:
  0.0 76.0 jit_solution(1641358073833476047)
XLA Ops:
  0.6 0.0 copy-start
  0.6 1.7 %copy.14 = f32[128,16,128]{0,2,1:T(8,128)S(1)} copy(f32[128,16,128]{2,1,0:T(8,128)} %param.6) | data formatting | bytes 2097152 | tf_op args[1]
  2.3 0.0 copy-done
  2.3 0.0 copy-start.2
  2.4 0.0 copy-start.3
  2.4 0.0 copy-start.4
  2.4 0.4 copy.13
  2.9 2.4 %collective-permute-start = (f32[128,3,128]{2,0,1:T(8,128)S(1)}, f32[128,3,128]{2,0,1:T(8,128)S(1)}, u32[]{:S(2)}, u32[]{:S(2)}) collective-permute-start(f32[128,3,128]{2,0,1:T(8,128)S(1)} %pad_maximum_fusion.7), channel_id=1, source_target_pairs={{0,4},{4,8},{8,12},{12,16},{16,20},{20,24},{24,28},{1,5},{5,9},{9,... | collective-permute-start | bytes 589832 | tf_op jit(solution)/shard_map/ppermute | solution.py:135
  5.3 1.3 %collective-permute-start.1 = (f32[128,3,128]{2,0,1:T(8,128)S(1)}, f32[128,3,128]{2,0,1:T(8,128)S(1)}, u32[]{:S(2)}, u32[]{:S(2)}) collective-permute-start(f32[128,3,128]{2,0,1:T(8,128)S(1)} %pad_maximum_fusion.8), channel_id=1, source_target_pairs={{4,0},{8,4},{12,8},{16,12},{20,16},{24,20},{28,24},{5,1},{9,5},{13... | collective-permute-start | bytes 589832 | tf_op jit(solution)/shard_map/ppermute | solution.py:135
  6.6 0.0 copy-done.2
  6.6 0.0 copy-done.3
  6.6 0.0 copy-done.4
  6.7 0.4 fusion.27
  7.1 0.0 collective-permute-done
  7.1 3.6 %collective-permute-done.1 = f32[128,3,128]{2,0,1:T(8,128)S(1)} collective-permute-done((f32[128,3,128]{2,0,1:T(8,128)S(1)}, f32[128,3,128]{2,0,1:T(8,128)S(1)}, u32[]{:S(2)}, u32[]{:S(2)}) %collective-permute-start.1) | collective-permute-done | bytes 196640 | tf_op jit(solution)/shard_map/ppermute | solution.py:135
  10.8 1.3 %collective-permute-start.3 = (f32[3,20,128]{2,1,0:T(8,128)S(1)}, f32[3,20,128]{2,1,0:T(8,128)S(1)}, u32[]{:S(2)}, u32[]{:S(2)}) collective-permute-start(f32[3,20,128]{2,1,0:T(8,128)S(1)} %pad_maximum_fusion.11), channel_id=1, source_target_pairs={{1,0},{2,1},{3,2},{5,4},{6,5},{7,6},{9,8},{10,9},{11,10},{13,12},{... | collective-permute-start | bytes 92168 | tf_op jit(solution)/shard_map/ppermute | solution.py:135
  12.2 4.5 %collective-permute-start.2 = (f32[3,20,128]{2,1,0:T(8,128)S(1)}, f32[3,20,128]{2,1,0:T(8,128)S(1)}, u32[]{:S(2)}, u32[]{:S(2)}) collective-permute-start(f32[3,20,128]{2,1,0:T(8,128)S(1)} %pad_maximum_fusion.10), channel_id=1, source_target_pairs={{0,1},{1,2},{2,3},{4,5},{5,6},{6,7},{8,9},{9,10},{10,11},{12,13},{... | collective-permute-start | bytes 92168 | tf_op jit(solution)/shard_map/ppermute | solution.py:135
  16.7 0.1 or_or_fusion
  16.8 0.0 collective-permute-done.3
  16.8 1.5 %collective-permute-done.2 = f32[3,20,128]{2,1,0:T(8,128)S(1)} collective-permute-done((f32[3,20,128]{2,1,0:T(8,128)S(1)}, f32[3,20,128]{2,1,0:T(8,128)S(1)}, u32[]{:S(2)}, u32[]{:S(2)}) %collective-permute-start.2) | collective-permute-done | bytes 30752 | tf_op jit(solution)/shard_map/ppermute | solution.py:135
  18.4 0.1 pad_maximum_fusion
  18.5 2.1 %fusion.9 = f32[130,18,128]{2,0,1:T(8,128)S(1)} fusion(f32[2,20,128]{2,0,1:T(2,128)S(1)} %copy.19, f32[128,2,128]{2,0,1:T(8,128)S(1)} %slice.121, f32[128,16,128]{2,0,1:T(8,128)S(1)} %bitcast.42, f32[128,2,128]{2,0,1:T(8,128)S(1)} %slice.118, f32[2,20,128]{2,0,1:T(2,128)S(1)} %copy.20, f32[132,20,128]{2,0,1:T(8,128)S(1)} %pad_maximum_fusion, ...), kind=kLoop, calls=%fused_computation.13 | loop fusion | flops 5990400 | bytes 7344420 | tf_op jit(solution)/shard_map/jit(_where)/select_n | solution.py:177
  20.7 0.9 %fusion.44 = (f32[128,16]{0,1:T(8,128)S(1)}, f32[128,16,128]{2,0,1:T(8,128)S(1)}, f32[128,16]{0,1:T(8,128)S(1)}) fusion(f32[128,16,128]{0,2,1:T(8,128)S(1)} %copy.14, f32[130,18,128]{2,0,1:T(8,128)S(1)} %fusion.9), kind=kLoop, calls=%fused_computation.90 | loop fusion | flops 2879488 | bytes 7356416 | tf_op jit(solution)/shard_map/reduce_sum | solution.py:192
  21.6 2.7 %fusion.11 = f32[128,128]{1,0:T(8,128)S(1)} fusion(f32[128,16,128]{2,0,1:T(8,128)S(1)} %get-tuple-element.7, f32[128,16]{0,1:T(8,128)S(1)} %get-tuple-element.17, f32[128,16]{0,1:T(8,128)S(1)} %get-tuple-element.20), kind=kOutput, calls=%fused_computation.22 | convolution fusion | flops 403439616 | bytes 1130496 | tf_op jit(solution)/shard_map/dot_general | solution.py:215
  24.3 0.8 %convolution_bitcast_fusion.2 = f32[1,128]{1,0:T(1,128)S(1)} fusion(f32[128,16,1]{0,2,1:T(1,128)S(1)} %bitcast.43, f32[128,16,128]{2,0,1:T(8,128)S(1)} %get-tuple-element.7, f32[128,16]{0,1:T(8,128)S(1)} %get-tuple-element.20), kind=kOutput, calls=%fused_computation.23 | convolution fusion | flops 3407872 | bytes 1065472 | tf_op jit(solution)/shard_map/dot_general | solution.py:221
  25.1 3.1 %collective-permute-start.4 = (f32[129,128]{1,0:T(8,128)S(1)}, f32[129,128]{1,0:T(8,128)S(1)}, u32[]{:S(2)}, u32[]{:S(2)}) collective-permute-start(f32[129,128]{1,0:T(8,128)S(1)} %pad_maximum_fusion.9), channel_id=1, source_target_pairs={{0,4},{4,0},{8,12},{12,8},{16,20},{20,16},{24,28},{28,24},{1,5},{5... | collective-permute-start | bytes 198152 | tf_op jit(solution)/shard_map/ppermute | solution.py:38
  28.2 0.9 %collective-permute-done.4 = f32[129,128]{1,0:T(8,128)S(1)} collective-permute-done((f32[129,128]{1,0:T(8,128)S(1)}, f32[129,128]{1,0:T(8,128)S(1)}, u32[]{:S(2)}, u32[]{:S(2)}) %collective-permute-start.4) | collective-permute-done | bytes 66080 | tf_op jit(solution)/shard_map/ppermute | solution.py:38
  29.1 2.5 %collective-permute-start.5 = (f32[129,128]{1,0:T(8,128)S(1)}, f32[129,128]{1,0:T(8,128)S(1)}, u32[]{:S(2)}, u32[]{:S(2)}) collective-permute-start(f32[129,128]{1,0:T(8,128)S(1)} %fusion.43), channel_id=1, source_target_pairs={{0,8},{4,12},{8,0},{12,4},{16,24},{20,28},{24,16},{28,20},{1,9},{5... | collective-permute-start | bytes 198152 | tf_op jit(solution)/shard_map/ppermute | solution.py:38
  31.5 2.7 %collective-permute-done.5 = f32[129,128]{1,0:T(8,128)S(1)} collective-permute-done((f32[129,128]{1,0:T(8,128)S(1)}, f32[129,128]{1,0:T(8,128)S(1)}, u32[]{:S(2)}, u32[]{:S(2)}) %collective-permute-start.5) | collective-permute-done | bytes 66080 | tf_op jit(solution)/shard_map/ppermute | solution.py:38
  34.3 1.4 %collective-permute-start.6 = (f32[129,128]{1,0:T(8,128)S(1)}, f32[129,128]{1,0:T(8,128)S(1)}, u32[]{:S(2)}, u32[]{:S(2)}) collective-permute-start(f32[129,128]{1,0:T(8,128)S(1)} %add.88), channel_id=1, source_target_pairs={{0,16},{4,20},{8,24},{12,28},{16,0},{20,4},{24,8},{28,12},{1,17},{... | collective-permute-start | bytes 198152 | tf_op jit(solution)/shard_map/ppermute | solution.py:38
  35.7 3.0 %collective-permute-done.6 = f32[129,128]{1,0:T(8,128)S(1)} collective-permute-done((f32[129,128]{1,0:T(8,128)S(1)}, f32[129,128]{1,0:T(8,128)S(1)}, u32[]{:S(2)}, u32[]{:S(2)}) %collective-permute-start.6) | collective-permute-done | bytes 66080 | tf_op jit(solution)/shard_map/ppermute | solution.py:38
  38.6 2.1 %collective-permute-start.7 = (f32[129,128]{1,0:T(8,128)S(1)}, f32[129,128]{1,0:T(8,128)S(1)}, u32[]{:S(2)}, u32[]{:S(2)}) collective-permute-start(f32[129,128]{1,0:T(8,128)S(1)} %add.89), channel_id=1, source_target_pairs={{0,1},{1,0},{2,3},{3,2},{4,5},{5,4},{6,7},{7,6},{8,9},{9,8},{10,11... | collective-permute-start | bytes 198152 | tf_op jit(solution)/shard_map/ppermute | solution.py:38
  40.7 2.3 %collective-permute-done.7 = f32[129,128]{1,0:T(8,128)S(1)} collective-permute-done((f32[129,128]{1,0:T(8,128)S(1)}, f32[129,128]{1,0:T(8,128)S(1)}, u32[]{:S(2)}, u32[]{:S(2)}) %collective-permute-start.7) | collective-permute-done | bytes 66080 | tf_op jit(solution)/shard_map/ppermute | solution.py:38
  43.0 3.1 %collective-permute-start.8 = (f32[129,128]{1,0:T(8,128)S(1)}, f32[129,128]{1,0:T(8,128)S(1)}, u32[]{:S(2)}, u32[]{:S(2)}) collective-permute-start(f32[129,128]{1,0:T(8,128)S(1)} %add.90), channel_id=1, source_target_pairs={{0,2},{1,3},{2,0},{3,1},{4,6},{5,7},{6,4},{7,5},{8,10},{9,11},{10,... | collective-permute-start | bytes 198152 | tf_op jit(solution)/shard_map/ppermute | solution.py:38
  46.1 2.3 %collective-permute-done.8 = f32[129,128]{1,0:T(8,128)S(1)} collective-permute-done((f32[129,128]{1,0:T(8,128)S(1)}, f32[129,128]{1,0:T(8,128)S(1)}, u32[]{:S(2)}, u32[]{:S(2)}) %collective-permute-start.8) | collective-permute-done | bytes 66080 | tf_op jit(solution)/shard_map/ppermute | solution.py:38
  48.4 0.6 add.91.stacked_ref
  49.1 21.3 %shard_map.68 = f32[128,128]{1,0:T(8,128)} custom-call(f32[129,128]{1,0:T(8,128)} %add.91.stacked_ref), custom_call_target="tpu_custom_call" | custom-call | tf_op jit(solution)/shard_map/pallas_call | solution.py:99
  70.4 1.9 %fusion.2 = f32[128,16,128]{0,2,1:T(8,128)S(1)} fusion(f32[128,16]{0,1:T(8,128)S(1)} %get-tuple-element.22, f32[16,128]{1,0:T(8,128)S(1)} %get-tuple-element.21, f32[128,128]{1,0:T(8,128)} %shard_map.68, f32[128,16,128]{0,2,1:T(8,128)S(1)} %copy.14), kind=kOutput, calls=%fused_computation.4 | convolution fusion | flops 403177472 | bytes 2179072 | tf_op jit(solution)/shard_map/dot_general | solution.py:234
  72.2 0.0 copy-start.1
  72.2 1.4 %copy.27 = f32[128,16,128]{2,1,0:T(8,128)} copy(f32[128,16,128]{0,2,1:T(8,128)S(1)} %fusion.2) | data formatting | bytes 2097152
  73.6 0.0 copy-done.1
  73.6 1.0 %fusion.3 = f32[128,16,128]{0,2,1:T(8,128)S(1)} fusion(f32[128,16,128]{2,0,1:T(8,128)S(1)} %get-tuple-element.7, f32[128,16]{0,1:T(8,128)S(1)} %get-tuple-element.20, f32[16,128]{1,0:T(8,128)S(1)} %get-tuple-element.19, f32[128,128]{1,0:T(8,128)S(1)} %copy-done.1), kind=kOutput, calls=%fused_computation.6 | convolution fusion | flops 403177472 | bytes 2179072 | tf_op jit(solution)/shard_map/dot_general | solution.py:231
  74.7 1.4 %copy.26 = f32[128,16,128]{2,1,0:T(8,128)} copy(f32[128,16,128]{0,2,1:T(8,128)S(1)} %fusion.3) | data formatting | bytes 2097152
  (37 shorter events, 0.4 us)
Async XLA Ops:
  0.6 1.7 %copy-start = (f32[128,16,128]{2,1,0:T(8,128)S(1)}, f32[128,16,128]{2,1,0:T(8,128)}, u32[]{:S(2)}) copy-start(f32[128,16,128]{2,1,0:T(8,128)} %param.5) | copy-start | bytes 3145732
  2.3 4.2 %copy-start.2 = (s32[1024]{0:T(1024)S(1)}, s32[1024]{0:T(1024)}, u32[]{:S(2)}) copy-start(s32[1024]{0:T(1024)} %param.9) | copy-start | bytes 12292
  2.4 4.3 %copy-start.3 = (f32[1024]{0:T(1024)S(1)}, f32[1024]{0:T(1024)}, u32[]{:S(2)}) copy-start(f32[1024]{0:T(1024)} %param.8) | copy-start | bytes 12292
  2.4 4.3 %copy-start.4 = (f32[1024]{0:T(1024)S(1)}, f32[1024]{0:T(1024)}, u32[]{:S(2)}) copy-start(f32[1024]{0:T(1024)} %param.7) | copy-start | bytes 12292
  2.9 4.2 %collective-permute-start = (f32[128,3,128]{2,0,1:T(8,128)S(1)}, f32[128,3,128]{2,0,1:T(8,128)S(1)}, u32[]{:S(2)}, u32[]{:S(2)}) collective-permute-start(f32[128,3,128]{2,0,1:T(8,128)S(1)} %pad_maximum_fusion.7), channel_id=1, source_target_pairs={{0,4},{4,8},{8,12},{12,16},{16,20},{20,24},{24,28},{1,5},{5,9},{9,... | collective-permute-start | bytes 589832 | tf_op jit(solution)/shard_map/ppermute | solution.py:135
  5.3 5.4 %collective-permute-start.1 = (f32[128,3,128]{2,0,1:T(8,128)S(1)}, f32[128,3,128]{2,0,1:T(8,128)S(1)}, u32[]{:S(2)}, u32[]{:S(2)}) collective-permute-start(f32[128,3,128]{2,0,1:T(8,128)S(1)} %pad_maximum_fusion.8), channel_id=1, source_target_pairs={{4,0},{8,4},{12,8},{16,12},{20,16},{24,20},{28,24},{5,1},{9,5},{13... | collective-permute-start | bytes 589832 | tf_op jit(solution)/shard_map/ppermute | solution.py:135
  10.8 6.0 %collective-permute-start.3 = (f32[3,20,128]{2,1,0:T(8,128)S(1)}, f32[3,20,128]{2,1,0:T(8,128)S(1)}, u32[]{:S(2)}, u32[]{:S(2)}) collective-permute-start(f32[3,20,128]{2,1,0:T(8,128)S(1)} %pad_maximum_fusion.11), channel_id=1, source_target_pairs={{1,0},{2,1},{3,2},{5,4},{6,5},{7,6},{9,8},{10,9},{11,10},{13,12},{... | collective-permute-start | bytes 92168 | tf_op jit(solution)/shard_map/ppermute | solution.py:135
  12.2 6.2 %collective-permute-start.2 = (f32[3,20,128]{2,1,0:T(8,128)S(1)}, f32[3,20,128]{2,1,0:T(8,128)S(1)}, u32[]{:S(2)}, u32[]{:S(2)}) collective-permute-start(f32[3,20,128]{2,1,0:T(8,128)S(1)} %pad_maximum_fusion.10), channel_id=1, source_target_pairs={{0,1},{1,2},{2,3},{4,5},{5,6},{6,7},{8,9},{9,10},{10,11},{12,13},{... | collective-permute-start | bytes 92168 | tf_op jit(solution)/shard_map/ppermute | solution.py:135
  25.1 4.0 %collective-permute-start.4 = (f32[129,128]{1,0:T(8,128)S(1)}, f32[129,128]{1,0:T(8,128)S(1)}, u32[]{:S(2)}, u32[]{:S(2)}) collective-permute-start(f32[129,128]{1,0:T(8,128)S(1)} %pad_maximum_fusion.9), channel_id=1, source_target_pairs={{0,4},{4,0},{8,12},{12,8},{16,20},{20,16},{24,28},{28,24},{1,5},{5... | collective-permute-start | bytes 198152 | tf_op jit(solution)/shard_map/ppermute | solution.py:38
  29.1 5.2 %collective-permute-start.5 = (f32[129,128]{1,0:T(8,128)S(1)}, f32[129,128]{1,0:T(8,128)S(1)}, u32[]{:S(2)}, u32[]{:S(2)}) collective-permute-start(f32[129,128]{1,0:T(8,128)S(1)} %fusion.43), channel_id=1, source_target_pairs={{0,8},{4,12},{8,0},{12,4},{16,24},{20,28},{24,16},{28,20},{1,9},{5... | collective-permute-start | bytes 198152 | tf_op jit(solution)/shard_map/ppermute | solution.py:38
  34.3 4.4 %collective-permute-start.6 = (f32[129,128]{1,0:T(8,128)S(1)}, f32[129,128]{1,0:T(8,128)S(1)}, u32[]{:S(2)}, u32[]{:S(2)}) collective-permute-start(f32[129,128]{1,0:T(8,128)S(1)} %add.88), channel_id=1, source_target_pairs={{0,16},{4,20},{8,24},{12,28},{16,0},{20,4},{24,8},{28,12},{1,17},{... | collective-permute-start | bytes 198152 | tf_op jit(solution)/shard_map/ppermute | solution.py:38
  38.6 4.4 %collective-permute-start.7 = (f32[129,128]{1,0:T(8,128)S(1)}, f32[129,128]{1,0:T(8,128)S(1)}, u32[]{:S(2)}, u32[]{:S(2)}) collective-permute-start(f32[129,128]{1,0:T(8,128)S(1)} %add.89), channel_id=1, source_target_pairs={{0,1},{1,0},{2,3},{3,2},{4,5},{5,4},{6,7},{7,6},{8,9},{9,8},{10,11... | collective-permute-start | bytes 198152 | tf_op jit(solution)/shard_map/ppermute | solution.py:38
  43.0 5.4 %collective-permute-start.8 = (f32[129,128]{1,0:T(8,128)S(1)}, f32[129,128]{1,0:T(8,128)S(1)}, u32[]{:S(2)}, u32[]{:S(2)}) collective-permute-start(f32[129,128]{1,0:T(8,128)S(1)} %add.90), channel_id=1, source_target_pairs={{0,2},{1,3},{2,0},{3,1},{4,6},{5,7},{6,4},{7,5},{8,10},{9,11},{10,... | collective-permute-start | bytes 198152 | tf_op jit(solution)/shard_map/ppermute | solution.py:38
  72.2 1.4 %copy-start.1 = (f32[128,128]{1,0:T(8,128)S(1)}, f32[128,128]{1,0:T(8,128)}, u32[]{:S(2)}) copy-start(f32[128,128]{1,0:T(8,128)} %shard_map.68) | copy-start | bytes 196612

commit v18 on v16

--- a/solution.py
+++ b/solution.py
@@ -57,11 +57,11 @@
         sublane = lax.broadcasted_iota(jnp.int32, (span, 1), 0) + first
         band_col = lax.broadcasted_iota(jnp.int32, (span, size), 1)
 
-        def step(pair, carry, first=first, sublane=sublane, band_col=band_col):
+        def step(pair, carry, sublane=sublane, band_col=band_col):
+            band, inverse_band = carry
             k = 2 * pair
-            row0 = work_ref[pl.ds(k, 1), :]
-            row1 = work_ref[pl.ds(k + 1, 1), :]
-            band = work_ref[first:, :]
+            row0 = pick(band, sublane == k, 0)
+            row1 = pick(band, sublane == k + 1, 0)
             col0 = pick(band, band_col == k, 1)
             col1 = pick(band, band_col == k + 1, 1)
             scale0 = 1.0 / jnp.sqrt(pick(row0, lane == k, 1))
@@ -73,19 +73,25 @@
             factor_col1 = jnp.where(
                 sublane >= k + 1, (col1 - factor_col0 * coupling) * scale1, 0.0
             )
-            work_ref[first:, :] = band - factor_col0 * factor_row0 - factor_col1 * factor_row1
-            inverse_row0 = inverse_ref[pl.ds(k, 1), :] * scale0
-            inverse_row1 = (inverse_ref[pl.ds(k + 1, 1), :] - coupling * inverse_row0) * scale1
+            band = band - factor_col0 * factor_row0 - factor_col1 * factor_row1
+            inverse_row0 = pick(inverse_band, sublane == k, 0) * scale0
+            inverse_row1 = (pick(inverse_band, sublane == k + 1, 0) - coupling * inverse_row0) * scale1
             below0 = jnp.where(sublane > k + 1, factor_col0, 0.0)
             below1 = jnp.where(sublane > k + 1, factor_col1, 0.0)
-            inverse_ref[first:, :] = (
-                inverse_ref[first:, :] - below0 * inverse_row0 - below1 * inverse_row1
+            inverse_band = inverse_band - below0 * inverse_row0 - below1 * inverse_row1
+            inverse_band = jnp.where(
+                sublane == k, inverse_row0, jnp.where(sublane == k + 1, inverse_row1, inverse_band)
             )
-            inverse_ref[pl.ds(k, 1), :] = inverse_row0
-            inverse_ref[pl.ds(k + 1, 1), :] = inverse_row1
-            return carry
-
-        lax.fori_loop(first // 2, min(first + 8, size) // 2, step, 0)
+            return (band, inverse_band)
+
+        band, inverse_band = lax.fori_loop(
+            first // 2,
+            min(first + 8, size) // 2,
+            step,
+            (work_ref[first:, :], inverse_ref[first:, :]),
+        )
+        work_ref[first:, :] = band
+        inverse_ref[first:, :] = inverse_band
     lower_inverse = inverse_ref[...]
     projected_row = stacked_ref[size : size + 1, :]
     whitened = jnp.sum(lower_inverse * projected_row, axis=1, keepdims=True)

time: 64.9 us -> 66.2 us (1.020)
  Pallas kernels: 9.64 us -> 10.9 us
    pallas_call x1, Pallas kernels: 9.64 us -> 10.9 us  [combination_transposed_of(): pl.pallas_call(combination_kernel, out_shape=jax.ShapeDtypeStruct((size,...]
where the time goes in v18:
time: 66.2 us; the launch traced here: 65.7 us
  starting transfers between devices  21.7 us (33%)
  waiting for transfers between devices  16.2 us (24%)
  Pallas kernels  10.9 us (16%)
  matrix products  6.78 us (10%)
  local copies, waits for them, and re-layouts  5.02 us (8%)
  other arithmetic  4.04 us (6%)
  between operations  1.04 us (2%)
    ppermute x5, starting transfers between devices, butterfly_sum(): received[offset] = lax.ppermute(value, axis, pairs)  12.1 us
    ppermute x5, waiting for transfers between devices, butterfly_sum(): received[offset] = lax.ppermute(value, axis, pairs)  11.1 us
    pallas_call x1, Pallas kernels, combination_transposed_of(): pl.pallas_call(combination_kernel, out_shape=jax.ShapeDtypeStruct((size,...  10.9 us
    ppermute x4, starting transfers between devices, from_neighbour(): return lax.ppermute(block, axis, pairs)  9.5 us
    ppermute x4, waiting for transfers between devices, from_neighbour(): return lax.ppermute(block, axis, pairs)  5.09 us
    unnamed x14, local copies, waits for them, and re-layouts  4.87 us
    dot_general x1, matrix products, shards(): lax.dot_general(deviation_t * cell_weight[:, :, None], deviation_t, (((0,...  2.7 us
    select_n x1, other arithmetic, forecast_two_steps(): first = jnp.where(outside[:, :, None], 0.0, first)  2.12 us
  transfers between devices with their start and end apart: 9, of which 7 were waited for; matrix products, arithmetic and copies ran while one was open for 1% of the time, Pallas kernels for 0%

profile of v18, /device:TPU:0, one launch (start us, length us, event | category | flops | bytes accessed | tf_op | source)
XLA Modules:
  0.0 65.7 jit_solution(9012559113295233212)
XLA Ops:
  0.6 0.0 copy-start
  0.6 1.7 %copy.14 = f32[128,16,128]{0,2,1:T(8,128)S(1)} copy(f32[128,16,128]{2,1,0:T(8,128)} %param.6) | data formatting | bytes 2097152 | tf_op args[1]
  2.3 0.0 copy-done
  2.3 0.0 copy-start.2
  2.4 0.0 copy-start.3
  2.4 0.0 copy-start.4
  2.4 0.4 copy.13
  2.9 2.4 %collective-permute-start = (f32[128,3,128]{2,0,1:T(8,128)S(1)}, f32[128,3,128]{2,0,1:T(8,128)S(1)}, u32[]{:S(2)}, u32[]{:S(2)}) collective-permute-start(f32[128,3,128]{2,0,1:T(8,128)S(1)} %pad_maximum_fusion.7), channel_id=1, source_target_pairs={{0,4},{4,8},{8,12},{12,16},{16,20},{20,24},{24,28},{1,5},{5,9},{9,... | collective-permute-start | bytes 589832 | tf_op jit(solution)/shard_map/ppermute | solution.py:140
  5.3 1.3 %collective-permute-start.1 = (f32[128,3,128]{2,0,1:T(8,128)S(1)}, f32[128,3,128]{2,0,1:T(8,128)S(1)}, u32[]{:S(2)}, u32[]{:S(2)}) collective-permute-start(f32[128,3,128]{2,0,1:T(8,128)S(1)} %pad_maximum_fusion.8), channel_id=1, source_target_pairs={{4,0},{8,4},{12,8},{16,12},{20,16},{24,20},{28,24},{5,1},{9,5},{13... | collective-permute-start | bytes 589832 | tf_op jit(solution)/shard_map/ppermute | solution.py:140
  6.6 0.0 copy-done.2
  6.6 0.0 copy-done.3
  6.6 0.0 copy-done.4
  6.7 0.4 fusion.27
  7.1 0.0 collective-permute-done
  7.1 3.6 %collective-permute-done.1 = f32[128,3,128]{2,0,1:T(8,128)S(1)} collective-permute-done((f32[128,3,128]{2,0,1:T(8,128)S(1)}, f32[128,3,128]{2,0,1:T(8,128)S(1)}, u32[]{:S(2)}, u32[]{:S(2)}) %collective-permute-start.1) | collective-permute-done | bytes 196640 | tf_op jit(solution)/shard_map/ppermute | solution.py:140
  10.8 1.3 %collective-permute-start.3 = (f32[3,20,128]{2,1,0:T(8,128)S(1)}, f32[3,20,128]{2,1,0:T(8,128)S(1)}, u32[]{:S(2)}, u32[]{:S(2)}) collective-permute-start(f32[3,20,128]{2,1,0:T(8,128)S(1)} %pad_maximum_fusion.11), channel_id=1, source_target_pairs={{1,0},{2,1},{3,2},{5,4},{6,5},{7,6},{9,8},{10,9},{11,10},{13,12},{... | collective-permute-start | bytes 92168 | tf_op jit(solution)/shard_map/ppermute | solution.py:140
  12.2 4.5 %collective-permute-start.2 = (f32[3,20,128]{2,1,0:T(8,128)S(1)}, f32[3,20,128]{2,1,0:T(8,128)S(1)}, u32[]{:S(2)}, u32[]{:S(2)}) collective-permute-start(f32[3,20,128]{2,1,0:T(8,128)S(1)} %pad_maximum_fusion.10), channel_id=1, source_target_pairs={{0,1},{1,2},{2,3},{4,5},{5,6},{6,7},{8,9},{9,10},{10,11},{12,13},{... | collective-permute-start | bytes 92168 | tf_op jit(solution)/shard_map/ppermute | solution.py:140
  16.7 0.1 or_or_fusion
  16.8 0.0 collective-permute-done.3
  16.8 1.5 %collective-permute-done.2 = f32[3,20,128]{2,1,0:T(8,128)S(1)} collective-permute-done((f32[3,20,128]{2,1,0:T(8,128)S(1)}, f32[3,20,128]{2,1,0:T(8,128)S(1)}, u32[]{:S(2)}, u32[]{:S(2)}) %collective-permute-start.2) | collective-permute-done | bytes 30752 | tf_op jit(solution)/shard_map/ppermute | solution.py:140
  18.4 0.1 pad_maximum_fusion
  18.5 2.1 %fusion.9 = f32[130,18,128]{2,0,1:T(8,128)S(1)} fusion(f32[2,20,128]{2,0,1:T(2,128)S(1)} %copy.19, f32[128,2,128]{2,0,1:T(8,128)S(1)} %slice.121, f32[128,16,128]{2,0,1:T(8,128)S(1)} %bitcast.42, f32[128,2,128]{2,0,1:T(8,128)S(1)} %slice.118, f32[2,20,128]{2,0,1:T(2,128)S(1)} %copy.20, f32[132,20,128]{2,0,1:T(8,128)S(1)} %pad_maximum_fusion, ...), kind=kLoop, calls=%fused_computation.13 | loop fusion | flops 5990400 | bytes 7344420 | tf_op jit(solution)/shard_map/jit(_where)/select_n | solution.py:182
  20.7 0.9 %fusion.44 = (f32[128,16]{0,1:T(8,128)S(1)}, f32[128,16,128]{2,0,1:T(8,128)S(1)}, f32[128,16]{0,1:T(8,128)S(1)}) fusion(f32[128,16,128]{0,2,1:T(8,128)S(1)} %copy.14, f32[130,18,128]{2,0,1:T(8,128)S(1)} %fusion.9), kind=kLoop, calls=%fused_computation.90 | loop fusion | flops 2879488 | bytes 7356416 | tf_op jit(solution)/shard_map/reduce_sum | solution.py:197
  21.6 2.7 %fusion.11 = f32[128,128]{1,0:T(8,128)S(1)} fusion(f32[128,16,128]{2,0,1:T(8,128)S(1)} %get-tuple-element.7, f32[128,16]{0,1:T(8,128)S(1)} %get-tuple-element.17, f32[128,16]{0,1:T(8,128)S(1)} %get-tuple-element.20), kind=kOutput, calls=%fused_computation.22 | convolution fusion | flops 403439616 | bytes 1130496 | tf_op jit(solution)/shard_map/dot_general | solution.py:220
  24.3 0.8 %convolution_bitcast_fusion.2 = f32[1,128]{1,0:T(1,128)S(1)} fusion(f32[128,16,1]{0,2,1:T(1,128)S(1)} %bitcast.43, f32[128,16,128]{2,0,1:T(8,128)S(1)} %get-tuple-element.7, f32[128,16]{0,1:T(8,128)S(1)} %get-tuple-element.20), kind=kOutput, calls=%fused_computation.23 | convolution fusion | flops 3407872 | bytes 1065472 | tf_op jit(solution)/shard_map/dot_general | solution.py:226
  25.1 3.1 %collective-permute-start.4 = (f32[129,128]{1,0:T(8,128)S(1)}, f32[129,128]{1,0:T(8,128)S(1)}, u32[]{:S(2)}, u32[]{:S(2)}) collective-permute-start(f32[129,128]{1,0:T(8,128)S(1)} %pad_maximum_fusion.9), channel_id=1, source_target_pairs={{0,4},{4,0},{8,12},{12,8},{16,20},{20,16},{24,28},{28,24},{1,5},{5... | collective-permute-start | bytes 198152 | tf_op jit(solution)/shard_map/ppermute | solution.py:38
  28.2 0.9 %collective-permute-done.4 = f32[129,128]{1,0:T(8,128)S(1)} collective-permute-done((f32[129,128]{1,0:T(8,128)S(1)}, f32[129,128]{1,0:T(8,128)S(1)}, u32[]{:S(2)}, u32[]{:S(2)}) %collective-permute-start.4) | collective-permute-done | bytes 66080 | tf_op jit(solution)/shard_map/ppermute | solution.py:38
  29.1 2.5 %collective-permute-start.5 = (f32[129,128]{1,0:T(8,128)S(1)}, f32[129,128]{1,0:T(8,128)S(1)}, u32[]{:S(2)}, u32[]{:S(2)}) collective-permute-start(f32[129,128]{1,0:T(8,128)S(1)} %fusion.43), channel_id=1, source_target_pairs={{0,8},{4,12},{8,0},{12,4},{16,24},{20,28},{24,16},{28,20},{1,9},{5... | collective-permute-start | bytes 198152 | tf_op jit(solution)/shard_map/ppermute | solution.py:38
  31.5 2.7 %collective-permute-done.5 = f32[129,128]{1,0:T(8,128)S(1)} collective-permute-done((f32[129,128]{1,0:T(8,128)S(1)}, f32[129,128]{1,0:T(8,128)S(1)}, u32[]{:S(2)}, u32[]{:S(2)}) %collective-permute-start.5) | collective-permute-done | bytes 66080 | tf_op jit(solution)/shard_map/ppermute | solution.py:38
  34.3 1.4 %collective-permute-start.6 = (f32[129,128]{1,0:T(8,128)S(1)}, f32[129,128]{1,0:T(8,128)S(1)}, u32[]{:S(2)}, u32[]{:S(2)}) collective-permute-start(f32[129,128]{1,0:T(8,128)S(1)} %add.88), channel_id=1, source_target_pairs={{0,16},{4,20},{8,24},{12,28},{16,0},{20,4},{24,8},{28,12},{1,17},{... | collective-permute-start | bytes 198152 | tf_op jit(solution)/shard_map/ppermute | solution.py:38
  35.7 3.0 %collective-permute-done.6 = f32[129,128]{1,0:T(8,128)S(1)} collective-permute-done((f32[129,128]{1,0:T(8,128)S(1)}, f32[129,128]{1,0:T(8,128)S(1)}, u32[]{:S(2)}, u32[]{:S(2)}) %collective-permute-start.6) | collective-permute-done | bytes 66080 | tf_op jit(solution)/shard_map/ppermute | solution.py:38
  38.6 2.1 %collective-permute-start.7 = (f32[129,128]{1,0:T(8,128)S(1)}, f32[129,128]{1,0:T(8,128)S(1)}, u32[]{:S(2)}, u32[]{:S(2)}) collective-permute-start(f32[129,128]{1,0:T(8,128)S(1)} %add.89), channel_id=1, source_target_pairs={{0,1},{1,0},{2,3},{3,2},{4,5},{5,4},{6,7},{7,6},{8,9},{9,8},{10,11... | collective-permute-start | bytes 198152 | tf_op jit(solution)/shard_map/ppermute | solution.py:38
  40.7 2.3 %collective-permute-done.7 = f32[129,128]{1,0:T(8,128)S(1)} collective-permute-done((f32[129,128]{1,0:T(8,128)S(1)}, f32[129,128]{1,0:T(8,128)S(1)}, u32[]{:S(2)}, u32[]{:S(2)}) %collective-permute-start.7) | collective-permute-done | bytes 66080 | tf_op jit(solution)/shard_map/ppermute | solution.py:38
  43.0 3.1 %collective-permute-start.8 = (f32[129,128]{1,0:T(8,128)S(1)}, f32[129,128]{1,0:T(8,128)S(1)}, u32[]{:S(2)}, u32[]{:S(2)}) collective-permute-start(f32[129,128]{1,0:T(8,128)S(1)} %add.90), channel_id=1, source_target_pairs={{0,2},{1,3},{2,0},{3,1},{4,6},{5,7},{6,4},{7,5},{8,10},{9,11},{10,... | collective-permute-start | bytes 198152 | tf_op jit(solution)/shard_map/ppermute | solution.py:38
  46.1 2.3 %collective-permute-done.8 = f32[129,128]{1,0:T(8,128)S(1)} collective-permute-done((f32[129,128]{1,0:T(8,128)S(1)}, f32[129,128]{1,0:T(8,128)S(1)}, u32[]{:S(2)}, u32[]{:S(2)}) %collective-permute-start.8) | collective-permute-done | bytes 66080 | tf_op jit(solution)/shard_map/ppermute | solution.py:38
  48.4 0.6 add.91.stacked_ref
  49.1 10.9 %shard_map.68 = f32[128,128]{1,0:T(8,128)} custom-call(f32[129,128]{1,0:T(8,128)} %add.91.stacked_ref), custom_call_target="tpu_custom_call" | custom-call | tf_op jit(solution)/shard_map/pallas_call | solution.py:104
  60.0 1.9 %fusion.2 = f32[128,16,128]{0,2,1:T(8,128)S(1)} fusion(f32[128,16]{0,1:T(8,128)S(1)} %get-tuple-element.22, f32[16,128]{1,0:T(8,128)S(1)} %get-tuple-element.21, f32[128,128]{1,0:T(8,128)} %shard_map.68, f32[128,16,128]{0,2,1:T(8,128)S(1)} %copy.14), kind=kOutput, calls=%fused_computation.4 | convolution fusion | flops 403177472 | bytes 2179072 | tf_op jit(solution)/shard_map/dot_general | solution.py:239
  61.9 0.0 copy-start.1
  61.9 1.4 %copy.27 = f32[128,16,128]{2,1,0:T(8,128)} copy(f32[128,16,128]{0,2,1:T(8,128)S(1)} %fusion.2) | data formatting | bytes 2097152
  63.3 0.0 copy-done.1
  63.3 1.0 %fusion.3 = f32[128,16,128]{0,2,1:T(8,128)S(1)} fusion(f32[128,16,128]{2,0,1:T(8,128)S(1)} %get-tuple-element.7, f32[128,16]{0,1:T(8,128)S(1)} %get-tuple-element.20, f32[16,128]{1,0:T(8,128)S(1)} %get-tuple-element.19, f32[128,128]{1,0:T(8,128)S(1)} %copy-done.1), kind=kOutput, calls=%fused_computation.6 | convolution fusion | flops 403177472 | bytes 2179072 | tf_op jit(solution)/shard_map/dot_general | solution.py:236
  64.3 1.4 %copy.26 = f32[128,16,128]{2,1,0:T(8,128)} copy(f32[128,16,128]{0,2,1:T(8,128)S(1)} %fusion.3) | data formatting | bytes 2097152
  (37 shorter events, 0.4 us)
Async XLA Ops:
  0.6 1.7 %copy-start = (f32[128,16,128]{2,1,0:T(8,128)S(1)}, f32[128,16,128]{2,1,0:T(8,128)}, u32[]{:S(2)}) copy-start(f32[128,16,128]{2,1,0:T(8,128)} %param.5) | copy-start | bytes 3145732
  2.3 4.2 %copy-start.2 = (s32[1024]{0:T(1024)S(1)}, s32[1024]{0:T(1024)}, u32[]{:S(2)}) copy-start(s32[1024]{0:T(1024)} %param.9) | copy-start | bytes 12292
  2.4 4.3 %copy-start.3 = (f32[1024]{0:T(1024)S(1)}, f32[1024]{0:T(1024)}, u32[]{:S(2)}) copy-start(f32[1024]{0:T(1024)} %param.8) | copy-start | bytes 12292
  2.4 4.3 %copy-start.4 = (f32[1024]{0:T(1024)S(1)}, f32[1024]{0:T(1024)}, u32[]{:S(2)}) copy-start(f32[1024]{0:T(1024)} %param.7) | copy-start | bytes 12292
  2.9 4.2 %collective-permute-start = (f32[128,3,128]{2,0,1:T(8,128)S(1)}, f32[128,3,128]{2,0,1:T(8,128)S(1)}, u32[]{:S(2)}, u32[]{:S(2)}) collective-permute-start(f32[128,3,128]{2,0,1:T(8,128)S(1)} %pad_maximum_fusion.7), channel_id=1, source_target_pairs={{0,4},{4,8},{8,12},{12,16},{16,20},{20,24},{24,28},{1,5},{5,9},{9,... | collective-permute-start | bytes 589832 | tf_op jit(solution)/shard_map/ppermute | solution.py:140
  5.3 5.4 %collective-permute-start.1 = (f32[128,3,128]{2,0,1:T(8,128)S(1)}, f32[128,3,128]{2,0,1:T(8,128)S(1)}, u32[]{:S(2)}, u32[]{:S(2)}) collective-permute-start(f32[128,3,128]{2,0,1:T(8,128)S(1)} %pad_maximum_fusion.8), channel_id=1, source_target_pairs={{4,0},{8,4},{12,8},{16,12},{20,16},{24,20},{28,24},{5,1},{9,5},{13... | collective-permute-start | bytes 589832 | tf_op jit(solution)/shard_map/ppermute | solution.py:140
  10.8 6.0 %collective-permute-start.3 = (f32[3,20,128]{2,1,0:T(8,128)S(1)}, f32[3,20,128]{2,1,0:T(8,128)S(1)}, u32[]{:S(2)}, u32[]{:S(2)}) collective-permute-start(f32[3,20,128]{2,1,0:T(8,128)S(1)} %pad_maximum_fusion.11), channel_id=1, source_target_pairs={{1,0},{2,1},{3,2},{5,4},{6,5},{7,6},{9,8},{10,9},{11,10},{13,12},{... | collective-permute-start | bytes 92168 | tf_op jit(solution)/shard_map/ppermute | solution.py:140
  12.2 6.2 %collective-permute-start.2 = (f32[3,20,128]{2,1,0:T(8,128)S(1)}, f32[3,20,128]{2,1,0:T(8,128)S(1)}, u32[]{:S(2)}, u32[]{:S(2)}) collective-permute-start(f32[3,20,128]{2,1,0:T(8,128)S(1)} %pad_maximum_fusion.10), channel_id=1, source_target_pairs={{0,1},{1,2},{2,3},{4,5},{5,6},{6,7},{8,9},{9,10},{10,11},{12,13},{... | collective-permute-start | bytes 92168 | tf_op jit(solution)/shard_map/ppermute | solution.py:140
  25.1 4.0 %collective-permute-start.4 = (f32[129,128]{1,0:T(8,128)S(1)}, f32[129,128]{1,0:T(8,128)S(1)}, u32[]{:S(2)}, u32[]{:S(2)}) collective-permute-start(f32[129,128]{1,0:T(8,128)S(1)} %pad_maximum_fusion.9), channel_id=1, source_target_pairs={{0,4},{4,0},{8,12},{12,8},{16,20},{20,16},{24,28},{28,24},{1,5},{5... | collective-permute-start | bytes 198152 | tf_op jit(solution)/shard_map/ppermute | solution.py:38
  29.1 5.2 %collective-permute-start.5 = (f32[129,128]{1,0:T(8,128)S(1)}, f32[129,128]{1,0:T(8,128)S(1)}, u32[]{:S(2)}, u32[]{:S(2)}) collective-permute-start(f32[129,128]{1,0:T(8,128)S(1)} %fusion.43), channel_id=1, source_target_pairs={{0,8},{4,12},{8,0},{12,4},{16,24},{20,28},{24,16},{28,20},{1,9},{5... | collective-permute-start | bytes 198152 | tf_op jit(solution)/shard_map/ppermute | solution.py:38
  34.3 4.4 %collective-permute-start.6 = (f32[129,128]{1,0:T(8,128)S(1)}, f32[129,128]{1,0:T(8,128)S(1)}, u32[]{:S(2)}, u32[]{:S(2)}) collective-permute-start(f32[129,128]{1,0:T(8,128)S(1)} %add.88), channel_id=1, source_target_pairs={{0,16},{4,20},{8,24},{12,28},{16,0},{20,4},{24,8},{28,12},{1,17},{... | collective-permute-start | bytes 198152 | tf_op jit(solution)/shard_map/ppermute | solution.py:38
  38.6 4.4 %collective-permute-start.7 = (f32[129,128]{1,0:T(8,128)S(1)}, f32[129,128]{1,0:T(8,128)S(1)}, u32[]{:S(2)}, u32[]{:S(2)}) collective-permute-start(f32[129,128]{1,0:T(8,128)S(1)} %add.89), channel_id=1, source_target_pairs={{0,1},{1,0},{2,3},{3,2},{4,5},{5,4},{6,7},{7,6},{8,9},{9,8},{10,11... | collective-permute-start | bytes 198152 | tf_op jit(solution)/shard_map/ppermute | solution.py:38
  43.0 5.4 %collective-permute-start.8 = (f32[129,128]{1,0:T(8,128)S(1)}, f32[129,128]{1,0:T(8,128)S(1)}, u32[]{:S(2)}, u32[]{:S(2)}) collective-permute-start(f32[129,128]{1,0:T(8,128)S(1)} %add.90), channel_id=1, source_target_pairs={{0,2},{1,3},{2,0},{3,1},{4,6},{5,7},{6,4},{7,5},{8,10},{9,11},{10,... | collective-permute-start | bytes 198152 | tf_op jit(solution)/shard_map/ppermute | solution.py:38
  61.9 1.4 %copy-start.1 = (f32[128,128]{1,0:T(8,128)S(1)}, f32[128,128]{1,0:T(8,128)}, u32[]{:S(2)}) copy-start(f32[128,128]{1,0:T(8,128)} %shard_map.68) | copy-start | bytes 196612

commit v19 on v16

--- a/solution.py
+++ b/solution.py
@@ -134,7 +134,7 @@
     return lax.ppermute(block, axis, pairs)
 
 
-def forecast_two_steps(warmth, heat):
+def forecast_in_pieces(warmth, heat):
     width, height = warmth.shape[0], warmth.shape[1]
     top = from_neighbour(
         jnp.concatenate([warmth[:, -2:], heat[:, -1:]], axis=1), "gx", 1
@@ -161,20 +161,35 @@
         "gy",
         -1,
     )
-    warmth_wide = jnp.concatenate([left[:2], warmth_tall, right[:2]], axis=0)
-    heat_wide = jnp.concatenate([left[2:, 1:-1], heat_tall, right[2:, 1:-1]], axis=0)
-    first = propagate_members_last(warmth_wide, heat_wide)
-    col = lax.broadcasted_iota(jnp.int32, (width + 2, height + 2), 0)
-    row = lax.broadcasted_iota(jnp.int32, (width + 2, height + 2), 1)
     at_x, at_y = lax.axis_index("gx"), lax.axis_index("gy")
-    outside = (
-        ((row == 0) & (at_x == 0))
-        | ((row == height + 1) & (at_x == lax.axis_size("gx") - 1))
-        | ((col == 0) & (at_y == 0))
-        | ((col == width + 1) & (at_y == lax.axis_size("gy") - 1))
-    )
-    first = jnp.where(outside[:, :, None], 0.0, first)
-    return propagate_members_last(first, heat)
+    row = lax.broadcasted_iota(jnp.int32, (1, height + 2, 1), 1)
+    off_grid = ((row == 0) & (at_x == 0)) | (
+        (row == height + 1) & (at_x == lax.axis_size("gx") - 1)
+    )
+    first_inner = jnp.where(
+        off_grid, 0.0, propagate_members_last(warmth_tall, heat_tall[1:-1])
+    )
+    second_inner = propagate_members_last(first_inner, heat[2:-2])
+    first_left = propagate_members_last(
+        jnp.concatenate([left[:2], warmth_tall[:2]], axis=0),
+        jnp.concatenate([left[2:, 1:-1], heat_tall[:1]], axis=0),
+    )
+    first_right = propagate_members_last(
+        jnp.concatenate([warmth_tall[-2:], right[:2]], axis=0),
+        jnp.concatenate([heat_tall[-1:], right[2:, 1:-1]], axis=0),
+    )
+    col = lax.broadcasted_iota(jnp.int32, (2, 1, 1), 0)
+    first_left = jnp.where(off_grid | ((col == 0) & (at_y == 0)), 0.0, first_left)
+    first_right = jnp.where(
+        off_grid | ((col == 1) & (at_y == lax.axis_size("gy") - 1)), 0.0, first_right
+    )
+    second_left = propagate_members_last(
+        jnp.concatenate([first_left, first_inner[:2]], axis=0), heat[:2]
+    )
+    second_right = propagate_members_last(
+        jnp.concatenate([first_inner[-2:], first_right], axis=0), heat[-2:]
+    )
+    return [(0, second_left), (2, second_inner), (width - 2, second_right)]
 
 
 def shards(
@@ -187,10 +202,8 @@
     sample_number, block_height_number, block_width_number = prior_gas_warmth.shape
     warmth_t = jnp.transpose(prior_gas_warmth, (2, 1, 0))
     heat_t = jnp.transpose(fire_power_output, (2, 1, 0))
-    predicted_t = forecast_two_steps(warmth_t, heat_t)
-    average_t = jnp.mean(predicted_t, axis=2)
+    pieces = forecast_in_pieces(warmth_t, heat_t)
     mean_heat_t = jnp.mean(heat_t, axis=2)
-    deviation_t = predicted_t - average_t[:, :, None]
     heat_anomaly_t = heat_t - mean_heat_t[:, :, None]
     coefficient_line = 1.0 / (reading_noise_spread * math.sqrt(sample_number - 1))
     weight_line = coefficient_line * coefficient_line
@@ -209,20 +222,29 @@
     cell_sums = lax.dot_general(
         col_hot, weighted_rows, (((0,), (0,)), ((), ())), precision=lax.Precision.HIGHEST
     )
-    cell_weight = cell_sums[:, :block_height_number]
-    cell_residual = cell_sums[:, block_height_number:] - average_t * cell_weight
-    gram_local = lax.dot_general(
-        deviation_t * cell_weight[:, :, None],
-        deviation_t,
-        (((0, 1), (0, 1)), ((), ())),
-        precision=lax.Precision.HIGHEST,
-    )
-    projected = lax.dot_general(
-        deviation_t,
-        cell_residual,
-        (((0, 1), (0, 1)), ((), ())),
-        precision=lax.Precision.HIGHEST,
-    )
+    averages, deviations, gram_local, projected = [], [], 0.0, 0.0
+    for start, piece in pieces:
+        count = piece.shape[0]
+        average = jnp.mean(piece, axis=2)
+        deviation = piece - average[:, :, None]
+        cell_weight = cell_sums[start : start + count, :block_height_number]
+        cell_residual = cell_sums[start : start + count, block_height_number:] - average * cell_weight
+        gram_local = gram_local + lax.dot_general(
+            deviation * cell_weight[:, :, None],
+            deviation,
+            (((0, 1), (0, 1)), ((), ())),
+            precision=lax.Precision.HIGHEST,
+        )
+        projected = projected + lax.dot_general(
+            deviation,
+            cell_residual,
+            (((0, 1), (0, 1)), ((), ())),
+            precision=lax.Precision.HIGHEST,
+        )
+        averages.append(average)
+        deviations.append(deviation)
+    average_t = jnp.concatenate(averages, axis=0)
+    deviation_t = jnp.concatenate(deviations, axis=0)
     combination_transposed = combination_transposed_of(
         butterfly_sum(jnp.concatenate([gram_local, projected[None, :]], axis=0), ("gx", "gy"))
     )

time: 64.9 us -> 63.8 us (0.983)
  waiting for transfers between devices: 16.2 us -> 11.8 us
  starting transfers between devices: 21.7 us -> 24.7 us
    ppermute x4, waiting for transfers between devices: 5.09 us -> 1.49 us  [from_neighbour(): return lax.ppermute(block, axis, pairs)]
    ppermute x5, starting transfers between devices: 12.1 us -> 13.9 us  [butterfly_sum(): received[offset] = lax.ppermute(value, axis, pairs)]
    ppermute x4, starting transfers between devices: 9.5 us -> 10.7 us  [from_neighbour(): return lax.ppermute(block, axis, pairs)]
    select_n x1 -> x3, other arithmetic: 2.12 us -> 0.95 us  [the longest x1 0.77 us: forecast_in_pieces(): jnp.where(off_grid, 0.0, propagate_members_last(warmth_tall, heat_tall[1:...]
    dot_general x1, matrix products: 1.03 us -> 1.91 us  [shards(): lax.dot_general(deviation_t, combination_transposed, contract, precision=...]
    ppermute x5, waiting for transfers between devices: 11.1 us -> 10.3 us  [butterfly_sum(): received[offset] = lax.ppermute(value, axis, pairs)]
    dot_general x1, matrix products: 1.86 us -> 1.03 us  [shards(): lax.dot_general(heat_anomaly_t, combination_transposed, contract, precisi...]
    dot_general x2 -> x6, matrix products: 3.49 us -> 3.86 us  [the longest x3 2.76 us: shards(): lax.dot_general(deviation * cell_weight[:, :, None], deviation, (((0, 1),...]
  transfers between devices with their start and end apart: 9 -> 9, of which waited for: 7 -> 7; matrix products, arithmetic and copies ran while one was open for 1% -> 7% of each run, Pallas kernels for 0% -> 0%
where the time goes in v19:
time: 63.8 us; the launch traced here: 63.4 us
  starting transfers between devices  24.7 us (39%)
  waiting for transfers between devices  11.8 us (18%)
  Pallas kernels  9.64 us (15%)
  matrix products  7.18 us (11%)
  local copies, waits for them, and re-layouts  5.16 us (8%)
  other arithmetic  3.96 us (6%)
  between operations  1.02 us (2%)
    ppermute x5, starting transfers between devices, butterfly_sum(): received[offset] = lax.ppermute(value, axis, pairs)  13.9 us
    ppermute x4, starting transfers between devices, from_neighbour(): return lax.ppermute(block, axis, pairs)  10.7 us
    ppermute x5, waiting for transfers between devices, butterfly_sum(): received[offset] = lax.ppermute(value, axis, pairs)  10.3 us
    pallas_call x1, Pallas kernels, combination_transposed_of(): pl.pallas_call(combination_kernel, out_shape=jax.ShapeDtypeStruct((size,...  9.64 us
    unnamed x14, local copies, waits for them, and re-layouts  4.87 us
    dot_general x3, matrix products, shards(): lax.dot_general(deviation * cell_weight[:, :, None], deviation, (((0, 1),...  2.76 us
    dot_general x1, matrix products, shards(): lax.dot_general(deviation_t, combination_transposed, contract, precision=...  1.91 us
    ppermute x4, waiting for transfers between devices, from_neighbour(): return lax.ppermute(block, axis, pairs)  1.49 us
  transfers between devices with their start and end apart: 9, of which 7 were waited for; matrix products, arithmetic and copies ran while one was open for 7% of the time, Pallas kernels for 0%

profile of v19, /device:TPU:0, one launch (start us, length us, event | category | flops | bytes accessed | tf_op | source)
XLA Modules:
  0.0 63.4 jit_solution(12685963103037000633)
XLA Ops:
  0.6 0.0 copy-start
  0.6 1.7 %copy.17 = f32[128,16,128]{0,2,1:T(8,128)S(1)} copy(f32[128,16,128]{2,1,0:T(8,128)} %param.6) | data formatting | bytes 2097152 | tf_op args[1]
  2.3 0.0 copy-done
  2.3 0.4 copy.16
  2.8 0.0 copy-start.2
  2.8 0.0 copy-start.3
  2.8 0.0 copy-start.4
  2.9 1.3 %collective-permute-start.1 = (f32[128,3,128]{2,0,1:T(8,128)S(1)}, f32[128,3,128]{2,0,1:T(8,128)S(1)}, u32[]{:S(2)}, u32[]{:S(2)}) collective-permute-start(f32[128,3,128]{2,0,1:T(8,128)S(1)} %pad_maximum_fusion.6), channel_id=1, source_target_pairs={{4,0},{8,4},{12,8},{16,12},{20,16},{24,20},{28,24},{5,1},{9,5},{13... | collective-permute-start | bytes 589832 | tf_op jit(solution)/shard_map/ppermute | solution.py:134
  4.2 3.0 %collective-permute-start = (f32[128,3,128]{2,0,1:T(8,128)S(1)}, f32[128,3,128]{2,0,1:T(8,128)S(1)}, u32[]{:S(2)}, u32[]{:S(2)}) collective-permute-start(f32[128,3,128]{2,0,1:T(8,128)S(1)} %pad_maximum_fusion.5), channel_id=1, source_target_pairs={{0,4},{4,8},{8,12},{12,16},{16,20},{20,24},{24,28},{1,5},{5,9},{9,... | collective-permute-start | bytes 589832 | tf_op jit(solution)/shard_map/ppermute | solution.py:134
  7.2 0.0 copy-done.2
  7.3 0.0 copy-done.3
  7.3 0.0 copy-done.4
  7.4 0.4 fusion.31
  7.8 0.1 broadcast_or_fusion.1
  7.8 0.0 collective-permute-done.1
  7.8 0.4 collective-permute-done
  8.3 0.1 pad_maximum_fusion
  8.5 0.8 %fusion.6 = f32[126,18,128]{2,0,1:T(8,128)S(1)} fusion(f32[128,1,128]{2,0,1:T(8,128)S(1)} %slice.257, f32[128,16,128]{2,0,1:T(8,128)S(1)} %bitcast.68, f32[128,1,128]{2,0,1:T(8,128)S(1)} %slice.256, f32[128,20,128]{2,0,1:T(8,128)S(1)} %pad_maximum_fusion, f32[128,16,128]{2,0,1:T(8,128)S(1)} %bitcast.63, f32[128,2,128]{2,0,1:T(8,128)S(1)} %slice.252, ...), kind=kLoop, calls=%fused_computation.10 | loop fusion | flops 4064256 | bytes 7135250 | tf_op jit(solution)/shard_map/jit(_where)/select_n | solution.py:169
  9.3 0.7 %fusion.90 = (f32[124,16]{0,1:T(8,128)S(1)}, f32[124,16,128]{2,0,1:T(8,128)S(1)}) fusion(f32[128,16,128]{2,0,1:T(8,128)S(1)} %bitcast.69, f32[126,18,128]{2,0,1:T(8,128)S(1)} %fusion.6), kind=kLoop, calls=%fused_computation.168 | loop fusion | flops 2537536 | bytes 7118592 | tf_op jit(solution)/shard_map/reduce_sum | solution.py:228
  10.0 4.9 %collective-permute-start.2 = (f32[3,20,128]{2,0,1:T(4,128)S(1)}, f32[3,20,128]{2,0,1:T(4,128)S(1)}, u32[]{:S(2)}, u32[]{:S(2)}) collective-permute-start(f32[3,20,128]{2,0,1:T(4,128)S(1)} %get-tuple-element.47), channel_id=1, source_target_pairs={{0,1},{1,2},{2,3},{4,5},{5,6},{6,7},{8,9},{9,10},{10,11},{12,13},{... | collective-permute-start | bytes 92168 | tf_op jit(solution)/shard_map/ppermute | solution.py:134
  15.0 1.5 %collective-permute-start.3 = (f32[3,20,128]{2,0,1:T(4,128)S(1)}, f32[3,20,128]{2,0,1:T(4,128)S(1)}, u32[]{:S(2)}, u32[]{:S(2)}) collective-permute-start(f32[3,20,128]{2,0,1:T(4,128)S(1)} %get-tuple-element.48), channel_id=1, source_target_pairs={{1,0},{2,1},{3,2},{5,4},{6,5},{7,6},{9,8},{10,9},{11,10},{13,12},{... | collective-permute-start | bytes 92168 | tf_op jit(solution)/shard_map/ppermute | solution.py:134
  16.4 0.1 fusion.97
  16.5 0.3 broadcast_subtract_fusion
  16.9 2.2 %fusion.11 = f32[128,128]{1,0:T(8,128)S(1)} fusion(f32[124,16,128]{2,0,1:T(8,128)S(1)} %broadcast_subtract_fusion, f32[124,16]{0,1:T(8,128)S(1)} %get-tuple-element.28), kind=kOutput, calls=%fused_computation.20 | convolution fusion | flops 390324224 | bytes 1089280 | tf_op jit(solution)/shard_map/dot_general | solution.py:232
  19.0 0.7 %convolution_bitcast_fusion.5 = f32[128]{0:T(128)S(1)} fusion(f32[124,16,128]{2,0,1:T(8,128)S(1)} %broadcast_subtract_fusion, f32[124,16,1]{0,2,1:T(1,128)S(1)} %bitcast.71), kind=kOutput, calls=%fused_computation.26 | convolution fusion | flops 3047424 | bytes 1024256 | tf_op jit(solution)/shard_map/dot_general | solution.py:238
  19.7 0.0 collective-permute-done.2
  19.8 1.1 %collective-permute-done.3 = f32[3,20,128]{2,0,1:T(4,128)S(1)} collective-permute-done((f32[3,20,128]{2,0,1:T(4,128)S(1)}, f32[3,20,128]{2,0,1:T(4,128)S(1)}, u32[]{:S(2)}, u32[]{:S(2)}) %collective-permute-start.3) | collective-permute-done | bytes 30752 | tf_op jit(solution)/shard_map/ppermute | solution.py:134
  20.9 0.1 fusion.55
  21.0 0.1 fusion.57
  21.1 0.2 fusion.88
  21.3 0.1 fusion.79
  21.3 0.1 copy.26
  21.4 0.1 copy.28
  21.5 0.1 broadcast_multiply_fusion
  21.6 0.2 convolution_bitcast_fusion.4
  21.8 0.3 convolution_bitcast_fusion.2
  22.1 0.1 broadcast_multiply_fusion.1
  22.2 0.2 fusion.18
  22.4 0.3 fusion.15
  22.7 1.4 %collective-permute-start.4 = (f32[129,128]{1,0:T(8,128)S(1)}, f32[129,128]{1,0:T(8,128)S(1)}, u32[]{:S(2)}, u32[]{:S(2)}) collective-permute-start(f32[129,128]{1,0:T(8,128)S(1)} %pad_maximum_fusion.7), channel_id=1, source_target_pairs={{0,4},{4,0},{8,12},{12,8},{16,20},{20,16},{24,28},{28,24},{1,5},{5... | collective-permute-start | bytes 198152 | tf_op jit(solution)/shard_map/ppermute | solution.py:38
  24.1 0.9 %collective-permute-done.4 = f32[129,128]{1,0:T(8,128)S(1)} collective-permute-done((f32[129,128]{1,0:T(8,128)S(1)}, f32[129,128]{1,0:T(8,128)S(1)}, u32[]{:S(2)}, u32[]{:S(2)}) %collective-permute-start.4) | collective-permute-done | bytes 66080 | tf_op jit(solution)/shard_map/ppermute | solution.py:38
  25.0 4.1 %collective-permute-start.5 = (f32[129,128]{1,0:T(8,128)S(1)}, f32[129,128]{1,0:T(8,128)S(1)}, u32[]{:S(2)}, u32[]{:S(2)}) collective-permute-start(f32[129,128]{1,0:T(8,128)S(1)} %fusion.87), channel_id=1, source_target_pairs={{0,8},{4,12},{8,0},{12,4},{16,24},{20,28},{24,16},{28,20},{1,9},{5... | collective-permute-start | bytes 198152 | tf_op jit(solution)/shard_map/ppermute | solution.py:38
  29.1 2.5 %collective-permute-done.5 = f32[129,128]{1,0:T(8,128)S(1)} collective-permute-done((f32[129,128]{1,0:T(8,128)S(1)}, f32[129,128]{1,0:T(8,128)S(1)}, u32[]{:S(2)}, u32[]{:S(2)}) %collective-permute-start.5) | collective-permute-done | bytes 66080 | tf_op jit(solution)/shard_map/ppermute | solution.py:38
  31.7 3.7 %collective-permute-start.6 = (f32[129,128]{1,0:T(8,128)S(1)}, f32[129,128]{1,0:T(8,128)S(1)}, u32[]{:S(2)}, u32[]{:S(2)}) collective-permute-start(f32[129,128]{1,0:T(8,128)S(1)} %add.184), channel_id=1, source_target_pairs={{0,16},{4,20},{8,24},{12,28},{16,0},{20,4},{24,8},{28,12},{1,17},{... | collective-permute-start | bytes 198152 | tf_op jit(solution)/shard_map/ppermute | solution.py:38
  35.3 0.3 bitcast_reduce_fusion
  35.7 1.9 %collective-permute-done.6 = f32[129,128]{1,0:T(8,128)S(1)} collective-permute-done((f32[129,128]{1,0:T(8,128)S(1)}, f32[129,128]{1,0:T(8,128)S(1)}, u32[]{:S(2)}, u32[]{:S(2)}) %collective-permute-start.6) | collective-permute-done | bytes 66080 | tf_op jit(solution)/shard_map/ppermute | solution.py:38
  37.6 1.7 %collective-permute-start.7 = (f32[129,128]{1,0:T(8,128)S(1)}, f32[129,128]{1,0:T(8,128)S(1)}, u32[]{:S(2)}, u32[]{:S(2)}) collective-permute-start(f32[129,128]{1,0:T(8,128)S(1)} %add.185), channel_id=1, source_target_pairs={{0,1},{1,0},{2,3},{3,2},{4,5},{5,4},{6,7},{7,6},{8,9},{9,8},{10,11... | collective-permute-start | bytes 198152 | tf_op jit(solution)/shard_map/ppermute | solution.py:38
  39.3 2.7 %collective-permute-done.7 = f32[129,128]{1,0:T(8,128)S(1)} collective-permute-done((f32[129,128]{1,0:T(8,128)S(1)}, f32[129,128]{1,0:T(8,128)S(1)}, u32[]{:S(2)}, u32[]{:S(2)}) %collective-permute-start.7) | collective-permute-done | bytes 66080 | tf_op jit(solution)/shard_map/ppermute | solution.py:38
  42.0 3.1 %collective-permute-start.8 = (f32[129,128]{1,0:T(8,128)S(1)}, f32[129,128]{1,0:T(8,128)S(1)}, u32[]{:S(2)}, u32[]{:S(2)}) collective-permute-start(f32[129,128]{1,0:T(8,128)S(1)} %add.186), channel_id=1, source_target_pairs={{0,2},{1,3},{2,0},{3,1},{4,6},{5,7},{6,4},{7,5},{8,10},{9,11},{10,... | collective-permute-start | bytes 198152 | tf_op jit(solution)/shard_map/ppermute | solution.py:38
  45.1 0.1 maximum_bitcast_fusion
  45.2 2.2 %collective-permute-done.8 = f32[129,128]{1,0:T(8,128)S(1)} collective-permute-done((f32[129,128]{1,0:T(8,128)S(1)}, f32[129,128]{1,0:T(8,128)S(1)}, u32[]{:S(2)}, u32[]{:S(2)}) %collective-permute-start.8) | collective-permute-done | bytes 66080 | tf_op jit(solution)/shard_map/ppermute | solution.py:38
  47.4 0.6 %add.187.stacked_ref = f32[129,128]{1,0:T(8,128)} add(f32[129,128]{1,0:T(8,128)S(1)} %add.186, f32[129,128]{1,0:T(8,128)S(1)} %collective-permute-done.8) | non-fusion elementwise | flops 16512 | bytes 198144 | tf_op jit(solution)/shard_map/add | solution.py:17
  48.1 9.6 %shard_map.68 = f32[128,128]{1,0:T(8,128)} custom-call(f32[129,128]{1,0:T(8,128)} %add.187.stacked_ref), custom_call_target="tpu_custom_call" | custom-call | tf_op jit(solution)/shard_map/pallas_call | solution.py:98
  57.7 0.0 copy-start.1
  57.7 1.9 %fusion.3 = f32[128,16,128]{0,2,1:T(8,128)S(1)} fusion(f32[2,16,128]{2,0,1:T(2,128)S(1)} %get-tuple-element.9, f32[124,16,128]{2,0,1:T(8,128)S(1)} %broadcast_subtract_fusion, f32[2,16,128]{2,0,1:T(2,128)S(1)} %get-tuple-element.7, f32[16,128]{1,0:T(8,128)S(1)} %maximum_bitcast_fusion, f32[128,128]{1,0:T(8,128)} %shard_map.68), kind=kOutput, calls=%fused_computation.5 | convolution fusion | flops 403439616 | bytes 2170880 | tf_op jit(solution)/shard_map/dot_general | solution.py:252
  59.6 0.0 copy-done.1
  59.6 1.0 %fusion.2 = f32[128,16,128]{0,2,1:T(8,128)S(1)} fusion(f32[128,16]{0,1:T(8,128)S(1)} %get-tuple-element.37, f32[16,128]{1,0:T(8,128)S(1)} %get-tuple-element.36, f32[128,128]{1,0:T(8,128)S(1)} %copy-done.1, f32[128,16,128]{0,2,1:T(8,128)S(1)} %copy.17), kind=kOutput, calls=%fused_computation.3 | convolution fusion | flops 403177472 | bytes 2179072 | tf_op jit(solution)/shard_map/dot_general | solution.py:255
  60.7 1.4 %copy.24 = f32[128,16,128]{2,1,0:T(8,128)} copy(f32[128,16,128]{0,2,1:T(8,128)S(1)} %fusion.2) | data formatting | bytes 2097152
  62.0 1.4 %copy.23 = f32[128,16,128]{2,1,0:T(8,128)} copy(f32[128,16,128]{0,2,1:T(8,128)S(1)} %fusion.3) | data formatting | bytes 2097152
  (28 shorter events, 0.3 us)
Async XLA Ops:
  0.6 1.7 %copy-start = (f32[128,16,128]{2,1,0:T(8,128)S(1)}, f32[128,16,128]{2,1,0:T(8,128)}, u32[]{:S(2)}) copy-start(f32[128,16,128]{2,1,0:T(8,128)} %param.5) | copy-start | bytes 3145732
  2.8 4.5 %copy-start.2 = (s32[1024]{0:T(1024)S(1)}, s32[1024]{0:T(1024)}, u32[]{:S(2)}) copy-start(s32[1024]{0:T(1024)} %param.9) | copy-start | bytes 12292
  2.8 4.5 %copy-start.3 = (f32[1024]{0:T(1024)S(1)}, f32[1024]{0:T(1024)}, u32[]{:S(2)}) copy-start(f32[1024]{0:T(1024)} %param.8) | copy-start | bytes 12292
  2.8 4.5 %copy-start.4 = (f32[1024]{0:T(1024)S(1)}, f32[1024]{0:T(1024)}, u32[]{:S(2)}) copy-start(f32[1024]{0:T(1024)} %param.7) | copy-start | bytes 12292
  2.9 5.0 %collective-permute-start.1 = (f32[128,3,128]{2,0,1:T(8,128)S(1)}, f32[128,3,128]{2,0,1:T(8,128)S(1)}, u32[]{:S(2)}, u32[]{:S(2)}) collective-permute-start(f32[128,3,128]{2,0,1:T(8,128)S(1)} %pad_maximum_fusion.6), channel_id=1, source_target_pairs={{4,0},{8,4},{12,8},{16,12},{20,16},{24,20},{28,24},{5,1},{9,5},{13... | collective-permute-start | bytes 589832 | tf_op jit(solution)/shard_map/ppermute | solution.py:134
  4.2 4.1 %collective-permute-start = (f32[128,3,128]{2,0,1:T(8,128)S(1)}, f32[128,3,128]{2,0,1:T(8,128)S(1)}, u32[]{:S(2)}, u32[]{:S(2)}) collective-permute-start(f32[128,3,128]{2,0,1:T(8,128)S(1)} %pad_maximum_fusion.5), channel_id=1, source_target_pairs={{0,4},{4,8},{8,12},{12,16},{16,20},{20,24},{24,28},{1,5},{5,9},{9,... | collective-permute-start | bytes 589832 | tf_op jit(solution)/shard_map/ppermute | solution.py:134
  10.0 9.7 %collective-permute-start.2 = (f32[3,20,128]{2,0,1:T(4,128)S(1)}, f32[3,20,128]{2,0,1:T(4,128)S(1)}, u32[]{:S(2)}, u32[]{:S(2)}) collective-permute-start(f32[3,20,128]{2,0,1:T(4,128)S(1)} %get-tuple-element.47), channel_id=1, source_target_pairs={{0,1},{1,2},{2,3},{4,5},{5,6},{6,7},{8,9},{9,10},{10,11},{12,13},{... | collective-permute-start | bytes 92168 | tf_op jit(solution)/shard_map/ppermute | solution.py:134
  15.0 5.9 %collective-permute-start.3 = (f32[3,20,128]{2,0,1:T(4,128)S(1)}, f32[3,20,128]{2,0,1:T(4,128)S(1)}, u32[]{:S(2)}, u32[]{:S(2)}) collective-permute-start(f32[3,20,128]{2,0,1:T(4,128)S(1)} %get-tuple-element.48), channel_id=1, source_target_pairs={{1,0},{2,1},{3,2},{5,4},{6,5},{7,6},{9,8},{10,9},{11,10},{13,12},{... | collective-permute-start | bytes 92168 | tf_op jit(solution)/shard_map/ppermute | solution.py:134
  22.7 2.3 %collective-permute-start.4 = (f32[129,128]{1,0:T(8,128)S(1)}, f32[129,128]{1,0:T(8,128)S(1)}, u32[]{:S(2)}, u32[]{:S(2)}) collective-permute-start(f32[129,128]{1,0:T(8,128)S(1)} %pad_maximum_fusion.7), channel_id=1, source_target_pairs={{0,4},{4,0},{8,12},{12,8},{16,20},{20,16},{24,28},{28,24},{1,5},{5... | collective-permute-start | bytes 198152 | tf_op jit(solution)/shard_map/ppermute | solution.py:38
  25.0 6.6 %collective-permute-start.5 = (f32[129,128]{1,0:T(8,128)S(1)}, f32[129,128]{1,0:T(8,128)S(1)}, u32[]{:S(2)}, u32[]{:S(2)}) collective-permute-start(f32[129,128]{1,0:T(8,128)S(1)} %fusion.87), channel_id=1, source_target_pairs={{0,8},{4,12},{8,0},{12,4},{16,24},{20,28},{24,16},{28,20},{1,9},{5... | collective-permute-start | bytes 198152 | tf_op jit(solution)/shard_map/ppermute | solution.py:38
  31.7 6.0 %collective-permute-start.6 = (f32[129,128]{1,0:T(8,128)S(1)}, f32[129,128]{1,0:T(8,128)S(1)}, u32[]{:S(2)}, u32[]{:S(2)}) collective-permute-start(f32[129,128]{1,0:T(8,128)S(1)} %add.184), channel_id=1, source_target_pairs={{0,16},{4,20},{8,24},{12,28},{16,0},{20,4},{24,8},{28,12},{1,17},{... | collective-permute-start | bytes 198152 | tf_op jit(solution)/shard_map/ppermute | solution.py:38
  37.6 4.4 %collective-permute-start.7 = (f32[129,128]{1,0:T(8,128)S(1)}, f32[129,128]{1,0:T(8,128)S(1)}, u32[]{:S(2)}, u32[]{:S(2)}) collective-permute-start(f32[129,128]{1,0:T(8,128)S(1)} %add.185), channel_id=1, source_target_pairs={{0,1},{1,0},{2,3},{3,2},{4,5},{5,4},{6,7},{7,6},{8,9},{9,8},{10,11... | collective-permute-start | bytes 198152 | tf_op jit(solution)/shard_map/ppermute | solution.py:38
  42.0 5.4 %collective-permute-start.8 = (f32[129,128]{1,0:T(8,128)S(1)}, f32[129,128]{1,0:T(8,128)S(1)}, u32[]{:S(2)}, u32[]{:S(2)}) collective-permute-start(f32[129,128]{1,0:T(8,128)S(1)} %add.186), channel_id=1, source_target_pairs={{0,2},{1,3},{2,0},{3,1},{4,6},{5,7},{6,4},{7,5},{8,10},{9,11},{10,... | collective-permute-start | bytes 198152 | tf_op jit(solution)/shard_map/ppermute | solution.py:38
  57.7 1.9 %copy-start.1 = (f32[128,128]{1,0:T(8,128)S(1)}, f32[128,128]{1,0:T(8,128)}, u32[]{:S(2)}) copy-start(f32[128,128]{1,0:T(8,128)} %shard_map.68) | copy-start | bytes 196612

commit v20 on v19

--- a/solution.py
+++ b/solution.py
@@ -103,6 +103,27 @@
         scratch_shapes=[pltpu.VMEM((size, size), jnp.float32)] * 2,
     )(stacked)
 
+def analysis_kernel(combination_ref, deviation_ref, average_ref, out_ref):
+    for level in range(deviation_ref.shape[0]):
+        product = lax.dot_general(
+            combination_ref[...],
+            deviation_ref[level],
+            (((1,), (1,)), ((), ())),
+            precision=lax.Precision.HIGHEST,
+            preferred_element_type=jnp.float32,
+        )
+        out_ref[:, level, :] = product + average_ref[level : level + 1, :]
+
+
+def analysis_of(combination, deviation_hwm, average_hw):
+    levels, width, members = deviation_hwm.shape
+    return pl.pallas_call(
+        analysis_kernel,
+        out_shape=jax.ShapeDtypeStruct((members, levels, width), jnp.float32),
+        in_specs=[pl.BlockSpec(memory_space=pltpu.VMEM)] * 3,
+        out_specs=pl.BlockSpec(memory_space=pltpu.VMEM),
+    )(combination, deviation_hwm, average_hw)
+
 def propagate_model(padded_field, source_term):
     laplacian = (
         padded_field[:, 2:, 1:-1]
@@ -248,14 +269,17 @@
     combination_transposed = combination_transposed_of(
         butterfly_sum(jnp.concatenate([gram_local, projected[None, :]], axis=0), ("gx", "gy"))
     )
-    contract = (((2,), (1,)), ((), ()))
-    updated_t = average_t[:, :, None] + lax.dot_general(
-        deviation_t, combination_transposed, contract, precision=lax.Precision.HIGHEST
-    )
-    heat_out_t = mean_heat_t[:, :, None] + lax.dot_general(
-        heat_anomaly_t, combination_transposed, contract, precision=lax.Precision.HIGHEST
-    )
-    return (jnp.transpose(updated_t, (2, 1, 0)), jnp.transpose(heat_out_t, (2, 1, 0)))
+    updated = analysis_of(
+        combination_transposed,
+        jnp.transpose(deviation_t, (1, 0, 2)),
+        jnp.transpose(average_t),
+    )
+    heat_out = analysis_of(
+        combination_transposed,
+        jnp.transpose(heat_anomaly_t, (1, 0, 2)),
+        jnp.transpose(mean_heat_t),
+    )
+    return (updated, heat_out)
 
 
 def solution(mesh):

time: 63.8 us -> 67 us (1.050)
  Pallas kernels: 9.64 us -> 18.6 us
  waiting for transfers between devices: 11.8 us -> 8.78 us
  other arithmetic: 3.96 us -> 6.95 us
  matrix products: 7.18 us -> 4.25 us
  local copies, waits for them, and re-layouts: 5.16 us -> 2.41 us
    pallas_call x0 -> x2, Pallas kernels: none -> 8.93 us  [analysis_of(): pl.pallas_call(analysis_kernel, out_shape=jax.ShapeDtypeStruct((members,...]
    ppermute x5, waiting for transfers between devices: 10.3 us -> 7.29 us  [butterfly_sum(): received[offset] = lax.ppermute(value, axis, pairs)]
    dot_general x2 -> x0, matrix products: 2.93 us -> none  [the longest x1 1.91 us: shards(): lax.dot_general(deviation_t, combination_transposed, contract, precision=...]
    unnamed x14 -> x12, local copies, waits for them, and re-layouts: 4.87 us -> 2.12 us
    transpose x0 -> x2, other arithmetic: none -> 1.76 us  [the longest x1 1.09 us: shards(): jnp.transpose(deviation_t, (1, 0, 2))]
    sub x1, other arithmetic: 0.08 us -> 1.31 us  [shards(): heat_anomaly_t = heat_t - mean_heat_t[:, :, None]]
  transfers between devices with their start and end apart: 9 -> 9, of which waited for: 7 -> 7; matrix products, arithmetic and copies ran while one was open for 7% -> 11% of each run, Pallas kernels for 0% -> 0%
where the time goes in v20:
time: 67 us; the launch traced here: 66.6 us
  starting transfers between devices  24.7 us (37%)
  Pallas kernels  18.6 us (28%)
  waiting for transfers between devices  8.78 us (13%)
  other arithmetic  6.95 us (10%)
  matrix products  4.25 us (6%)
  local copies, waits for them, and re-layouts  2.41 us (4%)
  between operations  1.01 us (2%)
    ppermute x5, starting transfers between devices, butterfly_sum(): received[offset] = lax.ppermute(value, axis, pairs)  13.9 us
    ppermute x4, starting transfers between devices, from_neighbour(): return lax.ppermute(block, axis, pairs)  10.7 us
    pallas_call x1, Pallas kernels, combination_transposed_of(): pl.pallas_call(combination_kernel, out_shape=jax.ShapeDtypeStruct((size,...  9.63 us
    pallas_call x2, Pallas kernels, analysis_of(): pl.pallas_call(analysis_kernel, out_shape=jax.ShapeDtypeStruct((members,...  8.93 us
    ppermute x5, waiting for transfers between devices, butterfly_sum(): received[offset] = lax.ppermute(value, axis, pairs)  7.29 us
    dot_general x3, matrix products, shards(): lax.dot_general(deviation * cell_weight[:, :, None], deviation, (((0, 1),...  2.76 us
    unnamed x12, local copies, waits for them, and re-layouts  2.12 us
    ppermute x4, waiting for transfers between devices, from_neighbour(): return lax.ppermute(block, axis, pairs)  1.49 us
  transfers between devices with their start and end apart: 9, of which 7 were waited for; matrix products, arithmetic and copies ran while one was open for 11% of the time, Pallas kernels for 0%

profile of v20, /device:TPU:0, one launch (start us, length us, event | category | flops | bytes accessed | tf_op | source)
XLA Modules:
  0.0 66.6 jit_solution(17067751068962638024)
XLA Ops:
  0.6 0.0 copy-start
  0.6 1.7 %copy.16 = f32[128,16,128]{0,2,1:T(8,128)S(1)} copy(f32[128,16,128]{2,1,0:T(8,128)} %param.6) | data formatting | bytes 2097152 | tf_op args[1]
  2.3 0.0 copy-done
  2.3 0.4 copy.15
  2.8 0.0 copy-start.2
  2.8 0.0 copy-start.3
  2.8 0.0 copy-start.4
  2.9 1.3 %collective-permute-start.1 = (f32[128,3,128]{2,0,1:T(8,128)S(1)}, f32[128,3,128]{2,0,1:T(8,128)S(1)}, u32[]{:S(2)}, u32[]{:S(2)}) collective-permute-start(f32[128,3,128]{2,0,1:T(8,128)S(1)} %pad_maximum_fusion.6), channel_id=1, source_target_pairs={{4,0},{8,4},{12,8},{16,12},{20,16},{24,20},{28,24},{5,1},{9,5},{13... | collective-permute-start | bytes 589832 | tf_op jit(solution)/shard_map/ppermute | solution.py:155
  4.2 3.0 %collective-permute-start = (f32[128,3,128]{2,0,1:T(8,128)S(1)}, f32[128,3,128]{2,0,1:T(8,128)S(1)}, u32[]{:S(2)}, u32[]{:S(2)}) collective-permute-start(f32[128,3,128]{2,0,1:T(8,128)S(1)} %pad_maximum_fusion.5), channel_id=1, source_target_pairs={{0,4},{4,8},{8,12},{12,16},{16,20},{20,24},{24,28},{1,5},{5,9},{9,... | collective-permute-start | bytes 589832 | tf_op jit(solution)/shard_map/ppermute | solution.py:155
  7.2 0.0 copy-done.2
  7.3 0.0 copy-done.3
  7.3 0.0 copy-done.4
  7.4 0.4 fusion.22
  7.8 0.1 broadcast_or_fusion.1
  7.8 0.0 collective-permute-done.1
  7.9 0.4 collective-permute-done
  8.3 0.1 pad_maximum_fusion
  8.5 0.8 %fusion.4 = f32[126,18,128]{2,0,1:T(8,128)S(1)} fusion(f32[128,1,128]{2,0,1:T(8,128)S(1)} %slice.257, f32[128,16,128]{2,0,1:T(8,128)S(1)} %bitcast.55, f32[128,1,128]{2,0,1:T(8,128)S(1)} %slice.256, f32[128,20,128]{2,0,1:T(8,128)S(1)} %pad_maximum_fusion, f32[128,16,128]{2,0,1:T(8,128)S(1)} %bitcast.50, f32[128,2,128]{2,0,1:T(8,128)S(1)} %slice.252, ...), kind=kLoop, calls=%fused_computation.6 | loop fusion | flops 4064256 | bytes 7135250 | tf_op jit(solution)/shard_map/jit(_where)/select_n | solution.py:190
  9.3 0.7 %fusion.76 = (f32[124,16]{0,1:T(8,128)S(1)}, f32[124,16,128]{2,0,1:T(8,128)S(1)}) fusion(f32[128,16,128]{2,0,1:T(8,128)S(1)} %bitcast.56, f32[126,18,128]{2,0,1:T(8,128)S(1)} %fusion.4), kind=kLoop, calls=%fused_computation.154 | loop fusion | flops 2537536 | bytes 7118592 | tf_op jit(solution)/shard_map/reduce_sum | solution.py:249
  10.0 4.9 %collective-permute-start.2 = (f32[3,20,128]{2,0,1:T(4,128)S(1)}, f32[3,20,128]{2,0,1:T(4,128)S(1)}, u32[]{:S(2)}, u32[]{:S(2)}) collective-permute-start(f32[3,20,128]{2,0,1:T(4,128)S(1)} %get-tuple-element.41), channel_id=1, source_target_pairs={{0,1},{1,2},{2,3},{4,5},{5,6},{6,7},{8,9},{9,10},{10,11},{12,13},{... | collective-permute-start | bytes 92168 | tf_op jit(solution)/shard_map/ppermute | solution.py:155
  15.0 1.5 %collective-permute-start.3 = (f32[3,20,128]{2,0,1:T(4,128)S(1)}, f32[3,20,128]{2,0,1:T(4,128)S(1)}, u32[]{:S(2)}, u32[]{:S(2)}) collective-permute-start(f32[3,20,128]{2,0,1:T(4,128)S(1)} %get-tuple-element.42), channel_id=1, source_target_pairs={{1,0},{2,1},{3,2},{5,4},{6,5},{7,6},{9,8},{10,9},{11,10},{13,12},{... | collective-permute-start | bytes 92168 | tf_op jit(solution)/shard_map/ppermute | solution.py:155
  16.4 0.1 fusion.83
  16.5 0.3 broadcast_subtract_fusion
  16.9 2.2 %fusion.9 = f32[128,128]{1,0:T(8,128)S(1)} fusion(f32[124,16,128]{2,0,1:T(8,128)S(1)} %broadcast_subtract_fusion, f32[124,16]{0,1:T(8,128)S(1)} %get-tuple-element.24), kind=kOutput, calls=%fused_computation.16 | convolution fusion | flops 390324224 | bytes 1089280 | tf_op jit(solution)/shard_map/dot_general | solution.py:253
  19.0 0.7 %convolution_bitcast_fusion.3 = f32[128]{0:T(128)S(1)} fusion(f32[124,16,128]{2,0,1:T(8,128)S(1)} %broadcast_subtract_fusion, f32[124,16,1]{0,2,1:T(1,128)S(1)} %bitcast.58), kind=kOutput, calls=%fused_computation.22 | convolution fusion | flops 3047424 | bytes 1024256 | tf_op jit(solution)/shard_map/dot_general | solution.py:259
  19.7 0.0 collective-permute-done.2
  19.8 1.1 %collective-permute-done.3 = f32[3,20,128]{2,0,1:T(4,128)S(1)} collective-permute-done((f32[3,20,128]{2,0,1:T(4,128)S(1)}, f32[3,20,128]{2,0,1:T(4,128)S(1)}, u32[]{:S(2)}, u32[]{:S(2)}) %collective-permute-start.3) | collective-permute-done | bytes 30752 | tf_op jit(solution)/shard_map/ppermute | solution.py:155
  20.9 0.1 fusion.44
  21.0 0.1 fusion.46
  21.1 0.2 fusion.74
  21.3 0.1 fusion.84
  21.3 0.1 copy.26
  21.4 0.1 copy.24
  21.5 0.1 broadcast_multiply_fusion
  21.6 0.2 convolution_bitcast_fusion.2
  21.8 0.3 convolution_bitcast_fusion
  22.1 0.1 broadcast_multiply_fusion.1
  22.2 0.2 fusion.16
  22.4 0.3 fusion.13
  22.7 1.4 %collective-permute-start.4 = (f32[129,128]{1,0:T(8,128)S(1)}, f32[129,128]{1,0:T(8,128)S(1)}, u32[]{:S(2)}, u32[]{:S(2)}) collective-permute-start(f32[129,128]{1,0:T(8,128)S(1)} %pad_maximum_fusion.7), channel_id=1, source_target_pairs={{0,4},{4,0},{8,12},{12,8},{16,20},{20,16},{24,28},{28,24},{1,5},{5... | collective-permute-start | bytes 198152 | tf_op jit(solution)/shard_map/ppermute | solution.py:38
  24.1 0.3 bitcast_reduce_fusion
  24.5 0.6 collective-permute-done.4
  25.0 4.1 %collective-permute-start.5 = (f32[129,128]{1,0:T(8,128)S(1)}, f32[129,128]{1,0:T(8,128)S(1)}, u32[]{:S(2)}, u32[]{:S(2)}) collective-permute-start(f32[129,128]{1,0:T(8,128)S(1)} %fusion.73), channel_id=1, source_target_pairs={{0,8},{4,12},{8,0},{12,4},{16,24},{20,28},{24,16},{28,20},{1,9},{5... | collective-permute-start | bytes 198152 | tf_op jit(solution)/shard_map/ppermute | solution.py:38
  29.1 0.0 copy-start.1
  29.1 2.5 %collective-permute-done.5 = f32[129,128]{1,0:T(8,128)S(1)} collective-permute-done((f32[129,128]{1,0:T(8,128)S(1)}, f32[129,128]{1,0:T(8,128)S(1)}, u32[]{:S(2)}, u32[]{:S(2)}) %collective-permute-start.5) | collective-permute-done | bytes 66080 | tf_op jit(solution)/shard_map/ppermute | solution.py:38
  31.7 3.7 %collective-permute-start.6 = (f32[129,128]{1,0:T(8,128)S(1)}, f32[129,128]{1,0:T(8,128)S(1)}, u32[]{:S(2)}, u32[]{:S(2)}) collective-permute-start(f32[129,128]{1,0:T(8,128)S(1)} %add.160), channel_id=1, source_target_pairs={{0,16},{4,20},{8,24},{12,28},{16,0},{20,4},{24,8},{28,12},{1,17},{... | collective-permute-start | bytes 198152 | tf_op jit(solution)/shard_map/ppermute | solution.py:38
  35.3 1.3 %subtract_bitcast_fusion.deviation_ref = f32[16,128,128]{2,1,0:T(8,128)} fusion(f32[128,16,128]{0,2,1:T(8,128)S(1)} %copy.16, f32[16,128]{1,0:T(8,128)S(1)} %multiply_bitcast_fusion.average_ref), kind=kLoop, calls=%fused_computation.36 | loop fusion | flops 262144 | bytes 2105344 | tf_op jit(solution)/shard_map/sub | solution.py:228
  36.6 1.0 %collective-permute-done.6 = f32[129,128]{1,0:T(8,128)S(1)} collective-permute-done((f32[129,128]{1,0:T(8,128)S(1)}, f32[129,128]{1,0:T(8,128)S(1)}, u32[]{:S(2)}, u32[]{:S(2)}) %collective-permute-start.6) | collective-permute-done | bytes 66080 | tf_op jit(solution)/shard_map/ppermute | solution.py:38
  37.6 0.0 copy-done.1
  37.6 1.7 %collective-permute-start.7 = (f32[129,128]{1,0:T(8,128)S(1)}, f32[129,128]{1,0:T(8,128)S(1)}, u32[]{:S(2)}, u32[]{:S(2)}) collective-permute-start(f32[129,128]{1,0:T(8,128)S(1)} %add.161), channel_id=1, source_target_pairs={{0,1},{1,0},{2,3},{3,2},{4,5},{5,4},{6,7},{7,6},{8,9},{9,8},{10,11... | collective-permute-start | bytes 198152 | tf_op jit(solution)/shard_map/ppermute | solution.py:38
  39.3 1.1 %maximum_bitcast_fusion.deviation_ref = f32[16,128,128]{2,1,0:T(8,128)} fusion(f32[2,16,128]{2,0,1:T(2,128)S(1)} %get-tuple-element.5, f32[124,16,128]{2,0,1:T(8,128)S(1)} %broadcast_subtract_fusion, f32[2,16,128]{2,0,1:T(2,128)S(1)} %get-tuple-element.3), kind=kLoop, calls=%fused_computation.35 | loop fusion | flops 524288 | bytes 2097152 | tf_op jit(solution)/shard_map/transpose | solution.py:274
  40.4 1.6 %collective-permute-done.7 = f32[129,128]{1,0:T(8,128)S(1)} collective-permute-done((f32[129,128]{1,0:T(8,128)S(1)}, f32[129,128]{1,0:T(8,128)S(1)}, u32[]{:S(2)}, u32[]{:S(2)}) %collective-permute-start.7) | collective-permute-done | bytes 66080 | tf_op jit(solution)/shard_map/ppermute | solution.py:38
  42.0 3.1 %collective-permute-start.8 = (f32[129,128]{1,0:T(8,128)S(1)}, f32[129,128]{1,0:T(8,128)S(1)}, u32[]{:S(2)}, u32[]{:S(2)}) collective-permute-start(f32[129,128]{1,0:T(8,128)S(1)} %add.162), channel_id=1, source_target_pairs={{0,2},{1,3},{2,0},{3,1},{4,6},{5,7},{6,4},{7,5},{8,10},{9,11},{10,... | collective-permute-start | bytes 198152 | tf_op jit(solution)/shard_map/ppermute | solution.py:38
  45.1 0.7 maximum_bitcast_fusion.1.average_ref
  45.8 1.6 %collective-permute-done.8 = f32[129,128]{1,0:T(8,128)S(1)} collective-permute-done((f32[129,128]{1,0:T(8,128)S(1)}, f32[129,128]{1,0:T(8,128)S(1)}, u32[]{:S(2)}, u32[]{:S(2)}) %collective-permute-start.8) | collective-permute-done | bytes 66080 | tf_op jit(solution)/shard_map/ppermute | solution.py:38
  47.4 0.6 add.163.stacked_ref
  48.1 9.6 %shard_map.68.combination_ref = f32[128,128]{1,0:T(8,128)} custom-call(f32[129,128]{1,0:T(8,128)} %add.163.stacked_ref), custom_call_target="tpu_custom_call" | custom-call | tf_op jit(solution)/shard_map/pallas_call | solution.py:98
  57.7 4.5 %shard_map.70 = f32[128,16,128]{2,1,0:T(8,128)} custom-call(f32[128,128]{1,0:T(8,128)} %shard_map.68.combination_ref, f32[16,128,128]{2,1,0:T(8,128)} %subtract_bitcast_fusion.deviation_ref, f32[16,128]{1,0:T(8,128)} %copy-done.1), custom_call_target="tpu_custom_call" | custom-call | tf_op jit(solution)/shard_map/pallas_call | solution.py:120
  62.2 4.5 %shard_map.69 = f32[128,16,128]{2,1,0:T(8,128)} custom-call(f32[128,128]{1,0:T(8,128)} %shard_map.68.combination_ref, f32[16,128,128]{2,1,0:T(8,128)} %maximum_bitcast_fusion.deviation_ref, f32[16,128]{1,0:T(8,128)} %maximum_bitcast_fusion.1.average_ref), custom_call_target="tpu_custom_call" | custom-call | tf_op jit(solution)/shard_map/pallas_call | solution.py:120
  (28 shorter events, 0.3 us)
Async XLA Ops:
  0.6 1.7 %copy-start = (f32[128,16,128]{2,1,0:T(8,128)S(1)}, f32[128,16,128]{2,1,0:T(8,128)}, u32[]{:S(2)}) copy-start(f32[128,16,128]{2,1,0:T(8,128)} %param.5) | copy-start | bytes 3145732
  2.8 4.5 %copy-start.2 = (s32[1024]{0:T(1024)S(1)}, s32[1024]{0:T(1024)}, u32[]{:S(2)}) copy-start(s32[1024]{0:T(1024)} %param.9) | copy-start | bytes 12292
  2.8 4.5 %copy-start.3 = (f32[1024]{0:T(1024)S(1)}, f32[1024]{0:T(1024)}, u32[]{:S(2)}) copy-start(f32[1024]{0:T(1024)} %param.8) | copy-start | bytes 12292
  2.8 4.5 %copy-start.4 = (f32[1024]{0:T(1024)S(1)}, f32[1024]{0:T(1024)}, u32[]{:S(2)}) copy-start(f32[1024]{0:T(1024)} %param.7) | copy-start | bytes 12292
  2.9 5.0 %collective-permute-start.1 = (f32[128,3,128]{2,0,1:T(8,128)S(1)}, f32[128,3,128]{2,0,1:T(8,128)S(1)}, u32[]{:S(2)}, u32[]{:S(2)}) collective-permute-start(f32[128,3,128]{2,0,1:T(8,128)S(1)} %pad_maximum_fusion.6), channel_id=1, source_target_pairs={{4,0},{8,4},{12,8},{16,12},{20,16},{24,20},{28,24},{5,1},{9,5},{13... | collective-permute-start | bytes 589832 | tf_op jit(solution)/shard_map/ppermute | solution.py:155
  4.2 4.1 %collective-permute-start = (f32[128,3,128]{2,0,1:T(8,128)S(1)}, f32[128,3,128]{2,0,1:T(8,128)S(1)}, u32[]{:S(2)}, u32[]{:S(2)}) collective-permute-start(f32[128,3,128]{2,0,1:T(8,128)S(1)} %pad_maximum_fusion.5), channel_id=1, source_target_pairs={{0,4},{4,8},{8,12},{12,16},{16,20},{20,24},{24,28},{1,5},{5,9},{9,... | collective-permute-start | bytes 589832 | tf_op jit(solution)/shard_map/ppermute | solution.py:155
  10.0 9.7 %collective-permute-start.2 = (f32[3,20,128]{2,0,1:T(4,128)S(1)}, f32[3,20,128]{2,0,1:T(4,128)S(1)}, u32[]{:S(2)}, u32[]{:S(2)}) collective-permute-start(f32[3,20,128]{2,0,1:T(4,128)S(1)} %get-tuple-element.41), channel_id=1, source_target_pairs={{0,1},{1,2},{2,3},{4,5},{5,6},{6,7},{8,9},{9,10},{10,11},{12,13},{... | collective-permute-start | bytes 92168 | tf_op jit(solution)/shard_map/ppermute | solution.py:155
  15.0 5.9 %collective-permute-start.3 = (f32[3,20,128]{2,0,1:T(4,128)S(1)}, f32[3,20,128]{2,0,1:T(4,128)S(1)}, u32[]{:S(2)}, u32[]{:S(2)}) collective-permute-start(f32[3,20,128]{2,0,1:T(4,128)S(1)} %get-tuple-element.42), channel_id=1, source_target_pairs={{1,0},{2,1},{3,2},{5,4},{6,5},{7,6},{9,8},{10,9},{11,10},{13,12},{... | collective-permute-start | bytes 92168 | tf_op jit(solution)/shard_map/ppermute | solution.py:155
  22.7 2.3 %collective-permute-start.4 = (f32[129,128]{1,0:T(8,128)S(1)}, f32[129,128]{1,0:T(8,128)S(1)}, u32[]{:S(2)}, u32[]{:S(2)}) collective-permute-start(f32[129,128]{1,0:T(8,128)S(1)} %pad_maximum_fusion.7), channel_id=1, source_target_pairs={{0,4},{4,0},{8,12},{12,8},{16,20},{20,16},{24,28},{28,24},{1,5},{5... | collective-permute-start | bytes 198152 | tf_op jit(solution)/shard_map/ppermute | solution.py:38
  25.0 6.6 %collective-permute-start.5 = (f32[129,128]{1,0:T(8,128)S(1)}, f32[129,128]{1,0:T(8,128)S(1)}, u32[]{:S(2)}, u32[]{:S(2)}) collective-permute-start(f32[129,128]{1,0:T(8,128)S(1)} %fusion.73), channel_id=1, source_target_pairs={{0,8},{4,12},{8,0},{12,4},{16,24},{20,28},{24,16},{28,20},{1,9},{5... | collective-permute-start | bytes 198152 | tf_op jit(solution)/shard_map/ppermute | solution.py:38
  29.1 8.5 %copy-start.1 = (f32[16,128]{1,0:T(8,128)}, f32[16,128]{1,0:T(8,128)S(1)}, u32[]{:S(2)}) copy-start(f32[16,128]{1,0:T(8,128)S(1)} %multiply_bitcast_fusion.average_ref) | copy-start | bytes 24580
  31.7 6.0 %collective-permute-start.6 = (f32[129,128]{1,0:T(8,128)S(1)}, f32[129,128]{1,0:T(8,128)S(1)}, u32[]{:S(2)}, u32[]{:S(2)}) collective-permute-start(f32[129,128]{1,0:T(8,128)S(1)} %add.160), channel_id=1, source_target_pairs={{0,16},{4,20},{8,24},{12,28},{16,0},{20,4},{24,8},{28,12},{1,17},{... | collective-permute-start | bytes 198152 | tf_op jit(solution)/shard_map/ppermute | solution.py:38
  37.6 4.4 %collective-permute-start.7 = (f32[129,128]{1,0:T(8,128)S(1)}, f32[129,128]{1,0:T(8,128)S(1)}, u32[]{:S(2)}, u32[]{:S(2)}) collective-permute-start(f32[129,128]{1,0:T(8,128)S(1)} %add.161), channel_id=1, source_target_pairs={{0,1},{1,0},{2,3},{3,2},{4,5},{5,4},{6,7},{7,6},{8,9},{9,8},{10,11... | collective-permute-start | bytes 198152 | tf_op jit(solution)/shard_map/ppermute | solution.py:38
  42.0 5.4 %collective-permute-start.8 = (f32[129,128]{1,0:T(8,128)S(1)}, f32[129,128]{1,0:T(8,128)S(1)}, u32[]{:S(2)}, u32[]{:S(2)}) collective-permute-start(f32[129,128]{1,0:T(8,128)S(1)} %add.162), channel_id=1, source_target_pairs={{0,2},{1,3},{2,0},{3,1},{4,6},{5,7},{6,4},{7,5},{8,10},{9,11},{10,... | collective-permute-start | bytes 198152 | tf_op jit(solution)/shard_map/ppermute | solution.py:38

commit v21 on v19

--- a/solution.py
+++ b/solution.py
@@ -136,60 +136,56 @@
 
 def forecast_in_pieces(warmth, heat):
     width, height = warmth.shape[0], warmth.shape[1]
+    left = from_neighbour(jnp.concatenate([warmth[-2:], heat[-1:]], axis=0), "gy", 1)
+    right = from_neighbour(jnp.concatenate([warmth[:2], heat[:1]], axis=0), "gy", -1)
+    warmth_wide = jnp.concatenate([left[:2], warmth, right[:2]], axis=0)
+    heat_wide = jnp.concatenate([left[2:], heat, right[2:]], axis=0)
+    edge = jnp.zeros_like(heat_wide[:1, :1])
     top = from_neighbour(
-        jnp.concatenate([warmth[:, -2:], heat[:, -1:]], axis=1), "gx", 1
+        jnp.concatenate(
+            [warmth_wide[:, -2:], jnp.concatenate([edge, heat_wide[:, -1:], edge], axis=0)],
+            axis=1,
+        ),
+        "gx",
+        1,
     )
     bottom = from_neighbour(
-        jnp.concatenate([warmth[:, :2], heat[:, :1]], axis=1), "gx", -1
-    )
-    warmth_tall = jnp.concatenate([top[:, :2], warmth, bottom[:, :2]], axis=1)
-    heat_tall = jnp.concatenate([top[:, 2:], heat, bottom[:, 2:]], axis=1)
-    edge = jnp.zeros_like(heat_tall[:1, :1])
-    left = from_neighbour(
         jnp.concatenate(
-            [warmth_tall[-2:], jnp.concatenate([edge, heat_tall[-1:], edge], axis=1)],
-            axis=0,
+            [warmth_wide[:, :2], jnp.concatenate([edge, heat_wide[:, :1], edge], axis=0)],
+            axis=1,
         ),
-        "gy",
-        1,
-    )
-    right = from_neighbour(
-        jnp.concatenate(
-            [warmth_tall[:2], jnp.concatenate([edge, heat_tall[:1], edge], axis=1)],
-            axis=0,
-        ),
-        "gy",
+        "gx",
         -1,
     )
     at_x, at_y = lax.axis_index("gx"), lax.axis_index("gy")
-    row = lax.broadcasted_iota(jnp.int32, (1, height + 2, 1), 1)
-    off_grid = ((row == 0) & (at_x == 0)) | (
-        (row == height + 1) & (at_x == lax.axis_size("gx") - 1)
+    col = lax.broadcasted_iota(jnp.int32, (width + 2, 1, 1), 0)
+    off_grid = ((col == 0) & (at_y == 0)) | (
+        (col == width + 1) & (at_y == lax.axis_size("gy") - 1)
     )
     first_inner = jnp.where(
-        off_grid, 0.0, propagate_members_last(warmth_tall, heat_tall[1:-1])
-    )
-    second_inner = propagate_members_last(first_inner, heat[2:-2])
-    first_left = propagate_members_last(
-        jnp.concatenate([left[:2], warmth_tall[:2]], axis=0),
-        jnp.concatenate([left[2:, 1:-1], heat_tall[:1]], axis=0),
-    )
-    first_right = propagate_members_last(
-        jnp.concatenate([warmth_tall[-2:], right[:2]], axis=0),
-        jnp.concatenate([heat_tall[-1:], right[2:, 1:-1]], axis=0),
-    )
-    col = lax.broadcasted_iota(jnp.int32, (2, 1, 1), 0)
-    first_left = jnp.where(off_grid | ((col == 0) & (at_y == 0)), 0.0, first_left)
-    first_right = jnp.where(
-        off_grid | ((col == 1) & (at_y == lax.axis_size("gy") - 1)), 0.0, first_right
-    )
-    second_left = propagate_members_last(
-        jnp.concatenate([first_left, first_inner[:2]], axis=0), heat[:2]
-    )
-    second_right = propagate_members_last(
-        jnp.concatenate([first_inner[-2:], first_right], axis=0), heat[-2:]
-    )
-    return [(0, second_left), (2, second_inner), (width - 2, second_right)]
+        off_grid, 0.0, propagate_members_last(warmth_wide, heat_wide[:, 1:-1])
+    )
+    second_inner = propagate_members_last(first_inner, heat[:, 2:-2])
+    first_top = propagate_members_last(
+        jnp.concatenate([top[:, :2], warmth_wide[:, :2]], axis=1),
+        jnp.concatenate([top[1:-1, 2:], heat_wide[:, :1]], axis=1),
+    )
+    first_bottom = propagate_members_last(
+        jnp.concatenate([warmth_wide[:, -2:], bottom[:, :2]], axis=1),
+        jnp.concatenate([heat_wide[:, -1:], bottom[1:-1, 2:]], axis=1),
+    )
+    row = lax.broadcasted_iota(jnp.int32, (1, 2, 1), 1)
+    first_top = jnp.where(off_grid | ((row == 0) & (at_x == 0)), 0.0, first_top)
+    first_bottom = jnp.where(
+        off_grid | ((row == 1) & (at_x == lax.axis_size("gx") - 1)), 0.0, first_bottom
+    )
+    second_top = propagate_members_last(
+        jnp.concatenate([first_top, first_inner[:, :2]], axis=1), heat[:, :2]
+    )
+    second_bottom = propagate_members_last(
+        jnp.concatenate([first_inner[:, -2:], first_bottom], axis=1), heat[:, -2:]
+    )
+    return [(0, second_top), (2, second_inner), (height - 2, second_bottom)]
 
 
 def shards(
@@ -224,11 +220,14 @@
     )
     averages, deviations, gram_local, projected = [], [], 0.0, 0.0
     for start, piece in pieces:
-        count = piece.shape[0]
+        count = piece.shape[1]
         average = jnp.mean(piece, axis=2)
         deviation = piece - average[:, :, None]
-        cell_weight = cell_sums[start : start + count, :block_height_number]
-        cell_residual = cell_sums[start : start + count, block_height_number:] - average * cell_weight
+        cell_weight = cell_sums[:, start : start + count]
+        cell_residual = (
+            cell_sums[:, block_height_number + start : block_height_number + start + count]
+            - average * cell_weight
+        )
         gram_local = gram_local + lax.dot_general(
             deviation * cell_weight[:, :, None],
             deviation,
@@ -243,8 +242,8 @@
         )
         averages.append(average)
         deviations.append(deviation)
-    average_t = jnp.concatenate(averages, axis=0)
-    deviation_t = jnp.concatenate(deviations, axis=0)
+    average_t = jnp.concatenate(averages, axis=1)
+    deviation_t = jnp.concatenate(deviations, axis=1)
     combination_transposed = combination_transposed_of(
         butterfly_sum(jnp.concatenate([gram_local, projected[None, :]], axis=0), ("gx", "gy"))
     )

time: 63.8 us -> 62.1 us (0.973)
  starting transfers between devices: 24.7 us -> 22.6 us
  waiting for transfers between devices: 11.8 us -> 13.3 us
    ppermute x4, starting transfers between devices: 10.7 us -> 9.44 us  [from_neighbour(): return lax.ppermute(block, axis, pairs)]
    ppermute x5, waiting for transfers between devices: 10.3 us -> 11.3 us  [butterfly_sum(): received[offset] = lax.ppermute(value, axis, pairs)]
    ppermute x5, starting transfers between devices: 13.9 us -> 13.2 us  [butterfly_sum(): received[offset] = lax.ppermute(value, axis, pairs)]
  transfers between devices with their start and end apart: 9 -> 9, of which waited for: 7 -> 7; matrix products, arithmetic and copies ran while one was open for 7% -> 6% of each run, Pallas kernels for 0% -> 0%
where the time goes in v21:
time: 62.1 us; the launch traced here: 61.8 us
  starting transfers between devices  22.6 us (36%)
  waiting for transfers between devices  13.3 us (21%)
  Pallas kernels  9.64 us (16%)
  matrix products  6.74 us (11%)
  local copies, waits for them, and re-layouts  5 us (8%)
  other arithmetic  3.4 us (5%)
  between operations  1.02 us (2%)
    ppermute x5, starting transfers between devices, butterfly_sum(): received[offset] = lax.ppermute(value, axis, pairs)  13.2 us
    ppermute x5, waiting for transfers between devices, butterfly_sum(): received[offset] = lax.ppermute(value, axis, pairs)  11.3 us
    pallas_call x1, Pallas kernels, combination_transposed_of(): pl.pallas_call(combination_kernel, out_shape=jax.ShapeDtypeStruct((size,...  9.64 us
    ppermute x4, starting transfers between devices, from_neighbour(): return lax.ppermute(block, axis, pairs)  9.44 us
    unnamed x14, local copies, waits for them, and re-layouts  4.87 us
    dot_general x3, matrix products, shards(): lax.dot_general(deviation * cell_weight[:, :, None], deviation, (((0, 1),...  2.62 us
    ppermute x4, waiting for transfers between devices, from_neighbour(): return lax.ppermute(block, axis, pairs)  2.05 us
    dot_general x1, matrix products, shards(): lax.dot_general(deviation_t, combination_transposed, contract, precision=...  1.83 us
  transfers between devices with their start and end apart: 9, of which 7 were waited for; matrix products, arithmetic and copies ran while one was open for 6% of the time, Pallas kernels for 0%

profile of v21, /device:TPU:0, one launch (start us, length us, event | category | flops | bytes accessed | tf_op | source)
XLA Modules:
  0.0 61.8 jit_solution(1958155362405210783)
XLA Ops:
  0.6 0.0 copy-start
  0.6 1.7 %copy.15 = f32[128,16,128]{0,2,1:T(8,128)S(1)} copy(f32[128,16,128]{2,1,0:T(8,128)} %param.6) | data formatting | bytes 2097152 | tf_op args[1]
  2.3 0.0 copy-done
  2.3 0.0 copy-start.2
  2.4 0.0 copy-start.3
  2.4 0.0 copy-start.4
  2.4 0.4 copy.14
  2.9 1.3 %collective-permute-start.1 = (f32[3,16,128]{2,0,1:T(4,128)S(1)}, f32[3,16,128]{2,0,1:T(4,128)S(1)}, u32[]{:S(2)}, u32[]{:S(2)}) collective-permute-start(f32[3,16,128]{2,0,1:T(4,128)S(1)} %pad_maximum_fusion.19), channel_id=1, source_target_pairs={{1,0},{2,1},{3,2},{5,4},{6,5},{7,6},{9,8},{10,9},{11,10},{13,12},{... | collective-permute-start | bytes 73736 | tf_op jit(solution)/shard_map/ppermute | solution.py:134
  4.2 5.6 %collective-permute-start = (f32[3,16,128]{2,0,1:T(4,128)S(1)}, f32[3,16,128]{2,0,1:T(4,128)S(1)}, u32[]{:S(2)}, u32[]{:S(2)}) collective-permute-start(f32[3,16,128]{2,0,1:T(4,128)S(1)} %pad_maximum_fusion.18), channel_id=1, source_target_pairs={{0,1},{1,2},{2,3},{4,5},{5,6},{6,7},{8,9},{9,10},{10,11},{12,13},{... | collective-permute-start | bytes 73736 | tf_op jit(solution)/shard_map/ppermute | solution.py:134
  9.8 0.0 copy-done.2
  9.8 0.0 copy-done.3
  9.8 0.0 copy-done.4
  9.9 0.4 fusion.31
  10.3 0.1 broadcast_or_fusion.1
  10.3 0.0 collective-permute-done.1
  10.4 1.0 %collective-permute-done = f32[3,16,128]{2,0,1:T(4,128)S(1)} collective-permute-done((f32[3,16,128]{2,0,1:T(4,128)S(1)}, f32[3,16,128]{2,0,1:T(4,128)S(1)}, u32[]{:S(2)}, u32[]{:S(2)}) %collective-permute-start) | collective-permute-done | bytes 24608 | tf_op jit(solution)/shard_map/ppermute | solution.py:134
  11.4 0.1 pad_maximum_fusion
  11.6 1.3 %collective-permute-start.2 = (f32[132,3,128]{2,0,1:T(8,128)S(1)}, f32[132,3,128]{2,0,1:T(8,128)S(1)}, u32[]{:S(2)}, u32[]{:S(2)}) collective-permute-start(f32[132,3,128]{2,0,1:T(8,128)S(1)} %get-tuple-element.43), channel_id=1, source_target_pairs={{0,4},{4,8},{8,12},{12,16},{16,20},{20,24},{24,28},{1,5},{5,9},{9,... | collective-permute-start | bytes 608264 | tf_op jit(solution)/shard_map/ppermute | solution.py:134
  12.9 1.3 %collective-permute-start.3 = (f32[132,3,128]{2,0,1:T(8,128)S(1)}, f32[132,3,128]{2,0,1:T(8,128)S(1)}, u32[]{:S(2)}, u32[]{:S(2)}) collective-permute-start(f32[132,3,128]{2,0,1:T(8,128)S(1)} %get-tuple-element.44), channel_id=1, source_target_pairs={{4,0},{8,4},{12,8},{16,12},{20,16},{24,20},{28,24},{5,1},{9,5},{13... | collective-permute-start | bytes 608264 | tf_op jit(solution)/shard_map/ppermute | solution.py:134
  14.2 0.6 fusion.20
  14.8 0.5 fusion.93
  15.3 0.3 broadcast_subtract_fusion
  15.6 1.7 %fusion.4 = f32[128,128]{1,0:T(8,128)S(1)} fusion(f32[128,12,128]{2,0,1:T(8,128)S(1)} %broadcast_subtract_fusion, f32[128,12]{0,1:T(8,128)S(1)} %get-tuple-element.28), kind=kOutput, calls=%fused_computation.8 | convolution fusion | flops 302186496 | bytes 858112 | tf_op jit(solution)/shard_map/dot_general | solution.py:231
  17.3 0.0 collective-permute-done.2
  17.3 1.1 %collective-permute-done.3 = f32[132,3,128]{2,0,1:T(8,128)S(1)} collective-permute-done((f32[132,3,128]{2,0,1:T(8,128)S(1)}, f32[132,3,128]{2,0,1:T(8,128)S(1)}, u32[]{:S(2)}, u32[]{:S(2)}) %collective-permute-start.3) | collective-permute-done | bytes 202784 | tf_op jit(solution)/shard_map/ppermute | solution.py:134
  18.4 0.1 fusion.54
  18.5 0.1 fusion.45
  18.7 0.2 fusion.91
  18.9 0.1 broadcast_subtract_fusion.1
  19.0 0.1 broadcast_subtract_fusion.2
  19.1 0.2 convolution_bitcast_fusion.6
  19.3 0.5 fusion.10
  19.8 0.5 convolution_bitcast_fusion.2
  20.3 0.2 fusion.11
  20.5 0.5 fusion.8
  21.0 4.3 %collective-permute-start.4 = (f32[129,128]{1,0:T(8,128)S(1)}, f32[129,128]{1,0:T(8,128)S(1)}, u32[]{:S(2)}, u32[]{:S(2)}) collective-permute-start(f32[129,128]{1,0:T(8,128)S(1)} %pad_maximum_fusion.17), channel_id=1, source_target_pairs={{0,4},{4,0},{8,12},{12,8},{16,20},{20,16},{24,28},{28,24},{1,5},{5... | collective-permute-start | bytes 198152 | tf_op jit(solution)/shard_map/ppermute | solution.py:38
  25.3 0.9 %collective-permute-done.4 = f32[129,128]{1,0:T(8,128)S(1)} collective-permute-done((f32[129,128]{1,0:T(8,128)S(1)}, f32[129,128]{1,0:T(8,128)S(1)}, u32[]{:S(2)}, u32[]{:S(2)}) %collective-permute-start.4) | collective-permute-done | bytes 66080 | tf_op jit(solution)/shard_map/ppermute | solution.py:38
  26.2 2.5 %collective-permute-start.5 = (f32[129,128]{1,0:T(8,128)S(1)}, f32[129,128]{1,0:T(8,128)S(1)}, u32[]{:S(2)}, u32[]{:S(2)}) collective-permute-start(f32[129,128]{1,0:T(8,128)S(1)} %fusion.90), channel_id=1, source_target_pairs={{0,8},{4,12},{8,0},{12,4},{16,24},{20,28},{24,16},{28,20},{1,9},{5... | collective-permute-start | bytes 198152 | tf_op jit(solution)/shard_map/ppermute | solution.py:38
  28.7 2.7 %collective-permute-done.5 = f32[129,128]{1,0:T(8,128)S(1)} collective-permute-done((f32[129,128]{1,0:T(8,128)S(1)}, f32[129,128]{1,0:T(8,128)S(1)}, u32[]{:S(2)}, u32[]{:S(2)}) %collective-permute-start.5) | collective-permute-done | bytes 66080 | tf_op jit(solution)/shard_map/ppermute | solution.py:38
  31.4 0.9 %collective-permute-start.6 = (f32[129,128]{1,0:T(8,128)S(1)}, f32[129,128]{1,0:T(8,128)S(1)}, u32[]{:S(2)}, u32[]{:S(2)}) collective-permute-start(f32[129,128]{1,0:T(8,128)S(1)} %add.184), channel_id=1, source_target_pairs={{0,16},{4,20},{8,24},{12,28},{16,0},{20,4},{24,8},{28,12},{1,17},{... | collective-permute-start | bytes 198152 | tf_op jit(solution)/shard_map/ppermute | solution.py:38
  32.3 0.3 bitcast_reduce_fusion
  32.7 3.1 %collective-permute-done.6 = f32[129,128]{1,0:T(8,128)S(1)} collective-permute-done((f32[129,128]{1,0:T(8,128)S(1)}, f32[129,128]{1,0:T(8,128)S(1)}, u32[]{:S(2)}, u32[]{:S(2)}) %collective-permute-start.6) | collective-permute-done | bytes 66080 | tf_op jit(solution)/shard_map/ppermute | solution.py:38
  35.8 2.4 %collective-permute-start.7 = (f32[129,128]{1,0:T(8,128)S(1)}, f32[129,128]{1,0:T(8,128)S(1)}, u32[]{:S(2)}, u32[]{:S(2)}) collective-permute-start(f32[129,128]{1,0:T(8,128)S(1)} %add.185), channel_id=1, source_target_pairs={{0,1},{1,0},{2,3},{3,2},{4,5},{5,4},{6,7},{7,6},{8,9},{9,8},{10,11... | collective-permute-start | bytes 198152 | tf_op jit(solution)/shard_map/ppermute | solution.py:38
  38.2 2.3 %collective-permute-done.7 = f32[129,128]{1,0:T(8,128)S(1)} collective-permute-done((f32[129,128]{1,0:T(8,128)S(1)}, f32[129,128]{1,0:T(8,128)S(1)}, u32[]{:S(2)}, u32[]{:S(2)}) %collective-permute-start.7) | collective-permute-done | bytes 66080 | tf_op jit(solution)/shard_map/ppermute | solution.py:38
  40.5 3.1 %collective-permute-start.8 = (f32[129,128]{1,0:T(8,128)S(1)}, f32[129,128]{1,0:T(8,128)S(1)}, u32[]{:S(2)}, u32[]{:S(2)}) collective-permute-start(f32[129,128]{1,0:T(8,128)S(1)} %add.186), channel_id=1, source_target_pairs={{0,2},{1,3},{2,0},{3,1},{4,6},{5,7},{6,4},{7,5},{8,10},{9,11},{10,... | collective-permute-start | bytes 198152 | tf_op jit(solution)/shard_map/ppermute | solution.py:38
  43.6 2.3 %collective-permute-done.8 = f32[129,128]{1,0:T(8,128)S(1)} collective-permute-done((f32[129,128]{1,0:T(8,128)S(1)}, f32[129,128]{1,0:T(8,128)S(1)}, u32[]{:S(2)}, u32[]{:S(2)}) %collective-permute-start.8) | collective-permute-done | bytes 66080 | tf_op jit(solution)/shard_map/ppermute | solution.py:38
  45.8 0.6 %add.187.stacked_ref = f32[129,128]{1,0:T(8,128)} add(f32[129,128]{1,0:T(8,128)S(1)} %add.186, f32[129,128]{1,0:T(8,128)S(1)} %collective-permute-done.8) | non-fusion elementwise | flops 16512 | bytes 198144 | tf_op jit(solution)/shard_map/add | solution.py:17
  46.5 9.6 %shard_map.68 = f32[128,128]{1,0:T(8,128)} custom-call(f32[129,128]{1,0:T(8,128)} %add.187.stacked_ref), custom_call_target="tpu_custom_call" | custom-call | tf_op jit(solution)/shard_map/pallas_call | solution.py:98
  56.1 1.8 %fusion.1 = f32[128,16,128]{0,2,1:T(8,128)S(1)} fusion(f32[128,2,128]{2,0,1:T(8,128)S(1)} %broadcast_subtract_fusion.1, f32[128,12,128]{2,0,1:T(8,128)S(1)} %broadcast_subtract_fusion, f32[128,2,128]{2,0,1:T(8,128)S(1)} %broadcast_subtract_fusion.2, f32[16,128]{1,0:T(8,128)S(1)} %maximum_bitcast_fusion, f32[128,128]{1,0:T(8,128)} %shard_map.68), kind=kOutput, calls=%fused_computation.3 | convolution fusion | flops 403439616 | bytes 2170880 | tf_op jit(solution)/shard_map/dot_general | solution.py:251
  58.0 0.0 copy-start.1
  58.0 1.4 %copy.19 = f32[128,16,128]{2,1,0:T(8,128)} copy(f32[128,16,128]{0,2,1:T(8,128)S(1)} %fusion.1) | data formatting | bytes 2097152
  59.3 0.0 copy-done.1
  59.4 1.0 %fusion = f32[128,16,128]{0,2,1:T(8,128)S(1)} fusion(f32[128,16]{0,1:T(8,128)S(1)} %get-tuple-element.32, f32[16,128]{1,0:T(8,128)S(1)} %get-tuple-element.31, f32[128,128]{1,0:T(8,128)S(1)} %copy-done.1, f32[128,16,128]{0,2,1:T(8,128)S(1)} %copy.15), kind=kOutput, calls=%fused_computation.1 | convolution fusion | flops 403177472 | bytes 2179072 | tf_op jit(solution)/shard_map/dot_general | solution.py:254
  60.4 1.4 %copy.20 = f32[128,16,128]{2,1,0:T(8,128)} copy(f32[128,16,128]{0,2,1:T(8,128)S(1)} %fusion) | data formatting | bytes 2097152
  (31 shorter events, 0.4 us)
Async XLA Ops:
  0.6 1.7 %copy-start = (f32[128,16,128]{2,1,0:T(8,128)S(1)}, f32[128,16,128]{2,1,0:T(8,128)}, u32[]{:S(2)}) copy-start(f32[128,16,128]{2,1,0:T(8,128)} %param.5) | copy-start | bytes 3145732
  2.3 7.4 %copy-start.2 = (s32[1024]{0:T(1024)S(1)}, s32[1024]{0:T(1024)}, u32[]{:S(2)}) copy-start(s32[1024]{0:T(1024)} %param.9) | copy-start | bytes 12292
  2.4 7.5 %copy-start.3 = (f32[1024]{0:T(1024)S(1)}, f32[1024]{0:T(1024)}, u32[]{:S(2)}) copy-start(f32[1024]{0:T(1024)} %param.8) | copy-start | bytes 12292
  2.4 7.5 %copy-start.4 = (f32[1024]{0:T(1024)S(1)}, f32[1024]{0:T(1024)}, u32[]{:S(2)}) copy-start(f32[1024]{0:T(1024)} %param.7) | copy-start | bytes 12292
  2.9 7.5 %collective-permute-start.1 = (f32[3,16,128]{2,0,1:T(4,128)S(1)}, f32[3,16,128]{2,0,1:T(4,128)S(1)}, u32[]{:S(2)}, u32[]{:S(2)}) collective-permute-start(f32[3,16,128]{2,0,1:T(4,128)S(1)} %pad_maximum_fusion.19), channel_id=1, source_target_pairs={{1,0},{2,1},{3,2},{5,4},{6,5},{7,6},{9,8},{10,9},{11,10},{13,12},{... | collective-permute-start | bytes 73736 | tf_op jit(solution)/shard_map/ppermute | solution.py:134
  4.2 7.1 %collective-permute-start = (f32[3,16,128]{2,0,1:T(4,128)S(1)}, f32[3,16,128]{2,0,1:T(4,128)S(1)}, u32[]{:S(2)}, u32[]{:S(2)}) collective-permute-start(f32[3,16,128]{2,0,1:T(4,128)S(1)} %pad_maximum_fusion.18), channel_id=1, source_target_pairs={{0,1},{1,2},{2,3},{4,5},{5,6},{6,7},{8,9},{9,10},{10,11},{12,13},{... | collective-permute-start | bytes 73736 | tf_op jit(solution)/shard_map/ppermute | solution.py:134
  11.6 5.7 %collective-permute-start.2 = (f32[132,3,128]{2,0,1:T(8,128)S(1)}, f32[132,3,128]{2,0,1:T(8,128)S(1)}, u32[]{:S(2)}, u32[]{:S(2)}) collective-permute-start(f32[132,3,128]{2,0,1:T(8,128)S(1)} %get-tuple-element.43), channel_id=1, source_target_pairs={{0,4},{4,8},{8,12},{12,16},{16,20},{20,24},{24,28},{1,5},{5,9},{9,... | collective-permute-start | bytes 608264 | tf_op jit(solution)/shard_map/ppermute | solution.py:134
  12.9 5.5 %collective-permute-start.3 = (f32[132,3,128]{2,0,1:T(8,128)S(1)}, f32[132,3,128]{2,0,1:T(8,128)S(1)}, u32[]{:S(2)}, u32[]{:S(2)}) collective-permute-start(f32[132,3,128]{2,0,1:T(8,128)S(1)} %get-tuple-element.44), channel_id=1, source_target_pairs={{4,0},{8,4},{12,8},{16,12},{20,16},{24,20},{28,24},{5,1},{9,5},{13... | collective-permute-start | bytes 608264 | tf_op jit(solution)/shard_map/ppermute | solution.py:134
  21.0 5.2 %collective-permute-start.4 = (f32[129,128]{1,0:T(8,128)S(1)}, f32[129,128]{1,0:T(8,128)S(1)}, u32[]{:S(2)}, u32[]{:S(2)}) collective-permute-start(f32[129,128]{1,0:T(8,128)S(1)} %pad_maximum_fusion.17), channel_id=1, source_target_pairs={{0,4},{4,0},{8,12},{12,8},{16,20},{20,16},{24,28},{28,24},{1,5},{5... | collective-permute-start | bytes 198152 | tf_op jit(solution)/shard_map/ppermute | solution.py:38
  26.2 5.2 %collective-permute-start.5 = (f32[129,128]{1,0:T(8,128)S(1)}, f32[129,128]{1,0:T(8,128)S(1)}, u32[]{:S(2)}, u32[]{:S(2)}) collective-permute-start(f32[129,128]{1,0:T(8,128)S(1)} %fusion.90), channel_id=1, source_target_pairs={{0,8},{4,12},{8,0},{12,4},{16,24},{20,28},{24,16},{28,20},{1,9},{5... | collective-permute-start | bytes 198152 | tf_op jit(solution)/shard_map/ppermute | solution.py:38
  31.4 4.4 %collective-permute-start.6 = (f32[129,128]{1,0:T(8,128)S(1)}, f32[129,128]{1,0:T(8,128)S(1)}, u32[]{:S(2)}, u32[]{:S(2)}) collective-permute-start(f32[129,128]{1,0:T(8,128)S(1)} %add.184), channel_id=1, source_target_pairs={{0,16},{4,20},{8,24},{12,28},{16,0},{20,4},{24,8},{28,12},{1,17},{... | collective-permute-start | bytes 198152 | tf_op jit(solution)/shard_map/ppermute | solution.py:38
  35.8 4.7 %collective-permute-start.7 = (f32[129,128]{1,0:T(8,128)S(1)}, f32[129,128]{1,0:T(8,128)S(1)}, u32[]{:S(2)}, u32[]{:S(2)}) collective-permute-start(f32[129,128]{1,0:T(8,128)S(1)} %add.185), channel_id=1, source_target_pairs={{0,1},{1,0},{2,3},{3,2},{4,5},{5,4},{6,7},{7,6},{8,9},{9,8},{10,11... | collective-permute-start | bytes 198152 | tf_op jit(solution)/shard_map/ppermute | solution.py:38
  40.5 5.4 %collective-permute-start.8 = (f32[129,128]{1,0:T(8,128)S(1)}, f32[129,128]{1,0:T(8,128)S(1)}, u32[]{:S(2)}, u32[]{:S(2)}) collective-permute-start(f32[129,128]{1,0:T(8,128)S(1)} %add.186), channel_id=1, source_target_pairs={{0,2},{1,3},{2,0},{3,1},{4,6},{5,7},{6,4},{7,5},{8,10},{9,11},{10,... | collective-permute-start | bytes 198152 | tf_op jit(solution)/shard_map/ppermute | solution.py:38
  58.0 1.4 %copy-start.1 = (f32[128,128]{1,0:T(8,128)S(1)}, f32[128,128]{1,0:T(8,128)}, u32[]{:S(2)}) copy-start(f32[128,128]{1,0:T(8,128)} %shard_map.68) | copy-start | bytes 196612

commit v22 on v21

--- a/solution.py
+++ b/solution.py
@@ -26,8 +26,8 @@
             value = lax.psum(value, axis)
             continue
         bits = [1 << b for b in range(count.bit_length() - 1)]
-        for first in range(len(bits)):
-            strides = bits[first : first + 1]
+        for first in range(0, len(bits), 2):
+            strides = bits[first : first + 2]
             received = {0: value}
             for mask in range(1, 1 << len(strides)):
                 offset = 0

time: 62.1 us -> 62 us (level)
  starting transfers between devices: 22.6 us -> 23.3 us
    ppermute x5 -> x7, waiting for transfers between devices: 11.3 us -> 10.6 us  [butterfly_sum(): received[offset] = lax.ppermute(value, axis, pairs)]
    ppermute x5 -> x7, starting transfers between devices: 13.2 us -> 13.8 us  [butterfly_sum(): received[offset] = lax.ppermute(value, axis, pairs)]
  transfers between devices with their start and end apart: 9 -> 11, of which waited for: 7 -> 6; matrix products, arithmetic and copies ran while one was open for 6% -> 6% of each run, Pallas kernels for 0% -> 0%
where the time goes in v22:
time: 62 us; the launch traced here: 61.7 us
  starting transfers between devices  23.3 us (38%)
  waiting for transfers between devices  12.7 us (20%)
  Pallas kernels  9.62 us (16%)
  matrix products  6.74 us (11%)
  local copies, waits for them, and re-layouts  5 us (8%)
  other arithmetic  3.4 us (5%)
  between operations  1.02 us (2%)
    ppermute x7, starting transfers between devices, butterfly_sum(): received[offset] = lax.ppermute(value, axis, pairs)  13.8 us
    ppermute x7, waiting for transfers between devices, butterfly_sum(): received[offset] = lax.ppermute(value, axis, pairs)  10.6 us
    pallas_call x1, Pallas kernels, combination_transposed_of(): pl.pallas_call(combination_kernel, out_shape=jax.ShapeDtypeStruct((size,...  9.62 us
    ppermute x4, starting transfers between devices, from_neighbour(): return lax.ppermute(block, axis, pairs)  9.44 us
    unnamed x14, local copies, waits for them, and re-layouts  4.87 us
    dot_general x3, matrix products, shards(): lax.dot_general(deviation * cell_weight[:, :, None], deviation, (((0, 1),...  2.62 us
    ppermute x4, waiting for transfers between devices, from_neighbour(): return lax.ppermute(block, axis, pairs)  2.05 us
    dot_general x1, matrix products, shards(): lax.dot_general(deviation_t, combination_transposed, contract, precision=...  1.82 us
  transfers between devices with their start and end apart: 11, of which 6 were waited for; matrix products, arithmetic and copies ran while one was open for 6% of the time, Pallas kernels for 0%

profile of v22, /device:TPU:0, one launch (start us, length us, event | category | flops | bytes accessed | tf_op | source)
XLA Modules:
  0.0 61.7 jit_solution(5260419926740128881)
XLA Ops:
  0.6 0.0 copy-start
  0.6 1.7 %copy.15 = f32[128,16,128]{0,2,1:T(8,128)S(1)} copy(f32[128,16,128]{2,1,0:T(8,128)} %param.6) | data formatting | bytes 2097152 | tf_op args[1]
  2.3 0.0 copy-done
  2.3 0.0 copy-start.2
  2.4 0.0 copy-start.3
  2.4 0.0 copy-start.4
  2.4 0.4 copy.14
  2.9 1.3 %collective-permute-start.1 = (f32[3,16,128]{2,0,1:T(4,128)S(1)}, f32[3,16,128]{2,0,1:T(4,128)S(1)}, u32[]{:S(2)}, u32[]{:S(2)}) collective-permute-start(f32[3,16,128]{2,0,1:T(4,128)S(1)} %pad_maximum_fusion.19), channel_id=1, source_target_pairs={{1,0},{2,1},{3,2},{5,4},{6,5},{7,6},{9,8},{10,9},{11,10},{13,12},{... | collective-permute-start | bytes 73736 | tf_op jit(solution)/shard_map/ppermute | solution.py:134
  4.2 5.6 %collective-permute-start = (f32[3,16,128]{2,0,1:T(4,128)S(1)}, f32[3,16,128]{2,0,1:T(4,128)S(1)}, u32[]{:S(2)}, u32[]{:S(2)}) collective-permute-start(f32[3,16,128]{2,0,1:T(4,128)S(1)} %pad_maximum_fusion.18), channel_id=1, source_target_pairs={{0,1},{1,2},{2,3},{4,5},{5,6},{6,7},{8,9},{9,10},{10,11},{12,13},{... | collective-permute-start | bytes 73736 | tf_op jit(solution)/shard_map/ppermute | solution.py:134
  9.8 0.0 copy-done.2
  9.8 0.0 copy-done.3
  9.8 0.0 copy-done.4
  9.9 0.4 fusion.31
  10.3 0.1 broadcast_or_fusion.1
  10.3 0.0 collective-permute-done.1
  10.4 1.0 %collective-permute-done = f32[3,16,128]{2,0,1:T(4,128)S(1)} collective-permute-done((f32[3,16,128]{2,0,1:T(4,128)S(1)}, f32[3,16,128]{2,0,1:T(4,128)S(1)}, u32[]{:S(2)}, u32[]{:S(2)}) %collective-permute-start) | collective-permute-done | bytes 24608 | tf_op jit(solution)/shard_map/ppermute | solution.py:134
  11.4 0.1 pad_maximum_fusion
  11.6 1.3 %collective-permute-start.2 = (f32[132,3,128]{2,0,1:T(8,128)S(1)}, f32[132,3,128]{2,0,1:T(8,128)S(1)}, u32[]{:S(2)}, u32[]{:S(2)}) collective-permute-start(f32[132,3,128]{2,0,1:T(8,128)S(1)} %get-tuple-element.43), channel_id=1, source_target_pairs={{0,4},{4,8},{8,12},{12,16},{16,20},{20,24},{24,28},{1,5},{5,9},{9,... | collective-permute-start | bytes 608264 | tf_op jit(solution)/shard_map/ppermute | solution.py:134
  12.9 1.3 %collective-permute-start.3 = (f32[132,3,128]{2,0,1:T(8,128)S(1)}, f32[132,3,128]{2,0,1:T(8,128)S(1)}, u32[]{:S(2)}, u32[]{:S(2)}) collective-permute-start(f32[132,3,128]{2,0,1:T(8,128)S(1)} %get-tuple-element.44), channel_id=1, source_target_pairs={{4,0},{8,4},{12,8},{16,12},{20,16},{24,20},{28,24},{5,1},{9,5},{13... | collective-permute-start | bytes 608264 | tf_op jit(solution)/shard_map/ppermute | solution.py:134
  14.2 0.6 fusion.20
  14.8 0.5 fusion.92
  15.3 0.3 broadcast_subtract_fusion
  15.6 1.7 %fusion.4 = f32[128,128]{1,0:T(8,128)S(1)} fusion(f32[128,12,128]{2,0,1:T(8,128)S(1)} %broadcast_subtract_fusion, f32[128,12]{0,1:T(8,128)S(1)} %get-tuple-element.28), kind=kOutput, calls=%fused_computation.8 | convolution fusion | flops 302186496 | bytes 858112 | tf_op jit(solution)/shard_map/dot_general | solution.py:231
  17.3 0.0 collective-permute-done.2
  17.3 1.1 %collective-permute-done.3 = f32[132,3,128]{2,0,1:T(8,128)S(1)} collective-permute-done((f32[132,3,128]{2,0,1:T(8,128)S(1)}, f32[132,3,128]{2,0,1:T(8,128)S(1)}, u32[]{:S(2)}, u32[]{:S(2)}) %collective-permute-start.3) | collective-permute-done | bytes 202784 | tf_op jit(solution)/shard_map/ppermute | solution.py:134
  18.4 0.1 fusion.54
  18.5 0.1 fusion.45
  18.7 0.2 fusion.90
  18.9 0.1 broadcast_subtract_fusion.1
  19.0 0.1 broadcast_subtract_fusion.2
  19.1 0.2 convolution_bitcast_fusion.6
  19.3 0.5 fusion.10
  19.8 0.5 convolution_bitcast_fusion.2
  20.3 0.2 fusion.11
  20.5 0.5 fusion.8
  21.0 4.0 %collective-permute-start.5 = (f32[129,128]{1,0:T(8,128)S(1)}, f32[129,128]{1,0:T(8,128)S(1)}, u32[]{:S(2)}, u32[]{:S(2)}) collective-permute-start(f32[129,128]{1,0:T(8,128)S(1)} %pad_maximum_fusion.17), channel_id=1, source_target_pairs={{0,8},{4,12},{8,0},{12,4},{16,24},{20,28},{24,16},{28,20},{1,9},{5... | collective-permute-start | bytes 198152 | tf_op jit(solution)/shard_map/ppermute | solution.py:38
  25.0 2.4 %collective-permute-start.6 = (f32[129,128]{1,0:T(8,128)S(1)}, f32[129,128]{1,0:T(8,128)S(1)}, u32[]{:S(2)}, u32[]{:S(2)}) collective-permute-start(f32[129,128]{1,0:T(8,128)S(1)} %pad_maximum_fusion.17), channel_id=1, source_target_pairs={{0,12},{4,8},{8,4},{12,0},{16,28},{20,24},{24,20},{28,16},{1,13},{... | collective-permute-start | bytes 198152 | tf_op jit(solution)/shard_map/ppermute | solution.py:38
  27.4 0.0 collective-permute-start.4
  27.4 0.3 bitcast_reduce_fusion
  27.8 0.0 collective-permute-done.5
  27.8 2.3 %collective-permute-done.6 = f32[129,128]{1,0:T(8,128)S(1)} collective-permute-done((f32[129,128]{1,0:T(8,128)S(1)}, f32[129,128]{1,0:T(8,128)S(1)}, u32[]{:S(2)}, u32[]{:S(2)}) %collective-permute-start.6) | collective-permute-done | bytes 66080 | tf_op jit(solution)/shard_map/ppermute | solution.py:38
  30.0 0.0 collective-permute-done.4
  30.1 2.3 %collective-permute-start.7 = (f32[129,128]{1,0:T(8,128)S(1)}, f32[129,128]{1,0:T(8,128)S(1)}, u32[]{:S(2)}, u32[]{:S(2)}) collective-permute-start(f32[129,128]{1,0:T(8,128)S(1)} %add_add_fusion.1), channel_id=1, source_target_pairs={{0,16},{4,20},{8,24},{12,28},{16,0},{20,4},{24,8},{28,12},{1,17},{... | collective-permute-start | bytes 198152 | tf_op jit(solution)/shard_map/ppermute | solution.py:38
  32.4 2.9 %collective-permute-done.7 = f32[129,128]{1,0:T(8,128)S(1)} collective-permute-done((f32[129,128]{1,0:T(8,128)S(1)}, f32[129,128]{1,0:T(8,128)S(1)}, u32[]{:S(2)}, u32[]{:S(2)}) %collective-permute-start.7) | collective-permute-done | bytes 66080 | tf_op jit(solution)/shard_map/ppermute | solution.py:38
  35.3 4.4 %collective-permute-start.10 = (f32[129,128]{1,0:T(8,128)S(1)}, f32[129,128]{1,0:T(8,128)S(1)}, u32[]{:S(2)}, u32[]{:S(2)}) collective-permute-start(f32[129,128]{1,0:T(8,128)S(1)} %add.192), channel_id=1, source_target_pairs={{0,3},{1,2},{2,1},{3,0},{4,7},{5,6},{6,5},{7,4},{8,11},{9,10},{10,... | collective-permute-start | bytes 198152 | tf_op jit(solution)/shard_map/ppermute | solution.py:38
  39.7 0.0 collective-permute-start.9
  39.7 0.6 %collective-permute-start.8 = (f32[129,128]{1,0:T(8,128)S(1)}, f32[129,128]{1,0:T(8,128)S(1)}, u32[]{:S(2)}, u32[]{:S(2)}) collective-permute-start(f32[129,128]{1,0:T(8,128)S(1)} %add.192), channel_id=1, source_target_pairs={{0,1},{1,0},{2,3},{3,2},{4,5},{5,4},{6,7},{7,6},{8,9},{9,8},{10,11... | collective-permute-start | bytes 198152 | tf_op jit(solution)/shard_map/ppermute | solution.py:38
  40.4 2.0 %collective-permute-done.10 = f32[129,128]{1,0:T(8,128)S(1)} collective-permute-done((f32[129,128]{1,0:T(8,128)S(1)}, f32[129,128]{1,0:T(8,128)S(1)}, u32[]{:S(2)}, u32[]{:S(2)}) %collective-permute-start.10) | collective-permute-done | bytes 66080 | tf_op jit(solution)/shard_map/ppermute | solution.py:38
  42.4 3.4 %collective-permute-done.9 = f32[129,128]{1,0:T(8,128)S(1)} collective-permute-done((f32[129,128]{1,0:T(8,128)S(1)}, f32[129,128]{1,0:T(8,128)S(1)}, u32[]{:S(2)}, u32[]{:S(2)}) %collective-permute-start.9) | collective-permute-done | bytes 66080 | tf_op jit(solution)/shard_map/ppermute | solution.py:38
  45.8 0.0 collective-permute-done.8
  45.8 0.6 %add_add_fusion.stacked_ref = f32[129,128]{1,0:T(8,128)} fusion(f32[129,128]{1,0:T(8,128)S(1)} %collective-permute-done.9, f32[129,128]{1,0:T(8,128)S(1)} %collective-permute-done.10, f32[129,128]{1,0:T(8,128)S(1)} %add.192, f32[129,128]{1,0:T(8,128)S(1)} %collective-permute-done.8), kind=kLoop, calls=%fused_computation.129 | loop fusion | flops 49536 | bytes 330240 | tf_op jit(solution)/shard_map/add | solution.py:17
  46.5 9.6 %shard_map.68 = f32[128,128]{1,0:T(8,128)} custom-call(f32[129,128]{1,0:T(8,128)} %add_add_fusion.stacked_ref), custom_call_target="tpu_custom_call" | custom-call | tf_op jit(solution)/shard_map/pallas_call | solution.py:98
  56.1 1.8 %fusion.1 = f32[128,16,128]{0,2,1:T(8,128)S(1)} fusion(f32[128,2,128]{2,0,1:T(8,128)S(1)} %broadcast_subtract_fusion.1, f32[128,12,128]{2,0,1:T(8,128)S(1)} %broadcast_subtract_fusion, f32[128,2,128]{2,0,1:T(8,128)S(1)} %broadcast_subtract_fusion.2, f32[16,128]{1,0:T(8,128)S(1)} %maximum_bitcast_fusion, f32[128,128]{1,0:T(8,128)} %shard_map.68), kind=kOutput, calls=%fused_computation.3 | convolution fusion | flops 403439616 | bytes 2170880 | tf_op jit(solution)/shard_map/dot_general | solution.py:251
  57.9 0.0 copy-start.1
  57.9 1.4 %copy.19 = f32[128,16,128]{2,1,0:T(8,128)} copy(f32[128,16,128]{0,2,1:T(8,128)S(1)} %fusion.1) | data formatting | bytes 2097152
  59.3 0.0 copy-done.1
  59.3 1.0 %fusion = f32[128,16,128]{0,2,1:T(8,128)S(1)} fusion(f32[128,16]{0,1:T(8,128)S(1)} %get-tuple-element.32, f32[16,128]{1,0:T(8,128)S(1)} %get-tuple-element.31, f32[128,128]{1,0:T(8,128)S(1)} %copy-done.1, f32[128,16,128]{0,2,1:T(8,128)S(1)} %copy.15), kind=kOutput, calls=%fused_computation.1 | convolution fusion | flops 403177472 | bytes 2179072 | tf_op jit(solution)/shard_map/dot_general | solution.py:254
  60.3 1.4 %copy.20 = f32[128,16,128]{2,1,0:T(8,128)} copy(f32[128,16,128]{0,2,1:T(8,128)S(1)} %fusion) | data formatting | bytes 2097152
  (29 shorter events, 0.4 us)
Async XLA Ops:
  0.6 1.7 %copy-start = (f32[128,16,128]{2,1,0:T(8,128)S(1)}, f32[128,16,128]{2,1,0:T(8,128)}, u32[]{:S(2)}) copy-start(f32[128,16,128]{2,1,0:T(8,128)} %param.5) | copy-start | bytes 3145732
  2.3 7.4 %copy-start.2 = (s32[1024]{0:T(1024)S(1)}, s32[1024]{0:T(1024)}, u32[]{:S(2)}) copy-start(s32[1024]{0:T(1024)} %param.9) | copy-start | bytes 12292
  2.4 7.5 %copy-start.3 = (f32[1024]{0:T(1024)S(1)}, f32[1024]{0:T(1024)}, u32[]{:S(2)}) copy-start(f32[1024]{0:T(1024)} %param.8) | copy-start | bytes 12292
  2.4 7.5 %copy-start.4 = (f32[1024]{0:T(1024)S(1)}, f32[1024]{0:T(1024)}, u32[]{:S(2)}) copy-start(f32[1024]{0:T(1024)} %param.7) | copy-start | bytes 12292
  2.9 7.5 %collective-permute-start.1 = (f32[3,16,128]{2,0,1:T(4,128)S(1)}, f32[3,16,128]{2,0,1:T(4,128)S(1)}, u32[]{:S(2)}, u32[]{:S(2)}) collective-permute-start(f32[3,16,128]{2,0,1:T(4,128)S(1)} %pad_maximum_fusion.19), channel_id=1, source_target_pairs={{1,0},{2,1},{3,2},{5,4},{6,5},{7,6},{9,8},{10,9},{11,10},{13,12},{... | collective-permute-start | bytes 73736 | tf_op jit(solution)/shard_map/ppermute | solution.py:134
  4.2 7.1 %collective-permute-start = (f32[3,16,128]{2,0,1:T(4,128)S(1)}, f32[3,16,128]{2,0,1:T(4,128)S(1)}, u32[]{:S(2)}, u32[]{:S(2)}) collective-permute-start(f32[3,16,128]{2,0,1:T(4,128)S(1)} %pad_maximum_fusion.18), channel_id=1, source_target_pairs={{0,1},{1,2},{2,3},{4,5},{5,6},{6,7},{8,9},{9,10},{10,11},{12,13},{... | collective-permute-start | bytes 73736 | tf_op jit(solution)/shard_map/ppermute | solution.py:134
  11.6 5.7 %collective-permute-start.2 = (f32[132,3,128]{2,0,1:T(8,128)S(1)}, f32[132,3,128]{2,0,1:T(8,128)S(1)}, u32[]{:S(2)}, u32[]{:S(2)}) collective-permute-start(f32[132,3,128]{2,0,1:T(8,128)S(1)} %get-tuple-element.43), channel_id=1, source_target_pairs={{0,4},{4,8},{8,12},{12,16},{16,20},{20,24},{24,28},{1,5},{5,9},{9,... | collective-permute-start | bytes 608264 | tf_op jit(solution)/shard_map/ppermute | solution.py:134
  12.9 5.5 %collective-permute-start.3 = (f32[132,3,128]{2,0,1:T(8,128)S(1)}, f32[132,3,128]{2,0,1:T(8,128)S(1)}, u32[]{:S(2)}, u32[]{:S(2)}) collective-permute-start(f32[132,3,128]{2,0,1:T(8,128)S(1)} %get-tuple-element.44), channel_id=1, source_target_pairs={{4,0},{8,4},{12,8},{16,12},{20,16},{24,20},{28,24},{5,1},{9,5},{13... | collective-permute-start | bytes 608264 | tf_op jit(solution)/shard_map/ppermute | solution.py:134
  21.0 6.8 %collective-permute-start.5 = (f32[129,128]{1,0:T(8,128)S(1)}, f32[129,128]{1,0:T(8,128)S(1)}, u32[]{:S(2)}, u32[]{:S(2)}) collective-permute-start(f32[129,128]{1,0:T(8,128)S(1)} %pad_maximum_fusion.17), channel_id=1, source_target_pairs={{0,8},{4,12},{8,0},{12,4},{16,24},{20,28},{24,16},{28,20},{1,9},{5... | collective-permute-start | bytes 198152 | tf_op jit(solution)/shard_map/ppermute | solution.py:38
  25.0 5.0 %collective-permute-start.6 = (f32[129,128]{1,0:T(8,128)S(1)}, f32[129,128]{1,0:T(8,128)S(1)}, u32[]{:S(2)}, u32[]{:S(2)}) collective-permute-start(f32[129,128]{1,0:T(8,128)S(1)} %pad_maximum_fusion.17), channel_id=1, source_target_pairs={{0,12},{4,8},{8,4},{12,0},{16,28},{20,24},{24,20},{28,16},{1,13},{... | collective-permute-start | bytes 198152 | tf_op jit(solution)/shard_map/ppermute | solution.py:38
  27.4 2.7 %collective-permute-start.4 = (f32[129,128]{1,0:T(8,128)S(1)}, f32[129,128]{1,0:T(8,128)S(1)}, u32[]{:S(2)}, u32[]{:S(2)}) collective-permute-start(f32[129,128]{1,0:T(8,128)S(1)} %pad_maximum_fusion.17), channel_id=1, source_target_pairs={{0,4},{4,0},{8,12},{12,8},{16,20},{20,16},{24,28},{28,24},{1,5},{5... | collective-permute-start | bytes 198152 | tf_op jit(solution)/shard_map/ppermute | solution.py:38
  30.1 5.3 %collective-permute-start.7 = (f32[129,128]{1,0:T(8,128)S(1)}, f32[129,128]{1,0:T(8,128)S(1)}, u32[]{:S(2)}, u32[]{:S(2)}) collective-permute-start(f32[129,128]{1,0:T(8,128)S(1)} %add_add_fusion.1), channel_id=1, source_target_pairs={{0,16},{4,20},{8,24},{12,28},{16,0},{20,4},{24,8},{28,12},{1,17},{... | collective-permute-start | bytes 198152 | tf_op jit(solution)/shard_map/ppermute | solution.py:38
  35.3 7.1 %collective-permute-start.10 = (f32[129,128]{1,0:T(8,128)S(1)}, f32[129,128]{1,0:T(8,128)S(1)}, u32[]{:S(2)}, u32[]{:S(2)}) collective-permute-start(f32[129,128]{1,0:T(8,128)S(1)} %add.192), channel_id=1, source_target_pairs={{0,3},{1,2},{2,1},{3,0},{4,7},{5,6},{6,5},{7,4},{8,11},{9,10},{10,... | collective-permute-start | bytes 198152 | tf_op jit(solution)/shard_map/ppermute | solution.py:38
  39.7 6.1 %collective-permute-start.9 = (f32[129,128]{1,0:T(8,128)S(1)}, f32[129,128]{1,0:T(8,128)S(1)}, u32[]{:S(2)}, u32[]{:S(2)}) collective-permute-start(f32[129,128]{1,0:T(8,128)S(1)} %add.192), channel_id=1, source_target_pairs={{0,2},{1,3},{2,0},{3,1},{4,6},{5,7},{6,4},{7,5},{8,10},{9,11},{10,... | collective-permute-start | bytes 198152 | tf_op jit(solution)/shard_map/ppermute | solution.py:38
  39.7 6.1 %collective-permute-start.8 = (f32[129,128]{1,0:T(8,128)S(1)}, f32[129,128]{1,0:T(8,128)S(1)}, u32[]{:S(2)}, u32[]{:S(2)}) collective-permute-start(f32[129,128]{1,0:T(8,128)S(1)} %add.192), channel_id=1, source_target_pairs={{0,1},{1,0},{2,3},{3,2},{4,5},{5,4},{6,7},{7,6},{8,9},{9,8},{10,11... | collective-permute-start | bytes 198152 | tf_op jit(solution)/shard_map/ppermute | solution.py:38
  57.9 1.4 %copy-start.1 = (f32[128,128]{1,0:T(8,128)S(1)}, f32[128,128]{1,0:T(8,128)}, u32[]{:S(2)}) copy-start(f32[128,128]{1,0:T(8,128)} %shard_map.68) | copy-start | bytes 196612

commit v23 on v21

--- a/solution.py
+++ b/solution.py
@@ -40,12 +40,33 @@
     return value
 
 
-def combination_kernel(stacked_ref, combination_ref, work_ref, inverse_ref):
-    size = stacked_ref.shape[1]
+def butterfly_terms(value, axes):
+    *early, last = axes
+    value = butterfly_sum(value, early)
+    count = lax.axis_size(last)
+    if count == 1 or count & (count - 1):
+        return butterfly_sum(value, [last]), jnp.zeros_like(value)
+    stride = count // 2
+    value = butterfly_sum_bits(value, last, count, stride)
+    pairs = [(i, i ^ stride) for i in range(count)]
+    return value, lax.ppermute(value, last, pairs)
+
+
+def butterfly_sum_bits(value, axis, count, limit):
+    stride = 1
+    while stride < limit:
+        pairs = [(i, i ^ stride) for i in range(count)]
+        value = value + lax.ppermute(value, axis, pairs)
+        stride *= 2
+    return value
+
+
+def combination_kernel(own_ref, other_ref, combination_ref, work_ref, inverse_ref):
+    size = own_ref.shape[1]
     square_row = lax.broadcasted_iota(jnp.int32, (size, size), 0)
     square_col = lax.broadcasted_iota(jnp.int32, (size, size), 1)
     unit = jnp.where(square_row == square_col, 1.0, 0.0).astype(jnp.float32)
-    work_ref[...] = stacked_ref[:size, :] + unit
+    work_ref[...] = (own_ref[:size, :] + other_ref[:size, :]) + unit
     inverse_ref[...] = unit
     lane = lax.broadcasted_iota(jnp.int32, (1, size), 1)
 
@@ -87,21 +108,21 @@
 
         lax.fori_loop(first // 2, min(first + 8, size) // 2, step, 0)
     lower_inverse = inverse_ref[...]
-    projected_row = stacked_ref[size : size + 1, :]
+    projected_row = own_ref[size : size + 1, :] + other_ref[size : size + 1, :]
     whitened = jnp.sum(lower_inverse * projected_row, axis=1, keepdims=True)
     mean_weights = jnp.sum(lower_inverse * whitened, axis=0, keepdims=True)
     combination_ref[...] = lower_inverse + mean_weights
 
 
-def combination_transposed_of(stacked):
-    size = stacked.shape[1]
+def combination_transposed_of(own, other):
+    size = own.shape[1]
     return pl.pallas_call(
         combination_kernel,
         out_shape=jax.ShapeDtypeStruct((size, size), jnp.float32),
-        in_specs=[pl.BlockSpec(memory_space=pltpu.VMEM)],
+        in_specs=[pl.BlockSpec(memory_space=pltpu.VMEM)] * 2,
         out_specs=pl.BlockSpec(memory_space=pltpu.VMEM),
         scratch_shapes=[pltpu.VMEM((size, size), jnp.float32)] * 2,
-    )(stacked)
+    )(own, other)
 
 def propagate_model(padded_field, source_term):
     laplacian = (
@@ -245,7 +266,7 @@
     average_t = jnp.concatenate(averages, axis=1)
     deviation_t = jnp.concatenate(deviations, axis=1)
     combination_transposed = combination_transposed_of(
-        butterfly_sum(jnp.concatenate([gram_local, projected[None, :]], axis=0), ("gx", "gy"))
+        *butterfly_terms(jnp.concatenate([gram_local, projected[None, :]], axis=0), ("gx", "gy"))
     )
     contract = (((2,), (1,)), ((), ()))
     updated_t = average_t[:, :, None] + lax.dot_general(

time: 62.1 us -> 62.1 us (level)
  other arithmetic: 3.4 us -> 2.76 us
  local copies, waits for them, and re-layouts: 5 us -> 5.64 us
    ppermute x5 -> x3, starting transfers between devices: 13.2 us -> 7.72 us  [butterfly_sum(): received[offset] = lax.ppermute(value, axis, pairs)]
    ppermute x0 -> x2, starting transfers between devices: none -> 5.48 us  [the longest x1 3.1 us: butterfly_terms(): return (value, lax.ppermute(value, last, pairs))]
    ppermute x5 -> x3, waiting for transfers between devices: 11.3 us -> 6.7 us  [butterfly_sum(): received[offset] = lax.ppermute(value, axis, pairs)]
    ppermute x0 -> x2, waiting for transfers between devices: none -> 4.57 us  [the longest x1 2.29 us: butterfly_sum_bits(): value = value + lax.ppermute(value, axis, pairs)]
    add x5 -> x3, other arithmetic: 0.68 us -> 0.03 us  [xor_tree(): xor_tree(received, base, strides[:-1])]
    unnamed x14 -> x18, local copies, waits for them, and re-layouts: 4.87 us -> 5.51 us
where the time goes in v23:
time: 62.1 us; the launch traced here: 61.8 us
  starting transfers between devices  22.6 us (36%)
  waiting for transfers between devices  13.3 us (21%)
  Pallas kernels  9.66 us (16%)
  matrix products  6.74 us (11%)
  local copies, waits for them, and re-layouts  5.64 us (9%)
  other arithmetic  2.76 us (4%)
  between operations  1.03 us (2%)
    pallas_call x1, Pallas kernels, combination_transposed_of(): pl.pallas_call(combination_kernel, out_shape=jax.ShapeDtypeStruct((size,...  9.66 us
    ppermute x4, starting transfers between devices, from_neighbour(): return lax.ppermute(block, axis, pairs)  9.44 us
    ppermute x3, starting transfers between devices, butterfly_sum(): received[offset] = lax.ppermute(value, axis, pairs)  7.72 us
    ppermute x3, waiting for transfers between devices, butterfly_sum(): received[offset] = lax.ppermute(value, axis, pairs)  6.7 us
    unnamed x18, local copies, waits for them, and re-layouts  5.51 us
    ppermute x1, starting transfers between devices, butterfly_terms(): return (value, lax.ppermute(value, last, pairs))  3.1 us
    dot_general x3, matrix products, shards(): lax.dot_general(deviation * cell_weight[:, :, None], deviation, (((0, 1),...  2.62 us
    ppermute x1, starting transfers between devices, butterfly_sum_bits(): value = value + lax.ppermute(value, axis, pairs)  2.38 us
  transfers between devices with their start and end apart: 9, of which 7 were waited for; matrix products, arithmetic and copies ran while one was open for 6% of the time, Pallas kernels for 0%

profile of v23, /device:TPU:0, one launch (start us, length us, event | category | flops | bytes accessed | tf_op | source)
XLA Modules:
  0.0 61.8 jit_solution(5817172465895662454)
XLA Ops:
  0.6 0.0 copy-start
  0.6 1.7 %copy.15 = f32[128,16,128]{0,2,1:T(8,128)S(1)} copy(f32[128,16,128]{2,1,0:T(8,128)} %param.6) | data formatting | bytes 2097152 | tf_op args[1]
  2.3 0.0 copy-done
  2.3 0.0 copy-start.4
  2.4 0.0 copy-start.5
  2.4 0.0 copy-start.6
  2.4 0.4 copy.14
  2.9 1.3 %collective-permute-start.1 = (f32[3,16,128]{2,0,1:T(4,128)S(1)}, f32[3,16,128]{2,0,1:T(4,128)S(1)}, u32[]{:S(2)}, u32[]{:S(2)}) collective-permute-start(f32[3,16,128]{2,0,1:T(4,128)S(1)} %pad_maximum_fusion.19), channel_id=1, source_target_pairs={{1,0},{2,1},{3,2},{5,4},{6,5},{7,6},{9,8},{10,9},{11,10},{13,12},{... | collective-permute-start | bytes 73736 | tf_op jit(solution)/shard_map/ppermute | solution.py:155
  4.2 5.6 %collective-permute-start = (f32[3,16,128]{2,0,1:T(4,128)S(1)}, f32[3,16,128]{2,0,1:T(4,128)S(1)}, u32[]{:S(2)}, u32[]{:S(2)}) collective-permute-start(f32[3,16,128]{2,0,1:T(4,128)S(1)} %pad_maximum_fusion.18), channel_id=1, source_target_pairs={{0,1},{1,2},{2,3},{4,5},{5,6},{6,7},{8,9},{9,10},{10,11},{12,13},{... | collective-permute-start | bytes 73736 | tf_op jit(solution)/shard_map/ppermute | solution.py:155
  9.8 0.0 copy-done.4
  9.8 0.0 copy-done.5
  9.8 0.0 copy-done.6
  9.9 0.4 fusion.31
  10.3 0.1 broadcast_or_fusion.1
  10.3 0.0 collective-permute-done.1
  10.4 1.0 %collective-permute-done = f32[3,16,128]{2,0,1:T(4,128)S(1)} collective-permute-done((f32[3,16,128]{2,0,1:T(4,128)S(1)}, f32[3,16,128]{2,0,1:T(4,128)S(1)}, u32[]{:S(2)}, u32[]{:S(2)}) %collective-permute-start) | collective-permute-done | bytes 24608 | tf_op jit(solution)/shard_map/ppermute | solution.py:155
  11.4 0.1 pad_maximum_fusion
  11.6 1.3 %collective-permute-start.2 = (f32[132,3,128]{2,0,1:T(8,128)S(1)}, f32[132,3,128]{2,0,1:T(8,128)S(1)}, u32[]{:S(2)}, u32[]{:S(2)}) collective-permute-start(f32[132,3,128]{2,0,1:T(8,128)S(1)} %get-tuple-element.43), channel_id=1, source_target_pairs={{0,4},{4,8},{8,12},{12,16},{16,20},{20,24},{24,28},{1,5},{5,9},{9,... | collective-permute-start | bytes 608264 | tf_op jit(solution)/shard_map/ppermute | solution.py:155
  12.9 1.3 %collective-permute-start.3 = (f32[132,3,128]{2,0,1:T(8,128)S(1)}, f32[132,3,128]{2,0,1:T(8,128)S(1)}, u32[]{:S(2)}, u32[]{:S(2)}) collective-permute-start(f32[132,3,128]{2,0,1:T(8,128)S(1)} %get-tuple-element.44), channel_id=1, source_target_pairs={{4,0},{8,4},{12,8},{16,12},{20,16},{24,20},{28,24},{5,1},{9,5},{13... | collective-permute-start | bytes 608264 | tf_op jit(solution)/shard_map/ppermute | solution.py:155
  14.2 0.6 fusion.20
  14.8 0.5 fusion.93
  15.3 0.3 broadcast_subtract_fusion
  15.6 1.7 %fusion.4 = f32[128,128]{1,0:T(8,128)S(1)} fusion(f32[128,12,128]{2,0,1:T(8,128)S(1)} %broadcast_subtract_fusion, f32[128,12]{0,1:T(8,128)S(1)} %get-tuple-element.28), kind=kOutput, calls=%fused_computation.8 | convolution fusion | flops 302186496 | bytes 858112 | tf_op jit(solution)/shard_map/dot_general | solution.py:252
  17.3 0.0 collective-permute-done.2
  17.3 1.1 %collective-permute-done.3 = f32[132,3,128]{2,0,1:T(8,128)S(1)} collective-permute-done((f32[132,3,128]{2,0,1:T(8,128)S(1)}, f32[132,3,128]{2,0,1:T(8,128)S(1)}, u32[]{:S(2)}, u32[]{:S(2)}) %collective-permute-start.3) | collective-permute-done | bytes 202784 | tf_op jit(solution)/shard_map/ppermute | solution.py:155
  18.4 0.1 fusion.54
  18.5 0.1 fusion.45
  18.7 0.2 fusion.91
  18.9 0.1 broadcast_subtract_fusion.1
  19.0 0.1 broadcast_subtract_fusion.2
  19.1 0.2 convolution_bitcast_fusion.6
  19.3 0.5 fusion.10
  19.8 0.5 convolution_bitcast_fusion.2
  20.3 0.2 fusion.11
  20.5 0.5 fusion.8
  21.0 4.3 %collective-permute-start.4 = (f32[129,128]{1,0:T(8,128)S(1)}, f32[129,128]{1,0:T(8,128)S(1)}, u32[]{:S(2)}, u32[]{:S(2)}) collective-permute-start(f32[129,128]{1,0:T(8,128)S(1)} %pad_maximum_fusion.17), channel_id=1, source_target_pairs={{0,4},{4,0},{8,12},{12,8},{16,20},{20,16},{24,28},{28,24},{1,5},{5... | collective-permute-start | bytes 198152 | tf_op jit(solution)/shard_map/ppermute | solution.py:38
  25.3 0.9 %collective-permute-done.4 = f32[129,128]{1,0:T(8,128)S(1)} collective-permute-done((f32[129,128]{1,0:T(8,128)S(1)}, f32[129,128]{1,0:T(8,128)S(1)}, u32[]{:S(2)}, u32[]{:S(2)}) %collective-permute-start.4) | collective-permute-done | bytes 66080 | tf_op jit(solution)/shard_map/ppermute | solution.py:38
  26.2 2.5 %collective-permute-start.5 = (f32[129,128]{1,0:T(8,128)S(1)}, f32[129,128]{1,0:T(8,128)S(1)}, u32[]{:S(2)}, u32[]{:S(2)}) collective-permute-start(f32[129,128]{1,0:T(8,128)S(1)} %fusion.90), channel_id=1, source_target_pairs={{0,8},{4,12},{8,0},{12,4},{16,24},{20,28},{24,16},{28,20},{1,9},{5... | collective-permute-start | bytes 198152 | tf_op jit(solution)/shard_map/ppermute | solution.py:38
  28.7 2.7 %collective-permute-done.5 = f32[129,128]{1,0:T(8,128)S(1)} collective-permute-done((f32[129,128]{1,0:T(8,128)S(1)}, f32[129,128]{1,0:T(8,128)S(1)}, u32[]{:S(2)}, u32[]{:S(2)}) %collective-permute-start.5) | collective-permute-done | bytes 66080 | tf_op jit(solution)/shard_map/ppermute | solution.py:38
  31.4 0.9 %collective-permute-start.6 = (f32[129,128]{1,0:T(8,128)S(1)}, f32[129,128]{1,0:T(8,128)S(1)}, u32[]{:S(2)}, u32[]{:S(2)}) collective-permute-start(f32[129,128]{1,0:T(8,128)S(1)} %add.181), channel_id=1, source_target_pairs={{0,16},{4,20},{8,24},{12,28},{16,0},{20,4},{24,8},{28,12},{1,17},{... | collective-permute-start | bytes 198152 | tf_op jit(solution)/shard_map/ppermute | solution.py:38
  32.3 0.3 bitcast_reduce_fusion
  32.7 3.1 %collective-permute-done.6 = f32[129,128]{1,0:T(8,128)S(1)} collective-permute-done((f32[129,128]{1,0:T(8,128)S(1)}, f32[129,128]{1,0:T(8,128)S(1)}, u32[]{:S(2)}, u32[]{:S(2)}) %collective-permute-start.6) | collective-permute-done | bytes 66080 | tf_op jit(solution)/shard_map/ppermute | solution.py:38
  35.8 2.4 %collective-permute-start.7 = (f32[129,128]{1,0:T(8,128)S(1)}, f32[129,128]{1,0:T(8,128)S(1)}, u32[]{:S(2)}, u32[]{:S(2)}) collective-permute-start(f32[129,128]{1,0:T(8,128)S(1)} %add.182), channel_id=1, source_target_pairs={{0,1},{1,0},{2,3},{3,2},{4,5},{5,4},{6,7},{7,6},{8,9},{9,8},{10,11... | collective-permute-start | bytes 198152 | tf_op jit(solution)/shard_map/ppermute | solution.py:59
  38.2 2.3 %collective-permute-done.7 = f32[129,128]{1,0:T(8,128)S(1)} collective-permute-done((f32[129,128]{1,0:T(8,128)S(1)}, f32[129,128]{1,0:T(8,128)S(1)}, u32[]{:S(2)}, u32[]{:S(2)}) %collective-permute-start.7) | collective-permute-done | bytes 66080 | tf_op jit(solution)/shard_map/ppermute | solution.py:59
  40.5 0.0 copy-start.2
  40.5 3.1 %collective-permute-start.8 = (f32[129,128]{1,0:T(8,128)S(1)}, f32[129,128]{1,0:T(8,128)S(1)}, u32[]{:S(2)}, u32[]{:S(2)}) collective-permute-start(f32[129,128]{1,0:T(8,128)S(1)} %add.183.own_ref), channel_id=1, source_target_pairs={{0,2},{1,3},{2,0},{3,1},{4,6},{5,7},{6,4},{7,5},{8,10},{9,11},{10,... | collective-permute-start | bytes 198152 | tf_op jit(solution)/shard_map/ppermute | solution.py:52
  43.6 2.3 %collective-permute-done.8.other_ref = f32[129,128]{1,0:T(8,128)S(1)} collective-permute-done((f32[129,128]{1,0:T(8,128)S(1)}, f32[129,128]{1,0:T(8,128)S(1)}, u32[]{:S(2)}, u32[]{:S(2)}) %collective-permute-start.8) | collective-permute-done | bytes 66080 | tf_op jit(solution)/shard_map/ppermute | solution.py:52
  45.9 0.0 copy-done.2
  45.9 0.0 copy-start.3
  45.9 0.6 %copy-done.3 = f32[129,128]{1,0:T(8,128)} copy-done((f32[129,128]{1,0:T(8,128)}, f32[129,128]{1,0:T(8,128)S(1)}, u32[]{:S(2)}) %copy-start.3) | copy-done | bytes 66072
  46.5 9.7 %shard_map.68 = f32[128,128]{1,0:T(8,128)} custom-call(f32[129,128]{1,0:T(8,128)} %copy-done.2, f32[129,128]{1,0:T(8,128)} %copy-done.3), custom_call_target="tpu_custom_call" | custom-call | tf_op jit(solution)/shard_map/pallas_call | solution.py:119
  56.2 1.8 %fusion.1 = f32[128,16,128]{0,2,1:T(8,128)S(1)} fusion(f32[128,2,128]{2,0,1:T(8,128)S(1)} %broadcast_subtract_fusion.1, f32[128,12,128]{2,0,1:T(8,128)S(1)} %broadcast_subtract_fusion, f32[128,2,128]{2,0,1:T(8,128)S(1)} %broadcast_subtract_fusion.2, f32[16,128]{1,0:T(8,128)S(1)} %maximum_bitcast_fusion, f32[128,128]{1,0:T(8,128)} %shard_map.68), kind=kOutput, calls=%fused_computation.3 | convolution fusion | flops 403439616 | bytes 2170880 | tf_op jit(solution)/shard_map/dot_general | solution.py:272
  58.0 0.0 copy-start.1
  58.0 1.4 %copy.19 = f32[128,16,128]{2,1,0:T(8,128)} copy(f32[128,16,128]{0,2,1:T(8,128)S(1)} %fusion.1) | data formatting | bytes 2097152
  59.4 0.0 copy-done.1
  59.4 1.0 %fusion = f32[128,16,128]{0,2,1:T(8,128)S(1)} fusion(f32[128,16]{0,1:T(8,128)S(1)} %get-tuple-element.32, f32[16,128]{1,0:T(8,128)S(1)} %get-tuple-element.31, f32[128,128]{1,0:T(8,128)S(1)} %copy-done.1, f32[128,16,128]{0,2,1:T(8,128)S(1)} %copy.15), kind=kOutput, calls=%fused_computation.1 | convolution fusion | flops 403177472 | bytes 2179072 | tf_op jit(solution)/shard_map/dot_general | solution.py:275
  60.4 1.4 %copy.20 = f32[128,16,128]{2,1,0:T(8,128)} copy(f32[128,16,128]{0,2,1:T(8,128)S(1)} %fusion) | data formatting | bytes 2097152
  (31 shorter events, 0.4 us)
Async XLA Ops:
  0.6 1.7 %copy-start = (f32[128,16,128]{2,1,0:T(8,128)S(1)}, f32[128,16,128]{2,1,0:T(8,128)}, u32[]{:S(2)}) copy-start(f32[128,16,128]{2,1,0:T(8,128)} %param.5) | copy-start | bytes 3145732
  2.3 7.4 %copy-start.4 = (s32[1024]{0:T(1024)S(1)}, s32[1024]{0:T(1024)}, u32[]{:S(2)}) copy-start(s32[1024]{0:T(1024)} %param.9) | copy-start | bytes 12292
  2.4 7.5 %copy-start.5 = (f32[1024]{0:T(1024)S(1)}, f32[1024]{0:T(1024)}, u32[]{:S(2)}) copy-start(f32[1024]{0:T(1024)} %param.8) | copy-start | bytes 12292
  2.4 7.5 %copy-start.6 = (f32[1024]{0:T(1024)S(1)}, f32[1024]{0:T(1024)}, u32[]{:S(2)}) copy-start(f32[1024]{0:T(1024)} %param.7) | copy-start | bytes 12292
  2.9 7.5 %collective-permute-start.1 = (f32[3,16,128]{2,0,1:T(4,128)S(1)}, f32[3,16,128]{2,0,1:T(4,128)S(1)}, u32[]{:S(2)}, u32[]{:S(2)}) collective-permute-start(f32[3,16,128]{2,0,1:T(4,128)S(1)} %pad_maximum_fusion.19), channel_id=1, source_target_pairs={{1,0},{2,1},{3,2},{5,4},{6,5},{7,6},{9,8},{10,9},{11,10},{13,12},{... | collective-permute-start | bytes 73736 | tf_op jit(solution)/shard_map/ppermute | solution.py:155
  4.2 7.1 %collective-permute-start = (f32[3,16,128]{2,0,1:T(4,128)S(1)}, f32[3,16,128]{2,0,1:T(4,128)S(1)}, u32[]{:S(2)}, u32[]{:S(2)}) collective-permute-start(f32[3,16,128]{2,0,1:T(4,128)S(1)} %pad_maximum_fusion.18), channel_id=1, source_target_pairs={{0,1},{1,2},{2,3},{4,5},{5,6},{6,7},{8,9},{9,10},{10,11},{12,13},{... | collective-permute-start | bytes 73736 | tf_op jit(solution)/shard_map/ppermute | solution.py:155
  11.6 5.7 %collective-permute-start.2 = (f32[132,3,128]{2,0,1:T(8,128)S(1)}, f32[132,3,128]{2,0,1:T(8,128)S(1)}, u32[]{:S(2)}, u32[]{:S(2)}) collective-permute-start(f32[132,3,128]{2,0,1:T(8,128)S(1)} %get-tuple-element.43), channel_id=1, source_target_pairs={{0,4},{4,8},{8,12},{12,16},{16,20},{20,24},{24,28},{1,5},{5,9},{9,... | collective-permute-start | bytes 608264 | tf_op jit(solution)/shard_map/ppermute | solution.py:155
  12.9 5.5 %collective-permute-start.3 = (f32[132,3,128]{2,0,1:T(8,128)S(1)}, f32[132,3,128]{2,0,1:T(8,128)S(1)}, u32[]{:S(2)}, u32[]{:S(2)}) collective-permute-start(f32[132,3,128]{2,0,1:T(8,128)S(1)} %get-tuple-element.44), channel_id=1, source_target_pairs={{4,0},{8,4},{12,8},{16,12},{20,16},{24,20},{28,24},{5,1},{9,5},{13... | collective-permute-start | bytes 608264 | tf_op jit(solution)/shard_map/ppermute | solution.py:155
  21.0 5.2 %collective-permute-start.4 = (f32[129,128]{1,0:T(8,128)S(1)}, f32[129,128]{1,0:T(8,128)S(1)}, u32[]{:S(2)}, u32[]{:S(2)}) collective-permute-start(f32[129,128]{1,0:T(8,128)S(1)} %pad_maximum_fusion.17), channel_id=1, source_target_pairs={{0,4},{4,0},{8,12},{12,8},{16,20},{20,16},{24,28},{28,24},{1,5},{5... | collective-permute-start | bytes 198152 | tf_op jit(solution)/shard_map/ppermute | solution.py:38
  26.2 5.2 %collective-permute-start.5 = (f32[129,128]{1,0:T(8,128)S(1)}, f32[129,128]{1,0:T(8,128)S(1)}, u32[]{:S(2)}, u32[]{:S(2)}) collective-permute-start(f32[129,128]{1,0:T(8,128)S(1)} %fusion.90), channel_id=1, source_target_pairs={{0,8},{4,12},{8,0},{12,4},{16,24},{20,28},{24,16},{28,20},{1,9},{5... | collective-permute-start | bytes 198152 | tf_op jit(solution)/shard_map/ppermute | solution.py:38
  31.4 4.4 %collective-permute-start.6 = (f32[129,128]{1,0:T(8,128)S(1)}, f32[129,128]{1,0:T(8,128)S(1)}, u32[]{:S(2)}, u32[]{:S(2)}) collective-permute-start(f32[129,128]{1,0:T(8,128)S(1)} %add.181), channel_id=1, source_target_pairs={{0,16},{4,20},{8,24},{12,28},{16,0},{20,4},{24,8},{28,12},{1,17},{... | collective-permute-start | bytes 198152 | tf_op jit(solution)/shard_map/ppermute | solution.py:38
  35.8 4.7 %collective-permute-start.7 = (f32[129,128]{1,0:T(8,128)S(1)}, f32[129,128]{1,0:T(8,128)S(1)}, u32[]{:S(2)}, u32[]{:S(2)}) collective-permute-start(f32[129,128]{1,0:T(8,128)S(1)} %add.182), channel_id=1, source_target_pairs={{0,1},{1,0},{2,3},{3,2},{4,5},{5,4},{6,7},{7,6},{8,9},{9,8},{10,11... | collective-permute-start | bytes 198152 | tf_op jit(solution)/shard_map/ppermute | solution.py:59
  40.5 5.4 %copy-start.2 = (f32[129,128]{1,0:T(8,128)}, f32[129,128]{1,0:T(8,128)S(1)}, u32[]{:S(2)}) copy-start(f32[129,128]{1,0:T(8,128)S(1)} %add.183.own_ref) | copy-start | bytes 198148
  40.5 5.4 %collective-permute-start.8 = (f32[129,128]{1,0:T(8,128)S(1)}, f32[129,128]{1,0:T(8,128)S(1)}, u32[]{:S(2)}, u32[]{:S(2)}) collective-permute-start(f32[129,128]{1,0:T(8,128)S(1)} %add.183.own_ref), channel_id=1, source_target_pairs={{0,2},{1,3},{2,0},{3,1},{4,6},{5,7},{6,4},{7,5},{8,10},{9,11},{10,... | collective-permute-start | bytes 198152 | tf_op jit(solution)/shard_map/ppermute | solution.py:52
  45.9 0.6 %copy-start.3 = (f32[129,128]{1,0:T(8,128)}, f32[129,128]{1,0:T(8,128)S(1)}, u32[]{:S(2)}) copy-start(f32[129,128]{1,0:T(8,128)S(1)} %collective-permute-done.8.other_ref) | copy-start | bytes 198148
  58.0 1.4 %copy-start.1 = (f32[128,128]{1,0:T(8,128)S(1)}, f32[128,128]{1,0:T(8,128)}, u32[]{:S(2)}) copy-start(f32[128,128]{1,0:T(8,128)} %shard_map.68) | copy-start | bytes 196612

commit v24 on v21

--- a/solution.py
+++ b/solution.py
@@ -243,7 +243,7 @@
         averages.append(average)
         deviations.append(deviation)
     average_t = jnp.concatenate(averages, axis=1)
-    deviation_t = jnp.concatenate(deviations, axis=1)
+    deviation_t = lax.optimization_barrier(jnp.concatenate(deviations, axis=1))
     combination_transposed = combination_transposed_of(
         butterfly_sum(jnp.concatenate([gram_local, projected[None, :]], axis=0), ("gx", "gy"))
     )

time: 62.1 us -> 89 us (1.43)
  other arithmetic: 3.4 us -> 18 us
  local copies, waits for them, and re-layouts: 5 us -> 17.2 us
  waiting for transfers between devices: 13.3 us -> 8.85 us
  matrix products: 6.74 us -> 9.71 us
    mul x0 -> x3, other arithmetic: none -> 3.8 us  [shards(): deviation * cell_weight[:, :, None]]
    sub x0 -> x3, local copies, waits for them, and re-layouts: none -> 2.57 us  [shards(): deviation = piece - average[:, :, None]]
    ppermute x5, waiting for transfers between devices: 11.3 us -> 8.84 us  [butterfly_sum(): received[offset] = lax.ppermute(value, axis, pairs)]
    reduce_sum x2, other arithmetic: 0.74 us -> 2.91 us  [shards(): average = jnp.mean(piece, axis=2)]
    sub x3, other arithmetic: 0.47 us -> 2.54 us  [the longest x2 2.21 us: shards(): cell_sums[:, block_height_number + start:block_height_number + start + co...]
    ppermute x4, waiting for transfers between devices: 2.05 us -> 0.01 us  [from_neighbour(): return lax.ppermute(block, axis, pairs)]
    dot_general x3, matrix products: 2.62 us -> 4.44 us  [shards(): lax.dot_general(deviation * cell_weight[:, :, None], deviation, (((0, 1),...]
    slice x0 -> x3, local copies, waits for them, and re-layouts: none -> 1.64 us  [shards(): cell_weight = cell_sums[:, start:start + count]]
  transfers between devices with their start and end apart: 9 -> 9, of which waited for: 7 -> 5; matrix products, arithmetic and copies ran while one was open for 6% -> 25% of each run, Pallas kernels for 0% -> 0%
where the time goes in v24:
time: 89 us; the launch traced here: 88.2 us
  starting transfers between devices  23.3 us (26%)
  other arithmetic  18 us (20%)
  local copies, waits for them, and re-layouts  17.2 us (19%)
  Pallas kernels  9.84 us (11%)
  matrix products  9.71 us (11%)
  waiting for transfers between devices  8.85 us (10%)
  between operations  1.18 us (1%)
    ppermute x5, starting transfers between devices, butterfly_sum(): received[offset] = lax.ppermute(value, axis, pairs)  12.9 us
    ppermute x4, starting transfers between devices, from_neighbour(): return lax.ppermute(block, axis, pairs)  10.5 us
    pallas_call x1, Pallas kernels, combination_transposed_of(): pl.pallas_call(combination_kernel, out_shape=jax.ShapeDtypeStruct((size,...  9.84 us
    ppermute x5, waiting for transfers between devices, butterfly_sum(): received[offset] = lax.ppermute(value, axis, pairs)  8.84 us
    unnamed x40, local copies, waits for them, and re-layouts  5.52 us
    dot_general x3, matrix products, shards(): lax.dot_general(deviation * cell_weight[:, :, None], deviation, (((0, 1),...  4.44 us
    mul x3, other arithmetic, shards(): deviation * cell_weight[:, :, None]  3.8 us
    reduce_sum x2, other arithmetic, shards(): average = jnp.mean(piece, axis=2)  2.91 us
  transfers between devices with their start and end apart: 9, of which 5 were waited for; matrix products, arithmetic and copies ran while one was open for 25% of the time, Pallas kernels for 0%

profile of v24, /device:TPU:0, one launch (start us, length us, event | category | flops | bytes accessed | tf_op | source)
XLA Modules:
  0.0 88.2 jit_solution(17151853615869716397)
XLA Ops:
  0.6 1.9 %copy.71 = f32[128,16,128]{0,1,2:T(8,128)S(1)} copy(f32[128,16,128]{2,1,0:T(8,128)} %param.6) | data formatting | bytes 2097152 | tf_op args[1]
  2.6 0.7 copy.70
  3.4 1.3 %collective-permute-start.1 = (f32[3,16,128]{2,1,0:T(8,128)S(1)}, f32[3,16,128]{2,1,0:T(8,128)S(1)}, u32[]{:S(2)}, u32[]{:S(2)}) collective-permute-start(f32[3,16,128]{2,1,0:T(8,128)S(1)} %pad_maximum_fusion.20), channel_id=1, source_target_pairs={{1,0},{2,1},{3,2},{5,4},{6,5},{7,6},{9,8},{10,9},{11,10},{13,12},{... | collective-permute-start | bytes 73736 | tf_op jit(solution)/shard_map/ppermute | solution.py:134
  4.7 5.6 %collective-permute-start = (f32[3,16,128]{2,1,0:T(8,128)S(1)}, f32[3,16,128]{2,1,0:T(8,128)S(1)}, u32[]{:S(2)}, u32[]{:S(2)}) collective-permute-start(f32[3,16,128]{2,1,0:T(8,128)S(1)} %pad_maximum_fusion.19), channel_id=1, source_target_pairs={{0,1},{1,2},{2,3},{4,5},{5,6},{6,7},{8,9},{9,10},{10,11},{12,13},{... | collective-permute-start | bytes 73736 | tf_op jit(solution)/shard_map/ppermute | solution.py:134
  10.4 0.7 broadcast_or_fusion.1
  11.1 1.0 %fusion.22 = f32[128,32]{0,1:T(8,128)} fusion(s32[1024]{0:T(1024)S(1)} %get-tuple-element.48, f32[1024,16]{0,1:T(8,128)S(1)} %get-tuple-element.44, f32[1024,16]{0,1:T(8,128)S(1)} %get-tuple-element.43), kind=kOutput, calls=%fused_computation.45 | convolution fusion | flops 50495488 | bytes 151552 | tf_op jit(solution)/shard_map/dot_general | solution.py:218
  12.2 0.1 pad_maximum_fusion.11
  12.3 0.1 pad_maximum_fusion.18
  12.4 1.7 %fusion.9 = f32[130,14,128]{2,1,0:T(8,128)S(1)} fusion(f32[1,16,128]{2,1,0:T(8,128)S(1)} %slice.257, f32[128,16,128]{2,1,0:T(8,128)S(1)} %bitcast.63, f32[1,16,128]{2,1,0:T(8,128)S(1)} %slice.256, f32[128,16,128]{2,1,0:T(8,128)S(1)} %bitcast.69, f32[2,16,128]{2,1,0:T(8,128)S(1)} %slice.252, f32[2,16,128]{2,1,0:T(8,128)S(1)} %slice.255, ...), kind=kLoop, calls=%fused_computation.19 | loop fusion | flops 3261440 | bytes 5873794 | tf_op jit(solution)/shard_map/jit(_where)/select_n | solution.py:165
  14.1 1.1 %fusion.23 = (f32[132,3,128]{2,1,0:T(4,128)}, f32[132,3,128]{2,1,0:T(4,128)}) fusion(f32[1,1,128]{2,1,0:T(1,128)S(1)} %broadcast_in_dim.51, f32[130,1,128]{2,1,0:T(1,128)S(1)} %get-tuple-element.28, f32[132,2,128]{2,1,0:T(2,128)S(1)} %get-tuple-element.24, f32[130,1,128]{2,1,0:T(1,128)S(1)} %get-tuple-element.29, f32[132,2,128]{2,1,0:T(2,128)S(1)} %get-tuple-element.25), kind=kLoop, calls=%fused_computation.66 | loop fusion | flops 304128 | bytes 809472 | tf_op jit(solution)/shard_map/concatenate | solution.py:145
  15.2 2.2 %collective-permute-start.2 = (f32[132,3,128]{2,1,0:T(4,128)}, f32[132,3,128]{2,1,0:T(4,128)}, u32[]{:S(2)}, u32[]{:S(2)}) collective-permute-start(f32[132,3,128]{2,1,0:T(4,128)} %get-tuple-element.53), channel_id=1, source_target_pairs={{0,4},{4,8},{8,12},{12,16},{16,20},{20,24},{24,28},{1,5},{5,9},{9,... | collective-permute-start | bytes 608264 | tf_op jit(solution)/shard_map/ppermute | solution.py:134
  17.4 1.5 %collective-permute-start.3 = (f32[132,3,128]{2,1,0:T(4,128)}, f32[132,3,128]{2,1,0:T(4,128)}, u32[]{:S(2)}, u32[]{:S(2)}) collective-permute-start(f32[132,3,128]{2,1,0:T(4,128)} %get-tuple-element.54), channel_id=1, source_target_pairs={{4,0},{8,4},{12,8},{16,12},{20,16},{24,20},{28,24},{5,1},{9,5},{13... | collective-permute-start | bytes 608264 | tf_op jit(solution)/shard_map/ppermute | solution.py:134
  18.8 2.1 %fusion.71 = (f32[128,12]{1,0:T(8,128)}, f32[128,12,128]{2,1,0:T(8,128)}) fusion(f32[128,16,128]{2,1,0:T(8,128)S(1)} %bitcast.64, f32[130,14,128]{2,1,0:T(8,128)S(1)} %fusion.9), kind=kLoop, calls=%fused_computation.158 | loop fusion | flops 1964544 | bytes 5511168 | tf_op jit(solution)/shard_map/reduce_sum | solution.py:224
  21.0 0.9 %copy.73 = f32[128,12]{0,1:T(8,128)S(1)} copy(f32[128,12]{1,0:T(8,128)} %get-tuple-element.18) | data formatting | bytes 12288 | tf_op jit(solution)/shard_map/reduce_sum | solution.py:224
  21.9 1.4 %fusion.61 = (f32[128,12,1]{0,1,2:T(8,128)}, f32[128,12]{0,1:T(8,128)}, f32[128,12]{0,1:T(8,128)S(1)}) fusion(f32[128,32]{0,1:T(8,128)} %fusion.22, f32[128,12]{0,1:T(8,128)S(1)} %copy.73), kind=kLoop, calls=%fused_computation.132 | loop fusion | flops 4608 | bytes 36864 | tf_op jit(solution)/shard_map/sub | solution.py:228
  23.3 1.4 %copy.81 = f32[128,12]{1,0:T(8,128)} copy(f32[128,12]{0,1:T(8,128)} %get-tuple-element.41) | data formatting | bytes 12288 | tf_op jit(solution)/shard_map/slice | solution.py:226
  24.7 0.7 copy.76
  25.4 3.1 %broadcast_multiply_fusion = (f32[128,12,128]{2,1,0:T(8,128)}, f32[128,12,128]{2,1,0:T(8,128)}) fusion(f32[128,12]{1,0:T(8,128)} %copy.81, f32[128,12,128]{2,1,0:T(8,128)} %get-tuple-element.19, f32[128,12]{1,0:T(8,128)} %copy.76), kind=kLoop, calls=%fused_computation.42 | loop fusion | flops 393216 | bytes 2371584 | tf_op jit(solution)/shard_map/mul | solution.py:232
  28.5 0.8 fusion.75
  29.3 2.4 %copy.94 = f32[128,12,128]{0,2,1:T(8,128)} copy(f32[128,12,128]{2,1,0:T(8,128)} %get-tuple-element.13) | data formatting | bytes 1572864 | tf_op jit(solution)/shard_map/sub | solution.py:225
  31.7 3.6 %convolution_bitcast_fusion.2 = f32[128,128]{1,0:T(8,128)} fusion(f32[128,12,128]{0,2,1:T(8,128)} %copy.94, f32[128,12,128]{2,1,0:T(8,128)} %get-tuple-element.12), kind=kOutput, calls=%fused_computation.4 | convolution fusion | flops 301989888 | bytes 1638400 | tf_op jit(solution)/shard_map/dot_general | solution.py:231
  35.3 1.0 %slice.264 = f32[130,1,128]{2,1,0:T(1,128)S(1)} slice(f32[132,3,128]{2,1,0:T(4,128)} %collective-permute-done.2), slice={[1:131], [2:3], [0:128]} | slice | bytes 133120 | tf_op jit(solution)/shard_map/slice | solution.py:171
  36.4 1.0 %slice.258 = f32[132,2,128]{2,1,0:T(2,128)S(1)} slice(f32[132,3,128]{2,1,0:T(4,128)} %collective-permute-done.2), slice={[0:132], [0:2], [0:128]} | slice | bytes 270336 | tf_op jit(solution)/shard_map/slice | solution.py:170
  37.4 1.0 %slice.289 = f32[130,1,128]{2,1,0:T(1,128)S(1)} slice(f32[132,3,128]{2,1,0:T(4,128)} %collective-permute-done.3), slice={[1:131], [2:3], [0:128]} | slice | bytes 133120 | tf_op jit(solution)/shard_map/slice | solution.py:175
  38.4 1.0 %slice.283 = f32[132,2,128]{2,1,0:T(2,128)S(1)} slice(f32[132,3,128]{2,1,0:T(4,128)} %collective-permute-done.3), slice={[0:132], [0:2], [0:128]} | slice | bytes 270336 | tf_op jit(solution)/shard_map/slice | solution.py:174
  39.4 1.4 %fusion.37 = f32[130,2,128]{2,1,0:T(2,128)S(1)} fusion(f32[130,1,128]{2,1,0:T(1,128)S(1)} %copy-done.4, f32[130,1,128]{2,1,0:T(1,128)S(1)} %slice.264, f32[132,2,128]{2,1,0:T(2,128)S(1)} %get-tuple-element.25, f32[132,2,128]{2,1,0:T(2,128)S(1)} %slice.258, f32[132,3,128]{2,1,0:T(4,128)} %collective-permute-done.2, f32[2,16,128]{2,1,0:T(8,128)S(1)} %slice.255, ...), kind=kLoop, calls=%fused_computation.87 | loop fusion | flops 532480 | bytes 1751300 | tf_op jit(solution)/shard_map/jit(_where)/select_n | solution.py:178
  40.9 1.5 %fusion.39 = f32[130,2,128]{2,1,0:T(2,128)S(1)} fusion(f32[130,1,128]{2,1,0:T(1,128)S(1)} %slice.289, f32[130,1,128]{2,1,0:T(1,128)S(1)} %get-tuple-element.28, f32[132,2,128]{2,1,0:T(2,128)S(1)} %slice.283, f32[132,2,128]{2,1,0:T(2,128)S(1)} %get-tuple-element.24, f32[2,16,128]{2,1,0:T(8,128)S(1)} %slice.255, f32[128,16,128]{2,1,0:T(8,128)S(1)} %bitcast.71, ...), kind=kLoop, calls=%fused_computation.90 | loop fusion | flops 532480 | bytes 1751300 | tf_op jit(solution)/shard_map/jit(_where)/select_n | solution.py:179
  42.4 0.8 fusion.69
  43.2 0.1 copy.72
  43.3 0.8 slice_subtract_fusion.1
  44.1 0.1 copy.84
  44.2 0.1 copy.77
  44.3 0.1 copy.78
  44.4 0.1 copy.75
  44.5 0.3 broadcast_multiply_fusion.2
  44.9 0.1 copy.92
  45.0 0.3 broadcast_multiply_fusion.1
  45.3 0.1 copy.96
  45.4 0.2 convolution_bitcast_fusion.7
  45.6 0.7 fusion.5
  46.4 0.4 convolution_bitcast_fusion.3
  46.8 0.2 fusion.6
  47.0 0.4 fusion.3
  47.4 2.5 %collective-permute-start.4 = (f32[129,128]{1,0:T(8,128)S(1)}, f32[129,128]{1,0:T(8,128)S(1)}, u32[]{:S(2)}, u32[]{:S(2)}) collective-permute-start(f32[129,128]{1,0:T(8,128)S(1)} %pad_maximum_fusion.16), channel_id=1, source_target_pairs={{0,4},{4,0},{8,12},{12,8},{16,20},{20,16},{24,28},{28,24},{1,5},{5... | collective-permute-start | bytes 198152 | tf_op jit(solution)/shard_map/ppermute | solution.py:38
  49.9 0.3 bitcast_reduce_fusion
  50.3 0.6 collective-permute-done.4
  50.8 2.0 %collective-permute-start.5 = (f32[129,128]{1,0:T(8,128)S(1)}, f32[129,128]{1,0:T(8,128)S(1)}, u32[]{:S(2)}, u32[]{:S(2)}) collective-permute-start(f32[129,128]{1,0:T(8,128)S(1)} %fusion.68), channel_id=1, source_target_pairs={{0,8},{4,12},{8,0},{12,4},{16,24},{20,28},{24,16},{28,20},{1,9},{5... | collective-permute-start | bytes 198152 | tf_op jit(solution)/shard_map/ppermute | solution.py:38
  52.9 2.5 %collective-permute-done.5 = f32[129,128]{1,0:T(8,128)S(1)} collective-permute-done((f32[129,128]{1,0:T(8,128)S(1)}, f32[129,128]{1,0:T(8,128)S(1)}, u32[]{:S(2)}, u32[]{:S(2)}) %collective-permute-start.5) | collective-permute-done | bytes 66080 | tf_op jit(solution)/shard_map/ppermute | solution.py:38
  55.4 2.8 %collective-permute-start.6 = (f32[129,128]{1,0:T(8,128)S(1)}, f32[129,128]{1,0:T(8,128)}, u32[]{:S(2)}, u32[]{:S(2)}) collective-permute-start(f32[129,128]{1,0:T(8,128)S(1)} %add.184), channel_id=1, source_target_pairs={{0,16},{4,20},{8,24},{12,28},{16,0},{20,4},{24,8},{28,12},{1,17},{... | collective-permute-start | bytes 198152 | tf_op jit(solution)/shard_map/ppermute | solution.py:38
  58.2 0.3 broadcast_subtract_fusion
  58.5 0.7 copy.88
  59.2 1.4 %collective-permute-done.6 = f32[129,128]{1,0:T(8,128)} collective-permute-done((f32[129,128]{1,0:T(8,128)S(1)}, f32[129,128]{1,0:T(8,128)}, u32[]{:S(2)}, u32[]{:S(2)}) %collective-permute-start.6) | collective-permute-done | bytes 66080 | tf_op jit(solution)/shard_map/ppermute | solution.py:38
  60.6 0.9 %add.185 = f32[129,128]{1,0:T(8,128)S(1)} add(f32[129,128]{1,0:T(8,128)S(1)} %add.184, f32[129,128]{1,0:T(8,128)} %collective-permute-done.6) | non-fusion elementwise | flops 16512 | bytes 198144 | tf_op jit(solution)/shard_map/add | solution.py:17
  61.5 2.0 %collective-permute-start.7 = (f32[129,128]{1,0:T(8,128)S(1)}, f32[129,128]{1,0:T(8,128)S(1)}, u32[]{:S(2)}, u32[]{:S(2)}) collective-permute-start(f32[129,128]{1,0:T(8,128)S(1)} %add.185), channel_id=1, source_target_pairs={{0,1},{1,0},{2,3},{3,2},{4,5},{5,4},{6,7},{7,6},{8,9},{9,8},{10,11... | collective-permute-start | bytes 198152 | tf_op jit(solution)/shard_map/ppermute | solution.py:38
  63.5 0.2 pad_maximum_fusion.5
  63.7 2.1 %collective-permute-done.7 = f32[129,128]{1,0:T(8,128)S(1)} collective-permute-done((f32[129,128]{1,0:T(8,128)S(1)}, f32[129,128]{1,0:T(8,128)S(1)}, u32[]{:S(2)}, u32[]{:S(2)}) %collective-permute-start.7) | collective-permute-done | bytes 66080 | tf_op jit(solution)/shard_map/ppermute | solution.py:38
  65.9 3.5 %collective-permute-start.8 = (f32[129,128]{1,0:T(8,128)S(1)}, f32[129,128]{1,0:T(8,128)S(1)}, u32[]{:S(2)}, u32[]{:S(2)}) collective-permute-start(f32[129,128]{1,0:T(8,128)S(1)} %add.186), channel_id=1, source_target_pairs={{0,2},{1,3},{2,0},{3,1},{4,6},{5,7},{6,4},{7,5},{8,10},{9,11},{10,... | collective-permute-start | bytes 198152 | tf_op jit(solution)/shard_map/ppermute | solution.py:38
  69.4 2.3 %collective-permute-done.8 = f32[129,128]{1,0:T(8,128)S(1)} collective-permute-done((f32[129,128]{1,0:T(8,128)S(1)}, f32[129,128]{1,0:T(8,128)S(1)}, u32[]{:S(2)}, u32[]{:S(2)}) %collective-permute-start.8) | collective-permute-done | bytes 66080 | tf_op jit(solution)/shard_map/ppermute | solution.py:38
  71.7 0.6 add.187.stacked_ref
  72.3 9.8 %shard_map.68 = f32[128,128]{1,0:T(8,128)} custom-call(f32[129,128]{1,0:T(8,128)} %add.187.stacked_ref), custom_call_target="tpu_custom_call" | custom-call | tf_op jit(solution)/shard_map/pallas_call | solution.py:98
  82.2 2.0 %fusion.1 = f32[128,16,128]{0,2,1:T(8,128)S(1)} fusion(f32[128,16,128]{2,1,0:T(8,128)S(1)} %pad_maximum_fusion.5, f32[16,128]{1,0:T(8,128)S(1)} %maximum_bitcast_fusion, f32[128,128]{1,0:T(8,128)} %shard_map.68), kind=kOutput, calls=%fused_computation.3 | convolution fusion | flops 402915328 | bytes 2170880 | tf_op jit(solution)/shard_map/dot_general | solution.py:251
  84.2 1.4 %copy.90 = f32[128,16,128]{2,1,0:T(8,128)} copy(f32[128,16,128]{0,2,1:T(8,128)S(1)} %fusion.1) | data formatting | bytes 2097152
  85.6 1.2 %fusion = f32[128,16,128]{0,2,1:T(8,128)S(1)} fusion(f32[128,16,128]{2,1,0:T(8,128)S(1)} %broadcast_subtract_fusion, f32[16,128]{1,0:T(8,128)S(1)} %copy-done.11, f32[128,128]{1,0:T(8,128)S(1)} %copy-done.5), kind=kOutput, calls=%fused_computation.1 | convolution fusion | flops 402915328 | bytes 2170880 | tf_op jit(solution)/shard_map/dot_general | solution.py:254
  86.8 1.4 %copy.91 = f32[128,16,128]{2,1,0:T(8,128)} copy(f32[128,16,128]{0,2,1:T(8,128)S(1)} %fusion) | data formatting | bytes 2097152
  (62 shorter events, 0.4 us)
Async XLA Ops:
  0.6 2.0 %copy-start.2 = (f32[128,16,128]{2,1,0:T(8,128)S(1)}, f32[128,16,128]{2,1,0:T(8,128)}, u32[]{:S(2)}) copy-start(f32[128,16,128]{2,1,0:T(8,128)} %param.5) | copy-start | bytes 3145732
  2.6 7.6 %copy-start.15 = (s32[1024]{0:T(1024)S(1)}, s32[1024]{0:T(1024)}, u32[]{:S(2)}) copy-start(s32[1024]{0:T(1024)} %param.9) | copy-start | bytes 12292
  2.6 7.7 %copy-start.16 = (f32[1024]{0:T(1024)S(1)}, f32[1024]{0:T(1024)}, u32[]{:S(2)}) copy-start(f32[1024]{0:T(1024)} %param.8) | copy-start | bytes 12292
  2.6 7.7 %copy-start.17 = (f32[1024]{0:T(1024)S(1)}, f32[1024]{0:T(1024)}, u32[]{:S(2)}) copy-start(f32[1024]{0:T(1024)} %param.7) | copy-start | bytes 12292
  3.4 8.7 %collective-permute-start.1 = (f32[3,16,128]{2,1,0:T(8,128)S(1)}, f32[3,16,128]{2,1,0:T(8,128)S(1)}, u32[]{:S(2)}, u32[]{:S(2)}) collective-permute-start(f32[3,16,128]{2,1,0:T(8,128)S(1)} %pad_maximum_fusion.20), channel_id=1, source_target_pairs={{1,0},{2,1},{3,2},{5,4},{6,5},{7,6},{9,8},{10,9},{11,10},{13,12},{... | collective-permute-start | bytes 73736 | tf_op jit(solution)/shard_map/ppermute | solution.py:134
  4.7 7.4 %collective-permute-start = (f32[3,16,128]{2,1,0:T(8,128)S(1)}, f32[3,16,128]{2,1,0:T(8,128)S(1)}, u32[]{:S(2)}, u32[]{:S(2)}) collective-permute-start(f32[3,16,128]{2,1,0:T(8,128)S(1)} %pad_maximum_fusion.19), channel_id=1, source_target_pairs={{0,1},{1,2},{2,3},{4,5},{5,6},{6,7},{8,9},{9,10},{10,11},{12,13},{... | collective-permute-start | bytes 73736 | tf_op jit(solution)/shard_map/ppermute | solution.py:134
  12.4 1.7 %copy-start.3 = (f32[130,1,128]{2,1,0:T(1,128)}, f32[130,1,128]{2,1,0:T(1,128)S(1)}, u32[]{:S(2)}) copy-start(f32[130,1,128]{2,1,0:T(1,128)S(1)} %get-tuple-element.29) | copy-start | bytes 199684
  15.2 20.2 %collective-permute-start.2 = (f32[132,3,128]{2,1,0:T(4,128)}, f32[132,3,128]{2,1,0:T(4,128)}, u32[]{:S(2)}, u32[]{:S(2)}) collective-permute-start(f32[132,3,128]{2,1,0:T(4,128)} %get-tuple-element.53), channel_id=1, source_target_pairs={{0,4},{4,8},{8,12},{12,16},{16,20},{20,24},{24,28},{1,5},{5,9},{9,... | collective-permute-start | bytes 608264 | tf_op jit(solution)/shard_map/ppermute | solution.py:134
  17.4 20.0 %collective-permute-start.3 = (f32[132,3,128]{2,1,0:T(4,128)}, f32[132,3,128]{2,1,0:T(4,128)}, u32[]{:S(2)}, u32[]{:S(2)}) collective-permute-start(f32[132,3,128]{2,1,0:T(4,128)} %get-tuple-element.54), channel_id=1, source_target_pairs={{4,0},{8,4},{12,8},{16,12},{20,16},{24,20},{28,24},{5,1},{9,5},{13... | collective-permute-start | bytes 608264 | tf_op jit(solution)/shard_map/ppermute | solution.py:134
  31.7 7.7 %copy-start.4 = (f32[130,1,128]{2,1,0:T(1,128)S(1)}, f32[130,1,128]{2,1,0:T(1,128)}, u32[]{:S(2)}) copy-start(f32[130,1,128]{2,1,0:T(1,128)} %copy-done.3) | copy-start | bytes 199684
  31.7 7.7 %copy-start.10 = (pred[130,2]{1,0:T(8,128)(4,1)S(1)}, pred[130,2]{1,0:T(8,128)(4,1)}, u32[]{:S(2)}) copy-start(pred[130,2]{1,0:T(8,128)(4,1)} %get-tuple-element.51) | copy-start | bytes 784
  37.4 3.5 %copy-start.9 = (pred[130,2]{1,0:T(8,128)(4,1)S(1)}, pred[130,2]{1,0:T(8,128)(4,1)}, u32[]{:S(2)}) copy-start(pred[130,2]{1,0:T(8,128)(4,1)} %get-tuple-element.52) | copy-start | bytes 784
  40.8 1.5 %copy-start.6 = (f32[130,2,128]{2,1,0:T(2,128)S(1)}, f32[130,2,128]{2,1,0:T(2,128)}, u32[]{:S(2)}) copy-start(f32[130,2,128]{2,1,0:T(2,128)} %get-tuple-element.26) | copy-start | bytes 399364
  40.9 1.5 %copy-start.7 = (f32[130,2,128]{2,1,0:T(2,128)S(1)}, f32[130,2,128]{2,1,0:T(2,128)}, u32[]{:S(2)}) copy-start(f32[130,2,128]{2,1,0:T(2,128)} %get-tuple-element.27) | copy-start | bytes 399364
  43.1 2.5 %copy-start.1 = (f32[128,12,128]{0,2,1:T(8,128)S(1)}, f32[128,12,128]{0,2,1:T(8,128)}, u32[]{:S(2)}) copy-start(f32[128,12,128]{0,2,1:T(8,128)} %copy.94) | copy-start | bytes 2359300
  43.1 2.5 %copy-start.12 = (f32[128,12,1]{0,1,2:T(8,128)S(1)}, f32[128,12,1]{0,1,2:T(8,128)}, u32[]{:S(2)}) copy-start(f32[128,12,1]{0,1,2:T(8,128)} %get-tuple-element.40) | copy-start | bytes 18436
  44.1 2.3 %copy-start.13 = (f32[128,2]{0,1:T(2,128)}, f32[128,2]{0,1:T(2,128)S(1)}, u32[]{:S(2)}) copy-start(f32[128,2]{0,1:T(2,128)S(1)} %get-tuple-element.50) | copy-start | bytes 3076
  45.0 2.0 %copy-start.8 = (f32[128,128]{1,0:T(8,128)S(1)}, f32[128,128]{1,0:T(8,128)}, u32[]{:S(2)}) copy-start(f32[128,128]{1,0:T(8,128)} %convolution_bitcast_fusion.2) | copy-start | bytes 196612
  47.4 3.4 %collective-permute-start.4 = (f32[129,128]{1,0:T(8,128)S(1)}, f32[129,128]{1,0:T(8,128)S(1)}, u32[]{:S(2)}, u32[]{:S(2)}) collective-permute-start(f32[129,128]{1,0:T(8,128)S(1)} %pad_maximum_fusion.16), channel_id=1, source_target_pairs={{0,4},{4,0},{8,12},{12,8},{16,20},{20,16},{24,28},{28,24},{1,5},{5... | collective-permute-start | bytes 198152 | tf_op jit(solution)/shard_map/ppermute | solution.py:38
  50.8 4.5 %collective-permute-start.5 = (f32[129,128]{1,0:T(8,128)S(1)}, f32[129,128]{1,0:T(8,128)S(1)}, u32[]{:S(2)}, u32[]{:S(2)}) collective-permute-start(f32[129,128]{1,0:T(8,128)S(1)} %fusion.68), channel_id=1, source_target_pairs={{0,8},{4,12},{8,0},{12,4},{16,24},{20,28},{24,16},{28,20},{1,9},{5... | collective-permute-start | bytes 198152 | tf_op jit(solution)/shard_map/ppermute | solution.py:38
  55.4 5.2 %collective-permute-start.6 = (f32[129,128]{1,0:T(8,128)S(1)}, f32[129,128]{1,0:T(8,128)}, u32[]{:S(2)}, u32[]{:S(2)}) collective-permute-start(f32[129,128]{1,0:T(8,128)S(1)} %add.184), channel_id=1, source_target_pairs={{0,16},{4,20},{8,24},{12,28},{16,0},{20,4},{24,8},{28,12},{1,17},{... | collective-permute-start | bytes 198152 | tf_op jit(solution)/shard_map/ppermute | solution.py:38
  58.2 5.3 %copy-start = (f32[128,12,128]{2,1,0:T(8,128)S(1)}, f32[128,12,128]{2,1,0:T(8,128)}, u32[]{:S(2)}) copy-start(f32[128,12,128]{2,1,0:T(8,128)} %get-tuple-element.13) | copy-start | bytes 2359300
  61.5 7.9 %copy-start.14 = (f32[128,2]{0,1:T(2,128)S(1)}, f32[128,2]{0,1:T(2,128)}, u32[]{:S(2)}) copy-start(f32[128,2]{0,1:T(2,128)} %copy-done.13) | copy-start | bytes 3076
  61.5 4.4 %collective-permute-start.7 = (f32[129,128]{1,0:T(8,128)S(1)}, f32[129,128]{1,0:T(8,128)S(1)}, u32[]{:S(2)}, u32[]{:S(2)}) collective-permute-start(f32[129,128]{1,0:T(8,128)S(1)} %add.185), channel_id=1, source_target_pairs={{0,1},{1,0},{2,3},{3,2},{4,5},{5,4},{6,7},{7,6},{8,9},{9,8},{10,11... | collective-permute-start | bytes 198152 | tf_op jit(solution)/shard_map/ppermute | solution.py:38
  65.9 5.8 %collective-permute-start.8 = (f32[129,128]{1,0:T(8,128)S(1)}, f32[129,128]{1,0:T(8,128)S(1)}, u32[]{:S(2)}, u32[]{:S(2)}) collective-permute-start(f32[129,128]{1,0:T(8,128)S(1)} %add.186), channel_id=1, source_target_pairs={{0,2},{1,3},{2,0},{3,1},{4,6},{5,7},{6,4},{7,5},{8,10},{9,11},{10,... | collective-permute-start | bytes 198152 | tf_op jit(solution)/shard_map/ppermute | solution.py:38
  84.2 1.4 %copy-start.5 = (f32[128,128]{1,0:T(8,128)S(1)}, f32[128,128]{1,0:T(8,128)}, u32[]{:S(2)}) copy-start(f32[128,128]{1,0:T(8,128)} %shard_map.68) | copy-start | bytes 196612
  84.2 1.4 %copy-start.11 = (f32[16,128]{1,0:T(8,128)S(1)}, f32[16,128]{1,0:T(8,128)}, u32[]{:S(2)}) copy-start(f32[16,128]{1,0:T(8,128)} %copy.88) | copy-start | bytes 24580

commit v25 on v24

--- a/solution.py
+++ b/solution.py
@@ -242,14 +242,19 @@
         )
         averages.append(average)
         deviations.append(deviation)
-    average_t = jnp.concatenate(averages, axis=1)
-    deviation_t = lax.optimization_barrier(jnp.concatenate(deviations, axis=1))
     combination_transposed = combination_transposed_of(
         butterfly_sum(jnp.concatenate([gram_local, projected[None, :]], axis=0), ("gx", "gy"))
     )
     contract = (((2,), (1,)), ((), ()))
-    updated_t = average_t[:, :, None] + lax.dot_general(
-        deviation_t, combination_transposed, contract, precision=lax.Precision.HIGHEST
+    updated_t = jnp.concatenate(
+        [
+            average[:, :, None]
+            + lax.dot_general(
+                deviation, combination_transposed, contract, precision=lax.Precision.HIGHEST
+            )
+            for average, deviation in zip(averages, deviations)
+        ],
+        axis=1,
     )
     heat_out_t = mean_heat_t[:, :, None] + lax.dot_general(
         heat_anomaly_t, combination_transposed, contract, precision=lax.Precision.HIGHEST

time: 89 us -> 64 us (0.72)
  other arithmetic: 18 us -> 2.99 us
  local copies, waits for them, and re-layouts: 17.2 us -> 5 us
  waiting for transfers between devices: 8.85 us -> 14.3 us
  matrix products: 9.71 us -> 8.07 us
    mul x3 -> x0, other arithmetic: 3.8 us -> none  [shards(): deviation * cell_weight[:, :, None]]
    ppermute x4, waiting for transfers between devices: 0.01 us -> 3.02 us  [from_neighbour(): return lax.ppermute(block, axis, pairs)]
    sub x3 -> x0, local copies, waits for them, and re-layouts: 2.57 us -> none  [shards(): deviation = piece - average[:, :, None]]
    sub x3 -> x0, other arithmetic: 2.54 us -> none  [the longest x2 2.21 us: shards(): cell_sums[:, block_height_number + start:block_height_number + start + co...]
    ppermute x5, waiting for transfers between devices: 8.84 us -> 11.3 us  [butterfly_sum(): received[offset] = lax.ppermute(value, axis, pairs)]
    reduce_sum x2, other arithmetic: 2.91 us -> 0.74 us  [shards(): average = jnp.mean(piece, axis=2)]
    slice x3 -> x0, local copies, waits for them, and re-layouts: 1.64 us -> none  [shards(): cell_weight = cell_sums[:, start:start + count]]
    div x4 -> x0, local copies, waits for them, and re-layouts: 1.61 us -> none  [the longest x3 0.95 us: shards(): average = jnp.mean(piece, axis=2)]
  transfers between devices with their start and end apart: 9 -> 9, of which waited for: 5 -> 7; matrix products, arithmetic and copies ran while one was open for 25% -> 5% of each run, Pallas kernels for 0% -> 0%
where the time goes in v25:
time: 64 us; the launch traced here: 63.7 us
  starting transfers between devices  22.6 us (35%)
  waiting for transfers between devices  14.3 us (22%)
  Pallas kernels  9.64 us (15%)
  matrix products  8.07 us (13%)
  local copies, waits for them, and re-layouts  5 us (8%)
  other arithmetic  2.99 us (5%)
  between operations  1.03 us (2%)
    ppermute x5, starting transfers between devices, butterfly_sum(): received[offset] = lax.ppermute(value, axis, pairs)  13.2 us
    ppermute x5, waiting for transfers between devices, butterfly_sum(): received[offset] = lax.ppermute(value, axis, pairs)  11.3 us
    pallas_call x1, Pallas kernels, combination_transposed_of(): pl.pallas_call(combination_kernel, out_shape=jax.ShapeDtypeStruct((size,...  9.64 us
    ppermute x4, starting transfers between devices, from_neighbour(): return lax.ppermute(block, axis, pairs)  9.44 us
    unnamed x14, local copies, waits for them, and re-layouts  4.87 us
    dot_general x3, matrix products, shards(): lax.dot_general(deviation * cell_weight[:, :, None], deviation, (((0, 1),...  3.15 us
    ppermute x4, waiting for transfers between devices, from_neighbour(): return lax.ppermute(block, axis, pairs)  3.02 us
    dot_general x3, matrix products, shards(): lax.dot_general(deviation, combination_transposed, contract, precision=la...  2.36 us
  transfers between devices with their start and end apart: 9, of which 7 were waited for; matrix products, arithmetic and copies ran while one was open for 5% of the time, Pallas kernels for 0%

profile of v25, /device:TPU:0, one launch (start us, length us, event | category | flops | bytes accessed | tf_op | source)
XLA Modules:
  0.0 63.7 jit_solution(4901018937138677045)
XLA Ops:
  0.6 0.0 copy-start.1
  0.6 1.7 %copy.15 = f32[128,16,128]{0,2,1:T(8,128)S(1)} copy(f32[128,16,128]{2,1,0:T(8,128)} %param.6) | data formatting | bytes 2097152 | tf_op args[1]
  2.3 0.0 copy-done.1
  2.3 0.0 copy-start.2
  2.4 0.0 copy-start.3
  2.4 0.0 copy-start.4
  2.4 0.4 copy.14
  2.9 1.3 %collective-permute-start.1 = (f32[3,16,128]{2,0,1:T(4,128)S(1)}, f32[3,16,128]{2,0,1:T(4,128)S(1)}, u32[]{:S(2)}, u32[]{:S(2)}) collective-permute-start(f32[3,16,128]{2,0,1:T(4,128)S(1)} %pad_maximum_fusion.19), channel_id=1, source_target_pairs={{1,0},{2,1},{3,2},{5,4},{6,5},{7,6},{9,8},{10,9},{11,10},{13,12},{... | collective-permute-start | bytes 73736 | tf_op jit(solution)/shard_map/ppermute | solution.py:134
  4.2 5.6 %collective-permute-start = (f32[3,16,128]{2,0,1:T(4,128)S(1)}, f32[3,16,128]{2,0,1:T(4,128)S(1)}, u32[]{:S(2)}, u32[]{:S(2)}) collective-permute-start(f32[3,16,128]{2,0,1:T(4,128)S(1)} %pad_maximum_fusion.18), channel_id=1, source_target_pairs={{0,1},{1,2},{2,3},{4,5},{5,6},{6,7},{8,9},{9,10},{10,11},{12,13},{... | collective-permute-start | bytes 73736 | tf_op jit(solution)/shard_map/ppermute | solution.py:134
  9.8 0.0 copy-done.2
  9.8 0.0 copy-done.3
  9.8 0.0 copy-done.4
  9.9 0.4 fusion.28
  10.3 0.1 broadcast_or_fusion.1
  10.3 0.0 collective-permute-done.1
  10.4 1.0 %collective-permute-done = f32[3,16,128]{2,0,1:T(4,128)S(1)} collective-permute-done((f32[3,16,128]{2,0,1:T(4,128)S(1)}, f32[3,16,128]{2,0,1:T(4,128)S(1)}, u32[]{:S(2)}, u32[]{:S(2)}) %collective-permute-start) | collective-permute-done | bytes 24608 | tf_op jit(solution)/shard_map/ppermute | solution.py:134
  11.4 0.1 pad_maximum_fusion
  11.5 0.6 fusion.14
  12.1 0.5 fusion.106
  12.7 1.3 %collective-permute-start.2 = (f32[132,3,128]{2,0,1:T(8,128)S(1)}, f32[132,3,128]{2,0,1:T(8,128)S(1)}, u32[]{:S(2)}, u32[]{:S(2)}) collective-permute-start(f32[132,3,128]{2,0,1:T(8,128)S(1)} %get-tuple-element.43), channel_id=1, source_target_pairs={{0,4},{4,8},{8,12},{12,16},{16,20},{20,24},{24,28},{1,5},{5,9},{9,... | collective-permute-start | bytes 608264 | tf_op jit(solution)/shard_map/ppermute | solution.py:134
  14.0 1.3 %collective-permute-start.3 = (f32[132,3,128]{2,0,1:T(8,128)S(1)}, f32[132,3,128]{2,0,1:T(8,128)S(1)}, u32[]{:S(2)}, u32[]{:S(2)}) collective-permute-start(f32[132,3,128]{2,0,1:T(8,128)S(1)} %get-tuple-element.44), channel_id=1, source_target_pairs={{4,0},{8,4},{12,8},{16,12},{20,16},{24,20},{28,24},{5,1},{9,5},{13... | collective-permute-start | bytes 608264 | tf_op jit(solution)/shard_map/ppermute | solution.py:134
  15.3 2.1 %fusion.3 = f32[128,128]{1,0:T(8,128)S(1)} fusion(f32[128,12,128]{2,0,1:T(8,128)S(1)} %get-tuple-element.9, f32[128,12]{0,1:T(8,128)S(1)} %get-tuple-element.28, f32[128,12]{0,1:T(8,128)S(1)} %get-tuple-element.30), kind=kOutput, calls=%fused_computation.9 | convolution fusion | flops 302579712 | bytes 864256 | tf_op jit(solution)/shard_map/dot_general | solution.py:231
  17.4 0.0 collective-permute-done.2
  17.4 2.1 %collective-permute-done.3 = f32[132,3,128]{2,0,1:T(8,128)S(1)} collective-permute-done((f32[132,3,128]{2,0,1:T(8,128)S(1)}, f32[132,3,128]{2,0,1:T(8,128)S(1)}, u32[]{:S(2)}, u32[]{:S(2)}) %collective-permute-start.3) | collective-permute-done | bytes 202784 | tf_op jit(solution)/shard_map/ppermute | solution.py:134
  19.5 0.1 fusion.54
  19.6 0.1 fusion.45
  19.8 0.2 fusion.108
  20.0 0.2 convolution_bitcast_fusion.5
  20.3 0.6 %fusion.9 = f32[128]{0:T(128)S(1)} fusion(f32[128]{0:T(128)S(1)} %convolution_bitcast_fusion.5, f32[128,12,128]{2,0,1:T(8,128)S(1)} %get-tuple-element.9, f32[128,12]{0,1:T(8,128)S(1)} %get-tuple-element.30, f32[128,12,1]{0,1,2:T(8,128)S(1)} %get-tuple-element.29), kind=kOutput, calls=%fused_computation.16 | convolution fusion | flops 2556032 | bytes 799744 | tf_op jit(solution)/shard_map/dot_general | solution.py:237
  20.9 0.5 convolution_bitcast_fusion.1
  21.4 0.2 fusion.10
  21.7 0.5 fusion.7
  22.2 4.3 %collective-permute-start.4 = (f32[129,128]{1,0:T(8,128)S(1)}, f32[129,128]{1,0:T(8,128)S(1)}, u32[]{:S(2)}, u32[]{:S(2)}) collective-permute-start(f32[129,128]{1,0:T(8,128)S(1)} %pad_maximum_fusion.17), channel_id=1, source_target_pairs={{0,4},{4,0},{8,12},{12,8},{16,20},{20,16},{24,28},{28,24},{1,5},{5... | collective-permute-start | bytes 198152 | tf_op jit(solution)/shard_map/ppermute | solution.py:38
  26.6 0.9 %collective-permute-done.4 = f32[129,128]{1,0:T(8,128)S(1)} collective-permute-done((f32[129,128]{1,0:T(8,128)S(1)}, f32[129,128]{1,0:T(8,128)S(1)}, u32[]{:S(2)}, u32[]{:S(2)}) %collective-permute-start.4) | collective-permute-done | bytes 66080 | tf_op jit(solution)/shard_map/ppermute | solution.py:38
  27.5 2.5 %collective-permute-start.5 = (f32[129,128]{1,0:T(8,128)S(1)}, f32[129,128]{1,0:T(8,128)S(1)}, u32[]{:S(2)}, u32[]{:S(2)}) collective-permute-start(f32[129,128]{1,0:T(8,128)S(1)} %fusion.103), channel_id=1, source_target_pairs={{0,8},{4,12},{8,0},{12,4},{16,24},{20,28},{24,16},{28,20},{1,9},{5... | collective-permute-start | bytes 198152 | tf_op jit(solution)/shard_map/ppermute | solution.py:38
  30.0 2.7 %collective-permute-done.5 = f32[129,128]{1,0:T(8,128)S(1)} collective-permute-done((f32[129,128]{1,0:T(8,128)S(1)}, f32[129,128]{1,0:T(8,128)S(1)}, u32[]{:S(2)}, u32[]{:S(2)}) %collective-permute-start.5) | collective-permute-done | bytes 66080 | tf_op jit(solution)/shard_map/ppermute | solution.py:38
  32.7 0.9 %collective-permute-start.6 = (f32[129,128]{1,0:T(8,128)S(1)}, f32[129,128]{1,0:T(8,128)S(1)}, u32[]{:S(2)}, u32[]{:S(2)}) collective-permute-start(f32[129,128]{1,0:T(8,128)S(1)} %add.192), channel_id=1, source_target_pairs={{0,16},{4,20},{8,24},{12,28},{16,0},{20,4},{24,8},{28,12},{1,17},{... | collective-permute-start | bytes 198152 | tf_op jit(solution)/shard_map/ppermute | solution.py:38
  33.6 3.4 %collective-permute-done.6 = f32[129,128]{1,0:T(8,128)S(1)} collective-permute-done((f32[129,128]{1,0:T(8,128)S(1)}, f32[129,128]{1,0:T(8,128)S(1)}, u32[]{:S(2)}, u32[]{:S(2)}) %collective-permute-start.6) | collective-permute-done | bytes 66080 | tf_op jit(solution)/shard_map/ppermute | solution.py:38
  37.1 2.4 %collective-permute-start.7 = (f32[129,128]{1,0:T(8,128)S(1)}, f32[129,128]{1,0:T(8,128)S(1)}, u32[]{:S(2)}, u32[]{:S(2)}) collective-permute-start(f32[129,128]{1,0:T(8,128)S(1)} %add.193), channel_id=1, source_target_pairs={{0,1},{1,0},{2,3},{3,2},{4,5},{5,4},{6,7},{7,6},{8,9},{9,8},{10,11... | collective-permute-start | bytes 198152 | tf_op jit(solution)/shard_map/ppermute | solution.py:38
  39.4 0.3 bitcast_reduce_fusion
  39.8 1.9 %collective-permute-done.7 = f32[129,128]{1,0:T(8,128)S(1)} collective-permute-done((f32[129,128]{1,0:T(8,128)S(1)}, f32[129,128]{1,0:T(8,128)S(1)}, u32[]{:S(2)}, u32[]{:S(2)}) %collective-permute-start.7) | collective-permute-done | bytes 66080 | tf_op jit(solution)/shard_map/ppermute | solution.py:38
  41.7 3.1 %collective-permute-start.8 = (f32[129,128]{1,0:T(8,128)S(1)}, f32[129,128]{1,0:T(8,128)S(1)}, u32[]{:S(2)}, u32[]{:S(2)}) collective-permute-start(f32[129,128]{1,0:T(8,128)S(1)} %add.194), channel_id=1, source_target_pairs={{0,2},{1,3},{2,0},{3,1},{4,6},{5,7},{6,4},{7,5},{8,10},{9,11},{10,... | collective-permute-start | bytes 198152 | tf_op jit(solution)/shard_map/ppermute | solution.py:38
  44.8 2.3 %collective-permute-done.8 = f32[129,128]{1,0:T(8,128)S(1)} collective-permute-done((f32[129,128]{1,0:T(8,128)S(1)}, f32[129,128]{1,0:T(8,128)S(1)}, u32[]{:S(2)}, u32[]{:S(2)}) %collective-permute-start.8) | collective-permute-done | bytes 66080 | tf_op jit(solution)/shard_map/ppermute | solution.py:38
  47.1 0.6 %add.195.stacked_ref = f32[129,128]{1,0:T(8,128)} add(f32[129,128]{1,0:T(8,128)S(1)} %add.194, f32[129,128]{1,0:T(8,128)S(1)} %collective-permute-done.8) | non-fusion elementwise | flops 16512 | bytes 198144 | tf_op jit(solution)/shard_map/add | solution.py:17
  47.8 9.6 %shard_map.68 = f32[128,128]{1,0:T(8,128)} custom-call(f32[129,128]{1,0:T(8,128)} %add.195.stacked_ref), custom_call_target="tpu_custom_call" | custom-call | tf_op jit(solution)/shard_map/pallas_call | solution.py:98
  57.4 0.0 copy-start
  57.4 1.7 %convolution_add_fusion = f32[128,12,128]{2,0,1:T(8,128)S(1)} fusion(f32[128,12,128]{2,0,1:T(8,128)S(1)} %get-tuple-element.9, f32[128,12]{0,1:T(8,128)S(1)} %get-tuple-element.30, f32[128,128]{1,0:T(8,128)} %shard_map.68), kind=kOutput, calls=%fused_computation.2 | convolution fusion | flops 302383104 | bytes 1644544 | tf_op jit(solution)/shard_map/dot_general | solution.py:252
  59.1 0.0 copy-done
  59.2 0.3 convolution_add_fusion.1
  59.5 0.3 convolution_add_fusion.2
  59.8 0.1 maximum_bitcast_fusion
  59.9 1.4 %copy.19 = f32[128,16,128]{2,1,0:T(8,128)} copy(f32[128,16,128]{0,2,1:T(8,128)S(1)} %maximum_bitcast_fusion) | data formatting | bytes 2097152
  61.3 1.0 %fusion = f32[128,16,128]{0,2,1:T(8,128)S(1)} fusion(f32[128,16]{0,1:T(8,128)S(1)} %get-tuple-element.32, f32[16,128]{1,0:T(8,128)S(1)} %get-tuple-element.31, f32[128,128]{1,0:T(8,128)S(1)} %copy-done, f32[128,16,128]{0,2,1:T(8,128)S(1)} %copy.15), kind=kOutput, calls=%fused_computation.1 | convolution fusion | flops 403177472 | bytes 2179072 | tf_op jit(solution)/shard_map/dot_general | solution.py:259
  62.3 1.4 %copy.20 = f32[128,16,128]{2,1,0:T(8,128)} copy(f32[128,16,128]{0,2,1:T(8,128)S(1)} %fusion) | data formatting | bytes 2097152
  (30 shorter events, 0.4 us)
Async XLA Ops:
  0.6 1.7 %copy-start.1 = (f32[128,16,128]{2,1,0:T(8,128)S(1)}, f32[128,16,128]{2,1,0:T(8,128)}, u32[]{:S(2)}) copy-start(f32[128,16,128]{2,1,0:T(8,128)} %param.5) | copy-start | bytes 3145732
  2.3 7.4 %copy-start.2 = (s32[1024]{0:T(1024)S(1)}, s32[1024]{0:T(1024)}, u32[]{:S(2)}) copy-start(s32[1024]{0:T(1024)} %param.9) | copy-start | bytes 12292
  2.4 7.5 %copy-start.3 = (f32[1024]{0:T(1024)S(1)}, f32[1024]{0:T(1024)}, u32[]{:S(2)}) copy-start(f32[1024]{0:T(1024)} %param.8) | copy-start | bytes 12292
  2.4 7.5 %copy-start.4 = (f32[1024]{0:T(1024)S(1)}, f32[1024]{0:T(1024)}, u32[]{:S(2)}) copy-start(f32[1024]{0:T(1024)} %param.7) | copy-start | bytes 12292
  2.9 7.5 %collective-permute-start.1 = (f32[3,16,128]{2,0,1:T(4,128)S(1)}, f32[3,16,128]{2,0,1:T(4,128)S(1)}, u32[]{:S(2)}, u32[]{:S(2)}) collective-permute-start(f32[3,16,128]{2,0,1:T(4,128)S(1)} %pad_maximum_fusion.19), channel_id=1, source_target_pairs={{1,0},{2,1},{3,2},{5,4},{6,5},{7,6},{9,8},{10,9},{11,10},{13,12},{... | collective-permute-start | bytes 73736 | tf_op jit(solution)/shard_map/ppermute | solution.py:134
  4.2 7.1 %collective-permute-start = (f32[3,16,128]{2,0,1:T(4,128)S(1)}, f32[3,16,128]{2,0,1:T(4,128)S(1)}, u32[]{:S(2)}, u32[]{:S(2)}) collective-permute-start(f32[3,16,128]{2,0,1:T(4,128)S(1)} %pad_maximum_fusion.18), channel_id=1, source_target_pairs={{0,1},{1,2},{2,3},{4,5},{5,6},{6,7},{8,9},{9,10},{10,11},{12,13},{... | collective-permute-start | bytes 73736 | tf_op jit(solution)/shard_map/ppermute | solution.py:134
  12.7 4.7 %collective-permute-start.2 = (f32[132,3,128]{2,0,1:T(8,128)S(1)}, f32[132,3,128]{2,0,1:T(8,128)S(1)}, u32[]{:S(2)}, u32[]{:S(2)}) collective-permute-start(f32[132,3,128]{2,0,1:T(8,128)S(1)} %get-tuple-element.43), channel_id=1, source_target_pairs={{0,4},{4,8},{8,12},{12,16},{16,20},{20,24},{24,28},{1,5},{5,9},{9,... | collective-permute-start | bytes 608264 | tf_op jit(solution)/shard_map/ppermute | solution.py:134
  14.0 5.5 %collective-permute-start.3 = (f32[132,3,128]{2,0,1:T(8,128)S(1)}, f32[132,3,128]{2,0,1:T(8,128)S(1)}, u32[]{:S(2)}, u32[]{:S(2)}) collective-permute-start(f32[132,3,128]{2,0,1:T(8,128)S(1)} %get-tuple-element.44), channel_id=1, source_target_pairs={{4,0},{8,4},{12,8},{16,12},{20,16},{24,20},{28,24},{5,1},{9,5},{13... | collective-permute-start | bytes 608264 | tf_op jit(solution)/shard_map/ppermute | solution.py:134
  22.2 5.2 %collective-permute-start.4 = (f32[129,128]{1,0:T(8,128)S(1)}, f32[129,128]{1,0:T(8,128)S(1)}, u32[]{:S(2)}, u32[]{:S(2)}) collective-permute-start(f32[129,128]{1,0:T(8,128)S(1)} %pad_maximum_fusion.17), channel_id=1, source_target_pairs={{0,4},{4,0},{8,12},{12,8},{16,20},{20,16},{24,28},{28,24},{1,5},{5... | collective-permute-start | bytes 198152 | tf_op jit(solution)/shard_map/ppermute | solution.py:38
  27.5 5.2 %collective-permute-start.5 = (f32[129,128]{1,0:T(8,128)S(1)}, f32[129,128]{1,0:T(8,128)S(1)}, u32[]{:S(2)}, u32[]{:S(2)}) collective-permute-start(f32[129,128]{1,0:T(8,128)S(1)} %fusion.103), channel_id=1, source_target_pairs={{0,8},{4,12},{8,0},{12,4},{16,24},{20,28},{24,16},{28,20},{1,9},{5... | collective-permute-start | bytes 198152 | tf_op jit(solution)/shard_map/ppermute | solution.py:38
  32.7 4.4 %collective-permute-start.6 = (f32[129,128]{1,0:T(8,128)S(1)}, f32[129,128]{1,0:T(8,128)S(1)}, u32[]{:S(2)}, u32[]{:S(2)}) collective-permute-start(f32[129,128]{1,0:T(8,128)S(1)} %add.192), channel_id=1, source_target_pairs={{0,16},{4,20},{8,24},{12,28},{16,0},{20,4},{24,8},{28,12},{1,17},{... | collective-permute-start | bytes 198152 | tf_op jit(solution)/shard_map/ppermute | solution.py:38
  37.1 4.7 %collective-permute-start.7 = (f32[129,128]{1,0:T(8,128)S(1)}, f32[129,128]{1,0:T(8,128)S(1)}, u32[]{:S(2)}, u32[]{:S(2)}) collective-permute-start(f32[129,128]{1,0:T(8,128)S(1)} %add.193), channel_id=1, source_target_pairs={{0,1},{1,0},{2,3},{3,2},{4,5},{5,4},{6,7},{7,6},{8,9},{9,8},{10,11... | collective-permute-start | bytes 198152 | tf_op jit(solution)/shard_map/ppermute | solution.py:38
  41.7 5.4 %collective-permute-start.8 = (f32[129,128]{1,0:T(8,128)S(1)}, f32[129,128]{1,0:T(8,128)S(1)}, u32[]{:S(2)}, u32[]{:S(2)}) collective-permute-start(f32[129,128]{1,0:T(8,128)S(1)} %add.194), channel_id=1, source_target_pairs={{0,2},{1,3},{2,0},{3,1},{4,6},{5,7},{6,4},{7,5},{8,10},{9,11},{10,... | collective-permute-start | bytes 198152 | tf_op jit(solution)/shard_map/ppermute | solution.py:38
  57.4 1.7 %copy-start = (f32[128,128]{1,0:T(8,128)S(1)}, f32[128,128]{1,0:T(8,128)}, u32[]{:S(2)}) copy-start(f32[128,128]{1,0:T(8,128)} %shard_map.68) | copy-start | bytes 196612

commit v26 on v21

--- a/solution.py
+++ b/solution.py
@@ -76,10 +76,8 @@
             work_ref[first:, :] = band - factor_col0 * factor_row0 - factor_col1 * factor_row1
             inverse_row0 = inverse_ref[pl.ds(k, 1), :] * scale0
             inverse_row1 = (inverse_ref[pl.ds(k + 1, 1), :] - coupling * inverse_row0) * scale1
-            below0 = jnp.where(sublane > k + 1, factor_col0, 0.0)
-            below1 = jnp.where(sublane > k + 1, factor_col1, 0.0)
             inverse_ref[first:, :] = (
-                inverse_ref[first:, :] - below0 * inverse_row0 - below1 * inverse_row1
+                inverse_ref[first:, :] - factor_col0 * inverse_row0 - factor_col1 * inverse_row1
             )
             inverse_ref[pl.ds(k, 1), :] = inverse_row0
             inverse_ref[pl.ds(k + 1, 1), :] = inverse_row1

time: 62.1 us -> 62 us (level)
  no operation moved by 1% of the time
where the time goes in v26:
time: 62 us; the launch traced here: 61.7 us
  starting transfers between devices  22.6 us (36%)
  waiting for transfers between devices  13.3 us (21%)
  Pallas kernels  9.55 us (15%)
  matrix products  6.74 us (11%)
  local copies, waits for them, and re-layouts  5 us (8%)
  other arithmetic  3.4 us (5%)
  between operations  1.02 us (2%)
    ppermute x5, starting transfers between devices, butterfly_sum(): received[offset] = lax.ppermute(value, axis, pairs)  13.2 us
    ppermute x5, waiting for transfers between devices, butterfly_sum(): received[offset] = lax.ppermute(value, axis, pairs)  11.3 us
    pallas_call x1, Pallas kernels, combination_transposed_of(): pl.pallas_call(combination_kernel, out_shape=jax.ShapeDtypeStruct((size,...  9.55 us
    ppermute x4, starting transfers between devices, from_neighbour(): return lax.ppermute(block, axis, pairs)  9.44 us
    unnamed x14, local copies, waits for them, and re-layouts  4.87 us
    dot_general x3, matrix products, shards(): lax.dot_general(deviation * cell_weight[:, :, None], deviation, (((0, 1),...  2.62 us
    ppermute x4, waiting for transfers between devices, from_neighbour(): return lax.ppermute(block, axis, pairs)  2.05 us
    dot_general x1, matrix products, shards(): lax.dot_general(deviation_t, combination_transposed, contract, precision=...  1.82 us
  transfers between devices with their start and end apart: 9, of which 7 were waited for; matrix products, arithmetic and copies ran while one was open for 6% of the time, Pallas kernels for 0%

profile of v26, /device:TPU:0, one launch (start us, length us, event | category | flops | bytes accessed | tf_op | source)
XLA Modules:
  0.0 61.7 jit_solution(11097902536887333368)
XLA Ops:
  0.6 0.0 copy-start
  0.6 1.7 %copy.15 = f32[128,16,128]{0,2,1:T(8,128)S(1)} copy(f32[128,16,128]{2,1,0:T(8,128)} %param.6) | data formatting | bytes 2097152 | tf_op args[1]
  2.3 0.0 copy-done
  2.3 0.0 copy-start.2
  2.4 0.0 copy-start.3
  2.4 0.0 copy-start.4
  2.4 0.4 copy.14
  2.9 1.3 %collective-permute-start.1 = (f32[3,16,128]{2,0,1:T(4,128)S(1)}, f32[3,16,128]{2,0,1:T(4,128)S(1)}, u32[]{:S(2)}, u32[]{:S(2)}) collective-permute-start(f32[3,16,128]{2,0,1:T(4,128)S(1)} %pad_maximum_fusion.19), channel_id=1, source_target_pairs={{1,0},{2,1},{3,2},{5,4},{6,5},{7,6},{9,8},{10,9},{11,10},{13,12},{... | collective-permute-start | bytes 73736 | tf_op jit(solution)/shard_map/ppermute | solution.py:132
  4.2 5.6 %collective-permute-start = (f32[3,16,128]{2,0,1:T(4,128)S(1)}, f32[3,16,128]{2,0,1:T(4,128)S(1)}, u32[]{:S(2)}, u32[]{:S(2)}) collective-permute-start(f32[3,16,128]{2,0,1:T(4,128)S(1)} %pad_maximum_fusion.18), channel_id=1, source_target_pairs={{0,1},{1,2},{2,3},{4,5},{5,6},{6,7},{8,9},{9,10},{10,11},{12,13},{... | collective-permute-start | bytes 73736 | tf_op jit(solution)/shard_map/ppermute | solution.py:132
  9.8 0.0 copy-done.2
  9.8 0.0 copy-done.3
  9.8 0.0 copy-done.4
  9.9 0.4 fusion.31
  10.3 0.1 broadcast_or_fusion.1
  10.3 0.0 collective-permute-done.1
  10.4 1.0 %collective-permute-done = f32[3,16,128]{2,0,1:T(4,128)S(1)} collective-permute-done((f32[3,16,128]{2,0,1:T(4,128)S(1)}, f32[3,16,128]{2,0,1:T(4,128)S(1)}, u32[]{:S(2)}, u32[]{:S(2)}) %collective-permute-start) | collective-permute-done | bytes 24608 | tf_op jit(solution)/shard_map/ppermute | solution.py:132
  11.4 0.1 pad_maximum_fusion
  11.6 1.3 %collective-permute-start.2 = (f32[132,3,128]{2,0,1:T(8,128)S(1)}, f32[132,3,128]{2,0,1:T(8,128)S(1)}, u32[]{:S(2)}, u32[]{:S(2)}) collective-permute-start(f32[132,3,128]{2,0,1:T(8,128)S(1)} %get-tuple-element.43), channel_id=1, source_target_pairs={{0,4},{4,8},{8,12},{12,16},{16,20},{20,24},{24,28},{1,5},{5,9},{9,... | collective-permute-start | bytes 608264 | tf_op jit(solution)/shard_map/ppermute | solution.py:132
  12.9 1.3 %collective-permute-start.3 = (f32[132,3,128]{2,0,1:T(8,128)S(1)}, f32[132,3,128]{2,0,1:T(8,128)S(1)}, u32[]{:S(2)}, u32[]{:S(2)}) collective-permute-start(f32[132,3,128]{2,0,1:T(8,128)S(1)} %get-tuple-element.44), channel_id=1, source_target_pairs={{4,0},{8,4},{12,8},{16,12},{20,16},{24,20},{28,24},{5,1},{9,5},{13... | collective-permute-start | bytes 608264 | tf_op jit(solution)/shard_map/ppermute | solution.py:132
  14.2 0.6 fusion.20
  14.8 0.5 fusion.93
  15.3 0.3 broadcast_subtract_fusion
  15.6 1.7 %fusion.4 = f32[128,128]{1,0:T(8,128)S(1)} fusion(f32[128,12,128]{2,0,1:T(8,128)S(1)} %broadcast_subtract_fusion, f32[128,12]{0,1:T(8,128)S(1)} %get-tuple-element.28), kind=kOutput, calls=%fused_computation.8 | convolution fusion | flops 302186496 | bytes 858112 | tf_op jit(solution)/shard_map/dot_general | solution.py:229
  17.3 0.0 collective-permute-done.2
  17.3 1.1 %collective-permute-done.3 = f32[132,3,128]{2,0,1:T(8,128)S(1)} collective-permute-done((f32[132,3,128]{2,0,1:T(8,128)S(1)}, f32[132,3,128]{2,0,1:T(8,128)S(1)}, u32[]{:S(2)}, u32[]{:S(2)}) %collective-permute-start.3) | collective-permute-done | bytes 202784 | tf_op jit(solution)/shard_map/ppermute | solution.py:132
  18.4 0.1 fusion.54
  18.5 0.1 fusion.45
  18.7 0.2 fusion.91
  18.9 0.1 broadcast_subtract_fusion.1
  19.0 0.1 broadcast_subtract_fusion.2
  19.1 0.2 convolution_bitcast_fusion.6
  19.3 0.5 fusion.10
  19.8 0.5 convolution_bitcast_fusion.2
  20.3 0.2 fusion.11
  20.5 0.5 fusion.8
  21.0 4.3 %collective-permute-start.4 = (f32[129,128]{1,0:T(8,128)S(1)}, f32[129,128]{1,0:T(8,128)S(1)}, u32[]{:S(2)}, u32[]{:S(2)}) collective-permute-start(f32[129,128]{1,0:T(8,128)S(1)} %pad_maximum_fusion.17), channel_id=1, source_target_pairs={{0,4},{4,0},{8,12},{12,8},{16,20},{20,16},{24,28},{28,24},{1,5},{5... | collective-permute-start | bytes 198152 | tf_op jit(solution)/shard_map/ppermute | solution.py:38
  25.3 0.9 %collective-permute-done.4 = f32[129,128]{1,0:T(8,128)S(1)} collective-permute-done((f32[129,128]{1,0:T(8,128)S(1)}, f32[129,128]{1,0:T(8,128)S(1)}, u32[]{:S(2)}, u32[]{:S(2)}) %collective-permute-start.4) | collective-permute-done | bytes 66080 | tf_op jit(solution)/shard_map/ppermute | solution.py:38
  26.2 2.5 %collective-permute-start.5 = (f32[129,128]{1,0:T(8,128)S(1)}, f32[129,128]{1,0:T(8,128)S(1)}, u32[]{:S(2)}, u32[]{:S(2)}) collective-permute-start(f32[129,128]{1,0:T(8,128)S(1)} %fusion.90), channel_id=1, source_target_pairs={{0,8},{4,12},{8,0},{12,4},{16,24},{20,28},{24,16},{28,20},{1,9},{5... | collective-permute-start | bytes 198152 | tf_op jit(solution)/shard_map/ppermute | solution.py:38
  28.7 2.7 %collective-permute-done.5 = f32[129,128]{1,0:T(8,128)S(1)} collective-permute-done((f32[129,128]{1,0:T(8,128)S(1)}, f32[129,128]{1,0:T(8,128)S(1)}, u32[]{:S(2)}, u32[]{:S(2)}) %collective-permute-start.5) | collective-permute-done | bytes 66080 | tf_op jit(solution)/shard_map/ppermute | solution.py:38
  31.4 0.9 %collective-permute-start.6 = (f32[129,128]{1,0:T(8,128)S(1)}, f32[129,128]{1,0:T(8,128)S(1)}, u32[]{:S(2)}, u32[]{:S(2)}) collective-permute-start(f32[129,128]{1,0:T(8,128)S(1)} %add.184), channel_id=1, source_target_pairs={{0,16},{4,20},{8,24},{12,28},{16,0},{20,4},{24,8},{28,12},{1,17},{... | collective-permute-start | bytes 198152 | tf_op jit(solution)/shard_map/ppermute | solution.py:38
  32.3 0.3 bitcast_reduce_fusion
  32.7 3.1 %collective-permute-done.6 = f32[129,128]{1,0:T(8,128)S(1)} collective-permute-done((f32[129,128]{1,0:T(8,128)S(1)}, f32[129,128]{1,0:T(8,128)S(1)}, u32[]{:S(2)}, u32[]{:S(2)}) %collective-permute-start.6) | collective-permute-done | bytes 66080 | tf_op jit(solution)/shard_map/ppermute | solution.py:38
  35.8 2.4 %collective-permute-start.7 = (f32[129,128]{1,0:T(8,128)S(1)}, f32[129,128]{1,0:T(8,128)S(1)}, u32[]{:S(2)}, u32[]{:S(2)}) collective-permute-start(f32[129,128]{1,0:T(8,128)S(1)} %add.185), channel_id=1, source_target_pairs={{0,1},{1,0},{2,3},{3,2},{4,5},{5,4},{6,7},{7,6},{8,9},{9,8},{10,11... | collective-permute-start | bytes 198152 | tf_op jit(solution)/shard_map/ppermute | solution.py:38
  38.2 2.3 %collective-permute-done.7 = f32[129,128]{1,0:T(8,128)S(1)} collective-permute-done((f32[129,128]{1,0:T(8,128)S(1)}, f32[129,128]{1,0:T(8,128)S(1)}, u32[]{:S(2)}, u32[]{:S(2)}) %collective-permute-start.7) | collective-permute-done | bytes 66080 | tf_op jit(solution)/shard_map/ppermute | solution.py:38
  40.5 3.1 %collective-permute-start.8 = (f32[129,128]{1,0:T(8,128)S(1)}, f32[129,128]{1,0:T(8,128)S(1)}, u32[]{:S(2)}, u32[]{:S(2)}) collective-permute-start(f32[129,128]{1,0:T(8,128)S(1)} %add.186), channel_id=1, source_target_pairs={{0,2},{1,3},{2,0},{3,1},{4,6},{5,7},{6,4},{7,5},{8,10},{9,11},{10,... | collective-permute-start | bytes 198152 | tf_op jit(solution)/shard_map/ppermute | solution.py:38
  43.6 2.3 %collective-permute-done.8 = f32[129,128]{1,0:T(8,128)S(1)} collective-permute-done((f32[129,128]{1,0:T(8,128)S(1)}, f32[129,128]{1,0:T(8,128)S(1)}, u32[]{:S(2)}, u32[]{:S(2)}) %collective-permute-start.8) | collective-permute-done | bytes 66080 | tf_op jit(solution)/shard_map/ppermute | solution.py:38
  45.8 0.6 %add.187.stacked_ref = f32[129,128]{1,0:T(8,128)} add(f32[129,128]{1,0:T(8,128)S(1)} %add.186, f32[129,128]{1,0:T(8,128)S(1)} %collective-permute-done.8) | non-fusion elementwise | flops 16512 | bytes 198144 | tf_op jit(solution)/shard_map/add | solution.py:17
  46.5 9.6 %shard_map.68 = f32[128,128]{1,0:T(8,128)} custom-call(f32[129,128]{1,0:T(8,128)} %add.187.stacked_ref), custom_call_target="tpu_custom_call" | custom-call | tf_op jit(solution)/shard_map/pallas_call | solution.py:96
  56.0 1.8 %fusion.1 = f32[128,16,128]{0,2,1:T(8,128)S(1)} fusion(f32[128,2,128]{2,0,1:T(8,128)S(1)} %broadcast_subtract_fusion.1, f32[128,12,128]{2,0,1:T(8,128)S(1)} %broadcast_subtract_fusion, f32[128,2,128]{2,0,1:T(8,128)S(1)} %broadcast_subtract_fusion.2, f32[16,128]{1,0:T(8,128)S(1)} %maximum_bitcast_fusion, f32[128,128]{1,0:T(8,128)} %shard_map.68), kind=kOutput, calls=%fused_computation.3 | convolution fusion | flops 403439616 | bytes 2170880 | tf_op jit(solution)/shard_map/dot_general | solution.py:249
  57.9 0.0 copy-start.1
  57.9 1.4 %copy.19 = f32[128,16,128]{2,1,0:T(8,128)} copy(f32[128,16,128]{0,2,1:T(8,128)S(1)} %fusion.1) | data formatting | bytes 2097152
  59.3 0.0 copy-done.1
  59.3 1.0 %fusion = f32[128,16,128]{0,2,1:T(8,128)S(1)} fusion(f32[128,16]{0,1:T(8,128)S(1)} %get-tuple-element.32, f32[16,128]{1,0:T(8,128)S(1)} %get-tuple-element.31, f32[128,128]{1,0:T(8,128)S(1)} %copy-done.1, f32[128,16,128]{0,2,1:T(8,128)S(1)} %copy.15), kind=kOutput, calls=%fused_computation.1 | convolution fusion | flops 403177472 | bytes 2179072 | tf_op jit(solution)/shard_map/dot_general | solution.py:252
  60.3 1.4 %copy.20 = f32[128,16,128]{2,1,0:T(8,128)} copy(f32[128,16,128]{0,2,1:T(8,128)S(1)} %fusion) | data formatting | bytes 2097152
  (31 shorter events, 0.4 us)
Async XLA Ops:
  0.6 1.7 %copy-start = (f32[128,16,128]{2,1,0:T(8,128)S(1)}, f32[128,16,128]{2,1,0:T(8,128)}, u32[]{:S(2)}) copy-start(f32[128,16,128]{2,1,0:T(8,128)} %param.5) | copy-start | bytes 3145732
  2.3 7.4 %copy-start.2 = (s32[1024]{0:T(1024)S(1)}, s32[1024]{0:T(1024)}, u32[]{:S(2)}) copy-start(s32[1024]{0:T(1024)} %param.9) | copy-start | bytes 12292
  2.4 7.5 %copy-start.3 = (f32[1024]{0:T(1024)S(1)}, f32[1024]{0:T(1024)}, u32[]{:S(2)}) copy-start(f32[1024]{0:T(1024)} %param.8) | copy-start | bytes 12292
  2.4 7.5 %copy-start.4 = (f32[1024]{0:T(1024)S(1)}, f32[1024]{0:T(1024)}, u32[]{:S(2)}) copy-start(f32[1024]{0:T(1024)} %param.7) | copy-start | bytes 12292
  2.9 7.5 %collective-permute-start.1 = (f32[3,16,128]{2,0,1:T(4,128)S(1)}, f32[3,16,128]{2,0,1:T(4,128)S(1)}, u32[]{:S(2)}, u32[]{:S(2)}) collective-permute-start(f32[3,16,128]{2,0,1:T(4,128)S(1)} %pad_maximum_fusion.19), channel_id=1, source_target_pairs={{1,0},{2,1},{3,2},{5,4},{6,5},{7,6},{9,8},{10,9},{11,10},{13,12},{... | collective-permute-start | bytes 73736 | tf_op jit(solution)/shard_map/ppermute | solution.py:132
  4.2 7.1 %collective-permute-start = (f32[3,16,128]{2,0,1:T(4,128)S(1)}, f32[3,16,128]{2,0,1:T(4,128)S(1)}, u32[]{:S(2)}, u32[]{:S(2)}) collective-permute-start(f32[3,16,128]{2,0,1:T(4,128)S(1)} %pad_maximum_fusion.18), channel_id=1, source_target_pairs={{0,1},{1,2},{2,3},{4,5},{5,6},{6,7},{8,9},{9,10},{10,11},{12,13},{... | collective-permute-start | bytes 73736 | tf_op jit(solution)/shard_map/ppermute | solution.py:132
  11.6 5.7 %collective-permute-start.2 = (f32[132,3,128]{2,0,1:T(8,128)S(1)}, f32[132,3,128]{2,0,1:T(8,128)S(1)}, u32[]{:S(2)}, u32[]{:S(2)}) collective-permute-start(f32[132,3,128]{2,0,1:T(8,128)S(1)} %get-tuple-element.43), channel_id=1, source_target_pairs={{0,4},{4,8},{8,12},{12,16},{16,20},{20,24},{24,28},{1,5},{5,9},{9,... | collective-permute-start | bytes 608264 | tf_op jit(solution)/shard_map/ppermute | solution.py:132
  12.9 5.5 %collective-permute-start.3 = (f32[132,3,128]{2,0,1:T(8,128)S(1)}, f32[132,3,128]{2,0,1:T(8,128)S(1)}, u32[]{:S(2)}, u32[]{:S(2)}) collective-permute-start(f32[132,3,128]{2,0,1:T(8,128)S(1)} %get-tuple-element.44), channel_id=1, source_target_pairs={{4,0},{8,4},{12,8},{16,12},{20,16},{24,20},{28,24},{5,1},{9,5},{13... | collective-permute-start | bytes 608264 | tf_op jit(solution)/shard_map/ppermute | solution.py:132
  21.0 5.2 %collective-permute-start.4 = (f32[129,128]{1,0:T(8,128)S(1)}, f32[129,128]{1,0:T(8,128)S(1)}, u32[]{:S(2)}, u32[]{:S(2)}) collective-permute-start(f32[129,128]{1,0:T(8,128)S(1)} %pad_maximum_fusion.17), channel_id=1, source_target_pairs={{0,4},{4,0},{8,12},{12,8},{16,20},{20,16},{24,28},{28,24},{1,5},{5... | collective-permute-start | bytes 198152 | tf_op jit(solution)/shard_map/ppermute | solution.py:38
  26.2 5.2 %collective-permute-start.5 = (f32[129,128]{1,0:T(8,128)S(1)}, f32[129,128]{1,0:T(8,128)S(1)}, u32[]{:S(2)}, u32[]{:S(2)}) collective-permute-start(f32[129,128]{1,0:T(8,128)S(1)} %fusion.90), channel_id=1, source_target_pairs={{0,8},{4,12},{8,0},{12,4},{16,24},{20,28},{24,16},{28,20},{1,9},{5... | collective-permute-start | bytes 198152 | tf_op jit(solution)/shard_map/ppermute | solution.py:38
  31.4 4.4 %collective-permute-start.6 = (f32[129,128]{1,0:T(8,128)S(1)}, f32[129,128]{1,0:T(8,128)S(1)}, u32[]{:S(2)}, u32[]{:S(2)}) collective-permute-start(f32[129,128]{1,0:T(8,128)S(1)} %add.184), channel_id=1, source_target_pairs={{0,16},{4,20},{8,24},{12,28},{16,0},{20,4},{24,8},{28,12},{1,17},{... | collective-permute-start | bytes 198152 | tf_op jit(solution)/shard_map/ppermute | solution.py:38
  35.8 4.7 %collective-permute-start.7 = (f32[129,128]{1,0:T(8,128)S(1)}, f32[129,128]{1,0:T(8,128)S(1)}, u32[]{:S(2)}, u32[]{:S(2)}) collective-permute-start(f32[129,128]{1,0:T(8,128)S(1)} %add.185), channel_id=1, source_target_pairs={{0,1},{1,0},{2,3},{3,2},{4,5},{5,4},{6,7},{7,6},{8,9},{9,8},{10,11... | collective-permute-start | bytes 198152 | tf_op jit(solution)/shard_map/ppermute | solution.py:38
  40.5 5.4 %collective-permute-start.8 = (f32[129,128]{1,0:T(8,128)S(1)}, f32[129,128]{1,0:T(8,128)S(1)}, u32[]{:S(2)}, u32[]{:S(2)}) collective-permute-start(f32[129,128]{1,0:T(8,128)S(1)} %add.186), channel_id=1, source_target_pairs={{0,2},{1,3},{2,0},{3,1},{4,6},{5,7},{6,4},{7,5},{8,10},{9,11},{10,... | collective-permute-start | bytes 198152 | tf_op jit(solution)/shard_map/ppermute | solution.py:38
  57.9 1.4 %copy-start.1 = (f32[128,128]{1,0:T(8,128)S(1)}, f32[128,128]{1,0:T(8,128)}, u32[]{:S(2)}) copy-start(f32[128,128]{1,0:T(8,128)} %shard_map.68) | copy-start | bytes 196612

commit v27 on v21

--- a/solution.py
+++ b/solution.py
@@ -85,7 +85,7 @@
             inverse_ref[pl.ds(k + 1, 1), :] = inverse_row1
             return carry
 
-        lax.fori_loop(first // 2, min(first + 8, size) // 2, step, 0)
+        lax.fori_loop(first // 2, min(first + 8, size) // 2, step, 0, unroll=True)
     lower_inverse = inverse_ref[...]
     projected_row = stacked_ref[size : size + 1, :]
     whitened = jnp.sum(lower_inverse * projected_row, axis=1, keepdims=True)

time: 62.1 us -> 62.3 us (level)
  no operation moved by 1% of the time
where the time goes in v27:
time: 62.3 us; the launch traced here: 62 us
  starting transfers between devices  22.6 us (36%)
  waiting for transfers between devices  13.3 us (21%)
  Pallas kernels  9.89 us (16%)
  matrix products  6.74 us (11%)
  local copies, waits for them, and re-layouts  5 us (8%)
  other arithmetic  3.4 us (5%)
  between operations  1.02 us (2%)
    ppermute x5, starting transfers between devices, butterfly_sum(): received[offset] = lax.ppermute(value, axis, pairs)  13.2 us
    ppermute x5, waiting for transfers between devices, butterfly_sum(): received[offset] = lax.ppermute(value, axis, pairs)  11.3 us
    pallas_call x1, Pallas kernels, combination_transposed_of(): pl.pallas_call(combination_kernel, out_shape=jax.ShapeDtypeStruct((size,...  9.89 us
    ppermute x4, starting transfers between devices, from_neighbour(): return lax.ppermute(block, axis, pairs)  9.44 us
    unnamed x14, local copies, waits for them, and re-layouts  4.87 us
    dot_general x3, matrix products, shards(): lax.dot_general(deviation * cell_weight[:, :, None], deviation, (((0, 1),...  2.62 us
    ppermute x4, waiting for transfers between devices, from_neighbour(): return lax.ppermute(block, axis, pairs)  2.05 us
    dot_general x1, matrix products, shards(): lax.dot_general(deviation_t, combination_transposed, contract, precision=...  1.82 us
  transfers between devices with their start and end apart: 9, of which 7 were waited for; matrix products, arithmetic and copies ran while one was open for 6% of the time, Pallas kernels for 0%

profile of v27, /device:TPU:0, one launch (start us, length us, event | category | flops | bytes accessed | tf_op | source)
XLA Modules:
  0.0 62.0 jit_solution(8695327538979236461)
XLA Ops:
  0.6 0.0 copy-start
  0.6 1.7 %copy.15 = f32[128,16,128]{0,2,1:T(8,128)S(1)} copy(f32[128,16,128]{2,1,0:T(8,128)} %param.6) | data formatting | bytes 2097152 | tf_op args[1]
  2.3 0.0 copy-done
  2.3 0.0 copy-start.2
  2.4 0.0 copy-start.3
  2.4 0.0 copy-start.4
  2.4 0.4 copy.14
  2.9 1.3 %collective-permute-start.1 = (f32[3,16,128]{2,0,1:T(4,128)S(1)}, f32[3,16,128]{2,0,1:T(4,128)S(1)}, u32[]{:S(2)}, u32[]{:S(2)}) collective-permute-start(f32[3,16,128]{2,0,1:T(4,128)S(1)} %pad_maximum_fusion.19), channel_id=1, source_target_pairs={{1,0},{2,1},{3,2},{5,4},{6,5},{7,6},{9,8},{10,9},{11,10},{13,12},{... | collective-permute-start | bytes 73736 | tf_op jit(solution)/shard_map/ppermute | solution.py:134
  4.2 5.6 %collective-permute-start = (f32[3,16,128]{2,0,1:T(4,128)S(1)}, f32[3,16,128]{2,0,1:T(4,128)S(1)}, u32[]{:S(2)}, u32[]{:S(2)}) collective-permute-start(f32[3,16,128]{2,0,1:T(4,128)S(1)} %pad_maximum_fusion.18), channel_id=1, source_target_pairs={{0,1},{1,2},{2,3},{4,5},{5,6},{6,7},{8,9},{9,10},{10,11},{12,13},{... | collective-permute-start | bytes 73736 | tf_op jit(solution)/shard_map/ppermute | solution.py:134
  9.8 0.0 copy-done.2
  9.8 0.0 copy-done.3
  9.8 0.0 copy-done.4
  9.9 0.4 fusion.31
  10.3 0.1 broadcast_or_fusion.1
  10.3 0.0 collective-permute-done.1
  10.4 1.0 %collective-permute-done = f32[3,16,128]{2,0,1:T(4,128)S(1)} collective-permute-done((f32[3,16,128]{2,0,1:T(4,128)S(1)}, f32[3,16,128]{2,0,1:T(4,128)S(1)}, u32[]{:S(2)}, u32[]{:S(2)}) %collective-permute-start) | collective-permute-done | bytes 24608 | tf_op jit(solution)/shard_map/ppermute | solution.py:134
  11.4 0.1 pad_maximum_fusion
  11.6 1.3 %collective-permute-start.2 = (f32[132,3,128]{2,0,1:T(8,128)S(1)}, f32[132,3,128]{2,0,1:T(8,128)S(1)}, u32[]{:S(2)}, u32[]{:S(2)}) collective-permute-start(f32[132,3,128]{2,0,1:T(8,128)S(1)} %get-tuple-element.43), channel_id=1, source_target_pairs={{0,4},{4,8},{8,12},{12,16},{16,20},{20,24},{24,28},{1,5},{5,9},{9,... | collective-permute-start | bytes 608264 | tf_op jit(solution)/shard_map/ppermute | solution.py:134
  12.9 1.3 %collective-permute-start.3 = (f32[132,3,128]{2,0,1:T(8,128)S(1)}, f32[132,3,128]{2,0,1:T(8,128)S(1)}, u32[]{:S(2)}, u32[]{:S(2)}) collective-permute-start(f32[132,3,128]{2,0,1:T(8,128)S(1)} %get-tuple-element.44), channel_id=1, source_target_pairs={{4,0},{8,4},{12,8},{16,12},{20,16},{24,20},{28,24},{5,1},{9,5},{13... | collective-permute-start | bytes 608264 | tf_op jit(solution)/shard_map/ppermute | solution.py:134
  14.2 0.6 fusion.20
  14.8 0.5 fusion.93
  15.3 0.3 broadcast_subtract_fusion
  15.6 1.7 %fusion.4 = f32[128,128]{1,0:T(8,128)S(1)} fusion(f32[128,12,128]{2,0,1:T(8,128)S(1)} %broadcast_subtract_fusion, f32[128,12]{0,1:T(8,128)S(1)} %get-tuple-element.28), kind=kOutput, calls=%fused_computation.8 | convolution fusion | flops 302186496 | bytes 858112 | tf_op jit(solution)/shard_map/dot_general | solution.py:231
  17.3 0.0 collective-permute-done.2
  17.3 1.1 %collective-permute-done.3 = f32[132,3,128]{2,0,1:T(8,128)S(1)} collective-permute-done((f32[132,3,128]{2,0,1:T(8,128)S(1)}, f32[132,3,128]{2,0,1:T(8,128)S(1)}, u32[]{:S(2)}, u32[]{:S(2)}) %collective-permute-start.3) | collective-permute-done | bytes 202784 | tf_op jit(solution)/shard_map/ppermute | solution.py:134
  18.4 0.1 fusion.54
  18.5 0.1 fusion.45
  18.7 0.2 fusion.91
  18.9 0.1 broadcast_subtract_fusion.1
  19.0 0.1 broadcast_subtract_fusion.2
  19.1 0.2 convolution_bitcast_fusion.6
  19.3 0.5 fusion.10
  19.8 0.5 convolution_bitcast_fusion.2
  20.3 0.2 fusion.11
  20.5 0.5 fusion.8
  21.0 4.3 %collective-permute-start.4 = (f32[129,128]{1,0:T(8,128)S(1)}, f32[129,128]{1,0:T(8,128)S(1)}, u32[]{:S(2)}, u32[]{:S(2)}) collective-permute-start(f32[129,128]{1,0:T(8,128)S(1)} %pad_maximum_fusion.17), channel_id=1, source_target_pairs={{0,4},{4,0},{8,12},{12,8},{16,20},{20,16},{24,28},{28,24},{1,5},{5... | collective-permute-start | bytes 198152 | tf_op jit(solution)/shard_map/ppermute | solution.py:38
  25.3 0.9 %collective-permute-done.4 = f32[129,128]{1,0:T(8,128)S(1)} collective-permute-done((f32[129,128]{1,0:T(8,128)S(1)}, f32[129,128]{1,0:T(8,128)S(1)}, u32[]{:S(2)}, u32[]{:S(2)}) %collective-permute-start.4) | collective-permute-done | bytes 66080 | tf_op jit(solution)/shard_map/ppermute | solution.py:38
  26.2 2.5 %collective-permute-start.5 = (f32[129,128]{1,0:T(8,128)S(1)}, f32[129,128]{1,0:T(8,128)S(1)}, u32[]{:S(2)}, u32[]{:S(2)}) collective-permute-start(f32[129,128]{1,0:T(8,128)S(1)} %fusion.90), channel_id=1, source_target_pairs={{0,8},{4,12},{8,0},{12,4},{16,24},{20,28},{24,16},{28,20},{1,9},{5... | collective-permute-start | bytes 198152 | tf_op jit(solution)/shard_map/ppermute | solution.py:38
  28.7 2.7 %collective-permute-done.5 = f32[129,128]{1,0:T(8,128)S(1)} collective-permute-done((f32[129,128]{1,0:T(8,128)S(1)}, f32[129,128]{1,0:T(8,128)S(1)}, u32[]{:S(2)}, u32[]{:S(2)}) %collective-permute-start.5) | collective-permute-done | bytes 66080 | tf_op jit(solution)/shard_map/ppermute | solution.py:38
  31.4 0.9 %collective-permute-start.6 = (f32[129,128]{1,0:T(8,128)S(1)}, f32[129,128]{1,0:T(8,128)S(1)}, u32[]{:S(2)}, u32[]{:S(2)}) collective-permute-start(f32[129,128]{1,0:T(8,128)S(1)} %add.184), channel_id=1, source_target_pairs={{0,16},{4,20},{8,24},{12,28},{16,0},{20,4},{24,8},{28,12},{1,17},{... | collective-permute-start | bytes 198152 | tf_op jit(solution)/shard_map/ppermute | solution.py:38
  32.3 0.3 bitcast_reduce_fusion
  32.7 3.1 %collective-permute-done.6 = f32[129,128]{1,0:T(8,128)S(1)} collective-permute-done((f32[129,128]{1,0:T(8,128)S(1)}, f32[129,128]{1,0:T(8,128)S(1)}, u32[]{:S(2)}, u32[]{:S(2)}) %collective-permute-start.6) | collective-permute-done | bytes 66080 | tf_op jit(solution)/shard_map/ppermute | solution.py:38
  35.8 2.4 %collective-permute-start.7 = (f32[129,128]{1,0:T(8,128)S(1)}, f32[129,128]{1,0:T(8,128)S(1)}, u32[]{:S(2)}, u32[]{:S(2)}) collective-permute-start(f32[129,128]{1,0:T(8,128)S(1)} %add.185), channel_id=1, source_target_pairs={{0,1},{1,0},{2,3},{3,2},{4,5},{5,4},{6,7},{7,6},{8,9},{9,8},{10,11... | collective-permute-start | bytes 198152 | tf_op jit(solution)/shard_map/ppermute | solution.py:38
  38.2 2.3 %collective-permute-done.7 = f32[129,128]{1,0:T(8,128)S(1)} collective-permute-done((f32[129,128]{1,0:T(8,128)S(1)}, f32[129,128]{1,0:T(8,128)S(1)}, u32[]{:S(2)}, u32[]{:S(2)}) %collective-permute-start.7) | collective-permute-done | bytes 66080 | tf_op jit(solution)/shard_map/ppermute | solution.py:38
  40.5 3.1 %collective-permute-start.8 = (f32[129,128]{1,0:T(8,128)S(1)}, f32[129,128]{1,0:T(8,128)S(1)}, u32[]{:S(2)}, u32[]{:S(2)}) collective-permute-start(f32[129,128]{1,0:T(8,128)S(1)} %add.186), channel_id=1, source_target_pairs={{0,2},{1,3},{2,0},{3,1},{4,6},{5,7},{6,4},{7,5},{8,10},{9,11},{10,... | collective-permute-start | bytes 198152 | tf_op jit(solution)/shard_map/ppermute | solution.py:38
  43.6 2.3 %collective-permute-done.8 = f32[129,128]{1,0:T(8,128)S(1)} collective-permute-done((f32[129,128]{1,0:T(8,128)S(1)}, f32[129,128]{1,0:T(8,128)S(1)}, u32[]{:S(2)}, u32[]{:S(2)}) %collective-permute-start.8) | collective-permute-done | bytes 66080 | tf_op jit(solution)/shard_map/ppermute | solution.py:38
  45.8 0.6 %add.187.stacked_ref = f32[129,128]{1,0:T(8,128)} add(f32[129,128]{1,0:T(8,128)S(1)} %add.186, f32[129,128]{1,0:T(8,128)S(1)} %collective-permute-done.8) | non-fusion elementwise | flops 16512 | bytes 198144 | tf_op jit(solution)/shard_map/add | solution.py:17
  46.5 9.9 %shard_map.68 = f32[128,128]{1,0:T(8,128)} custom-call(f32[129,128]{1,0:T(8,128)} %add.187.stacked_ref), custom_call_target="tpu_custom_call" | custom-call | tf_op jit(solution)/shard_map/pallas_call | solution.py:98
  56.4 1.8 %fusion.1 = f32[128,16,128]{0,2,1:T(8,128)S(1)} fusion(f32[128,2,128]{2,0,1:T(8,128)S(1)} %broadcast_subtract_fusion.1, f32[128,12,128]{2,0,1:T(8,128)S(1)} %broadcast_subtract_fusion, f32[128,2,128]{2,0,1:T(8,128)S(1)} %broadcast_subtract_fusion.2, f32[16,128]{1,0:T(8,128)S(1)} %maximum_bitcast_fusion, f32[128,128]{1,0:T(8,128)} %shard_map.68), kind=kOutput, calls=%fused_computation.3 | convolution fusion | flops 403439616 | bytes 2170880 | tf_op jit(solution)/shard_map/dot_general | solution.py:251
  58.2 0.0 copy-start.1
  58.2 1.4 %copy.19 = f32[128,16,128]{2,1,0:T(8,128)} copy(f32[128,16,128]{0,2,1:T(8,128)S(1)} %fusion.1) | data formatting | bytes 2097152
  59.6 0.0 copy-done.1
  59.6 1.0 %fusion = f32[128,16,128]{0,2,1:T(8,128)S(1)} fusion(f32[128,16]{0,1:T(8,128)S(1)} %get-tuple-element.32, f32[16,128]{1,0:T(8,128)S(1)} %get-tuple-element.31, f32[128,128]{1,0:T(8,128)S(1)} %copy-done.1, f32[128,16,128]{0,2,1:T(8,128)S(1)} %copy.15), kind=kOutput, calls=%fused_computation.1 | convolution fusion | flops 403177472 | bytes 2179072 | tf_op jit(solution)/shard_map/dot_general | solution.py:254
  60.6 1.4 %copy.20 = f32[128,16,128]{2,1,0:T(8,128)} copy(f32[128,16,128]{0,2,1:T(8,128)S(1)} %fusion) | data formatting | bytes 2097152
  (31 shorter events, 0.4 us)
Async XLA Ops:
  0.6 1.7 %copy-start = (f32[128,16,128]{2,1,0:T(8,128)S(1)}, f32[128,16,128]{2,1,0:T(8,128)}, u32[]{:S(2)}) copy-start(f32[128,16,128]{2,1,0:T(8,128)} %param.5) | copy-start | bytes 3145732
  2.3 7.4 %copy-start.2 = (s32[1024]{0:T(1024)S(1)}, s32[1024]{0:T(1024)}, u32[]{:S(2)}) copy-start(s32[1024]{0:T(1024)} %param.9) | copy-start | bytes 12292
  2.4 7.5 %copy-start.3 = (f32[1024]{0:T(1024)S(1)}, f32[1024]{0:T(1024)}, u32[]{:S(2)}) copy-start(f32[1024]{0:T(1024)} %param.8) | copy-start | bytes 12292
  2.4 7.5 %copy-start.4 = (f32[1024]{0:T(1024)S(1)}, f32[1024]{0:T(1024)}, u32[]{:S(2)}) copy-start(f32[1024]{0:T(1024)} %param.7) | copy-start | bytes 12292
  2.9 7.5 %collective-permute-start.1 = (f32[3,16,128]{2,0,1:T(4,128)S(1)}, f32[3,16,128]{2,0,1:T(4,128)S(1)}, u32[]{:S(2)}, u32[]{:S(2)}) collective-permute-start(f32[3,16,128]{2,0,1:T(4,128)S(1)} %pad_maximum_fusion.19), channel_id=1, source_target_pairs={{1,0},{2,1},{3,2},{5,4},{6,5},{7,6},{9,8},{10,9},{11,10},{13,12},{... | collective-permute-start | bytes 73736 | tf_op jit(solution)/shard_map/ppermute | solution.py:134
  4.2 7.1 %collective-permute-start = (f32[3,16,128]{2,0,1:T(4,128)S(1)}, f32[3,16,128]{2,0,1:T(4,128)S(1)}, u32[]{:S(2)}, u32[]{:S(2)}) collective-permute-start(f32[3,16,128]{2,0,1:T(4,128)S(1)} %pad_maximum_fusion.18), channel_id=1, source_target_pairs={{0,1},{1,2},{2,3},{4,5},{5,6},{6,7},{8,9},{9,10},{10,11},{12,13},{... | collective-permute-start | bytes 73736 | tf_op jit(solution)/shard_map/ppermute | solution.py:134
  11.6 5.7 %collective-permute-start.2 = (f32[132,3,128]{2,0,1:T(8,128)S(1)}, f32[132,3,128]{2,0,1:T(8,128)S(1)}, u32[]{:S(2)}, u32[]{:S(2)}) collective-permute-start(f32[132,3,128]{2,0,1:T(8,128)S(1)} %get-tuple-element.43), channel_id=1, source_target_pairs={{0,4},{4,8},{8,12},{12,16},{16,20},{20,24},{24,28},{1,5},{5,9},{9,... | collective-permute-start | bytes 608264 | tf_op jit(solution)/shard_map/ppermute | solution.py:134
  12.9 5.5 %collective-permute-start.3 = (f32[132,3,128]{2,0,1:T(8,128)S(1)}, f32[132,3,128]{2,0,1:T(8,128)S(1)}, u32[]{:S(2)}, u32[]{:S(2)}) collective-permute-start(f32[132,3,128]{2,0,1:T(8,128)S(1)} %get-tuple-element.44), channel_id=1, source_target_pairs={{4,0},{8,4},{12,8},{16,12},{20,16},{24,20},{28,24},{5,1},{9,5},{13... | collective-permute-start | bytes 608264 | tf_op jit(solution)/shard_map/ppermute | solution.py:134
  21.0 5.2 %collective-permute-start.4 = (f32[129,128]{1,0:T(8,128)S(1)}, f32[129,128]{1,0:T(8,128)S(1)}, u32[]{:S(2)}, u32[]{:S(2)}) collective-permute-start(f32[129,128]{1,0:T(8,128)S(1)} %pad_maximum_fusion.17), channel_id=1, source_target_pairs={{0,4},{4,0},{8,12},{12,8},{16,20},{20,16},{24,28},{28,24},{1,5},{5... | collective-permute-start | bytes 198152 | tf_op jit(solution)/shard_map/ppermute | solution.py:38
  26.2 5.2 %collective-permute-start.5 = (f32[129,128]{1,0:T(8,128)S(1)}, f32[129,128]{1,0:T(8,128)S(1)}, u32[]{:S(2)}, u32[]{:S(2)}) collective-permute-start(f32[129,128]{1,0:T(8,128)S(1)} %fusion.90), channel_id=1, source_target_pairs={{0,8},{4,12},{8,0},{12,4},{16,24},{20,28},{24,16},{28,20},{1,9},{5... | collective-permute-start | bytes 198152 | tf_op jit(solution)/shard_map/ppermute | solution.py:38
  31.4 4.4 %collective-permute-start.6 = (f32[129,128]{1,0:T(8,128)S(1)}, f32[129,128]{1,0:T(8,128)S(1)}, u32[]{:S(2)}, u32[]{:S(2)}) collective-permute-start(f32[129,128]{1,0:T(8,128)S(1)} %add.184), channel_id=1, source_target_pairs={{0,16},{4,20},{8,24},{12,28},{16,0},{20,4},{24,8},{28,12},{1,17},{... | collective-permute-start | bytes 198152 | tf_op jit(solution)/shard_map/ppermute | solution.py:38
  35.8 4.7 %collective-permute-start.7 = (f32[129,128]{1,0:T(8,128)S(1)}, f32[129,128]{1,0:T(8,128)S(1)}, u32[]{:S(2)}, u32[]{:S(2)}) collective-permute-start(f32[129,128]{1,0:T(8,128)S(1)} %add.185), channel_id=1, source_target_pairs={{0,1},{1,0},{2,3},{3,2},{4,5},{5,4},{6,7},{7,6},{8,9},{9,8},{10,11... | collective-permute-start | bytes 198152 | tf_op jit(solution)/shard_map/ppermute | solution.py:38
  40.5 5.4 %collective-permute-start.8 = (f32[129,128]{1,0:T(8,128)S(1)}, f32[129,128]{1,0:T(8,128)S(1)}, u32[]{:S(2)}, u32[]{:S(2)}) collective-permute-start(f32[129,128]{1,0:T(8,128)S(1)} %add.186), channel_id=1, source_target_pairs={{0,2},{1,3},{2,0},{3,1},{4,6},{5,7},{6,4},{7,5},{8,10},{9,11},{10,... | collective-permute-start | bytes 198152 | tf_op jit(solution)/shard_map/ppermute | solution.py:38
  58.2 1.4 %copy-start.1 = (f32[128,128]{1,0:T(8,128)S(1)}, f32[128,128]{1,0:T(8,128)}, u32[]{:S(2)}) copy-start(f32[128,128]{1,0:T(8,128)} %shard_map.68) | copy-start | bytes 196612
